TPU v7x, 512 devices: a whole 4x8x8 slice. The times are simulated.
512 devices in a mesh: seq: 32 (over x, y), head: 8 (over z_hi, core), var: 2 (over z_lo).
Axes of the slice: x: 4, y: 8, z: 8 (z_hi: 4, z_lo: 2; z = z_hi * 2 + z_lo), core: 2. Of those that a mesh axis runs over, the one named last changes fastest.
Arguments:
- inner: bfloat16 [2048, 4096], P('seq', 'head'), may hold values from -4.5 to 4.5
- residual_in: bfloat16 [2048, 4096], P('seq', 'head'), may hold values from -6 to 6
- erase: int32 [2, 2048], P('var', 'seq'), parts along dimension 0, may hold values from 0 to 1, as said below
- conv_weight: float32 [4, 4096], P(None, 'head'), may hold values from -3 to 3
- qkv_weight: bfloat16 [8, 512, 1536], P('head'), may hold values from -0.25 to 0.25
- gate_weight: bfloat16 [8, 2, 512], P('head'), may hold values from -0.4075734 to 0.4075734, as said below
- gate_bias: float32 [8, 2], P('head'), as said below
- norm_gain: float32 [4096], P('head'), may hold values from 0.5 to 1.5
- down_weight: bfloat16 [4096, 4096], P('head', 'seq'), may hold values from -0.09375 to 0.09375
Outputs:
- mixed: bfloat16 [2, 2048, 4096], P('var', 'seq', 'head'), parts along dimension 0
There are 2 independent parts, one for each index of `var`. A program takes and returns all parts, laid end to end along the dimension named above; an argument that names none is the same for every part. Nothing has to cross between parts.
Inputs may be any that keep to these rules, and one draw needn't show every extreme that they name: `erase`: each variant erases a few runs of consecutive tokens. `gate_weight`: row 0 of each head holds the input gate projection and row 1 the forget gate projection. `gate_bias`: column 0 is the input gate bias and column 1 the forget gate bias of each head.
All inputs are finite; a program needn't handle non-finite values.
Results may differ from a plain program's by a relative error of at most 0.014.
Values may be sent and summed in bfloat16 or wider, within the bound.
No kernel may reach another device: no remote copies, remote signals or barrier semaphores. Data moves between devices by JAX's collectives and lax.ppermute only.
A program may use at most 128 MiB of HBM per device.

v0:
```python
import jax
import jax.numpy as jnp
from jax import lax
from jax.sharding import Mesh
from jax.sharding import PartitionSpec as P

CONV = 4
SEQ = ("seq_0", "seq_1")


def neutral_like(x, identity):
    return jax.tree.map(
        lambda part, zero: jnp.zeros_like(part) + jnp.asarray(zero, part.dtype), x, identity
    )


def entering(x, axes, combine, identity):
    before = start = neutral_like(x, identity)
    subtotal = x
    for axis in reversed(axes):
        size, index = (lax.axis_size(axis), lax.axis_index(axis))
        pieces = jax.tree.map(lambda part: lax.all_gather(part, axis), subtotal)
        inside, subtotal = (start, start)
        for k in range(size):
            passed = k < index
            subtotal = combine(subtotal, jax.tree.map(lambda part: part[k], pieces))
            inside = jax.tree.map(lambda new, old: jnp.where(passed, new, old), subtotal, inside)
        before = combine(inside, before)
    return before


def laid_out(blocks, dim):
    blocks = jnp.moveaxis(blocks, 0, dim)
    lengths = blocks.shape
    return blocks.reshape(*lengths[:dim], lengths[dim] * lengths[dim + 1], *lengths[dim + 2 :])


def gather_in_order(x, axes, sequence):
    blocks = x[None]
    for k in sequence:
        blocks = lax.all_gather(blocks, axes[k], axis=0, tiled=True)
    current = [lax.axis_size(axes[k]) for k in reversed(sequence)]
    blocks = blocks.reshape(*current, *x.shape)
    turned = sorted(range(len(sequence)), key=lambda place: sequence[len(sequence) - 1 - place])
    return blocks.transpose(*turned, *range(len(sequence), blocks.ndim)).reshape(-1, *x.shape)


def gather_axes(x, axes, sequence, dim):
    return laid_out(gather_in_order(x, axes, sequence), dim)


def from_behind(value, axis, steps):
    count = lax.axis_size(axis)
    initial, last = (max(0, -steps), min(count, count - steps))
    return lax.ppermute(value, axis, [(source, source + steps) for source in range(initial, last)])


def split_up(x, dim, size):
    lengths = x.shape
    blocks = x.reshape(*lengths[:dim], size, lengths[dim] // size, *lengths[dim + 1 :])
    return jnp.moveaxis(blocks, dim, 0)


def sent_and_summed(x, axis, dim):
    blocks = split_up(x, dim, lax.axis_size(axis))
    arrived = lax.all_to_all(blocks, axis, split_axis=0, concat_axis=0, tiled=True)
    return arrived.astype(jnp.float32).sum(axis=0)


def combine_states(earlier, later):
    return (earlier[0] + later[0], jnp.exp(later[0])[:, None, None] * earlier[1] + later[1])


def entering_state(block_decay, own_memory):
    identity = (jnp.zeros_like(block_decay), jnp.zeros_like(own_memory))
    return entering((block_decay, own_memory), SEQ, combine_states, identity)


def local_terms(queries, key_rows, values, cumulated, input_log):
    token_count = queries.shape[1]
    causal = jnp.arange(token_count)[:, None] >= jnp.arange(token_count)[None, :]
    scores = jnp.einsum("vtd,vsd->vts", queries, key_rows, preferred_element_type=jnp.float32)
    exponent = cumulated[:, :, None] - cumulated[:, None, :] + input_log[:, None, :]
    weights = (scores * jnp.exp(jnp.where(causal, exponent, -jnp.inf))).astype(jnp.bfloat16)
    return jnp.einsum("vts,vse->vte", weights, values, preferred_element_type=jnp.float32)


def body(
    inner,
    residual_in,
    erase,
    conv_weight,
    qkv_weight,
    gate_weight,
    gate_bias,
    norm_gain,
    down_weight,
):
    columns_all = gather_axes(down_weight, SEQ, (0, 1), 1)
    kept_mask = (1 - erase).astype(jnp.bfloat16)
    erased = inner[None, :, :] * kept_mask[:, :, None]
    row_count = inner.shape[0]
    last_rows = erased[:, row_count - (CONV - 1) :, :]
    prior_rows = from_behind(last_rows, SEQ, 1)
    window = jnp.concatenate([prior_rows, erased], axis=1).astype(jnp.float32)
    convolved = jnp.zeros(erased.shape, jnp.float32)
    for offset in range(CONV):
        convolved = (
            convolved
            + conv_weight[offset] * window[:, CONV - 1 - offset : CONV - 1 - offset + row_count]
        )
    activated = jax.nn.silu(convolved).astype(jnp.bfloat16)
    proj_head = qkv_weight[0]
    head_size = proj_head.shape[0]
    query_key = jnp.einsum(
        "vtd,de->vte", activated, proj_head[:, : 2 * head_size], preferred_element_type=jnp.float32
    )
    queries = query_key[..., :head_size].astype(jnp.bfloat16)
    key_rows = (query_key[..., head_size:] * head_size ** (-0.5)).astype(jnp.bfloat16)
    values = jnp.einsum(
        "vtd,de->vte", erased, proj_head[:, 2 * head_size :], preferred_element_type=jnp.float32
    ).astype(jnp.bfloat16)
    gate_pre = (
        jnp.einsum("vtd,gd->vtg", activated, gate_weight[0], preferred_element_type=jnp.float32)
        + gate_bias[0]
    )
    input_log = 15.0 * jnp.tanh(gate_pre[..., 0] / 15.0)
    forget_log = jax.nn.log_sigmoid(gate_pre[..., 1])
    cumulated = jnp.cumsum(forget_log, axis=1)
    block_decay = cumulated[:, -1]
    key_scale = jnp.exp(block_decay[:, None] - cumulated + input_log)
    scaled_keys = (key_scale[..., None] * key_rows.astype(jnp.float32)).astype(jnp.bfloat16)
    own_memory = jnp.einsum("vsd,vse->vde", scaled_keys, values, preferred_element_type=jnp.float32)
    prior_decay, memory = entering_state(block_decay, own_memory)
    intra_part = local_terms(queries, key_rows, values, cumulated, input_log)
    memory_rounded = memory.astype(jnp.bfloat16)
    carry_part = jnp.einsum(
        "vtd,vde->vte", queries, memory_rounded, preferred_element_type=jnp.float32
    )
    numerator = jnp.exp(cumulated)[..., None] * carry_part + intra_part
    row_mean = jnp.mean(numerator, axis=-1, keepdims=True)
    centred = numerator - row_mean
    row_var = jnp.mean(centred * centred, axis=-1, keepdims=True)
    normed = (centred * lax.rsqrt(row_var + 1e-05) * norm_gain).astype(jnp.bfloat16)
    head_terms = (
        jnp.einsum("vtd,dc->vtc", normed, columns_all, preferred_element_type=jnp.float32)
        .astype(jnp.bfloat16)
        .astype(jnp.float32)
    )
    summed = sent_and_summed(head_terms.astype(jnp.bfloat16), "head", 2)
    return (residual_in[None, :, :].astype(jnp.float32) + summed).astype(jnp.bfloat16)


def solution(mesh):
    split = Mesh(
        mesh.devices.reshape(4, 8, mesh.shape["head"], mesh.shape["var"]),
        ("seq_0", "seq_1", "head", "var"),
    )
    placed = (
        P(SEQ, "head"),
        P(SEQ, "head"),
        P("var", SEQ),
        P(None, "head"),
        P("head", None, None),
        P("head", None, None),
        P("head", None),
        P("head"),
        P("head", SEQ),
    )
    return jax.shard_map(
        body, mesh=split, in_specs=placed, out_specs=P("var", SEQ, "head"), check_vma=False
    )
```

profile of v0, /device:TPU:1, one launch (start us, length us, event | category | flops | bytes accessed | tf_op | source)
XLA Modules:
  0.0 273.9 jit_solution(2478660386260614011)
XLA Ops:
  6.5 0.7 convert_bitcast_fusion
  7.2 0.9 multiply_bitcast_fusion
  8.2 4.0 %collective-permute-start = (bf16[1,3,512]{2,1,0:T(4,128)(2,1)S(1)}, bf16[1,3,512]{2,1,0:T(4,128)(2,1)S(1)}, u32[]{:S(2)}, u32[]{:S(2)}) collective-permute-start(bf16[1,3,512]{2,1,0:T(4,128)(2,1)S(1)} %slice.181), channel_id=1, source_target_pairs={{0,16},{16,32},{32,48},{48,64},{64,80},{80,96},{96,112},{112,128},... | collective-permute-start | bytes 9224 | tf_op jit(solution)/shard_map/ppermute | solution.py:55
  12.2 1.3 convolution_convert_fusion.1
  13.5 0.9 fusion.70
  14.4 0.0 collective-permute-done
  14.4 0.1 multiply_convert_fusion.2
  14.5 1.5 convolution_bitcast_fusion
  16.1 0.0 copy-done
  16.1 0.7 fusion.3
  16.8 0.1 fusion.56
  16.9 0.2 reduce_window_sum.13
  17.1 0.6 slice.133
  17.7 0.7 fusion.58
  18.4 1.4 fusion.27
  19.8 0.0 all-gather.11.cloned.1.call-update
  19.8 0.0 all-gather.9.cloned.1.call-start
  19.9 13.1 %all-gather.2 = bf16[2048,128]{1,0:T(8,128)(2,1)} all-gather(bf16[512,128]{1,0:T(8,128)(2,1)S(1)} %copy-done.3), channel_id=4, replica_groups=mesh['seq_0'=4,'seq_1'=8,'head'=8,'var'=2] {'seq_0'}, dimensions={0}, use_global_device_ids=true | all-gather | bytes 655360 | tf_op jit(solution)/shard_map/all_gather | solution.py:41
  33.0 0.0 all-gather.9.cloned.1.call-update
  33.0 0.0 all-gather.7.cloned.1.call-start
  33.0 1.3 dynamic-slice
  34.4 1.3 bitcast_dynamic-update-slice_fusion
  35.7 13.9 %all-reduce = f32[8]{0:T(128)S(1)} all-reduce(f32[8]{0:T(128)S(1)} %bitcast_dynamic-update-slice_fusion), channel_id=1, replica_groups=mesh['seq_0'=4,'seq_1'=8,'head'=8,'var'=2] {'seq_1'}, use_global_device_ids=true, to_apply=%add | all-reduce | flops 8 | bytes 64
  49.6 0.7 slice_add_fusion.10
  50.3 1.3 slice_add_fusion.9
  56.8 65.6 %all-gather.11.cloned.1.call-done = f32[4096,512]{1,0:T(8,128)} async-done(((f32[512,512]{1,0:T(8,128)}), f32[4096,512]{1,0:T(8,128)}) %all-gather.11.cloned.1.call-update) | async-done | bytes 8388624 | tf_op jit(solution)/shard_map/all_gather | solution.py:22
  122.4 5.4 %fusion.8 = (f32[1,1,512,512]{3,2,1,0:T(8,128)}, f32[1,1,512,512]{3,2,1,0:T(8,128)S(1)}) fusion(f32[4096,512]{1,0:T(8,128)} %all-gather.11.cloned.1.call-done, f32[]{:T(128)} %bitcast.32, f32[]{:T(128)} %bitcast.31, f32[]{:T(128)} %bitcast.38, f32[]{:T(128)} %bitcast.37, f32[]{:T(128)} %bitcast.36, f32[]{:T(128)} %bitcast.35, f32[]{:T(128)} %bitcast.34, ...), kind=kLoop, calls=%fused_computation.19 | loop fusion | flops 3932160 | bytes 10485792 | tf_op jit(solution)/shard_map/add | solution.py:71
  127.8 0.0 all-gather.7.cloned.1.call-update
  127.9 1.3 dynamic-slice.1
  129.2 1.3 dynamic-update-slice.1
  130.5 8.4 %all-reduce.1 = f32[4]{0:T(128)S(1)} all-reduce(f32[4]{0:T(128)S(1)} %dynamic-update-slice.1), channel_id=2, replica_groups=mesh['seq_0'=4,'seq_1'=8,'head'=8,'var'=2] {'seq_0'}, use_global_device_ids=true, to_apply=%add.1 | all-reduce | flops 4 | bytes 32
  143.9 0.7 fusion.71
  147.2 0.3 fusion.2
  147.5 33.2 %all-gather.9.cloned.1.call-done = bf16[32,512,128]{2,1,0:T(8,128)(2,1)} async-done(((bf16[4,512,128]{2,1,0:T(8,128)(2,1)}), bf16[32,512,128]{2,1,0:T(8,128)(2,1)}) %all-gather.9.cloned.1.call-update) | async-done | bytes 4194320 | tf_op jit(solution)/shard_map/all_gather | solution.py:41
  180.7 4.6 %copy.13 = bf16[4,8,512,128]{3,2,1,0:T(8,128)(2,1)} copy(bf16[4,8,512,128]{3,2,0,1:T(8,128)(2,1)} %bitcast.179) | data formatting | bytes 8388608 | tf_op jit(solution)/shard_map/transpose | solution.py:45
  185.3 6.6 %copy.14 = bf16[512,32,128]{0,2,1:T(8,128)(2,1)} copy(bf16[512,32,128]{2,0,1:T(8,128)(2,1)} %bitcast.178) | data formatting | bytes 8388608 | tf_op jit(solution)/shard_map/transpose | solution.py:33
  191.8 43.6 %all-gather.7.cloned.1.call-done = f32[4,1,512,512]{3,2,1,0:T(8,128)} async-done(((f32[1,1,512,512]{3,2,1,0:T(8,128)}), f32[4,1,512,512]{3,2,1,0:T(8,128)}) %all-gather.7.cloned.1.call-update) | async-done | bytes 4194320 | tf_op jit(solution)/shard_map/all_gather | solution.py:22
  235.4 5.6 %fusion.72 = (f32[64]{0:T(128)S(1)}, f32[64,512]{1,0:T(8,128)S(1)}) fusion(f32[64,512]{1,0:T(8,128)S(1)} %fusion.2, f32[1,1,512,512]{3,2,1,0:T(8,128)S(1)} %copy-done.2, f32[1,1,512,512]{3,2,1,0:T(8,128)S(1)} %get-tuple-element.6, f32[4096,512]{1,0:T(8,128)} %all-gather.11.cloned.1.call-done, f32[]{:T(128)} %bitcast.38, pred[]{:T(512)} %gt.43, pred[]{:T(512)} %gt.42, ...), kind=kOutput, calls=%fused_computation.112 | convolution fusion | flops 42303424 | bytes 12921092 | tf_op jit(solution)/shard_map/vtd,vde->vte/dot_general | solution.py:137
  241.0 0.2 multiply_reduce_fusion
  241.2 0.0 copy-done.1
  241.2 0.0 copy-done.5
  241.3 0.0 copy-start.4
  241.3 1.4 convolution_convert_fusion
  242.7 0.2 copy.16
  242.8 0.2 copy.18
  243.0 23.6 %all_to_all.5 = bf16[8,1,64,512]{3,2,1,0:T(8,128)(2,1)S(1)} all-to-all(bf16[8,1,64,512]{3,2,1,0:T(8,128)(2,1)S(1)} %bitcast.183), channel_id=1, replica_groups=mesh['seq_0'=4,'seq_1'=8,'head'=8,'var'=2] {'head'}, dimensions={0} | all-to-all | bytes 1048576 | tf_op jit(solution)/shard_map/all_to_all | solution.py:66
  266.6 0.1 convert_reduce_fusion
  266.7 0.6 fusion.29
  (16 shorter events, 0.1 us)
Async XLA Ops:
  6.5 9.5 %copy-start = (bf16[1,2,512]{2,1,0:T(2,128)(2,1)S(1)}, bf16[1,2,512]{2,1,0:T(2,128)(2,1)}, u32[]{:S(2)}) copy-start(bf16[1,2,512]{2,1,0:T(2,128)(2,1)} %param.14) | copy-start | bytes 6148
  6.5 13.3 %copy-start.3 = (bf16[512,128]{1,0:T(8,128)(2,1)S(1)}, bf16[512,128]{1,0:T(8,128)(2,1)}, u32[]{:S(2)}) copy-start(bf16[512,128]{1,0:T(8,128)(2,1)} %param.17) | copy-start | bytes 393220
  6.5 115.9 %all-gather.11.cloned.1.call-start = ((), (), s32[]{:S(2)}) async-start(), calls=%async_computation.3 | async-start | bytes 9437184 | tf_op jit(solution)/shard_map/all_gather | solution.py:22
  8.2 6.2 %collective-permute-start = (bf16[1,3,512]{2,1,0:T(4,128)(2,1)S(1)}, bf16[1,3,512]{2,1,0:T(4,128)(2,1)S(1)}, u32[]{:S(2)}, u32[]{:S(2)}) collective-permute-start(bf16[1,3,512]{2,1,0:T(4,128)(2,1)S(1)} %slice.181), channel_id=1, source_target_pairs={{0,16},{16,32},{32,48},{48,64},{64,80},{80,96},{96,112},{112,128},... | collective-permute-start | bytes 9224 | tf_op jit(solution)/shard_map/ppermute | solution.py:55
  19.8 160.9 %all-gather.9.cloned.1.call-start = ((), (), s32[]{:S(2)}) async-start(), calls=%async_computation.2 | async-start | bytes 4718592 | tf_op jit(solution)/shard_map/all_gather | solution.py:41
  33.0 202.4 %all-gather.7.cloned.1.call-start = ((), (), s32[]{:S(2)}) async-start(), calls=%async_computation.1 | async-start | bytes 5242880 | tf_op jit(solution)/shard_map/all_gather | solution.py:22
  185.3 50.1 %copy-start.2 = (f32[1,1,512,512]{3,2,1,0:T(8,128)S(1)}, f32[1,1,512,512]{3,2,1,0:T(8,128)}, u32[]{:S(2)}) copy-start(f32[1,1,512,512]{3,2,1,0:T(8,128)} %get-tuple-element.5) | copy-start | bytes 3145732
  235.4 5.8 %copy-start.1 = (bf16[512,32,128]{0,2,1:T(8,128)(2,1)S(1)}, bf16[512,32,128]{0,2,1:T(8,128)(2,1)}, u32[]{:S(2)}) copy-start(bf16[512,32,128]{0,2,1:T(8,128)(2,1)} %copy.14) | copy-start | bytes 12582916
  235.4 5.8 %copy-start.5 = (f32[512]{0:T(512)S(1)}, f32[512]{0:T(512)}, u32[]{:S(2)}) copy-start(f32[512]{0:T(512)} %param.16) | copy-start | bytes 6148
  241.3 25.5 %copy-start.4 = (bf16[64,512]{1,0:T(8,128)(2,1)S(1)}, bf16[64,512]{1,0:T(8,128)(2,1)}, u32[]{:S(2)}) copy-start(bf16[64,512]{1,0:T(8,128)(2,1)} %param.10) | copy-start | bytes 196612
Sparse Core Ops, SparseCore 0:
  19.9 102.4 all-gather.10
  124.5 56.1 all-gather.8
  182.8 52.5 all-gather.6
where the time goes:
time: 275 us; the launch traced here: 274 us
  waiting for transfers between devices  142 us (52%)
  blocking collectives  59 us (21%)
  between operations  26.2 us (10%)
  local copies, waits for them, and re-layouts  18.9 us (7%)
  matrix products  12.3 us (4%)
  other arithmetic  11 us (4%)
  starting transfers between devices  4.1 us (1%)
    all_gather x2, waiting for transfers between devices, entering(): pieces = jax.tree.map(lambda part: lax.all_gather(part, axis), subtotal)  109 us
    all_gather x1, waiting for transfers between devices, gather_in_order(): blocks = lax.all_gather(blocks, axes[k], axis=0, tiled=True)  33.2 us
    all_to_all x1, blocking collectives, sent_and_summed(): lax.all_to_all(blocks, axis, split_axis=0, concat_axis=0, tiled=True)  23.6 us
    unnamed x2, blocking collectives  22.3 us
    all_gather x1, blocking collectives, gather_in_order(): blocks = lax.all_gather(blocks, axes[k], axis=0, tiled=True)  13.1 us
    transpose x1, local copies, waits for them, and re-layouts, laid_out(): blocks = jnp.moveaxis(blocks, 0, dim)  6.56 us
    dot_general x1, matrix products, body(): jnp.einsum('vtd,vde->vte', queries, memory_rounded, preferred_element_typ...  5.62 us
  transfers between devices with their start and end apart: 4, of which 3 were waited for; matrix products, arithmetic and copies ran while one was open for 10% of the time, Pallas kernels for 0%

commit v1 on v0

v1 whole, which is shorter than its diff:
```python
import jax
import jax.numpy as jnp
from jax import lax
from jax.sharding import Mesh
from jax.sharding import PartitionSpec as P

CONV = 4
SEQ = ("seq_0", "seq_1")
EXTRA = 16


def from_behind(value, axis, steps):
    count = lax.axis_size(axis)
    initial, last = (max(0, -steps), min(count, count - steps))
    return lax.ppermute(value, axis, [(source, source + steps) for source in range(initial, last)])


def split_up(x, dim, size):
    lengths = x.shape
    blocks = x.reshape(*lengths[:dim], size, lengths[dim] // size, *lengths[dim + 1 :])
    return jnp.moveaxis(blocks, dim, 0)


def sent_and_summed(x, axis, dim):
    blocks = split_up(x, dim, lax.axis_size(axis))
    arrived = lax.all_to_all(blocks, axis, split_axis=0, concat_axis=0, tiled=True)
    return arrived.astype(jnp.float32).sum(axis=0)


def three_parts(x):
    hi = lax.reduce_precision(x, exponent_bits=8, mantissa_bits=7)
    rest = x - hi
    mid = lax.reduce_precision(rest, exponent_bits=8, mantissa_bits=7)
    lo = rest - mid
    return jnp.stack([hi, mid, lo], axis=-1).astype(jnp.bfloat16)


def local_terms(queries, key_rows, values, cumulated, input_log):
    token_count = queries.shape[1]
    causal = jnp.arange(token_count)[:, None] >= jnp.arange(token_count)[None, :]
    scores = jnp.einsum("vtd,vsd->vts", queries, key_rows, preferred_element_type=jnp.float32)
    exponent = cumulated[:, :, None] - cumulated[:, None, :] + input_log[:, None, :]
    weights = (scores * jnp.exp(jnp.where(causal, exponent, -jnp.inf))).astype(jnp.bfloat16)
    return jnp.einsum("vts,vse->vte", weights, values, preferred_element_type=jnp.float32)


def carried_terms(queries, cumulated, gathered, block):
    blocks, rows, head_size = gathered.shape
    token_count = queries.shape[1]
    keys_all = gathered[:, :token_count, :].reshape(blocks * token_count, head_size)
    values_all = gathered[:, token_count : 2 * token_count, :].reshape(blocks * token_count, head_size)
    parts = gathered[:, 2 * token_count, :3].astype(jnp.float32)
    decay = (parts[:, 0] + parts[:, 1]) + parts[:, 2]
    through = jnp.cumsum(decay)
    before_own = jnp.sum(jnp.where(jnp.arange(blocks) < block, decay, 0.0))
    earlier = jnp.arange(blocks) < block
    block_exponent = jnp.where(earlier, before_own - through, -jnp.inf)
    exponent = cumulated[:, :, None, None] + block_exponent[None, None, :, None]
    scale = jnp.exp(jnp.broadcast_to(exponent, (*cumulated.shape, blocks, token_count)))
    scale = scale.reshape(*cumulated.shape, blocks * token_count)
    scores = jnp.einsum("vtd,sd->vts", queries, keys_all, preferred_element_type=jnp.float32)
    weights = scores * scale
    high = weights.astype(jnp.bfloat16)
    low = (weights - high.astype(jnp.float32)).astype(jnp.bfloat16)
    return jnp.einsum("vts,se->vte", high, values_all, preferred_element_type=jnp.float32) + jnp.einsum(
        "vts,se->vte", low, values_all, preferred_element_type=jnp.float32
    )


def body(
    inner,
    residual_in,
    erase,
    conv_weight,
    qkv_weight,
    gate_weight,
    gate_bias,
    norm_gain,
    down_weight,
):
    columns_all = lax.all_gather(down_weight, SEQ, axis=0, tiled=False)
    kept_mask = (1 - erase).astype(jnp.bfloat16)
    erased = inner[None, :, :] * kept_mask[:, :, None]
    row_count = inner.shape[0]
    last_rows = erased[:, row_count - (CONV - 1) :, :]
    prior_rows = from_behind(last_rows, SEQ, 1)
    window = jnp.concatenate([prior_rows, erased], axis=1).astype(jnp.float32)
    convolved = jnp.zeros(erased.shape, jnp.float32)
    for offset in range(CONV):
        convolved = (
            convolved
            + conv_weight[offset] * window[:, CONV - 1 - offset : CONV - 1 - offset + row_count]
        )
    activated = jax.nn.silu(convolved).astype(jnp.bfloat16)
    proj_head = qkv_weight[0]
    head_size = proj_head.shape[0]
    query_key = jnp.einsum(
        "vtd,de->vte", activated, proj_head[:, : 2 * head_size], preferred_element_type=jnp.float32
    )
    queries = query_key[..., :head_size].astype(jnp.bfloat16)
    key_rows = (query_key[..., head_size:] * head_size ** (-0.5)).astype(jnp.bfloat16)
    values = jnp.einsum(
        "vtd,de->vte", erased, proj_head[:, 2 * head_size :], preferred_element_type=jnp.float32
    ).astype(jnp.bfloat16)
    gate_pre = (
        jnp.einsum("vtd,gd->vtg", activated, gate_weight[0], preferred_element_type=jnp.float32)
        + gate_bias[0]
    )
    input_log = 15.0 * jnp.tanh(gate_pre[..., 0] / 15.0)
    forget_log = jax.nn.log_sigmoid(gate_pre[..., 1])
    cumulated = jnp.cumsum(forget_log, axis=1)
    block_decay = cumulated[:, -1]
    key_scale = jnp.exp(block_decay[:, None] - cumulated + input_log)
    scaled_keys = (key_scale[..., None] * key_rows.astype(jnp.float32)).astype(jnp.bfloat16)
    extra = jnp.zeros((EXTRA, head_size), jnp.bfloat16)
    extra = extra.at[0, :3].set(three_parts(block_decay[0]))
    packed = jnp.concatenate([scaled_keys[0], values[0], extra], axis=0)
    gathered = lax.all_gather(packed, SEQ, axis=0, tiled=False)
    block = lax.axis_index(SEQ)
    intra_part = local_terms(queries, key_rows, values, cumulated, input_log)
    numerator = carried_terms(queries, cumulated, gathered, block) + intra_part
    row_mean = jnp.mean(numerator, axis=-1, keepdims=True)
    centred = numerator - row_mean
    row_var = jnp.mean(centred * centred, axis=-1, keepdims=True)
    normed = (centred * lax.rsqrt(row_var + 1e-05) * norm_gain).astype(jnp.bfloat16)
    head_terms = jnp.einsum(
        "vtd,kdc->vtkc", normed, columns_all, preferred_element_type=jnp.float32
    ).astype(jnp.bfloat16)
    head_terms = head_terms.reshape(*normed.shape[:2], -1)
    summed = sent_and_summed(head_terms, "head", 2)
    return (residual_in[None, :, :].astype(jnp.float32) + summed).astype(jnp.bfloat16)


def solution(mesh):
    split = Mesh(
        mesh.devices.reshape(4, 8, mesh.shape["head"], mesh.shape["var"]),
        ("seq_0", "seq_1", "head", "var"),
    )
    placed = (
        P(SEQ, "head"),
        P(SEQ, "head"),
        P("var", SEQ),
        P(None, "head"),
        P("head", None, None),
        P("head", None, None),
        P("head", None),
        P("head"),
        P("head", SEQ),
    )
    return jax.shard_map(
        body, mesh=split, in_specs=placed, out_specs=P("var", SEQ, "head"), check_vma=False
    )
```

time: 275 us -> 242 us (0.88)
  blocking collectives: 59 us -> 27 us
  waiting for transfers between devices: 142 us -> 170 us
  local copies, waits for them, and re-layouts: 18.9 us -> 6.52 us
  between operations: 26.2 us -> 18.7 us
  other arithmetic: 11 us -> 5.93 us
  matrix products: 12.3 us -> 8.76 us
    all_gather x3 -> x2, waiting for transfers between devices: 142 us -> 170 us  [the longest x1 89.9 us: body(): gathered = lax.all_gather(packed, SEQ, axis=0, tiled=False)]
    unnamed x2 -> x0, blocking collectives: 22.3 us -> none
    all_gather x1 -> x0, blocking collectives: 13.1 us -> none  [gather_in_order(): blocks = lax.all_gather(blocks, axes[k], axis=0, tiled=True)]
    transpose x2 -> x1, local copies, waits for them, and re-layouts: 11.1 us -> 0.16 us  [split_up(): return jnp.moveaxis(blocks, dim, 0)]
    add x3 -> x0, other arithmetic: 7.4 us -> none  [the longest x1 5.42 us: combine_states(): jnp.exp(later[0])[:, None, None] * earlier[1] + later[1]]
    unnamed x19 -> x7, local copies, waits for them, and re-layouts: 5.48 us -> 0.11 us
    dot_general x3 -> x4, matrix products: 8.43 us -> 4.89 us  [the longest x1 3.08 us: body(): jnp.einsum('vtd,kdc->vtkc', normed, columns_all, preferred_element_type=j...]
    all_to_all x1, blocking collectives: 23.6 us -> 27 us  [sent_and_summed(): lax.all_to_all(blocks, axis, split_axis=0, concat_axis=0, tiled=True)]
  transfers between devices with their start and end apart: 4 -> 3, of which waited for: 3 -> 2; matrix products, arithmetic and copies ran while one was open for 10% -> 4% of each run, Pallas kernels for 0% -> 0%
where the time goes in v1:
time: 242 us; the launch traced here: 241 us
  waiting for transfers between devices  170 us (70%)
  blocking collectives  27 us (11%)
  between operations  18.7 us (8%)
  matrix products  8.76 us (4%)
  local copies, waits for them, and re-layouts  6.52 us (3%)
  other arithmetic  5.93 us (2%)
  starting transfers between devices  4.06 us (2%)
    all_gather x1, waiting for transfers between devices, body(): gathered = lax.all_gather(packed, SEQ, axis=0, tiled=False)  89.9 us
    all_gather x1, waiting for transfers between devices, body(): columns_all = lax.all_gather(down_weight, SEQ, axis=0, tiled=False)  79.7 us
    all_to_all x1, blocking collectives, sent_and_summed(): lax.all_to_all(blocks, axis, split_axis=0, concat_axis=0, tiled=True)  27 us
  transfers between devices with their start and end apart: 3, of which 2 were waited for; matrix products, arithmetic and copies ran while one was open for 4% of the time, Pallas kernels for 0%

profile of v1, /device:TPU:1, one launch (start us, length us, event | category | flops | bytes accessed | tf_op | source)
XLA Modules:
  0.0 241.3 jit_solution(9596504596717116625)
XLA Ops:
  6.5 0.0 copy-start
  6.5 0.7 convert_bitcast_fusion
  7.2 0.9 multiply_bitcast_fusion
  8.1 4.0 %collective-permute-start = (bf16[1,3,512]{2,1,0:T(4,128)(2,1)S(1)}, bf16[1,3,512]{2,1,0:T(4,128)(2,1)S(1)}, u32[]{:S(2)}, u32[]{:S(2)}) collective-permute-start(bf16[1,3,512]{2,1,0:T(4,128)(2,1)S(1)} %slice.105), channel_id=1, source_target_pairs={{0,16},{16,32},{32,48},{48,64},{64,80},{80,96},{96,112},{112,128},... | collective-permute-start | bytes 9224 | tf_op jit(solution)/shard_map/ppermute | solution.py:15
  12.2 1.3 convolution_convert_fusion.1
  13.5 0.9 fusion.63
  14.4 0.0 collective-permute-done
  14.4 0.1 multiply_convert_fusion.2
  14.5 0.7 fusion.3
  15.2 0.1 fusion.51
  15.3 0.2 reduce_window_sum.18
  15.6 0.6 slice.95
  21.3 0.7 fusion.53
  21.9 1.5 convolution_bitcast_fusion
  23.5 0.1 fusion.13
  23.6 0.1 fusion.44
  23.6 0.7 pad_maximum_fusion
  24.3 0.0 all-gather.5.cloned.1.call-update
  24.3 0.0 all-gather.7.cloned.1.call-start
  24.4 0.7 all-gather.7.cloned.1.call-update
  25.1 0.3 fusion.2
  25.4 89.9 %all-gather.5.cloned.1.call-done = bf16[4608,512]{1,0:T(8,128)(2,1)} async-done(((bf16[144,512]{1,0:T(8,128)(2,1)}), bf16[4608,512]{1,0:T(8,128)(2,1)}) %all-gather.5.cloned.1.call-update) | async-done | bytes 4718608 | tf_op jit(solution)/shard_map/all_gather | solution.py:118
  115.3 0.8 slice.115
  116.1 0.1 copy.19
  116.2 0.6 fusion.50
  116.8 0.1 copy.16
  116.9 0.1 reduce-window.8
  117.0 0.8 subtract_reduce_fusion
  117.7 0.1 add_exponential_fusion
  117.8 0.3 broadcast_in_dim.19
  118.2 0.4 broadcast_in_dim.20
  118.5 2.5 %fusion.62 = (bf16[32,64,512]{2,1,0:T(8,128)(2,1)S(1)}, bf16[32,64,512]{2,1,0:T(8,128)(2,1)S(1)}) fusion(bf16[32,144,512]{2,1,0:T(8,128)(2,1)} %bitcast.89), kind=kLoop, calls=%fused_computation.94 | loop fusion | bytes 8388608 | tf_op jit(solution)/shard_map/slice | solution.py:50
  121.0 0.8 convolution_multiply_fusion
  121.8 0.5 fusion.11
  122.3 0.0 copy-start.2
  122.3 0.6 fusion.64
  122.9 0.2 multiply_reduce_fusion
  123.1 79.7 %all-gather.7.cloned.1.call-done = bf16[16384,128]{1,0:T(8,128)(2,1)} async-done(((bf16[512,128]{1,0:T(8,128)(2,1)}), bf16[16384,128]{1,0:T(8,128)(2,1)}) %all-gather.7.cloned.1.call-update) | async-done | bytes 4194320 | tf_op jit(solution)/shard_map/all_gather | solution.py:81
  202.8 0.0 copy-done.2
  202.8 3.1 %convolution_convert_fusion = bf16[64,32,128]{2,0,1:T(8,128)(2,1)S(1)} fusion(bf16[32,512,128]{2,1,0:T(8,128)(2,1)} %bitcast.87, f32[64,512]{1,0:T(8,128)S(1)} %get-tuple-element.28, f32[512]{0:T(512)S(1)} %copy-done.2, f32[64]{0:T(128)S(1)} %add_rsqrt_fusion, f32[64]{0:T(128)S(1)} %broadcast_multiply_fusion), kind=kOutput, calls=%fused_computation.1 | convolution fusion | flops 268828672 | bytes 4852224 | tf_op jit(solution)/shard_map/vtd,kdc->vtkc/dot_general | solution.py:126
  205.9 0.3 copy.17
  206.2 0.0 copy-start.1
  206.2 0.3 reshape_reshape.3
  206.6 0.2 copy.18
  206.7 27.0 %all_to_all.5 = bf16[8,1,64,512]{3,2,1,0:T(8,128)(2,1)S(1)} all-to-all(bf16[8,1,64,512]{3,2,1,0:T(8,128)(2,1)S(1)} %copy.18), channel_id=1, replica_groups=mesh['seq_0'=4,'seq_1'=8,'head'=8,'var'=2] {'head'}, dimensions={0} | all-to-all | bytes 1048576 | tf_op jit(solution)/shard_map/all_to_all | solution.py:26
  233.7 0.1 convert_reduce_fusion
  233.8 0.0 copy-done.1
  233.8 0.6 fusion.16
  (8 shorter events, 0.1 us)
Async XLA Ops:
  6.5 8.0 %copy-start = (bf16[1,2,512]{2,1,0:T(2,128)(2,1)S(1)}, bf16[1,2,512]{2,1,0:T(2,128)(2,1)}, u32[]{:S(2)}) copy-start(bf16[1,2,512]{2,1,0:T(2,128)(2,1)} %param.16) | copy-start | bytes 6148
  6.5 108.7 %all-gather.5.cloned.1.call-start = ((), (), s32[]{:S(2)}) async-start(), calls=%async_computation.1 | async-start | bytes 4866048 | tf_op jit(solution)/shard_map/all_gather | solution.py:118
  8.1 6.2 %collective-permute-start = (bf16[1,3,512]{2,1,0:T(4,128)(2,1)S(1)}, bf16[1,3,512]{2,1,0:T(4,128)(2,1)S(1)}, u32[]{:S(2)}, u32[]{:S(2)}) collective-permute-start(bf16[1,3,512]{2,1,0:T(4,128)(2,1)S(1)} %slice.105), channel_id=1, source_target_pairs={{0,16},{16,32},{32,48},{48,64},{64,80},{80,96},{96,112},{112,128},... | collective-permute-start | bytes 9224 | tf_op jit(solution)/shard_map/ppermute | solution.py:15
  24.3 178.5 %all-gather.7.cloned.1.call-start = ((), (), s32[]{:S(2)}) async-start(), calls=%async_computation.2 | async-start | bytes 4325376 | tf_op jit(solution)/shard_map/all_gather | solution.py:81
  122.3 80.5 %copy-start.2 = (f32[512]{0:T(512)S(1)}, f32[512]{0:T(512)}, u32[]{:S(2)}) copy-start(f32[512]{0:T(512)} %param.18) | copy-start | bytes 6148
  206.2 27.6 %copy-start.1 = (bf16[64,512]{1,0:T(8,128)(2,1)S(1)}, bf16[64,512]{1,0:T(8,128)(2,1)}, u32[]{:S(2)}) copy-start(bf16[64,512]{1,0:T(8,128)(2,1)} %param.12) | copy-start | bytes 196612
Sparse Core Ops, SparseCore 0:
  24.4 90.7 all-gather.4
  118.5 84.2 all-gather.6

commit v2 on v1

--- a/solution.py
+++ b/solution.py
@@ -25,6 +25,20 @@
     blocks = split_up(x, dim, lax.axis_size(axis))
     arrived = lax.all_to_all(blocks, axis, split_axis=0, concat_axis=0, tiled=True)
     return arrived.astype(jnp.float32).sum(axis=0)
+
+
+def ring_pieces(x, axis, count):
+    ahead = [(i, (i + 1) % count) for i in range(count)]
+    behind = [(i, (i - 1) % count) for i in range(count)]
+    before, after = [], []
+    forward = backward = x
+    for k in range(1, count // 2 + 1):
+        forward = lax.ppermute(forward, axis, ahead)
+        before.append(forward)
+        if k < count - k:
+            backward = lax.ppermute(backward, axis, behind)
+            after.append(backward)
+    return jnp.stack(before[::-1] + [x] + after)
 
 
 def three_parts(x):
@@ -78,7 +92,8 @@
     norm_gain,
     down_weight,
 ):
-    columns_all = lax.all_gather(down_weight, SEQ, axis=0, tiled=False)
+    outer, inner_size = (lax.axis_size(SEQ[0]), lax.axis_size(SEQ[1]))
+    columns_all = ring_pieces(ring_pieces(down_weight, SEQ[0], outer), SEQ[1], inner_size)
     kept_mask = (1 - erase).astype(jnp.bfloat16)
     erased = inner[None, :, :] * kept_mask[:, :, None]
     row_count = inner.shape[0]
@@ -124,9 +139,12 @@
     row_var = jnp.mean(centred * centred, axis=-1, keepdims=True)
     normed = (centred * lax.rsqrt(row_var + 1e-05) * norm_gain).astype(jnp.bfloat16)
     head_terms = jnp.einsum(
-        "vtd,kdc->vtkc", normed, columns_all, preferred_element_type=jnp.float32
+        "vtr,edrc->vtedc", normed, columns_all.reshape(inner_size, outer, head_size, -1),
+        preferred_element_type=jnp.float32,
     ).astype(jnp.bfloat16)
-    head_terms = head_terms.reshape(*normed.shape[:2], -1)
+    head_terms = jnp.roll(head_terms, lax.axis_index(SEQ[1]) - inner_size // 2, axis=2)
+    head_terms = jnp.roll(head_terms, lax.axis_index(SEQ[0]) - outer // 2, axis=3)
+    head_terms = jnp.swapaxes(head_terms, 2, 3).reshape(*normed.shape[:2], -1)
     summed = sent_and_summed(head_terms, "head", 2)
     return (residual_in[None, :, :].astype(jnp.float32) + summed).astype(jnp.bfloat16)
 

time: 242 us -> 176 us (0.73)
  waiting for transfers between devices: 170 us -> 57.8 us
  starting transfers between devices: 4.06 us -> 35.7 us
  local copies, waits for them, and re-layouts: 6.52 us -> 14.8 us
  matrix products: 8.76 us -> 11.3 us
    all_gather x1 -> x0, waiting for transfers between devices: 79.7 us -> none  [body(): columns_all = lax.all_gather(down_weight, SEQ, axis=0, tiled=False)]
    all_gather x1, waiting for transfers between devices: 89.9 us -> 14.5 us  [body(): gathered = lax.all_gather(packed, SEQ, axis=0, tiled=False)]
    ppermute x0 -> x10, waiting for transfers between devices: none -> 43.3 us  [the longest x6 42.9 us: ring_pieces(): forward = lax.ppermute(forward, axis, ahead)]
    ppermute x0 -> x10, starting transfers between devices: none -> 31.7 us  [the longest x6 19 us: ring_pieces(): forward = lax.ppermute(forward, axis, ahead)]
    unnamed x7 -> x29, local copies, waits for them, and re-layouts: 0.11 us -> 5.19 us
  transfers between devices with their start and end apart: 3 -> 12, of which waited for: 2 -> 8; matrix products, arithmetic and copies ran while one was open for 4% -> 6% of each run, Pallas kernels for 0% -> 0%
where the time goes in v2:
time: 176 us; the launch traced here: 174 us
  waiting for transfers between devices  57.8 us (33%)
  starting transfers between devices  35.7 us (20%)
  blocking collectives  27.3 us (16%)
  between operations  18.5 us (11%)
  local copies, waits for them, and re-layouts  14.8 us (8%)
  matrix products  11.3 us (6%)
  other arithmetic  8.18 us (5%)
    ppermute x6, waiting for transfers between devices, ring_pieces(): forward = lax.ppermute(forward, axis, ahead)  42.9 us
    all_to_all x1, blocking collectives, sent_and_summed(): lax.all_to_all(blocks, axis, split_axis=0, concat_axis=0, tiled=True)  27.3 us
    ppermute x6, starting transfers between devices, ring_pieces(): forward = lax.ppermute(forward, axis, ahead)  19 us
    all_gather x1, waiting for transfers between devices, body(): gathered = lax.all_gather(packed, SEQ, axis=0, tiled=False)  14.5 us
    ppermute x4, starting transfers between devices, ring_pieces(): backward = lax.ppermute(backward, axis, behind)  12.7 us
    unnamed x29, local copies, waits for them, and re-layouts  5.19 us
    ppermute x1, starting transfers between devices, from_behind(): lax.ppermute(value, axis, [(source, source + steps) for source in range(i...  4.02 us
    slice x1, local copies, waits for them, and re-layouts, carried_terms(): gathered[:, :token_count, :].reshape(blocks * token_count, head_size)  4.01 us
  transfers between devices with their start and end apart: 12, of which 8 were waited for; matrix products, arithmetic and copies ran while one was open for 6% of the time, Pallas kernels for 0%

profile of v2, /device:TPU:1, one launch (start us, length us, event | category | flops | bytes accessed | tf_op | source)
XLA Modules:
  0.0 173.6 jit_solution(16446140077314454384)
XLA Ops:
  6.5 0.7 convert_bitcast_fusion
  7.2 0.9 multiply_bitcast_fusion
  8.1 4.0 %collective-permute-start = (bf16[1,3,512]{2,1,0:T(4,128)(2,1)S(1)}, bf16[1,3,512]{2,1,0:T(4,128)(2,1)S(1)}, u32[]{:S(2)}, u32[]{:S(2)}) collective-permute-start(bf16[1,3,512]{2,1,0:T(4,128)(2,1)S(1)} %slice.105), channel_id=1, source_target_pairs={{0,16},{16,32},{32,48},{48,64},{64,80},{80,96},{96,112},{112,128},... | collective-permute-start | bytes 9224 | tf_op jit(solution)/shard_map/ppermute | solution.py:15
  12.2 1.3 convolution_convert_fusion.1
  13.5 0.9 fusion.67
  14.5 0.7 fusion.4
  15.6 0.6 slice.95
  20.9 0.6 fusion.57
  21.6 1.5 convolution_bitcast_fusion
  23.3 0.7 pad_maximum_fusion.1
  24.0 4.2 %collective-permute-start.1 = (bf16[512,128]{1,0:T(8,128)(2,1)}, bf16[512,128]{1,0:T(8,128)(2,1)S(1)}, u32[]{:S(2)}, u32[]{:S(2)}) collective-permute-start(bf16[512,128]{1,0:T(8,128)(2,1)} %param.19), channel_id=1, source_target_pairs={{0,128},{128,256},{256,384},{384,0},{1,129},{129,257},{257,385},{3... | collective-permute-start | bytes 393224 | tf_op jit(solution)/shard_map/ppermute | solution.py:36
  28.1 3.2 %collective-permute-start.3 = (bf16[512,128]{1,0:T(8,128)(2,1)}, bf16[512,128]{1,0:T(8,128)(2,1)S(1)}, u32[]{:S(2)}, u32[]{:S(2)}) collective-permute-start(bf16[512,128]{1,0:T(8,128)(2,1)} %param.19), channel_id=1, source_target_pairs={{0,384},{128,0},{256,128},{384,256},{1,385},{129,1},{257,129},{385... | collective-permute-start | bytes 393224 | tf_op jit(solution)/shard_map/ppermute | solution.py:39
  31.3 0.6 collective-permute-done.1
  31.9 2.1 %collective-permute-start.2 = (bf16[512,128]{1,0:T(8,128)(2,1)S(1)}, bf16[512,128]{1,0:T(8,128)(2,1)S(1)}, u32[]{:S(2)}, u32[]{:S(2)}) collective-permute-start(bf16[512,128]{1,0:T(8,128)(2,1)S(1)} %collective-permute-done.1), channel_id=1, source_target_pairs={{0,128},{128,256},{256,384},{384,0},{1,129},{129,257},{257,385},{3... | collective-permute-start | bytes 393224 | tf_op jit(solution)/shard_map/ppermute | solution.py:36
  34.1 4.8 %collective-permute-done.2 = bf16[512,128]{1,0:T(8,128)(2,1)S(1)} collective-permute-done((bf16[512,128]{1,0:T(8,128)(2,1)S(1)}, bf16[512,128]{1,0:T(8,128)(2,1)S(1)}, u32[]{:S(2)}, u32[]{:S(2)}) %collective-permute-start.2) | collective-permute-done | bytes 131104 | tf_op jit(solution)/shard_map/ppermute | solution.py:36
  38.9 1.0 pad_maximum_fusion
  39.9 2.4 %collective-permute-start.4 = (bf16[4,512,128]{2,1,0:T(8,128)(2,1)S(1)}, bf16[4,512,128]{2,1,0:T(8,128)(2,1)S(1)}, u32[]{:S(2)}, u32[]{:S(2)}) collective-permute-start(bf16[4,512,128]{2,1,0:T(8,128)(2,1)S(1)} %pad_maximum_fusion), channel_id=1, source_target_pairs={{0,16},{16,32},{32,48},{48,64},{64,80},{80,96},{96,112},{112,0},{1... | collective-permute-start | bytes 1572872 | tf_op jit(solution)/shard_map/ppermute | solution.py:36
  42.3 10.2 %collective-permute-done.4 = bf16[4,512,128]{2,1,0:T(8,128)(2,1)S(1)} collective-permute-done((bf16[4,512,128]{2,1,0:T(8,128)(2,1)S(1)}, bf16[4,512,128]{2,1,0:T(8,128)(2,1)S(1)}, u32[]{:S(2)}, u32[]{:S(2)}) %collective-permute-start.4) | collective-permute-done | bytes 524320 | tf_op jit(solution)/shard_map/ppermute | solution.py:36
  52.5 1.9 %collective-permute-start.5 = (bf16[4,512,128]{2,1,0:T(8,128)(2,1)S(1)}, bf16[4,512,128]{2,1,0:T(8,128)(2,1)S(1)}, u32[]{:S(2)}, u32[]{:S(2)}) collective-permute-start(bf16[4,512,128]{2,1,0:T(8,128)(2,1)S(1)} %collective-permute-done.4), channel_id=1, source_target_pairs={{0,16},{16,32},{32,48},{48,64},{64,80},{80,96},{96,112},{112,0},{1... | collective-permute-start | bytes 1572872 | tf_op jit(solution)/shard_map/ppermute | solution.py:36
  54.4 4.6 %collective-permute-start.8 = (bf16[4,512,128]{2,1,0:T(8,128)(2,1)S(1)}, bf16[4,512,128]{2,1,0:T(8,128)(2,1)S(1)}, u32[]{:S(2)}, u32[]{:S(2)}) collective-permute-start(bf16[4,512,128]{2,1,0:T(8,128)(2,1)S(1)} %pad_maximum_fusion), channel_id=1, source_target_pairs={{0,112},{16,0},{32,16},{48,32},{64,48},{80,64},{96,80},{112,96},{1... | collective-permute-start | bytes 1572872 | tf_op jit(solution)/shard_map/ppermute | solution.py:39
  59.0 7.7 %collective-permute-done.5 = bf16[4,512,128]{2,1,0:T(8,128)(2,1)S(1)} collective-permute-done((bf16[4,512,128]{2,1,0:T(8,128)(2,1)S(1)}, bf16[4,512,128]{2,1,0:T(8,128)(2,1)S(1)}, u32[]{:S(2)}, u32[]{:S(2)}) %collective-permute-start.5) | collective-permute-done | bytes 524320 | tf_op jit(solution)/shard_map/ppermute | solution.py:36
  66.7 4.9 %collective-permute-start.6 = (bf16[4,512,128]{2,1,0:T(8,128)(2,1)S(1)}, bf16[4,512,128]{2,1,0:T(8,128)(2,1)S(1)}, u32[]{:S(2)}, u32[]{:S(2)}) collective-permute-start(bf16[4,512,128]{2,1,0:T(8,128)(2,1)S(1)} %collective-permute-done.5), channel_id=1, source_target_pairs={{0,16},{16,32},{32,48},{48,64},{64,80},{80,96},{96,112},{112,0},{1... | collective-permute-start | bytes 1572872 | tf_op jit(solution)/shard_map/ppermute | solution.py:36
  71.6 1.9 %collective-permute-start.9 = (bf16[4,512,128]{2,1,0:T(8,128)(2,1)S(1)}, bf16[4,512,128]{2,1,0:T(8,128)(2,1)S(1)}, u32[]{:S(2)}, u32[]{:S(2)}) collective-permute-start(bf16[4,512,128]{2,1,0:T(8,128)(2,1)S(1)} %collective-permute-done.8), channel_id=1, source_target_pairs={{0,112},{16,0},{32,16},{48,32},{64,48},{80,64},{96,80},{112,96},{1... | collective-permute-start | bytes 1572872 | tf_op jit(solution)/shard_map/ppermute | solution.py:39
  73.5 5.6 %collective-permute-done.6 = bf16[4,512,128]{2,1,0:T(8,128)(2,1)S(1)} collective-permute-done((bf16[4,512,128]{2,1,0:T(8,128)(2,1)S(1)}, bf16[4,512,128]{2,1,0:T(8,128)(2,1)S(1)}, u32[]{:S(2)}, u32[]{:S(2)}) %collective-permute-start.6) | collective-permute-done | bytes 524320 | tf_op jit(solution)/shard_map/ppermute | solution.py:36
  79.2 3.6 %collective-permute-start.7 = (bf16[4,512,128]{2,1,0:T(8,128)(2,1)S(1)}, bf16[4,512,128]{2,1,0:T(8,128)(2,1)S(1)}, u32[]{:S(2)}, u32[]{:S(2)}) collective-permute-start(bf16[4,512,128]{2,1,0:T(8,128)(2,1)S(1)} %collective-permute-done.6), channel_id=1, source_target_pairs={{0,16},{16,32},{32,48},{48,64},{64,80},{80,96},{96,112},{112,0},{1... | collective-permute-start | bytes 1572872 | tf_op jit(solution)/shard_map/ppermute | solution.py:36
  82.8 1.1 fusion.3
  84.0 3.0 %collective-permute-start.10 = (bf16[4,512,128]{2,1,0:T(8,128)(2,1)S(1)}, bf16[4,512,128]{2,1,0:T(8,128)(2,1)S(1)}, u32[]{:S(2)}, u32[]{:S(2)}) collective-permute-start(bf16[4,512,128]{2,1,0:T(8,128)(2,1)S(1)} %collective-permute-done.9), channel_id=1, source_target_pairs={{0,112},{16,0},{32,16},{48,32},{64,48},{80,64},{96,80},{112,96},{1... | collective-permute-start | bytes 1572872 | tf_op jit(solution)/shard_map/ppermute | solution.py:39
  87.1 13.9 %collective-permute-done.7 = bf16[4,512,128]{2,1,0:T(8,128)(2,1)S(1)} collective-permute-done((bf16[4,512,128]{2,1,0:T(8,128)(2,1)S(1)}, bf16[4,512,128]{2,1,0:T(8,128)(2,1)S(1)}, u32[]{:S(2)}, u32[]{:S(2)}) %collective-permute-start.7) | collective-permute-done | bytes 524320 | tf_op jit(solution)/shard_map/ppermute | solution.py:36
  101.0 0.8 bitcast_dynamic-update-slice_fusion.7
  101.8 0.9 bitcast_dynamic-update-slice_fusion.6
  102.7 0.8 bitcast_dynamic-update-slice_fusion.5
  103.5 0.9 bitcast_dynamic-update-slice_fusion.4
  104.3 0.8 bitcast_dynamic-update-slice_fusion.3
  105.2 0.8 bitcast_dynamic-update-slice_fusion.2
  106.0 0.9 bitcast_dynamic-update-slice_fusion.1
  107.2 0.9 bitcast_dynamic-update-slice_fusion
  108.1 14.5 %all-gather.3.cloned.1.call-done = bf16[4608,512]{1,0:T(8,128)(2,1)} async-done(((bf16[144,512]{1,0:T(8,128)(2,1)}), bf16[4608,512]{1,0:T(8,128)(2,1)}) %all-gather.3.cloned.1.call-update) | async-done | bytes 4718608 | tf_op jit(solution)/shard_map/all_gather | solution.py:133
  122.6 0.8 slice.115
  123.5 4.0 %fusion.66 = (bf16[32,64,512]{2,1,0:T(8,128)(2,1)}, bf16[32,64,512]{2,1,0:T(8,128)(2,1)S(1)}) fusion(bf16[32,144,512]{2,1,0:T(8,128)(2,1)} %bitcast.115), kind=kLoop, calls=%fused_computation.111 | loop fusion | bytes 8388608 | tf_op jit(solution)/shard_map/slice | solution.py:64
  127.6 0.6 fusion.54
  128.4 0.8 subtract_reduce_fusion
  129.5 1.2 broadcast_in_dim.20
  130.7 2.4 %convolution_multiply_fusion = f32[64,2048]{1,0:T(8,128)S(1)} fusion(f32[64,2048]{1,0:T(8,128)} %broadcast_in_dim.20, bf16[2048,512]{1,0:T(8,128)(2,1)} %bitcast.113, f32[1,64,1024]{2,1,0:T(8,128)S(1)} %convolution_bitcast_fusion), kind=kOutput, calls=%fused_computation | convolution fusion | flops 134348800 | bytes 3211264 | tf_op jit(solution)/shard_map/vtd,sd->vts/dot_general | solution.py:75
  133.2 0.5 fusion.15
  133.6 0.6 fusion.68
  134.4 3.1 %fusion = bf16[1,64,8,4,128]{4,1,3,2,0:T(8,128)(2,1)S(1)} fusion(bf16[8,4,512,128]{3,2,1,0:T(8,128)(2,1)} %bitcast_dynamic-update-slice_fusion, f32[64,512]{1,0:T(8,128)S(1)} %get-tuple-element.28, f32[512]{0:T(512)S(1)} %copy-done.10, f32[64]{0:T(128)S(1)} %add_rsqrt_fusion, f32[64]{0:T(128)S(1)} %broadcast_multiply_fusion), kind=kOutput, calls=%fused_computation.2 | convolution fusion | flops 268828672 | bytes 4852224 | tf_op jit(solution)/shard_map/vtr,edrc->vtedc/dot_general | solution.py:141
  138.8 27.3 %all_to_all.5 = bf16[8,1,64,512]{3,2,1,0:T(8,128)(2,1)S(1)} all-to-all(bf16[8,1,64,512]{3,2,1,0:T(8,128)(2,1)S(1)} %copy.18), channel_id=1, replica_groups=mesh['seq_0'=4,'seq_1'=8,'head'=8,'var'=2] {'head'}, dimensions={0} | all-to-all | bytes 1048576 | tf_op jit(solution)/shard_map/all_to_all | solution.py:26
  166.1 0.6 fusion.20
  (52 shorter events, 3.2 us)
Async XLA Ops:
  6.5 8.0 %copy-start = (bf16[1,2,512]{2,1,0:T(2,128)(2,1)S(1)}, bf16[1,2,512]{2,1,0:T(2,128)(2,1)}, u32[]{:S(2)}) copy-start(bf16[1,2,512]{2,1,0:T(2,128)(2,1)} %param.16) | copy-start | bytes 6148
  6.5 116.1 %all-gather.3.cloned.1.call-start = ((), (), s32[]{:S(2)}) async-start(), calls=%async_computation.1 | async-start | bytes 4866048 | tf_op jit(solution)/shard_map/all_gather | solution.py:133
  8.1 6.2 %collective-permute-start = (bf16[1,3,512]{2,1,0:T(4,128)(2,1)S(1)}, bf16[1,3,512]{2,1,0:T(4,128)(2,1)S(1)}, u32[]{:S(2)}, u32[]{:S(2)}) collective-permute-start(bf16[1,3,512]{2,1,0:T(4,128)(2,1)S(1)} %slice.105), channel_id=1, source_target_pairs={{0,16},{16,32},{32,48},{48,64},{64,80},{80,96},{96,112},{112,128},... | collective-permute-start | bytes 9224 | tf_op jit(solution)/shard_map/ppermute | solution.py:15
  13.5 25.4 %copy-start.8 = (bf16[64,512]{1,0:T(8,128)(2,1)}, bf16[64,512]{1,0:T(8,128)(2,1)S(1)}, u32[]{:S(2)}) copy-start(bf16[64,512]{1,0:T(8,128)(2,1)S(1)} %convolution_convert_fusion.1) | copy-start | bytes 196612
  24.0 8.0 %collective-permute-start.1 = (bf16[512,128]{1,0:T(8,128)(2,1)}, bf16[512,128]{1,0:T(8,128)(2,1)S(1)}, u32[]{:S(2)}, u32[]{:S(2)}) collective-permute-start(bf16[512,128]{1,0:T(8,128)(2,1)} %param.19), channel_id=1, source_target_pairs={{0,128},{128,256},{256,384},{384,0},{1,129},{129,257},{257,385},{3... | collective-permute-start | bytes 393224 | tf_op jit(solution)/shard_map/ppermute | solution.py:36
  28.1 5.9 %collective-permute-start.3 = (bf16[512,128]{1,0:T(8,128)(2,1)}, bf16[512,128]{1,0:T(8,128)(2,1)S(1)}, u32[]{:S(2)}, u32[]{:S(2)}) collective-permute-start(bf16[512,128]{1,0:T(8,128)(2,1)} %param.19), channel_id=1, source_target_pairs={{0,384},{128,0},{256,128},{384,256},{1,385},{129,1},{257,129},{385... | collective-permute-start | bytes 393224 | tf_op jit(solution)/shard_map/ppermute | solution.py:39
  31.9 47.2 %copy-start.2 = (bf16[512,128]{1,0:T(8,128)(2,1)}, bf16[512,128]{1,0:T(8,128)(2,1)S(1)}, u32[]{:S(2)}) copy-start(bf16[512,128]{1,0:T(8,128)(2,1)S(1)} %collective-permute-done.1) | copy-start | bytes 393220
  31.9 6.9 %collective-permute-start.2 = (bf16[512,128]{1,0:T(8,128)(2,1)S(1)}, bf16[512,128]{1,0:T(8,128)(2,1)S(1)}, u32[]{:S(2)}, u32[]{:S(2)}) collective-permute-start(bf16[512,128]{1,0:T(8,128)(2,1)S(1)} %collective-permute-done.1), channel_id=1, source_target_pairs={{0,128},{128,256},{256,384},{384,0},{1,129},{129,257},{257,385},{3... | collective-permute-start | bytes 393224 | tf_op jit(solution)/shard_map/ppermute | solution.py:36
  34.0 48.7 %copy-start.4 = (bf16[512,128]{1,0:T(8,128)(2,1)}, bf16[512,128]{1,0:T(8,128)(2,1)S(1)}, u32[]{:S(2)}) copy-start(bf16[512,128]{1,0:T(8,128)(2,1)S(1)} %collective-permute-done.3) | copy-start | bytes 393220
  38.9 43.9 %copy-start.6 = (bf16[512,128]{1,0:T(8,128)(2,1)}, bf16[512,128]{1,0:T(8,128)(2,1)S(1)}, u32[]{:S(2)}) copy-start(bf16[512,128]{1,0:T(8,128)(2,1)S(1)} %collective-permute-done.2) | copy-start | bytes 393220
  39.9 12.6 %collective-permute-start.4 = (bf16[4,512,128]{2,1,0:T(8,128)(2,1)S(1)}, bf16[4,512,128]{2,1,0:T(8,128)(2,1)S(1)}, u32[]{:S(2)}, u32[]{:S(2)}) collective-permute-start(bf16[4,512,128]{2,1,0:T(8,128)(2,1)S(1)} %pad_maximum_fusion), channel_id=1, source_target_pairs={{0,16},{16,32},{32,48},{48,64},{64,80},{80,96},{96,112},{112,0},{1... | collective-permute-start | bytes 1572872 | tf_op jit(solution)/shard_map/ppermute | solution.py:36
  52.5 14.2 %collective-permute-start.5 = (bf16[4,512,128]{2,1,0:T(8,128)(2,1)S(1)}, bf16[4,512,128]{2,1,0:T(8,128)(2,1)S(1)}, u32[]{:S(2)}, u32[]{:S(2)}) collective-permute-start(bf16[4,512,128]{2,1,0:T(8,128)(2,1)S(1)} %collective-permute-done.4), channel_id=1, source_target_pairs={{0,16},{16,32},{32,48},{48,64},{64,80},{80,96},{96,112},{112,0},{1... | collective-permute-start | bytes 1572872 | tf_op jit(solution)/shard_map/ppermute | solution.py:36
  54.4 17.2 %collective-permute-start.8 = (bf16[4,512,128]{2,1,0:T(8,128)(2,1)S(1)}, bf16[4,512,128]{2,1,0:T(8,128)(2,1)S(1)}, u32[]{:S(2)}, u32[]{:S(2)}) collective-permute-start(bf16[4,512,128]{2,1,0:T(8,128)(2,1)S(1)} %pad_maximum_fusion), channel_id=1, source_target_pairs={{0,112},{16,0},{32,16},{48,32},{64,48},{80,64},{96,80},{112,96},{1... | collective-permute-start | bytes 1572872 | tf_op jit(solution)/shard_map/ppermute | solution.py:39
  66.7 12.5 %collective-permute-start.6 = (bf16[4,512,128]{2,1,0:T(8,128)(2,1)S(1)}, bf16[4,512,128]{2,1,0:T(8,128)(2,1)S(1)}, u32[]{:S(2)}, u32[]{:S(2)}) collective-permute-start(bf16[4,512,128]{2,1,0:T(8,128)(2,1)S(1)} %collective-permute-done.5), channel_id=1, source_target_pairs={{0,16},{16,32},{32,48},{48,64},{64,80},{80,96},{96,112},{112,0},{1... | collective-permute-start | bytes 1572872 | tf_op jit(solution)/shard_map/ppermute | solution.py:36
  71.6 12.4 %collective-permute-start.9 = (bf16[4,512,128]{2,1,0:T(8,128)(2,1)S(1)}, bf16[4,512,128]{2,1,0:T(8,128)(2,1)S(1)}, u32[]{:S(2)}, u32[]{:S(2)}) collective-permute-start(bf16[4,512,128]{2,1,0:T(8,128)(2,1)S(1)} %collective-permute-done.8), channel_id=1, source_target_pairs={{0,112},{16,0},{32,16},{48,32},{64,48},{80,64},{96,80},{112,96},{1... | collective-permute-start | bytes 1572872 | tf_op jit(solution)/shard_map/ppermute | solution.py:39
  79.2 21.8 %collective-permute-start.7 = (bf16[4,512,128]{2,1,0:T(8,128)(2,1)S(1)}, bf16[4,512,128]{2,1,0:T(8,128)(2,1)S(1)}, u32[]{:S(2)}, u32[]{:S(2)}) collective-permute-start(bf16[4,512,128]{2,1,0:T(8,128)(2,1)S(1)} %collective-permute-done.6), channel_id=1, source_target_pairs={{0,16},{16,32},{32,48},{48,64},{64,80},{80,96},{96,112},{112,0},{1... | collective-permute-start | bytes 1572872 | tf_op jit(solution)/shard_map/ppermute | solution.py:36
  84.0 20.3 %copy-start.1 = (bf16[512,128]{1,0:T(8,128)(2,1)S(1)}, bf16[512,128]{1,0:T(8,128)(2,1)}, u32[]{:S(2)}) copy-start(bf16[512,128]{1,0:T(8,128)(2,1)} %param.19) | copy-start | bytes 393220
  84.0 20.3 %copy-start.3 = (bf16[512,128]{1,0:T(8,128)(2,1)S(1)}, bf16[512,128]{1,0:T(8,128)(2,1)}, u32[]{:S(2)}) copy-start(bf16[512,128]{1,0:T(8,128)(2,1)} %copy-done.2) | copy-start | bytes 393220
  84.0 20.3 %copy-start.5 = (bf16[512,128]{1,0:T(8,128)(2,1)S(1)}, bf16[512,128]{1,0:T(8,128)(2,1)}, u32[]{:S(2)}) copy-start(bf16[512,128]{1,0:T(8,128)(2,1)} %copy-done.4) | copy-start | bytes 393220
  84.0 20.3 %copy-start.7 = (bf16[512,128]{1,0:T(8,128)(2,1)S(1)}, bf16[512,128]{1,0:T(8,128)(2,1)}, u32[]{:S(2)}) copy-start(bf16[512,128]{1,0:T(8,128)(2,1)} %copy-done.6) | copy-start | bytes 393220
  84.0 23.2 %collective-permute-start.10 = (bf16[4,512,128]{2,1,0:T(8,128)(2,1)S(1)}, bf16[4,512,128]{2,1,0:T(8,128)(2,1)S(1)}, u32[]{:S(2)}, u32[]{:S(2)}) collective-permute-start(bf16[4,512,128]{2,1,0:T(8,128)(2,1)S(1)} %collective-permute-done.9), channel_id=1, source_target_pairs={{0,112},{16,0},{32,16},{48,32},{64,48},{80,64},{96,80},{112,96},{1... | collective-permute-start | bytes 1572872 | tf_op jit(solution)/shard_map/ppermute | solution.py:39
  130.7 3.7 %copy-start.10 = (f32[512]{0:T(512)S(1)}, f32[512]{0:T(512)}, u32[]{:S(2)}) copy-start(f32[512]{0:T(512)} %param.18) | copy-start | bytes 6148
  137.5 28.6 %copy-start.9 = (bf16[64,512]{1,0:T(8,128)(2,1)S(1)}, bf16[64,512]{1,0:T(8,128)(2,1)}, u32[]{:S(2)}) copy-start(bf16[64,512]{1,0:T(8,128)(2,1)} %param.12) | copy-start | bytes 196612
Sparse Core Ops, SparseCore 0:
  24.1 98.5 all-gather.2

commit v3 on v2

--- a/solution.py
+++ b/solution.py
@@ -58,27 +58,47 @@
     return jnp.einsum("vts,vse->vte", weights, values, preferred_element_type=jnp.float32)
 
 
+def exact_pair(x):
+    high = x.astype(jnp.bfloat16)
+    return high, (x - high.astype(jnp.float32)).astype(jnp.bfloat16)
+
+
+def two_pass(spec, left, right):
+    high, low = exact_pair(left)
+    return jnp.einsum(spec, high, right, preferred_element_type=jnp.float32) + jnp.einsum(
+        spec, low, right, preferred_element_type=jnp.float32
+    )
+
+
+def block_decays(gathered, token_count):
+    parts = gathered[:, 2 * token_count, :3].astype(jnp.float32)
+    return (parts[:, 0] + parts[:, 1]) + parts[:, 2]
+
+
 def carried_terms(queries, cumulated, gathered, block):
     blocks, rows, head_size = gathered.shape
     token_count = queries.shape[1]
     keys_all = gathered[:, :token_count, :].reshape(blocks * token_count, head_size)
     values_all = gathered[:, token_count : 2 * token_count, :].reshape(blocks * token_count, head_size)
-    parts = gathered[:, 2 * token_count, :3].astype(jnp.float32)
-    decay = (parts[:, 0] + parts[:, 1]) + parts[:, 2]
+    decay = block_decays(gathered, token_count)
     through = jnp.cumsum(decay)
-    before_own = jnp.sum(jnp.where(jnp.arange(blocks) < block, decay, 0.0))
     earlier = jnp.arange(blocks) < block
+    before_own = jnp.sum(jnp.where(earlier, decay, 0.0))
     block_exponent = jnp.where(earlier, before_own - through, -jnp.inf)
     exponent = cumulated[:, :, None, None] + block_exponent[None, None, :, None]
     scale = jnp.exp(jnp.broadcast_to(exponent, (*cumulated.shape, blocks, token_count)))
     scale = scale.reshape(*cumulated.shape, blocks * token_count)
     scores = jnp.einsum("vtd,sd->vts", queries, keys_all, preferred_element_type=jnp.float32)
-    weights = scores * scale
-    high = weights.astype(jnp.bfloat16)
-    low = (weights - high.astype(jnp.float32)).astype(jnp.bfloat16)
-    return jnp.einsum("vts,se->vte", high, values_all, preferred_element_type=jnp.float32) + jnp.einsum(
-        "vts,se->vte", low, values_all, preferred_element_type=jnp.float32
-    )
+    return two_pass("vts,se->vte", scores * scale, values_all), before_own
+
+
+def group_rows(gathered, token_count, rows_at, row_count):
+    decay = block_decays(gathered, token_count)
+    tail = jnp.sum(decay) - jnp.cumsum(decay)
+    keys = lax.dynamic_slice_in_dim(gathered[:, :token_count, :], rows_at, row_count, 2)
+    values = gathered[:, token_count : 2 * token_count, :]
+    scaled = keys.astype(jnp.float32) * jnp.exp(tail)[:, None, None]
+    return two_pass("jtr,jte->re", scaled, values), jnp.sum(decay)
 
 
 def body(
@@ -130,10 +150,23 @@
     extra = jnp.zeros((EXTRA, head_size), jnp.bfloat16)
     extra = extra.at[0, :3].set(three_parts(block_decay[0]))
     packed = jnp.concatenate([scaled_keys[0], values[0], extra], axis=0)
-    gathered = lax.all_gather(packed, SEQ, axis=0, tiled=False)
-    block = lax.axis_index(SEQ)
+    gathered = lax.all_gather(packed, SEQ[1], axis=0, tiled=False)
+    place, group = (lax.axis_index(SEQ[1]), lax.axis_index(SEQ[0]))
+    slice_rows = head_size // inner_size
+    within, before_own = carried_terms(queries, cumulated, gathered, place)
+    leaving, group_decay = group_rows(gathered, row_count, place * slice_rows, slice_rows)
+    group_extra = jnp.zeros((8, head_size), jnp.float32).at[0, 0].set(group_decay)
+    across = lax.all_gather(jnp.concatenate([leaving, group_extra], axis=0), SEQ[0], axis=0, tiled=False)
+    decays = across[:, slice_rows, 0]
+    earlier = jnp.arange(outer) < group
+    before_group = jnp.sum(jnp.where(earlier, decays, 0.0))
+    factor = jnp.where(earlier, jnp.exp(jnp.where(earlier, before_group - jnp.cumsum(decays), 0.0)), 0.0)
+    entering_rows = jnp.sum(factor[:, None, None] * across[:, :slice_rows, :], axis=0)
+    entering = lax.all_gather(entering_rows, SEQ[1], axis=0, tiled=True)
+    carried = two_pass("vde,vtd->vte", entering[None], queries)
+    carried = jnp.exp(cumulated + before_own)[..., None] * carried
     intra_part = local_terms(queries, key_rows, values, cumulated, input_log)
-    numerator = carried_terms(queries, cumulated, gathered, block) + intra_part
+    numerator = (carried + within) + intra_part
     row_mean = jnp.mean(numerator, axis=-1, keepdims=True)
     centred = numerator - row_mean
     row_var = jnp.mean(centred * centred, axis=-1, keepdims=True)

time: 176 us -> 206 us (1.17)
  blocking collectives: 27.3 us -> 38.9 us
  waiting for transfers between devices: 57.8 us -> 66.4 us
  other arithmetic: 8.18 us -> 13.1 us
  matrix products: 11.3 us -> 14.3 us
    all_gather x1 -> x2, waiting for transfers between devices: 14.5 us -> 34.6 us  [the longest x1 34.6 us: body(): entering = lax.all_gather(entering_rows, SEQ[1], axis=0, tiled=True)]
    ppermute x6, waiting for transfers between devices: 42.9 us -> 31.8 us  [ring_pieces(): forward = lax.ppermute(forward, axis, ahead)]
    all_gather x0 -> x1, blocking collectives: none -> 10.6 us  [body(): lax.all_gather(jnp.concatenate([leaving, group_extra], axis=0), SEQ[0], a...]
    dot_general x2 -> x6, matrix products: 1.05 us -> 6.44 us  [the longest x3 3.45 us: two_pass(): jnp.einsum(spec, low, right, preferred_element_type=jnp.float32)]
    unnamed x29 -> x33, local copies, waits for them, and re-layouts: 5.19 us -> 8.36 us
    slice x2 -> x3, local copies, waits for them, and re-layouts: 4.86 us -> 2.02 us  [the longest x1 1.29 us: group_rows(): values = gathered[:, token_count:2 * token_count, :]]
    dot_general x1, matrix products: 2.44 us -> 0.28 us  [carried_terms(): jnp.einsum('vtd,sd->vts', queries, keys_all, preferred_element_type=jnp.f...]
  transfers between devices with their start and end apart: 12 -> 13, of which waited for: 8 -> 6; matrix products, arithmetic and copies ran while one was open for 6% -> 13% of each run, Pallas kernels for 0% -> 0%
where the time goes in v3:
time: 206 us; the launch traced here: 204 us
  waiting for transfers between devices  66.4 us (32%)
  blocking collectives  38.9 us (19%)
  starting transfers between devices  37.5 us (18%)
  between operations  18.8 us (9%)
  local copies, waits for them, and re-layouts  14.8 us (7%)
  matrix products  14.3 us (7%)
  other arithmetic  13.1 us (6%)
    all_gather x1, waiting for transfers between devices, body(): entering = lax.all_gather(entering_rows, SEQ[1], axis=0, tiled=True)  34.6 us
    ppermute x6, waiting for transfers between devices, ring_pieces(): forward = lax.ppermute(forward, axis, ahead)  31.8 us
    all_to_all x1, blocking collectives, sent_and_summed(): lax.all_to_all(blocks, axis, split_axis=0, concat_axis=0, tiled=True)  28.3 us
    ppermute x6, starting transfers between devices, ring_pieces(): forward = lax.ppermute(forward, axis, ahead)  19.6 us
    ppermute x4, starting transfers between devices, ring_pieces(): backward = lax.ppermute(backward, axis, behind)  13.8 us
    all_gather x1, blocking collectives, body(): lax.all_gather(jnp.concatenate([leaving, group_extra], axis=0), SEQ[0], a...  10.6 us
    unnamed x33, local copies, waits for them, and re-layouts  8.36 us
  transfers between devices with their start and end apart: 13, of which 6 were waited for; matrix products, arithmetic and copies ran while one was open for 13% of the time, Pallas kernels for 0%

profile of v3, /device:TPU:1, one launch (start us, length us, event | category | flops | bytes accessed | tf_op | source)
XLA Modules:
  0.0 203.9 jit_solution(1284970320818615073)
XLA Ops:
  6.5 0.7 convert_bitcast_fusion
  7.2 0.9 multiply_bitcast_fusion
  8.1 4.0 %collective-permute-start = (bf16[1,3,512]{2,1,0:T(4,128)(2,1)S(1)}, bf16[1,3,512]{2,1,0:T(4,128)(2,1)S(1)}, u32[]{:S(2)}, u32[]{:S(2)}) collective-permute-start(bf16[1,3,512]{2,1,0:T(4,128)(2,1)S(1)} %slice.135), channel_id=1, source_target_pairs={{0,16},{16,32},{32,48},{48,64},{64,80},{80,96},{96,112},{112,128},... | collective-permute-start | bytes 9224 | tf_op jit(solution)/shard_map/ppermute | solution.py:15
  12.2 1.3 convolution_convert_fusion.1
  13.5 0.9 fusion.84
  14.5 1.5 convolution_bitcast_fusion
  16.0 0.7 fusion.7
  17.7 0.7 fusion.72
  23.4 0.7 pad_maximum_fusion.1
  24.1 4.2 %collective-permute-start.1 = (bf16[512,128]{1,0:T(8,128)(2,1)}, bf16[512,128]{1,0:T(8,128)(2,1)S(1)}, u32[]{:S(2)}, u32[]{:S(2)}) collective-permute-start(bf16[512,128]{1,0:T(8,128)(2,1)} %param.21), channel_id=1, source_target_pairs={{0,128},{128,256},{256,384},{384,0},{1,129},{129,257},{257,385},{3... | collective-permute-start | bytes 393224 | tf_op jit(solution)/shard_map/ppermute | solution.py:36
  28.3 3.2 %collective-permute-start.3 = (bf16[512,128]{1,0:T(8,128)(2,1)}, bf16[512,128]{1,0:T(8,128)(2,1)S(1)}, u32[]{:S(2)}, u32[]{:S(2)}) collective-permute-start(bf16[512,128]{1,0:T(8,128)(2,1)} %param.21), channel_id=1, source_target_pairs={{0,384},{128,0},{256,128},{384,256},{1,385},{129,1},{257,129},{385... | collective-permute-start | bytes 393224 | tf_op jit(solution)/shard_map/ppermute | solution.py:39
  32.1 2.1 %collective-permute-start.2 = (bf16[512,128]{1,0:T(8,128)(2,1)S(1)}, bf16[512,128]{1,0:T(8,128)(2,1)S(1)}, u32[]{:S(2)}, u32[]{:S(2)}) collective-permute-start(bf16[512,128]{1,0:T(8,128)(2,1)S(1)} %collective-permute-done.1), channel_id=1, source_target_pairs={{0,128},{128,256},{256,384},{384,0},{1,129},{129,257},{257,385},{3... | collective-permute-start | bytes 393224 | tf_op jit(solution)/shard_map/ppermute | solution.py:36
  34.2 4.8 %collective-permute-done.2 = bf16[512,128]{1,0:T(8,128)(2,1)S(1)} collective-permute-done((bf16[512,128]{1,0:T(8,128)(2,1)S(1)}, bf16[512,128]{1,0:T(8,128)(2,1)S(1)}, u32[]{:S(2)}, u32[]{:S(2)}) %collective-permute-start.2) | collective-permute-done | bytes 131104 | tf_op jit(solution)/shard_map/ppermute | solution.py:36
  39.0 1.0 pad_maximum_fusion
  40.1 2.4 %collective-permute-start.4 = (bf16[4,512,128]{2,1,0:T(8,128)(2,1)S(1)}, bf16[4,512,128]{2,1,0:T(8,128)(2,1)S(1)}, u32[]{:S(2)}, u32[]{:S(2)}) collective-permute-start(bf16[4,512,128]{2,1,0:T(8,128)(2,1)S(1)} %pad_maximum_fusion), channel_id=1, source_target_pairs={{0,16},{16,32},{32,48},{48,64},{64,80},{80,96},{96,112},{112,0},{1... | collective-permute-start | bytes 1572872 | tf_op jit(solution)/shard_map/ppermute | solution.py:36
  42.4 4.1 %collective-permute-start.8 = (bf16[4,512,128]{2,1,0:T(8,128)(2,1)S(1)}, bf16[4,512,128]{2,1,0:T(8,128)(2,1)S(1)}, u32[]{:S(2)}, u32[]{:S(2)}) collective-permute-start(bf16[4,512,128]{2,1,0:T(8,128)(2,1)S(1)} %pad_maximum_fusion), channel_id=1, source_target_pairs={{0,112},{16,0},{32,16},{48,32},{64,48},{80,64},{96,80},{112,96},{1... | collective-permute-start | bytes 1572872 | tf_op jit(solution)/shard_map/ppermute | solution.py:39
  46.6 11.7 %collective-permute-done.4 = bf16[4,512,128]{2,1,0:T(8,128)(2,1)S(1)} collective-permute-done((bf16[4,512,128]{2,1,0:T(8,128)(2,1)S(1)}, bf16[4,512,128]{2,1,0:T(8,128)(2,1)S(1)}, u32[]{:S(2)}, u32[]{:S(2)}) %collective-permute-start.4) | collective-permute-done | bytes 524320 | tf_op jit(solution)/shard_map/ppermute | solution.py:36
  58.3 1.9 collective-permute-start.5
  60.2 4.6 %collective-permute-start.9 = (bf16[4,512,128]{2,1,0:T(8,128)(2,1)S(1)}, bf16[4,512,128]{2,1,0:T(8,128)(2,1)S(1)}, u32[]{:S(2)}, u32[]{:S(2)}) collective-permute-start(bf16[4,512,128]{2,1,0:T(8,128)(2,1)S(1)} %collective-permute-done.8), channel_id=1, source_target_pairs={{0,112},{16,0},{32,16},{48,32},{64,48},{80,64},{96,80},{112,96},{1... | collective-permute-start | bytes 1572872 | tf_op jit(solution)/shard_map/ppermute | solution.py:39
  64.8 9.4 %collective-permute-done.5 = bf16[4,512,128]{2,1,0:T(8,128)(2,1)S(1)} collective-permute-done((bf16[4,512,128]{2,1,0:T(8,128)(2,1)S(1)}, bf16[4,512,128]{2,1,0:T(8,128)(2,1)S(1)}, u32[]{:S(2)}, u32[]{:S(2)}) %collective-permute-start.5) | collective-permute-done | bytes 524320 | tf_op jit(solution)/shard_map/ppermute | solution.py:36
  74.2 4.9 %collective-permute-start.6 = (bf16[4,512,128]{2,1,0:T(8,128)(2,1)S(1)}, bf16[4,512,128]{2,1,0:T(8,128)(2,1)}, u32[]{:S(2)}, u32[]{:S(2)}) collective-permute-start(bf16[4,512,128]{2,1,0:T(8,128)(2,1)S(1)} %collective-permute-done.5), channel_id=1, source_target_pairs={{0,16},{16,32},{32,48},{48,64},{64,80},{80,96},{96,112},{112,0},{1... | collective-permute-start | bytes 1572872 | tf_op jit(solution)/shard_map/ppermute | solution.py:36
  79.1 1.0 fusion.6
  80.1 1.9 collective-permute-start.10
  82.0 5.3 %collective-permute-done.6 = bf16[4,512,128]{2,1,0:T(8,128)(2,1)} collective-permute-done((bf16[4,512,128]{2,1,0:T(8,128)(2,1)S(1)}, bf16[4,512,128]{2,1,0:T(8,128)(2,1)}, u32[]{:S(2)}, u32[]{:S(2)}) %collective-permute-start.6) | collective-permute-done | bytes 524320 | tf_op jit(solution)/shard_map/ppermute | solution.py:36
  87.3 4.2 %collective-permute-start.7 = (bf16[4,512,128]{2,1,0:T(8,128)(2,1)}, bf16[4,512,128]{2,1,0:T(8,128)(2,1)}, u32[]{:S(2)}, u32[]{:S(2)}) collective-permute-start(bf16[4,512,128]{2,1,0:T(8,128)(2,1)} %collective-permute-done.6), channel_id=1, source_target_pairs={{0,16},{16,32},{32,48},{48,64},{64,80},{80,96},{96,112},{112,0},{1... | collective-permute-start | bytes 1572872 | tf_op jit(solution)/shard_map/ppermute | solution.py:36
  91.6 0.7 slice.143
  93.0 0.7 reduce_sum.68
  93.9 1.3 fusion.83
  95.2 0.7 add_exponential_fusion.1
  96.5 0.7 exponential_bitcast_fusion
  97.2 1.4 convolution_bitcast_fusion.1
  98.5 1.4 fusion.4
  99.9 0.7 select_maximum_fusion
  100.6 10.6 %all-gather.1 = f32[288,512]{1,0:T(8,128)S(1)} all-gather(f32[72,512]{1,0:T(8,128)S(1)} %select_maximum_fusion), channel_id=3, replica_groups=mesh['seq_0'=4,'seq_1'=8,'head'=8,'var'=2] {'seq_0'}, dimensions={0}, use_global_device_ids=true | all-gather | bytes 737280 | tf_op jit(solution)/shard_map/all_gather | solution.py:159
  112.7 0.8 fusion.12
  114.5 1.9 bitcast_dynamic-update-slice_fusion.7
  116.3 1.9 bitcast_dynamic-update-slice_fusion.6
  118.2 1.9 bitcast_dynamic-update-slice_fusion.5
  120.1 0.8 bitcast_dynamic-update-slice_fusion.4
  120.9 0.8 bitcast_dynamic-update-slice_fusion.3
  121.8 0.8 bitcast_dynamic-update-slice_fusion.2
  122.6 0.8 bitcast_dynamic-update-slice_fusion.1
  123.4 1.9 bitcast_dynamic-update-slice_fusion
  125.3 34.6 %all-gather.5.cloned.1.call-done = f32[512,512]{1,0:T(8,128)} async-done(((f32[64,512]{1,0:T(8,128)}), f32[512,512]{1,0:T(8,128)}) %all-gather.5.cloned.1.call-update) | async-done | bytes 1048592 | tf_op jit(solution)/shard_map/all_gather | solution.py:165
  159.9 1.4 fusion.15
  161.3 1.8 fusion.3
  163.6 3.1 %fusion = bf16[1,64,8,4,128]{4,1,3,2,0:T(8,128)(2,1)S(1)} fusion(bf16[8,4,512,128]{3,2,1,0:T(8,128)(2,1)} %bitcast_dynamic-update-slice_fusion, f32[64,512]{1,0:T(8,128)S(1)} %get-tuple-element.40, f32[512]{0:T(512)S(1)} %copy-done.11, f32[64]{0:T(128)S(1)} %add_rsqrt_fusion, f32[64]{0:T(128)S(1)} %broadcast_multiply_fusion), kind=kOutput, calls=%fused_computation.1 | convolution fusion | flops 268828672 | bytes 4852224 | tf_op jit(solution)/shard_map/vtr,edrc->vtedc/dot_general | solution.py:174
  168.0 28.3 %all_to_all.5 = bf16[8,1,64,512]{3,2,1,0:T(8,128)(2,1)S(1)} all-to-all(bf16[8,1,64,512]{3,2,1,0:T(8,128)(2,1)S(1)} %copy.39), channel_id=1, replica_groups=mesh['seq_0'=4,'seq_1'=8,'head'=8,'var'=2] {'head'}, dimensions={0} | all-to-all | bytes 1048576 | tf_op jit(solution)/shard_map/all_to_all | solution.py:26
  (71 shorter events, 8.4 us)
Async XLA Ops:
  6.5 9.5 %copy-start = (bf16[1,2,512]{2,1,0:T(2,128)(2,1)S(1)}, bf16[1,2,512]{2,1,0:T(2,128)(2,1)}, u32[]{:S(2)}) copy-start(bf16[1,2,512]{2,1,0:T(2,128)(2,1)} %param.18) | copy-start | bytes 6148
  6.5 85.0 %all-gather.7.cloned.1.call-start = ((), (), s32[]{:S(2)}) async-start(), calls=%async_computation.2 | async-start | bytes 1327104 | tf_op jit(solution)/shard_map/all_gather | solution.py:153
  8.1 6.2 %collective-permute-start = (bf16[1,3,512]{2,1,0:T(4,128)(2,1)S(1)}, bf16[1,3,512]{2,1,0:T(4,128)(2,1)S(1)}, u32[]{:S(2)}, u32[]{:S(2)}) collective-permute-start(bf16[1,3,512]{2,1,0:T(4,128)(2,1)S(1)} %slice.135), channel_id=1, source_target_pairs={{0,16},{16,32},{32,48},{48,64},{64,80},{80,96},{96,112},{112,128},... | collective-permute-start | bytes 9224 | tf_op jit(solution)/shard_map/ppermute | solution.py:15
  24.1 135.8 %all-gather.5.cloned.1.call-start = ((), (), s32[]{:S(2)}) async-start(), calls=%async_computation.1 | async-start | bytes 1179648 | tf_op jit(solution)/shard_map/all_gather | solution.py:165
  24.1 8.0 %collective-permute-start.1 = (bf16[512,128]{1,0:T(8,128)(2,1)}, bf16[512,128]{1,0:T(8,128)(2,1)S(1)}, u32[]{:S(2)}, u32[]{:S(2)}) collective-permute-start(bf16[512,128]{1,0:T(8,128)(2,1)} %param.21), channel_id=1, source_target_pairs={{0,128},{128,256},{256,384},{384,0},{1,129},{129,257},{257,385},{3... | collective-permute-start | bytes 393224 | tf_op jit(solution)/shard_map/ppermute | solution.py:36
  28.3 5.9 %collective-permute-start.3 = (bf16[512,128]{1,0:T(8,128)(2,1)}, bf16[512,128]{1,0:T(8,128)(2,1)S(1)}, u32[]{:S(2)}, u32[]{:S(2)}) collective-permute-start(bf16[512,128]{1,0:T(8,128)(2,1)} %param.21), channel_id=1, source_target_pairs={{0,384},{128,0},{256,128},{384,256},{1,385},{129,1},{257,129},{385... | collective-permute-start | bytes 393224 | tf_op jit(solution)/shard_map/ppermute | solution.py:39
  32.1 7.9 %copy-start.4 = (bf16[512,128]{1,0:T(8,128)(2,1)}, bf16[512,128]{1,0:T(8,128)(2,1)S(1)}, u32[]{:S(2)}) copy-start(bf16[512,128]{1,0:T(8,128)(2,1)S(1)} %collective-permute-done.1) | copy-start | bytes 393220
  32.1 6.9 %collective-permute-start.2 = (bf16[512,128]{1,0:T(8,128)(2,1)S(1)}, bf16[512,128]{1,0:T(8,128)(2,1)S(1)}, u32[]{:S(2)}, u32[]{:S(2)}) collective-permute-start(bf16[512,128]{1,0:T(8,128)(2,1)S(1)} %collective-permute-done.1), channel_id=1, source_target_pairs={{0,128},{128,256},{256,384},{384,0},{1,129},{129,257},{257,385},{3... | collective-permute-start | bytes 393224 | tf_op jit(solution)/shard_map/ppermute | solution.py:36
  34.2 5.8 %copy-start.6 = (bf16[512,128]{1,0:T(8,128)(2,1)}, bf16[512,128]{1,0:T(8,128)(2,1)S(1)}, u32[]{:S(2)}) copy-start(bf16[512,128]{1,0:T(8,128)(2,1)S(1)} %collective-permute-done.3) | copy-start | bytes 393220
  39.0 1.0 copy-start.8
  40.1 18.2 %collective-permute-start.4 = (bf16[4,512,128]{2,1,0:T(8,128)(2,1)S(1)}, bf16[4,512,128]{2,1,0:T(8,128)(2,1)S(1)}, u32[]{:S(2)}, u32[]{:S(2)}) collective-permute-start(bf16[4,512,128]{2,1,0:T(8,128)(2,1)S(1)} %pad_maximum_fusion), channel_id=1, source_target_pairs={{0,16},{16,32},{32,48},{48,64},{64,80},{80,96},{96,112},{112,0},{1... | collective-permute-start | bytes 1572872 | tf_op jit(solution)/shard_map/ppermute | solution.py:36
  42.4 17.8 %collective-permute-start.8 = (bf16[4,512,128]{2,1,0:T(8,128)(2,1)S(1)}, bf16[4,512,128]{2,1,0:T(8,128)(2,1)S(1)}, u32[]{:S(2)}, u32[]{:S(2)}) collective-permute-start(bf16[4,512,128]{2,1,0:T(8,128)(2,1)S(1)} %pad_maximum_fusion), channel_id=1, source_target_pairs={{0,112},{16,0},{32,16},{48,32},{64,48},{80,64},{96,80},{112,96},{1... | collective-permute-start | bytes 1572872 | tf_op jit(solution)/shard_map/ppermute | solution.py:39
  58.3 15.9 %collective-permute-start.5 = (bf16[4,512,128]{2,1,0:T(8,128)(2,1)S(1)}, bf16[4,512,128]{2,1,0:T(8,128)(2,1)S(1)}, u32[]{:S(2)}, u32[]{:S(2)}) collective-permute-start(bf16[4,512,128]{2,1,0:T(8,128)(2,1)S(1)} %collective-permute-done.4), channel_id=1, source_target_pairs={{0,16},{16,32},{32,48},{48,64},{64,80},{80,96},{96,112},{112,0},{1... | collective-permute-start | bytes 1572872 | tf_op jit(solution)/shard_map/ppermute | solution.py:36
  60.2 19.9 %collective-permute-start.9 = (bf16[4,512,128]{2,1,0:T(8,128)(2,1)S(1)}, bf16[4,512,128]{2,1,0:T(8,128)(2,1)S(1)}, u32[]{:S(2)}, u32[]{:S(2)}) collective-permute-start(bf16[4,512,128]{2,1,0:T(8,128)(2,1)S(1)} %collective-permute-done.8), channel_id=1, source_target_pairs={{0,112},{16,0},{32,16},{48,32},{64,48},{80,64},{96,80},{112,96},{1... | collective-permute-start | bytes 1572872 | tf_op jit(solution)/shard_map/ppermute | solution.py:39
  74.2 19.5 %copy-start.1 = (bf16[4,512,128]{2,1,0:T(8,128)(2,1)}, bf16[4,512,128]{2,1,0:T(8,128)(2,1)S(1)}, u32[]{:S(2)}) copy-start(bf16[4,512,128]{2,1,0:T(8,128)(2,1)S(1)} %collective-permute-done.5) | copy-start | bytes 1572868
  74.2 13.2 %collective-permute-start.6 = (bf16[4,512,128]{2,1,0:T(8,128)(2,1)S(1)}, bf16[4,512,128]{2,1,0:T(8,128)(2,1)}, u32[]{:S(2)}, u32[]{:S(2)}) collective-permute-start(bf16[4,512,128]{2,1,0:T(8,128)(2,1)S(1)} %collective-permute-done.5), channel_id=1, source_target_pairs={{0,16},{16,32},{32,48},{48,64},{64,80},{80,96},{96,112},{112,0},{1... | collective-permute-start | bytes 1572872 | tf_op jit(solution)/shard_map/ppermute | solution.py:36
  80.1 43.3 %collective-permute-start.10 = (bf16[4,512,128]{2,1,0:T(8,128)(2,1)S(1)}, bf16[4,512,128]{2,1,0:T(8,128)(2,1)}, u32[]{:S(2)}, u32[]{:S(2)}) collective-permute-start(bf16[4,512,128]{2,1,0:T(8,128)(2,1)S(1)} %collective-permute-done.9), channel_id=1, source_target_pairs={{0,112},{16,0},{32,16},{48,32},{64,48},{80,64},{96,80},{112,96},{1... | collective-permute-start | bytes 1572872 | tf_op jit(solution)/shard_map/ppermute | solution.py:39
  87.3 27.1 %collective-permute-start.7 = (bf16[4,512,128]{2,1,0:T(8,128)(2,1)}, bf16[4,512,128]{2,1,0:T(8,128)(2,1)}, u32[]{:S(2)}, u32[]{:S(2)}) collective-permute-start(bf16[4,512,128]{2,1,0:T(8,128)(2,1)} %collective-permute-done.6), channel_id=1, source_target_pairs={{0,16},{16,32},{32,48},{48,64},{64,80},{80,96},{96,112},{112,0},{1... | collective-permute-start | bytes 1572872 | tf_op jit(solution)/shard_map/ppermute | solution.py:36
  113.5 7.4 %copy-start.3 = (bf16[512,128]{1,0:T(8,128)(2,1)S(1)}, bf16[512,128]{1,0:T(8,128)(2,1)}, u32[]{:S(2)}) copy-start(bf16[512,128]{1,0:T(8,128)(2,1)} %param.21) | copy-start | bytes 393220
  113.9 7.0 %copy-start.5 = (bf16[512,128]{1,0:T(8,128)(2,1)S(1)}, bf16[512,128]{1,0:T(8,128)(2,1)}, u32[]{:S(2)}) copy-start(bf16[512,128]{1,0:T(8,128)(2,1)} %copy-done.4) | copy-start | bytes 393220
  113.9 7.0 %copy-start.7 = (bf16[512,128]{1,0:T(8,128)(2,1)S(1)}, bf16[512,128]{1,0:T(8,128)(2,1)}, u32[]{:S(2)}) copy-start(bf16[512,128]{1,0:T(8,128)(2,1)} %copy-done.6) | copy-start | bytes 393220
  113.9 7.0 %copy-start.9 = (bf16[512,128]{1,0:T(8,128)(2,1)S(1)}, bf16[512,128]{1,0:T(8,128)(2,1)}, u32[]{:S(2)}) copy-start(bf16[512,128]{1,0:T(8,128)(2,1)} %copy-done.8) | copy-start | bytes 393220
  120.1 43.0 %copy-start.2 = (f32[64,512]{1,0:T(8,128)S(1)}, f32[64,512]{1,0:T(8,128)}, u32[]{:S(2)}) copy-start(f32[64,512]{1,0:T(8,128)} %fusion.6) | copy-start | bytes 393220
  120.9 42.7 %copy-start.11 = (f32[512]{0:T(512)S(1)}, f32[512]{0:T(512)}, u32[]{:S(2)}) copy-start(f32[512]{0:T(512)} %param.20) | copy-start | bytes 6148
  166.7 29.7 %copy-start.10 = (bf16[64,512]{1,0:T(8,128)(2,1)S(1)}, bf16[64,512]{1,0:T(8,128)(2,1)}, u32[]{:S(2)}) copy-start(bf16[64,512]{1,0:T(8,128)(2,1)} %param.14) | copy-start | bytes 196612
Sparse Core Ops, SparseCore 0:
  24.2 45.2 all-gather.6
  113.6 46.1 all-gather.4

commit v4 on v2

--- a/solution.py
+++ b/solution.py
@@ -25,6 +25,17 @@
     blocks = split_up(x, dim, lax.axis_size(axis))
     arrived = lax.all_to_all(blocks, axis, split_axis=0, concat_axis=0, tiled=True)
     return arrived.astype(jnp.float32).sum(axis=0)
+
+
+def exchanged_and_summed(x, axis, dim):
+    count = lax.axis_size(axis)
+    blocks = split_up(x, dim, count)
+    turned = jnp.roll(blocks, -lax.axis_index(axis), axis=0)
+    total = turned[0].astype(jnp.float32)
+    for k in range(1, count):
+        moved = lax.ppermute(turned[k], axis, [(i, (i + k) % count) for i in range(count)])
+        total = total + moved.astype(jnp.float32)
+    return total
 
 
 def ring_pieces(x, axis, count):
@@ -145,7 +156,7 @@
     head_terms = jnp.roll(head_terms, lax.axis_index(SEQ[1]) - inner_size // 2, axis=2)
     head_terms = jnp.roll(head_terms, lax.axis_index(SEQ[0]) - outer // 2, axis=3)
     head_terms = jnp.swapaxes(head_terms, 2, 3).reshape(*normed.shape[:2], -1)
-    summed = sent_and_summed(head_terms, "head", 2)
+    summed = exchanged_and_summed(head_terms, "head", 2)
     return (residual_in[None, :, :].astype(jnp.float32) + summed).astype(jnp.bfloat16)
 
 

time: 176 us -> 196 us (1.11)
  starting transfers between devices: 35.7 us -> 69.4 us
  blocking collectives: 27.3 us -> 0 us
  waiting for transfers between devices: 57.8 us -> 71 us
    ppermute x0 -> x7, starting transfers between devices: none -> 33.7 us  [exchanged_and_summed(): lax.ppermute(turned[k], axis, [(i, (i + k) % count) for i in range(count)])]
    all_to_all x1 -> x0, blocking collectives: 27.3 us -> none  [sent_and_summed(): lax.all_to_all(blocks, axis, split_axis=0, concat_axis=0, tiled=True)]
    ppermute x0 -> x7, waiting for transfers between devices: none -> 13.2 us  [exchanged_and_summed(): lax.ppermute(turned[k], axis, [(i, (i + k) % count) for i in range(count)])]
  transfers between devices with their start and end apart: 12 -> 19, of which waited for: 8 -> 12; matrix products, arithmetic and copies ran while one was open for 6% -> 6% of each run, Pallas kernels for 0% -> 0%
where the time goes in v4:
time: 196 us; the launch traced here: 195 us
  waiting for transfers between devices  71 us (36%)
  starting transfers between devices  69.4 us (35%)
  between operations  18.6 us (9%)
  local copies, waits for them, and re-layouts  16 us (8%)
  matrix products  11.3 us (6%)
  other arithmetic  8.43 us (4%)
    ppermute x6, waiting for transfers between devices, ring_pieces(): forward = lax.ppermute(forward, axis, ahead)  42.9 us
    ppermute x7, starting transfers between devices, exchanged_and_summed(): lax.ppermute(turned[k], axis, [(i, (i + k) % count) for i in range(count)])  33.7 us
    ppermute x6, starting transfers between devices, ring_pieces(): forward = lax.ppermute(forward, axis, ahead)  19 us
    all_gather x1, waiting for transfers between devices, body(): gathered = lax.all_gather(packed, SEQ, axis=0, tiled=False)  14.5 us
    ppermute x7, waiting for transfers between devices, exchanged_and_summed(): lax.ppermute(turned[k], axis, [(i, (i + k) % count) for i in range(count)])  13.2 us
    ppermute x4, starting transfers between devices, ring_pieces(): backward = lax.ppermute(backward, axis, behind)  12.7 us
    unnamed x29, local copies, waits for them, and re-layouts  5.2 us
    ppermute x1, starting transfers between devices, from_behind(): lax.ppermute(value, axis, [(source, source + steps) for source in range(i...  4.02 us
  transfers between devices with their start and end apart: 19, of which 12 were waited for; matrix products, arithmetic and copies ran while one was open for 6% of the time, Pallas kernels for 0%

profile of v4, /device:TPU:1, one launch (start us, length us, event | category | flops | bytes accessed | tf_op | source)
XLA Modules:
  0.0 194.8 jit_solution(8467813589799109394)
XLA Ops:
  7.2 0.9 multiply_bitcast_fusion
  8.1 4.0 %collective-permute-start = (bf16[1,3,512]{2,1,0:T(4,128)(2,1)S(1)}, bf16[1,3,512]{2,1,0:T(4,128)(2,1)S(1)}, u32[]{:S(2)}, u32[]{:S(2)}) collective-permute-start(bf16[1,3,512]{2,1,0:T(4,128)(2,1)S(1)} %slice.137), channel_id=1, source_target_pairs={{0,16},{16,32},{32,48},{48,64},{64,80},{80,96},{96,112},{112,128},... | collective-permute-start | bytes 9224 | tf_op jit(solution)/shard_map/ppermute | solution.py:15
  12.2 1.3 convolution_convert_fusion.1
  13.5 0.9 fusion.72
  21.4 1.5 convolution_bitcast_fusion
  23.8 4.2 %collective-permute-start.1 = (bf16[512,128]{1,0:T(8,128)(2,1)}, bf16[512,128]{1,0:T(8,128)(2,1)S(1)}, u32[]{:S(2)}, u32[]{:S(2)}) collective-permute-start(bf16[512,128]{1,0:T(8,128)(2,1)} %param.19), channel_id=1, source_target_pairs={{0,128},{128,256},{256,384},{384,0},{1,129},{129,257},{257,385},{3... | collective-permute-start | bytes 393224 | tf_op jit(solution)/shard_map/ppermute | solution.py:47
  28.0 3.2 %collective-permute-start.3 = (bf16[512,128]{1,0:T(8,128)(2,1)}, bf16[512,128]{1,0:T(8,128)(2,1)S(1)}, u32[]{:S(2)}, u32[]{:S(2)}) collective-permute-start(bf16[512,128]{1,0:T(8,128)(2,1)} %param.19), channel_id=1, source_target_pairs={{0,384},{128,0},{256,128},{384,256},{1,385},{129,1},{257,129},{385... | collective-permute-start | bytes 393224 | tf_op jit(solution)/shard_map/ppermute | solution.py:50
  31.8 2.1 %collective-permute-start.2 = (bf16[512,128]{1,0:T(8,128)(2,1)S(1)}, bf16[512,128]{1,0:T(8,128)(2,1)S(1)}, u32[]{:S(2)}, u32[]{:S(2)}) collective-permute-start(bf16[512,128]{1,0:T(8,128)(2,1)S(1)} %collective-permute-done.1), channel_id=1, source_target_pairs={{0,128},{128,256},{256,384},{384,0},{1,129},{129,257},{257,385},{3... | collective-permute-start | bytes 393224 | tf_op jit(solution)/shard_map/ppermute | solution.py:47
  33.9 4.8 %collective-permute-done.2 = bf16[512,128]{1,0:T(8,128)(2,1)S(1)} collective-permute-done((bf16[512,128]{1,0:T(8,128)(2,1)S(1)}, bf16[512,128]{1,0:T(8,128)(2,1)S(1)}, u32[]{:S(2)}, u32[]{:S(2)}) %collective-permute-start.2) | collective-permute-done | bytes 131104 | tf_op jit(solution)/shard_map/ppermute | solution.py:47
  38.7 1.0 pad_maximum_fusion
  39.7 2.4 %collective-permute-start.4 = (bf16[4,512,128]{2,1,0:T(8,128)(2,1)S(1)}, bf16[4,512,128]{2,1,0:T(8,128)(2,1)S(1)}, u32[]{:S(2)}, u32[]{:S(2)}) collective-permute-start(bf16[4,512,128]{2,1,0:T(8,128)(2,1)S(1)} %pad_maximum_fusion), channel_id=1, source_target_pairs={{0,16},{16,32},{32,48},{48,64},{64,80},{80,96},{96,112},{112,0},{1... | collective-permute-start | bytes 1572872 | tf_op jit(solution)/shard_map/ppermute | solution.py:47
  42.1 10.2 %collective-permute-done.4 = bf16[4,512,128]{2,1,0:T(8,128)(2,1)S(1)} collective-permute-done((bf16[4,512,128]{2,1,0:T(8,128)(2,1)S(1)}, bf16[4,512,128]{2,1,0:T(8,128)(2,1)S(1)}, u32[]{:S(2)}, u32[]{:S(2)}) %collective-permute-start.4) | collective-permute-done | bytes 524320 | tf_op jit(solution)/shard_map/ppermute | solution.py:47
  52.3 1.9 collective-permute-start.5
  54.3 4.6 %collective-permute-start.8 = (bf16[4,512,128]{2,1,0:T(8,128)(2,1)S(1)}, bf16[4,512,128]{2,1,0:T(8,128)(2,1)S(1)}, u32[]{:S(2)}, u32[]{:S(2)}) collective-permute-start(bf16[4,512,128]{2,1,0:T(8,128)(2,1)S(1)} %pad_maximum_fusion), channel_id=1, source_target_pairs={{0,112},{16,0},{32,16},{48,32},{64,48},{80,64},{96,80},{112,96},{1... | collective-permute-start | bytes 1572872 | tf_op jit(solution)/shard_map/ppermute | solution.py:50
  58.8 7.7 %collective-permute-done.5 = bf16[4,512,128]{2,1,0:T(8,128)(2,1)S(1)} collective-permute-done((bf16[4,512,128]{2,1,0:T(8,128)(2,1)S(1)}, bf16[4,512,128]{2,1,0:T(8,128)(2,1)S(1)}, u32[]{:S(2)}, u32[]{:S(2)}) %collective-permute-start.5) | collective-permute-done | bytes 524320 | tf_op jit(solution)/shard_map/ppermute | solution.py:47
  66.5 4.9 %collective-permute-start.6 = (bf16[4,512,128]{2,1,0:T(8,128)(2,1)S(1)}, bf16[4,512,128]{2,1,0:T(8,128)(2,1)S(1)}, u32[]{:S(2)}, u32[]{:S(2)}) collective-permute-start(bf16[4,512,128]{2,1,0:T(8,128)(2,1)S(1)} %collective-permute-done.5), channel_id=1, source_target_pairs={{0,16},{16,32},{32,48},{48,64},{64,80},{80,96},{96,112},{112,0},{1... | collective-permute-start | bytes 1572872 | tf_op jit(solution)/shard_map/ppermute | solution.py:47
  71.4 1.9 collective-permute-start.9
  73.4 5.7 %collective-permute-done.6 = bf16[4,512,128]{2,1,0:T(8,128)(2,1)S(1)} collective-permute-done((bf16[4,512,128]{2,1,0:T(8,128)(2,1)S(1)}, bf16[4,512,128]{2,1,0:T(8,128)(2,1)S(1)}, u32[]{:S(2)}, u32[]{:S(2)}) %collective-permute-start.6) | collective-permute-done | bytes 524320 | tf_op jit(solution)/shard_map/ppermute | solution.py:47
  79.0 3.6 %collective-permute-start.7 = (bf16[4,512,128]{2,1,0:T(8,128)(2,1)S(1)}, bf16[4,512,128]{2,1,0:T(8,128)(2,1)S(1)}, u32[]{:S(2)}, u32[]{:S(2)}) collective-permute-start(bf16[4,512,128]{2,1,0:T(8,128)(2,1)S(1)} %collective-permute-done.6), channel_id=1, source_target_pairs={{0,16},{16,32},{32,48},{48,64},{64,80},{80,96},{96,112},{112,0},{1... | collective-permute-start | bytes 1572872 | tf_op jit(solution)/shard_map/ppermute | solution.py:47
  82.7 1.1 fusion.3
  83.9 3.0 %collective-permute-start.10 = (bf16[4,512,128]{2,1,0:T(8,128)(2,1)S(1)}, bf16[4,512,128]{2,1,0:T(8,128)(2,1)S(1)}, u32[]{:S(2)}, u32[]{:S(2)}) collective-permute-start(bf16[4,512,128]{2,1,0:T(8,128)(2,1)S(1)} %collective-permute-done.9), channel_id=1, source_target_pairs={{0,112},{16,0},{32,16},{48,32},{64,48},{80,64},{96,80},{112,96},{1... | collective-permute-start | bytes 1572872 | tf_op jit(solution)/shard_map/ppermute | solution.py:50
  86.9 13.9 %collective-permute-done.7 = bf16[4,512,128]{2,1,0:T(8,128)(2,1)S(1)} collective-permute-done((bf16[4,512,128]{2,1,0:T(8,128)(2,1)S(1)}, bf16[4,512,128]{2,1,0:T(8,128)(2,1)S(1)}, u32[]{:S(2)}, u32[]{:S(2)}) %collective-permute-start.7) | collective-permute-done | bytes 524320 | tf_op jit(solution)/shard_map/ppermute | solution.py:47
  100.8 0.8 bitcast_dynamic-update-slice_fusion.7
  101.6 0.8 bitcast_dynamic-update-slice_fusion.6
  102.5 0.8 bitcast_dynamic-update-slice_fusion.5
  103.3 0.8 bitcast_dynamic-update-slice_fusion.4
  104.2 0.8 bitcast_dynamic-update-slice_fusion.3
  105.0 0.8 bitcast_dynamic-update-slice_fusion.2
  105.9 0.9 bitcast_dynamic-update-slice_fusion.1
  107.1 0.9 bitcast_dynamic-update-slice_fusion
  108.0 14.5 %all-gather.3.cloned.1.call-done = bf16[4608,512]{1,0:T(8,128)(2,1)} async-done(((bf16[144,512]{1,0:T(8,128)(2,1)}), bf16[4608,512]{1,0:T(8,128)(2,1)}) %all-gather.3.cloned.1.call-update) | async-done | bytes 4718608 | tf_op jit(solution)/shard_map/all_gather | solution.py:144
  122.5 0.8 slice.147
  123.3 3.9 %fusion.71 = (bf16[32,64,512]{2,1,0:T(8,128)(2,1)}, bf16[32,64,512]{2,1,0:T(8,128)(2,1)S(1)}) fusion(bf16[32,144,512]{2,1,0:T(8,128)(2,1)} %bitcast.140), kind=kLoop, calls=%fused_computation.125 | loop fusion | bytes 8388608 | tf_op jit(solution)/shard_map/slice | solution.py:75
  129.3 1.2 broadcast_in_dim.20
  130.5 2.4 %convolution_multiply_fusion = f32[64,2048]{1,0:T(8,128)S(1)} fusion(f32[64,2048]{1,0:T(8,128)} %broadcast_in_dim.20, bf16[2048,512]{1,0:T(8,128)(2,1)} %bitcast.138, f32[1,64,1024]{2,1,0:T(8,128)S(1)} %convolution_bitcast_fusion), kind=kOutput, calls=%fused_computation | convolution fusion | flops 134348800 | bytes 3211264 | tf_op jit(solution)/shard_map/vtd,sd->vts/dot_general | solution.py:86
  134.2 3.1 %fusion = bf16[1,64,8,4,128]{4,1,3,2,0:T(8,128)(2,1)S(1)} fusion(bf16[8,4,512,128]{3,2,1,0:T(8,128)(2,1)} %bitcast_dynamic-update-slice_fusion, f32[64,512]{1,0:T(8,128)S(1)} %get-tuple-element.35, f32[512]{0:T(512)S(1)} %copy-done.10, f32[64]{0:T(128)S(1)} %add_rsqrt_fusion, f32[64]{0:T(128)S(1)} %broadcast_multiply_fusion), kind=kOutput, calls=%fused_computation.2 | convolution fusion | flops 268828672 | bytes 4852224 | tf_op jit(solution)/shard_map/vtr,edrc->vtedc/dot_general | solution.py:152
  138.8 0.8 slice_bitcast_fusion.6
  139.6 7.2 %collective-permute-start.11 = (bf16[1,64,512]{2,0,1:T(2,128)(2,1)S(1)}, bf16[1,64,512]{2,0,1:T(2,128)(2,1)S(1)}, u32[]{:S(2)}, u32[]{:S(2)}) collective-permute-start(bf16[1,64,512]{2,0,1:T(2,128)(2,1)S(1)} %get-tuple-element.21), channel_id=1, source_target_pairs={{0,2},{2,4},{4,6},{6,8},{8,10},{10,12},{12,14},{14,0},{1,3},{3,5},... | collective-permute-start | bytes 196616 | tf_op jit(solution)/shard_map/ppermute | solution.py:36
  146.8 5.7 %collective-permute-start.12 = (bf16[1,64,512]{2,0,1:T(2,128)(2,1)S(1)}, bf16[1,64,512]{2,0,1:T(2,128)(2,1)S(1)}, u32[]{:S(2)}, u32[]{:S(2)}) collective-permute-start(bf16[1,64,512]{2,0,1:T(2,128)(2,1)S(1)} %get-tuple-element.26), channel_id=1, source_target_pairs={{0,4},{2,6},{4,8},{6,10},{8,12},{10,14},{12,0},{14,2},{1,5},{3,7},... | collective-permute-start | bytes 196616 | tf_op jit(solution)/shard_map/ppermute | solution.py:36
  152.5 7.0 %collective-permute-start.13 = (bf16[1,64,512]{2,0,1:T(2,128)(2,1)S(1)}, bf16[1,64,512]{2,0,1:T(2,128)(2,1)S(1)}, u32[]{:S(2)}, u32[]{:S(2)}) collective-permute-start(bf16[1,64,512]{2,0,1:T(2,128)(2,1)S(1)} %get-tuple-element.25), channel_id=1, source_target_pairs={{0,6},{2,8},{4,10},{6,12},{8,14},{10,0},{12,2},{14,4},{1,7},{3,9},... | collective-permute-start | bytes 196616 | tf_op jit(solution)/shard_map/ppermute | solution.py:36
  159.5 1.9 collective-permute-start.14
  161.4 5.8 %collective-permute-start.15 = (bf16[1,64,512]{2,0,1:T(2,128)(2,1)S(1)}, bf16[1,64,512]{2,0,1:T(2,128)(2,1)S(1)}, u32[]{:S(2)}, u32[]{:S(2)}) collective-permute-start(bf16[1,64,512]{2,0,1:T(2,128)(2,1)S(1)} %get-tuple-element.23), channel_id=1, source_target_pairs={{0,10},{2,12},{4,14},{6,0},{8,2},{10,4},{12,6},{14,8},{1,11},{3,13... | collective-permute-start | bytes 196616 | tf_op jit(solution)/shard_map/ppermute | solution.py:36
  167.2 4.3 %collective-permute-start.16 = (bf16[1,64,512]{2,0,1:T(2,128)(2,1)S(1)}, bf16[1,64,512]{2,0,1:T(2,128)(2,1)S(1)}, u32[]{:S(2)}, u32[]{:S(2)}) collective-permute-start(bf16[1,64,512]{2,0,1:T(2,128)(2,1)S(1)} %get-tuple-element.22), channel_id=1, source_target_pairs={{0,12},{2,14},{4,0},{6,2},{8,4},{10,6},{12,8},{14,10},{1,13},{3,15... | collective-permute-start | bytes 196616 | tf_op jit(solution)/shard_map/ppermute | solution.py:36
  171.5 1.9 collective-permute-start.17
  173.5 1.2 collective-permute-done.14
  174.6 4.3 %collective-permute-done.15 = bf16[1,64,512]{2,0,1:T(2,128)(2,1)S(1)} collective-permute-done((bf16[1,64,512]{2,0,1:T(2,128)(2,1)S(1)}, bf16[1,64,512]{2,0,1:T(2,128)(2,1)S(1)}, u32[]{:S(2)}, u32[]{:S(2)}) %collective-permute-start.15) | collective-permute-done | bytes 65568 | tf_op jit(solution)/shard_map/ppermute | solution.py:36
  178.9 6.3 %collective-permute-done.16 = bf16[1,64,512]{2,0,1:T(2,128)(2,1)S(1)} collective-permute-done((bf16[1,64,512]{2,0,1:T(2,128)(2,1)S(1)}, bf16[1,64,512]{2,0,1:T(2,128)(2,1)S(1)}, u32[]{:S(2)}, u32[]{:S(2)}) %collective-permute-start.16) | collective-permute-done | bytes 65568 | tf_op jit(solution)/shard_map/ppermute | solution.py:36
  185.3 1.4 collective-permute-done.17
  (67 shorter events, 10.9 us)
Async XLA Ops:
  6.5 8.0 %copy-start = (bf16[1,2,512]{2,1,0:T(2,128)(2,1)S(1)}, bf16[1,2,512]{2,1,0:T(2,128)(2,1)}, u32[]{:S(2)}) copy-start(bf16[1,2,512]{2,1,0:T(2,128)(2,1)} %param.16) | copy-start | bytes 6148
  6.5 115.9 %all-gather.3.cloned.1.call-start = ((), (), s32[]{:S(2)}) async-start(), calls=%async_computation | async-start | bytes 4866048 | tf_op jit(solution)/shard_map/all_gather | solution.py:144
  8.1 6.2 %collective-permute-start = (bf16[1,3,512]{2,1,0:T(4,128)(2,1)S(1)}, bf16[1,3,512]{2,1,0:T(4,128)(2,1)S(1)}, u32[]{:S(2)}, u32[]{:S(2)}) collective-permute-start(bf16[1,3,512]{2,1,0:T(4,128)(2,1)S(1)} %slice.137), channel_id=1, source_target_pairs={{0,16},{16,32},{32,48},{48,64},{64,80},{80,96},{96,112},{112,128},... | collective-permute-start | bytes 9224 | tf_op jit(solution)/shard_map/ppermute | solution.py:15
  13.5 25.2 %copy-start.8 = (bf16[64,512]{1,0:T(8,128)(2,1)}, bf16[64,512]{1,0:T(8,128)(2,1)S(1)}, u32[]{:S(2)}) copy-start(bf16[64,512]{1,0:T(8,128)(2,1)S(1)} %convolution_convert_fusion.1) | copy-start | bytes 196612
  23.8 8.0 %collective-permute-start.1 = (bf16[512,128]{1,0:T(8,128)(2,1)}, bf16[512,128]{1,0:T(8,128)(2,1)S(1)}, u32[]{:S(2)}, u32[]{:S(2)}) collective-permute-start(bf16[512,128]{1,0:T(8,128)(2,1)} %param.19), channel_id=1, source_target_pairs={{0,128},{128,256},{256,384},{384,0},{1,129},{129,257},{257,385},{3... | collective-permute-start | bytes 393224 | tf_op jit(solution)/shard_map/ppermute | solution.py:47
  28.0 5.9 %collective-permute-start.3 = (bf16[512,128]{1,0:T(8,128)(2,1)}, bf16[512,128]{1,0:T(8,128)(2,1)S(1)}, u32[]{:S(2)}, u32[]{:S(2)}) collective-permute-start(bf16[512,128]{1,0:T(8,128)(2,1)} %param.19), channel_id=1, source_target_pairs={{0,384},{128,0},{256,128},{384,256},{1,385},{129,1},{257,129},{385... | collective-permute-start | bytes 393224 | tf_op jit(solution)/shard_map/ppermute | solution.py:50
  31.8 47.2 %copy-start.2 = (bf16[512,128]{1,0:T(8,128)(2,1)}, bf16[512,128]{1,0:T(8,128)(2,1)S(1)}, u32[]{:S(2)}) copy-start(bf16[512,128]{1,0:T(8,128)(2,1)S(1)} %collective-permute-done.1) | copy-start | bytes 393220
  31.8 6.9 %collective-permute-start.2 = (bf16[512,128]{1,0:T(8,128)(2,1)S(1)}, bf16[512,128]{1,0:T(8,128)(2,1)S(1)}, u32[]{:S(2)}, u32[]{:S(2)}) collective-permute-start(bf16[512,128]{1,0:T(8,128)(2,1)S(1)} %collective-permute-done.1), channel_id=1, source_target_pairs={{0,128},{128,256},{256,384},{384,0},{1,129},{129,257},{257,385},{3... | collective-permute-start | bytes 393224 | tf_op jit(solution)/shard_map/ppermute | solution.py:47
  33.9 48.7 %copy-start.4 = (bf16[512,128]{1,0:T(8,128)(2,1)}, bf16[512,128]{1,0:T(8,128)(2,1)S(1)}, u32[]{:S(2)}) copy-start(bf16[512,128]{1,0:T(8,128)(2,1)S(1)} %collective-permute-done.3) | copy-start | bytes 393220
  38.7 43.9 %copy-start.6 = (bf16[512,128]{1,0:T(8,128)(2,1)}, bf16[512,128]{1,0:T(8,128)(2,1)S(1)}, u32[]{:S(2)}) copy-start(bf16[512,128]{1,0:T(8,128)(2,1)S(1)} %collective-permute-done.2) | copy-start | bytes 393220
  39.7 12.6 %collective-permute-start.4 = (bf16[4,512,128]{2,1,0:T(8,128)(2,1)S(1)}, bf16[4,512,128]{2,1,0:T(8,128)(2,1)S(1)}, u32[]{:S(2)}, u32[]{:S(2)}) collective-permute-start(bf16[4,512,128]{2,1,0:T(8,128)(2,1)S(1)} %pad_maximum_fusion), channel_id=1, source_target_pairs={{0,16},{16,32},{32,48},{48,64},{64,80},{80,96},{96,112},{112,0},{1... | collective-permute-start | bytes 1572872 | tf_op jit(solution)/shard_map/ppermute | solution.py:47
  52.3 14.2 %collective-permute-start.5 = (bf16[4,512,128]{2,1,0:T(8,128)(2,1)S(1)}, bf16[4,512,128]{2,1,0:T(8,128)(2,1)S(1)}, u32[]{:S(2)}, u32[]{:S(2)}) collective-permute-start(bf16[4,512,128]{2,1,0:T(8,128)(2,1)S(1)} %collective-permute-done.4), channel_id=1, source_target_pairs={{0,16},{16,32},{32,48},{48,64},{64,80},{80,96},{96,112},{112,0},{1... | collective-permute-start | bytes 1572872 | tf_op jit(solution)/shard_map/ppermute | solution.py:47
  54.3 17.2 %collective-permute-start.8 = (bf16[4,512,128]{2,1,0:T(8,128)(2,1)S(1)}, bf16[4,512,128]{2,1,0:T(8,128)(2,1)S(1)}, u32[]{:S(2)}, u32[]{:S(2)}) collective-permute-start(bf16[4,512,128]{2,1,0:T(8,128)(2,1)S(1)} %pad_maximum_fusion), channel_id=1, source_target_pairs={{0,112},{16,0},{32,16},{48,32},{64,48},{80,64},{96,80},{112,96},{1... | collective-permute-start | bytes 1572872 | tf_op jit(solution)/shard_map/ppermute | solution.py:50
  66.5 12.5 %collective-permute-start.6 = (bf16[4,512,128]{2,1,0:T(8,128)(2,1)S(1)}, bf16[4,512,128]{2,1,0:T(8,128)(2,1)S(1)}, u32[]{:S(2)}, u32[]{:S(2)}) collective-permute-start(bf16[4,512,128]{2,1,0:T(8,128)(2,1)S(1)} %collective-permute-done.5), channel_id=1, source_target_pairs={{0,16},{16,32},{32,48},{48,64},{64,80},{80,96},{96,112},{112,0},{1... | collective-permute-start | bytes 1572872 | tf_op jit(solution)/shard_map/ppermute | solution.py:47
  71.4 12.4 %collective-permute-start.9 = (bf16[4,512,128]{2,1,0:T(8,128)(2,1)S(1)}, bf16[4,512,128]{2,1,0:T(8,128)(2,1)S(1)}, u32[]{:S(2)}, u32[]{:S(2)}) collective-permute-start(bf16[4,512,128]{2,1,0:T(8,128)(2,1)S(1)} %collective-permute-done.8), channel_id=1, source_target_pairs={{0,112},{16,0},{32,16},{48,32},{64,48},{80,64},{96,80},{112,96},{1... | collective-permute-start | bytes 1572872 | tf_op jit(solution)/shard_map/ppermute | solution.py:50
  79.0 21.8 %collective-permute-start.7 = (bf16[4,512,128]{2,1,0:T(8,128)(2,1)S(1)}, bf16[4,512,128]{2,1,0:T(8,128)(2,1)S(1)}, u32[]{:S(2)}, u32[]{:S(2)}) collective-permute-start(bf16[4,512,128]{2,1,0:T(8,128)(2,1)S(1)} %collective-permute-done.6), channel_id=1, source_target_pairs={{0,16},{16,32},{32,48},{48,64},{64,80},{80,96},{96,112},{112,0},{1... | collective-permute-start | bytes 1572872 | tf_op jit(solution)/shard_map/ppermute | solution.py:47
  83.8 20.3 %copy-start.1 = (bf16[512,128]{1,0:T(8,128)(2,1)S(1)}, bf16[512,128]{1,0:T(8,128)(2,1)}, u32[]{:S(2)}) copy-start(bf16[512,128]{1,0:T(8,128)(2,1)} %param.19) | copy-start | bytes 393220
  83.9 20.3 %copy-start.3 = (bf16[512,128]{1,0:T(8,128)(2,1)S(1)}, bf16[512,128]{1,0:T(8,128)(2,1)}, u32[]{:S(2)}) copy-start(bf16[512,128]{1,0:T(8,128)(2,1)} %copy-done.2) | copy-start | bytes 393220
  83.9 20.3 %copy-start.5 = (bf16[512,128]{1,0:T(8,128)(2,1)S(1)}, bf16[512,128]{1,0:T(8,128)(2,1)}, u32[]{:S(2)}) copy-start(bf16[512,128]{1,0:T(8,128)(2,1)} %copy-done.4) | copy-start | bytes 393220
  83.9 20.3 %copy-start.7 = (bf16[512,128]{1,0:T(8,128)(2,1)S(1)}, bf16[512,128]{1,0:T(8,128)(2,1)}, u32[]{:S(2)}) copy-start(bf16[512,128]{1,0:T(8,128)(2,1)} %copy-done.6) | copy-start | bytes 393220
  83.9 23.2 %collective-permute-start.10 = (bf16[4,512,128]{2,1,0:T(8,128)(2,1)S(1)}, bf16[4,512,128]{2,1,0:T(8,128)(2,1)S(1)}, u32[]{:S(2)}, u32[]{:S(2)}) collective-permute-start(bf16[4,512,128]{2,1,0:T(8,128)(2,1)S(1)} %collective-permute-done.9), channel_id=1, source_target_pairs={{0,112},{16,0},{32,16},{48,32},{64,48},{80,64},{96,80},{112,96},{1... | collective-permute-start | bytes 1572872 | tf_op jit(solution)/shard_map/ppermute | solution.py:50
  130.5 3.7 %copy-start.10 = (f32[512]{0:T(512)S(1)}, f32[512]{0:T(512)}, u32[]{:S(2)}) copy-start(f32[512]{0:T(512)} %param.18) | copy-start | bytes 6148
  137.3 36.1 %copy-start.9 = (bf16[64,512]{1,0:T(8,128)(2,1)S(1)}, bf16[64,512]{1,0:T(8,128)(2,1)}, u32[]{:S(2)}) copy-start(bf16[64,512]{1,0:T(8,128)(2,1)} %param.12) | copy-start | bytes 196612
  139.6 27.6 %collective-permute-start.11 = (bf16[1,64,512]{2,0,1:T(2,128)(2,1)S(1)}, bf16[1,64,512]{2,0,1:T(2,128)(2,1)S(1)}, u32[]{:S(2)}, u32[]{:S(2)}) collective-permute-start(bf16[1,64,512]{2,0,1:T(2,128)(2,1)S(1)} %get-tuple-element.21), channel_id=1, source_target_pairs={{0,2},{2,4},{4,6},{6,8},{8,10},{10,12},{12,14},{14,0},{1,3},{3,5},... | collective-permute-start | bytes 196616 | tf_op jit(solution)/shard_map/ppermute | solution.py:36
  146.8 24.7 %collective-permute-start.12 = (bf16[1,64,512]{2,0,1:T(2,128)(2,1)S(1)}, bf16[1,64,512]{2,0,1:T(2,128)(2,1)S(1)}, u32[]{:S(2)}, u32[]{:S(2)}) collective-permute-start(bf16[1,64,512]{2,0,1:T(2,128)(2,1)S(1)} %get-tuple-element.26), channel_id=1, source_target_pairs={{0,4},{2,6},{4,8},{6,10},{8,12},{10,14},{12,0},{14,2},{1,5},{3,7},... | collective-permute-start | bytes 196616 | tf_op jit(solution)/shard_map/ppermute | solution.py:36
  152.5 20.9 %collective-permute-start.13 = (bf16[1,64,512]{2,0,1:T(2,128)(2,1)S(1)}, bf16[1,64,512]{2,0,1:T(2,128)(2,1)S(1)}, u32[]{:S(2)}, u32[]{:S(2)}) collective-permute-start(bf16[1,64,512]{2,0,1:T(2,128)(2,1)S(1)} %get-tuple-element.25), channel_id=1, source_target_pairs={{0,6},{2,8},{4,10},{6,12},{8,14},{10,0},{12,2},{14,4},{1,7},{3,9},... | collective-permute-start | bytes 196616 | tf_op jit(solution)/shard_map/ppermute | solution.py:36
  159.5 15.1 %collective-permute-start.14 = (bf16[1,64,512]{2,0,1:T(2,128)(2,1)S(1)}, bf16[1,64,512]{2,0,1:T(2,128)(2,1)S(1)}, u32[]{:S(2)}, u32[]{:S(2)}) collective-permute-start(bf16[1,64,512]{2,0,1:T(2,128)(2,1)S(1)} %get-tuple-element.24), channel_id=1, source_target_pairs={{0,8},{2,10},{4,12},{6,14},{8,0},{10,2},{12,4},{14,6},{1,9},{3,11}... | collective-permute-start | bytes 196616 | tf_op jit(solution)/shard_map/ppermute | solution.py:36
  161.4 17.5 %collective-permute-start.15 = (bf16[1,64,512]{2,0,1:T(2,128)(2,1)S(1)}, bf16[1,64,512]{2,0,1:T(2,128)(2,1)S(1)}, u32[]{:S(2)}, u32[]{:S(2)}) collective-permute-start(bf16[1,64,512]{2,0,1:T(2,128)(2,1)S(1)} %get-tuple-element.23), channel_id=1, source_target_pairs={{0,10},{2,12},{4,14},{6,0},{8,2},{10,4},{12,6},{14,8},{1,11},{3,13... | collective-permute-start | bytes 196616 | tf_op jit(solution)/shard_map/ppermute | solution.py:36
  167.2 18.1 %collective-permute-start.16 = (bf16[1,64,512]{2,0,1:T(2,128)(2,1)S(1)}, bf16[1,64,512]{2,0,1:T(2,128)(2,1)S(1)}, u32[]{:S(2)}, u32[]{:S(2)}) collective-permute-start(bf16[1,64,512]{2,0,1:T(2,128)(2,1)S(1)} %get-tuple-element.22), channel_id=1, source_target_pairs={{0,12},{2,14},{4,0},{6,2},{8,4},{10,6},{12,8},{14,10},{1,13},{3,15... | collective-permute-start | bytes 196616 | tf_op jit(solution)/shard_map/ppermute | solution.py:36
  171.5 15.2 %collective-permute-start.17 = (bf16[1,64,512]{2,0,1:T(2,128)(2,1)S(1)}, bf16[1,64,512]{2,0,1:T(2,128)(2,1)S(1)}, u32[]{:S(2)}, u32[]{:S(2)}) collective-permute-start(bf16[1,64,512]{2,0,1:T(2,128)(2,1)S(1)} %get-tuple-element.27), channel_id=1, source_target_pairs={{0,14},{2,0},{4,2},{6,4},{8,6},{10,8},{12,10},{14,12},{1,15},{3,1}... | collective-permute-start | bytes 196616 | tf_op jit(solution)/shard_map/ppermute | solution.py:36
Sparse Core Ops, SparseCore 0:
  23.9 98.5 all-gather.2

commit v5 on v2

--- a/solution.py
+++ b/solution.py
@@ -92,8 +92,7 @@
     norm_gain,
     down_weight,
 ):
-    outer, inner_size = (lax.axis_size(SEQ[0]), lax.axis_size(SEQ[1]))
-    columns_all = ring_pieces(ring_pieces(down_weight, SEQ[0], outer), SEQ[1], inner_size)
+    columns_all = lax.all_gather(down_weight, SEQ, axis=0, tiled=False)
     kept_mask = (1 - erase).astype(jnp.bfloat16)
     erased = inner[None, :, :] * kept_mask[:, :, None]
     row_count = inner.shape[0]
@@ -130,7 +129,9 @@
     extra = jnp.zeros((EXTRA, head_size), jnp.bfloat16)
     extra = extra.at[0, :3].set(three_parts(block_decay[0]))
     packed = jnp.concatenate([scaled_keys[0], values[0], extra], axis=0)
-    gathered = lax.all_gather(packed, SEQ, axis=0, tiled=False)
+    shards = lax.axis_size(SEQ)
+    copies = jnp.broadcast_to(packed[None], (shards, *packed.shape))
+    gathered = lax.all_to_all(copies, SEQ, split_axis=0, concat_axis=0, tiled=True)
     block = lax.axis_index(SEQ)
     intra_part = local_terms(queries, key_rows, values, cumulated, input_log)
     numerator = carried_terms(queries, cumulated, gathered, block) + intra_part
@@ -139,12 +140,9 @@
     row_var = jnp.mean(centred * centred, axis=-1, keepdims=True)
     normed = (centred * lax.rsqrt(row_var + 1e-05) * norm_gain).astype(jnp.bfloat16)
     head_terms = jnp.einsum(
-        "vtr,edrc->vtedc", normed, columns_all.reshape(inner_size, outer, head_size, -1),
-        preferred_element_type=jnp.float32,
+        "vtd,kdc->vtkc", normed, columns_all, preferred_element_type=jnp.float32
     ).astype(jnp.bfloat16)
-    head_terms = jnp.roll(head_terms, lax.axis_index(SEQ[1]) - inner_size // 2, axis=2)
-    head_terms = jnp.roll(head_terms, lax.axis_index(SEQ[0]) - outer // 2, axis=3)
-    head_terms = jnp.swapaxes(head_terms, 2, 3).reshape(*normed.shape[:2], -1)
+    head_terms = head_terms.reshape(*normed.shape[:2], -1)
     summed = sent_and_summed(head_terms, "head", 2)
     return (residual_in[None, :, :].astype(jnp.float32) + summed).astype(jnp.bfloat16)
 

time: 176 us -> 211 us (1.20)
  the two profiles are of different devices: /device:TPU:1 before, /device:TPU:10 now
where the time goes in v5:
time: 211 us
  waiting for transfers between devices  123 us (58%)
  blocking collectives  30.5 us (14%)
  between operations  18.7 us (9%)
  starting transfers between devices  14.7 us (7%)
  local copies, waits for them, and re-layouts  9.23 us (4%)
  matrix products  8.76 us (4%)
  other arithmetic  5.27 us (2%)
    all_to_all x1, waiting for transfers between devices, body(): lax.all_to_all(copies, SEQ, split_axis=0, concat_axis=0, tiled=True)  123 us
    all_to_all x1, blocking collectives, sent_and_summed(): lax.all_to_all(blocks, axis, split_axis=0, concat_axis=0, tiled=True)  30.5 us
    all_to_all x1, starting transfers between devices, body(): lax.all_to_all(copies, SEQ, split_axis=0, concat_axis=0, tiled=True)  11.2 us
  transfers between devices with their start and end apart: 3, of which 1 were waited for; matrix products, arithmetic and copies ran while one was open for 5% of the time, Pallas kernels for 0%

profile of v5, /device:TPU:10, one launch (start us, length us, event | category | flops | bytes accessed | tf_op | source)
XLA Modules:
  0.0 210.6 jit_solution(15682559262237797290)
XLA Ops:
  6.5 0.0 copy-start
  6.5 0.7 convert_bitcast_fusion
  7.2 0.9 multiply_bitcast_fusion
  8.1 3.5 %collective-permute-start = (bf16[1,3,512]{2,1,0:T(4,128)(2,1)S(1)}, bf16[1,3,512]{2,1,0:T(4,128)(2,1)S(1)}, u32[]{:S(2)}, u32[]{:S(2)}) collective-permute-start(bf16[1,3,512]{2,1,0:T(4,128)(2,1)S(1)} %slice.105), channel_id=1, source_target_pairs={{0,16},{16,32},{32,48},{48,64},{64,80},{80,96},{96,112},{112,128},... | collective-permute-start | bytes 9224 | tf_op jit(solution)/shard_map/ppermute | solution.py:15
  11.6 1.3 convolution_convert_fusion.1
  13.0 0.9 fusion.63
  13.8 0.0 collective-permute-done
  13.9 0.1 multiply_convert_fusion.2
  14.0 0.0 copy-done
  14.0 0.7 fusion.3
  14.7 0.1 fusion.51
  14.8 0.2 reduce_window_sum.18
  15.0 0.6 slice.95
  20.7 0.7 fusion.53
  21.4 1.5 convolution_bitcast_fusion
  22.9 0.1 fusion.13
  23.0 0.1 fusion.44
  23.1 2.7 %broadcast_in_dim.19 = bf16[32,144,512]{2,1,0:T(8,128)(2,1)} broadcast(bf16[144,512]{1,0:T(8,128)(2,1)S(1)} %pad_maximum_fusion), dimensions={1,2} | broadcast | bytes 4866048 | tf_op jit(solution)/shard_map/broadcast_in_dim | solution.py:133
  25.8 11.2 %all-to-all-start = ((bf16[32,144,512]{2,1,0:T(8,128)(2,1)}), bf16[32,144,512]{2,1,0:T(8,128)(2,1)}, u32[]{:S(2)}, u32[]{:S(2)}) async-start(bf16[32,144,512]{2,1,0:T(8,128)(2,1)} %broadcast_in_dim.19), calls=%async_computation | async-start | bytes 9437184 | tf_op jit(solution)/shard_map/all_to_all | solution.py:134
  37.0 0.0 all-gather.3.cloned.1.call-start
  37.1 0.7 all-gather.3.cloned.1.call-update
  37.8 0.3 fusion.2
  38.1 122.6 %all-to-all-done = bf16[32,144,512]{2,1,0:T(8,128)(2,1)} async-done(((bf16[32,144,512]{2,1,0:T(8,128)(2,1)}), bf16[32,144,512]{2,1,0:T(8,128)(2,1)}, u32[]{:S(2)}, u32[]{:S(2)}) %all-to-all-start) | async-done | bytes 4718624 | tf_op jit(solution)/shard_map/all_to_all | solution.py:134
  160.7 0.9 slice.115
  161.5 0.1 copy.29
  161.6 0.6 fusion.50
  162.3 0.1 copy.25
  162.3 0.1 reduce-window.8
  162.4 0.8 subtract_reduce_fusion
  163.2 0.1 add_exponential_fusion
  163.3 0.3 broadcast_in_dim.22
  163.6 0.4 broadcast_in_dim.23
  164.0 2.5 %fusion.62 = (bf16[32,64,512]{2,1,0:T(8,128)(2,1)S(1)}, bf16[32,64,512]{2,1,0:T(8,128)(2,1)S(1)}) fusion(bf16[32,144,512]{2,1,0:T(8,128)(2,1)} %all-to-all-done), kind=kLoop, calls=%fused_computation.94 | loop fusion | bytes 8388608 | tf_op jit(solution)/shard_map/slice | solution.py:64
  166.5 0.8 convolution_multiply_fusion
  167.2 0.5 fusion.11
  167.7 0.0 copy-start.2
  167.7 0.6 fusion.64
  168.3 0.2 multiply_reduce_fusion
  168.5 0.0 all-gather.3.cloned.1.call-done
  168.5 3.1 %convolution_convert_fusion = bf16[64,32,128]{2,0,1:T(8,128)(2,1)S(1)} fusion(bf16[32,512,128]{2,1,0:T(8,128)(2,1)} %bitcast.86, f32[64,512]{1,0:T(8,128)S(1)} %get-tuple-element.28, f32[512]{0:T(512)S(1)} %copy-done.2, f32[64]{0:T(128)S(1)} %add_rsqrt_fusion, f32[64]{0:T(128)S(1)} %broadcast_multiply_fusion), kind=kOutput, calls=%fused_computation.1 | convolution fusion | flops 268828672 | bytes 4852224 | tf_op jit(solution)/shard_map/vtd,kdc->vtkc/dot_general | solution.py:142
  171.6 0.3 copy.26
  172.0 0.0 copy-start.1
  172.0 0.3 reshape_reshape.3
  172.3 0.2 copy.27
  172.5 30.5 %all_to_all.10 = bf16[8,1,64,512]{3,2,1,0:T(8,128)(2,1)S(1)} all-to-all(bf16[8,1,64,512]{3,2,1,0:T(8,128)(2,1)S(1)} %copy.27), channel_id=1, replica_groups=mesh['seq_0'=4,'seq_1'=8,'head'=8,'var'=2] {'head'}, dimensions={0} | all-to-all | bytes 1048576 | tf_op jit(solution)/shard_map/all_to_all | solution.py:26
  203.0 0.1 convert_reduce_fusion
  203.1 0.0 copy-done.1
  203.1 0.6 fusion.16
  (8 shorter events, 0.1 us)
Async XLA Ops:
  6.5 7.4 %copy-start = (bf16[1,2,512]{2,1,0:T(2,128)(2,1)S(1)}, bf16[1,2,512]{2,1,0:T(2,128)(2,1)}, u32[]{:S(2)}) copy-start(bf16[1,2,512]{2,1,0:T(2,128)(2,1)} %param.16) | copy-start | bytes 6148
  8.1 5.7 %collective-permute-start = (bf16[1,3,512]{2,1,0:T(4,128)(2,1)S(1)}, bf16[1,3,512]{2,1,0:T(4,128)(2,1)S(1)}, u32[]{:S(2)}, u32[]{:S(2)}) collective-permute-start(bf16[1,3,512]{2,1,0:T(4,128)(2,1)S(1)} %slice.105), channel_id=1, source_target_pairs={{0,16},{16,32},{32,48},{48,64},{64,80},{80,96},{96,112},{112,128},... | collective-permute-start | bytes 9224 | tf_op jit(solution)/shard_map/ppermute | solution.py:15
  25.8 134.9 %all-to-all-start = ((bf16[32,144,512]{2,1,0:T(8,128)(2,1)}), bf16[32,144,512]{2,1,0:T(8,128)(2,1)}, u32[]{:S(2)}, u32[]{:S(2)}) async-start(bf16[32,144,512]{2,1,0:T(8,128)(2,1)} %broadcast_in_dim.19), calls=%async_computation | async-start | bytes 9437184 | tf_op jit(solution)/shard_map/all_to_all | solution.py:134
  37.0 131.5 %all-gather.3.cloned.1.call-start = ((), (), s32[]{:S(2)}) async-start(), calls=%async_computation.2 | async-start | bytes 4325376 | tf_op jit(solution)/shard_map/all_gather | solution.py:95
  167.7 0.8 copy-start.2
  172.0 31.1 %copy-start.1 = (bf16[64,512]{1,0:T(8,128)(2,1)S(1)}, bf16[64,512]{1,0:T(8,128)(2,1)}, u32[]{:S(2)}) copy-start(bf16[64,512]{1,0:T(8,128)(2,1)} %param.12) | copy-start | bytes 196612
Sparse Core Ops, SparseCore 0:
  41.0 126.1 all-gather.2

commit v6 on v2

--- a/solution.py
+++ b/solution.py
@@ -6,7 +6,7 @@
 
 CONV = 4
 SEQ = ("seq_0", "seq_1")
-EXTRA = 16
+EXTRA = 8
 
 
 def from_behind(value, axis, steps):
@@ -59,25 +59,22 @@
 
 
 def carried_terms(queries, cumulated, gathered, block):
-    blocks, rows, head_size = gathered.shape
+    blocks, rows, _ = gathered.shape
     token_count = queries.shape[1]
-    keys_all = gathered[:, :token_count, :].reshape(blocks * token_count, head_size)
-    values_all = gathered[:, token_count : 2 * token_count, :].reshape(blocks * token_count, head_size)
     parts = gathered[:, 2 * token_count, :3].astype(jnp.float32)
     decay = (parts[:, 0] + parts[:, 1]) + parts[:, 2]
     through = jnp.cumsum(decay)
-    before_own = jnp.sum(jnp.where(jnp.arange(blocks) < block, decay, 0.0))
     earlier = jnp.arange(blocks) < block
+    before_own = jnp.sum(jnp.where(earlier, decay, 0.0))
     block_exponent = jnp.where(earlier, before_own - through, -jnp.inf)
-    exponent = cumulated[:, :, None, None] + block_exponent[None, None, :, None]
-    scale = jnp.exp(jnp.broadcast_to(exponent, (*cumulated.shape, blocks, token_count)))
-    scale = scale.reshape(*cumulated.shape, blocks * token_count)
-    scores = jnp.einsum("vtd,sd->vts", queries, keys_all, preferred_element_type=jnp.float32)
-    weights = scores * scale
+    scale = jnp.exp(cumulated[:, :, None, None] + block_exponent[None, None, :, None])
+    scores = jnp.einsum("vtd,brd->vtbr", queries, gathered, preferred_element_type=jnp.float32)
+    weights = scores[..., :token_count] * scale
+    weights = jnp.pad(weights, ((0, 0), (0, 0), (0, 0), (token_count, rows - 2 * token_count)))
     high = weights.astype(jnp.bfloat16)
     low = (weights - high.astype(jnp.float32)).astype(jnp.bfloat16)
-    return jnp.einsum("vts,se->vte", high, values_all, preferred_element_type=jnp.float32) + jnp.einsum(
-        "vts,se->vte", low, values_all, preferred_element_type=jnp.float32
+    return jnp.einsum("vtbr,bre->vte", high, gathered, preferred_element_type=jnp.float32) + jnp.einsum(
+        "vtbr,bre->vte", low, gathered, preferred_element_type=jnp.float32
     )
 
 

time: 176 us -> 177 us (level)
  matrix products: 11.3 us -> 16.1 us
  local copies, waits for them, and re-layouts: 14.8 us -> 10.3 us
  blocking collectives: 27.3 us -> 29.5 us
    dot_general x3, matrix products: 3.49 us -> 9.04 us  [the longest x1 3.93 us: carried_terms(): jnp.einsum('vtd,brd->vtbr', queries, gathered, preferred_element_type=jnp...]
    slice x1 -> x0, local copies, waits for them, and re-layouts: 4.01 us -> none  [carried_terms(): gathered[:, :token_count, :].reshape(blocks * token_count, head_size)]
    all_to_all x1, blocking collectives: 27.3 us -> 29.5 us  [sent_and_summed(): lax.all_to_all(blocks, axis, split_axis=0, concat_axis=0, tiled=True)]
    unnamed x29 -> x20, local copies, waits for them, and re-layouts: 5.19 us -> 6.19 us
  transfers between devices with their start and end apart: 12 -> 12, of which waited for: 8 -> 9; matrix products, arithmetic and copies ran while one was open for 6% -> 6% of each run, Pallas kernels for 0% -> 0%
where the time goes in v6:
time: 177 us; the launch traced here: 175 us
  waiting for transfers between devices  57.9 us (33%)
  starting transfers between devices  34.4 us (19%)
  blocking collectives  29.5 us (17%)
  between operations  18.7 us (11%)
  matrix products  16.1 us (9%)
  local copies, waits for them, and re-layouts  10.3 us (6%)
  other arithmetic  8.48 us (5%)
    ppermute x6, waiting for transfers between devices, ring_pieces(): forward = lax.ppermute(forward, axis, ahead)  42.2 us
    all_to_all x1, blocking collectives, sent_and_summed(): lax.all_to_all(blocks, axis, split_axis=0, concat_axis=0, tiled=True)  29.5 us
    ppermute x6, starting transfers between devices, ring_pieces(): forward = lax.ppermute(forward, axis, ahead)  18.8 us
    all_gather x1, waiting for transfers between devices, body(): gathered = lax.all_gather(packed, SEQ, axis=0, tiled=False)  14.5 us
    ppermute x4, starting transfers between devices, ring_pieces(): backward = lax.ppermute(backward, axis, behind)  11.6 us
    unnamed x20, local copies, waits for them, and re-layouts  6.19 us
    ppermute x1, starting transfers between devices, from_behind(): lax.ppermute(value, axis, [(source, source + steps) for source in range(i...  4.02 us
    dot_general x1, matrix products, carried_terms(): jnp.einsum('vtd,brd->vtbr', queries, gathered, preferred_element_type=jnp...  3.93 us
  transfers between devices with their start and end apart: 12, of which 9 were waited for; matrix products, arithmetic and copies ran while one was open for 6% of the time, Pallas kernels for 0%

profile of v6, /device:TPU:1, one launch (start us, length us, event | category | flops | bytes accessed | tf_op | source)
XLA Modules:
  0.0 175.4 jit_solution(6932443636143668702)
XLA Ops:
  6.5 0.7 convert_bitcast_fusion
  7.2 0.9 multiply_bitcast_fusion
  8.1 4.0 %collective-permute-start = (bf16[1,3,512]{2,1,0:T(4,128)(2,1)S(1)}, bf16[1,3,512]{2,1,0:T(4,128)(2,1)S(1)}, u32[]{:S(2)}, u32[]{:S(2)}) collective-permute-start(bf16[1,3,512]{2,1,0:T(4,128)(2,1)S(1)} %slice.101), channel_id=1, source_target_pairs={{0,16},{16,32},{32,48},{48,64},{64,80},{80,96},{96,112},{112,128},... | collective-permute-start | bytes 9224 | tf_op jit(solution)/shard_map/ppermute | solution.py:15
  12.2 1.3 convolution_convert_fusion.1
  13.5 0.9 fusion.67
  14.5 0.7 fusion.4
  15.6 0.6 slice.92
  21.0 0.7 fusion.66
  21.7 1.5 convolution_bitcast_fusion.1
  23.4 0.7 pad_maximum_fusion.1
  24.1 4.2 %collective-permute-start.1 = (bf16[512,128]{1,0:T(8,128)(2,1)}, bf16[512,128]{1,0:T(8,128)(2,1)S(1)}, u32[]{:S(2)}, u32[]{:S(2)}) collective-permute-start(bf16[512,128]{1,0:T(8,128)(2,1)} %param.19), channel_id=1, source_target_pairs={{0,128},{128,256},{256,384},{384,0},{1,129},{129,257},{257,385},{3... | collective-permute-start | bytes 393224 | tf_op jit(solution)/shard_map/ppermute | solution.py:36
  28.3 3.2 %collective-permute-start.3 = (bf16[512,128]{1,0:T(8,128)(2,1)}, bf16[512,128]{1,0:T(8,128)(2,1)S(1)}, u32[]{:S(2)}, u32[]{:S(2)}) collective-permute-start(bf16[512,128]{1,0:T(8,128)(2,1)} %param.19), channel_id=1, source_target_pairs={{0,384},{128,0},{256,128},{384,256},{1,385},{129,1},{257,129},{385... | collective-permute-start | bytes 393224 | tf_op jit(solution)/shard_map/ppermute | solution.py:39
  31.5 0.6 collective-permute-done.1
  32.1 2.1 %collective-permute-start.2 = (bf16[512,128]{1,0:T(8,128)(2,1)S(1)}, bf16[512,128]{1,0:T(8,128)(2,1)S(1)}, u32[]{:S(2)}, u32[]{:S(2)}) collective-permute-start(bf16[512,128]{1,0:T(8,128)(2,1)S(1)} %collective-permute-done.1), channel_id=1, source_target_pairs={{0,128},{128,256},{256,384},{384,0},{1,129},{129,257},{257,385},{3... | collective-permute-start | bytes 393224 | tf_op jit(solution)/shard_map/ppermute | solution.py:36
  34.2 4.8 %collective-permute-done.2 = bf16[512,128]{1,0:T(8,128)(2,1)S(1)} collective-permute-done((bf16[512,128]{1,0:T(8,128)(2,1)S(1)}, bf16[512,128]{1,0:T(8,128)(2,1)S(1)}, u32[]{:S(2)}, u32[]{:S(2)}) %collective-permute-start.2) | collective-permute-done | bytes 131104 | tf_op jit(solution)/shard_map/ppermute | solution.py:36
  39.0 1.0 pad_maximum_fusion
  40.0 2.4 %collective-permute-start.4 = (bf16[4,512,128]{2,1,0:T(8,128)(2,1)S(1)}, bf16[4,512,128]{2,1,0:T(8,128)(2,1)S(1)}, u32[]{:S(2)}, u32[]{:S(2)}) collective-permute-start(bf16[4,512,128]{2,1,0:T(8,128)(2,1)S(1)} %pad_maximum_fusion), channel_id=1, source_target_pairs={{0,16},{16,32},{32,48},{48,64},{64,80},{80,96},{96,112},{112,0},{1... | collective-permute-start | bytes 1572872 | tf_op jit(solution)/shard_map/ppermute | solution.py:36
  42.3 10.1 %collective-permute-done.4 = bf16[4,512,128]{2,1,0:T(8,128)(2,1)S(1)} collective-permute-done((bf16[4,512,128]{2,1,0:T(8,128)(2,1)S(1)}, bf16[4,512,128]{2,1,0:T(8,128)(2,1)S(1)}, u32[]{:S(2)}, u32[]{:S(2)}) %collective-permute-start.4) | collective-permute-done | bytes 524320 | tf_op jit(solution)/shard_map/ppermute | solution.py:36
  52.5 1.9 %collective-permute-start.5 = (bf16[4,512,128]{2,1,0:T(8,128)(2,1)S(1)}, bf16[4,512,128]{2,1,0:T(8,128)(2,1)S(1)}, u32[]{:S(2)}, u32[]{:S(2)}) collective-permute-start(bf16[4,512,128]{2,1,0:T(8,128)(2,1)S(1)} %collective-permute-done.4), channel_id=1, source_target_pairs={{0,16},{16,32},{32,48},{48,64},{64,80},{80,96},{96,112},{112,0},{1... | collective-permute-start | bytes 1572872 | tf_op jit(solution)/shard_map/ppermute | solution.py:36
  54.4 4.6 %collective-permute-start.8 = (bf16[4,512,128]{2,1,0:T(8,128)(2,1)S(1)}, bf16[4,512,128]{2,1,0:T(8,128)(2,1)S(1)}, u32[]{:S(2)}, u32[]{:S(2)}) collective-permute-start(bf16[4,512,128]{2,1,0:T(8,128)(2,1)S(1)} %pad_maximum_fusion), channel_id=1, source_target_pairs={{0,112},{16,0},{32,16},{48,32},{64,48},{80,64},{96,80},{112,96},{1... | collective-permute-start | bytes 1572872 | tf_op jit(solution)/shard_map/ppermute | solution.py:39
  59.0 7.8 %collective-permute-done.5 = bf16[4,512,128]{2,1,0:T(8,128)(2,1)S(1)} collective-permute-done((bf16[4,512,128]{2,1,0:T(8,128)(2,1)S(1)}, bf16[4,512,128]{2,1,0:T(8,128)(2,1)S(1)}, u32[]{:S(2)}, u32[]{:S(2)}) %collective-permute-start.5) | collective-permute-done | bytes 524320 | tf_op jit(solution)/shard_map/ppermute | solution.py:36
  66.8 4.6 %collective-permute-start.6 = (bf16[4,512,128]{2,1,0:T(8,128)(2,1)S(1)}, bf16[4,512,128]{2,1,0:T(8,128)(2,1)S(1)}, u32[]{:S(2)}, u32[]{:S(2)}) collective-permute-start(bf16[4,512,128]{2,1,0:T(8,128)(2,1)S(1)} %collective-permute-done.5), channel_id=1, source_target_pairs={{0,16},{16,32},{32,48},{48,64},{64,80},{80,96},{96,112},{112,0},{1... | collective-permute-start | bytes 1572872 | tf_op jit(solution)/shard_map/ppermute | solution.py:36
  71.4 1.9 %collective-permute-start.9 = (bf16[4,512,128]{2,1,0:T(8,128)(2,1)S(1)}, bf16[4,512,128]{2,1,0:T(8,128)(2,1)S(1)}, u32[]{:S(2)}, u32[]{:S(2)}) collective-permute-start(bf16[4,512,128]{2,1,0:T(8,128)(2,1)S(1)} %collective-permute-done.8), channel_id=1, source_target_pairs={{0,112},{16,0},{32,16},{48,32},{64,48},{80,64},{96,80},{112,96},{1... | collective-permute-start | bytes 1572872 | tf_op jit(solution)/shard_map/ppermute | solution.py:39
  73.3 5.6 %collective-permute-done.6 = bf16[4,512,128]{2,1,0:T(8,128)(2,1)S(1)} collective-permute-done((bf16[4,512,128]{2,1,0:T(8,128)(2,1)S(1)}, bf16[4,512,128]{2,1,0:T(8,128)(2,1)S(1)}, u32[]{:S(2)}, u32[]{:S(2)}) %collective-permute-start.6) | collective-permute-done | bytes 524320 | tf_op jit(solution)/shard_map/ppermute | solution.py:36
  78.9 3.8 %collective-permute-start.7 = (bf16[4,512,128]{2,1,0:T(8,128)(2,1)S(1)}, bf16[4,512,128]{2,1,0:T(8,128)(2,1)}, u32[]{:S(2)}, u32[]{:S(2)}) collective-permute-start(bf16[4,512,128]{2,1,0:T(8,128)(2,1)S(1)} %collective-permute-done.6), channel_id=1, source_target_pairs={{0,16},{16,32},{32,48},{48,64},{64,80},{80,96},{96,112},{112,0},{1... | collective-permute-start | bytes 1572872 | tf_op jit(solution)/shard_map/ppermute | solution.py:36
  82.7 1.1 collective-permute-done.9
  83.8 1.9 %collective-permute-start.10 = (bf16[4,512,128]{2,1,0:T(8,128)(2,1)S(1)}, bf16[4,512,128]{2,1,0:T(8,128)(2,1)S(1)}, u32[]{:S(2)}, u32[]{:S(2)}) collective-permute-start(bf16[4,512,128]{2,1,0:T(8,128)(2,1)S(1)} %collective-permute-done.9), channel_id=1, source_target_pairs={{0,112},{16,0},{32,16},{48,32},{64,48},{80,64},{96,80},{112,96},{1... | collective-permute-start | bytes 1572872 | tf_op jit(solution)/shard_map/ppermute | solution.py:39
  85.8 13.2 %collective-permute-done.7 = bf16[4,512,128]{2,1,0:T(8,128)(2,1)} collective-permute-done((bf16[4,512,128]{2,1,0:T(8,128)(2,1)S(1)}, bf16[4,512,128]{2,1,0:T(8,128)(2,1)}, u32[]{:S(2)}, u32[]{:S(2)}) %collective-permute-start.7) | collective-permute-done | bytes 524320 | tf_op jit(solution)/shard_map/ppermute | solution.py:36
  99.0 1.9 %bitcast_dynamic-update-slice_fusion.7 = bf16[8,4,512,128]{3,2,1,0:T(8,128)(2,1)} fusion(bf16[4,512,128]{2,1,0:T(8,128)(2,1)} %collective-permute-done.7), kind=kLoop, calls=%fused_computation.37 | loop fusion | bytes 1048576
  100.8 0.8 bitcast_dynamic-update-slice_fusion.6
  101.6 0.8 bitcast_dynamic-update-slice_fusion.5
  102.5 0.8 bitcast_dynamic-update-slice_fusion.4
  103.3 0.8 bitcast_dynamic-update-slice_fusion.3
  104.2 0.8 bitcast_dynamic-update-slice_fusion.2
  105.0 0.8 bitcast_dynamic-update-slice_fusion.1
  105.9 0.9 bitcast_dynamic-update-slice_fusion
  106.8 14.5 %all-gather.3.cloned.1.call-done = bf16[4352,512]{1,0:T(8,128)(2,1)} async-done(((bf16[136,512]{1,0:T(8,128)(2,1)}), bf16[4352,512]{1,0:T(8,128)(2,1)}) %all-gather.3.cloned.1.call-update) | async-done | bytes 4456464 | tf_op jit(solution)/shard_map/all_gather | solution.py:130
  121.3 0.8 slice.111
  122.2 3.9 %convolution_bitcast_fusion = f32[1,64,32,136]{3,1,2,0:T(8,128)S(1)} fusion(bf16[32,136,512]{2,1,0:T(8,128)(2,1)} %bitcast.130, f32[1,64,1024]{2,1,0:T(8,128)S(1)} %convolution_bitcast_fusion.1), kind=kOutput, calls=%fused_computation.3 | convolution fusion | flops 285212672 | bytes 5636096 | tf_op jit(solution)/shard_map/vtd,brd->vtbr/dot_general | solution.py:71
  126.2 0.6 fusion.53
  127.0 0.8 subtract_reduce_fusion
  128.2 3.8 %convolution_bitcast_fusion.2 = f32[64,512]{1,0:T(8,128)S(1)} fusion(bf16[32,136,512]{2,1,0:T(8,128)(2,1)} %bitcast.131, f32[1,64,32,64]{3,1,2,0:T(8,128)S(1)} %slice_multiply_fusion), kind=kOutput, calls=%fused_computation.7 | convolution fusion | flops 286326784 | bytes 5111808 | tf_op jit(solution)/shard_map/vtbr,bre->vte/dot_general | solution.py:76
  132.0 1.3 fusion.2
  133.3 0.4 fusion.68
  133.9 3.1 %fusion.1 = bf16[1,64,8,4,128]{4,1,3,2,0:T(8,128)(2,1)S(1)} fusion(bf16[8,4,512,128]{3,2,1,0:T(8,128)(2,1)} %bitcast_dynamic-update-slice_fusion, f32[64,512]{1,0:T(8,128)S(1)} %get-tuple-element.26, f32[512]{0:T(512)S(1)} %copy-done.3, f32[64]{0:T(128)S(1)} %add_rsqrt_fusion, f32[64]{0:T(128)S(1)} %broadcast_multiply_fusion), kind=kOutput, calls=%fused_computation.5 | convolution fusion | flops 268828672 | bytes 4852224 | tf_op jit(solution)/shard_map/vtr,edrc->vtedc/dot_general | solution.py:138
  137.5 0.3 copy.27
  138.3 29.5 %all_to_all.5 = bf16[8,1,64,512]{3,2,1,0:T(8,128)(2,1)S(1)} all-to-all(bf16[8,1,64,512]{3,2,1,0:T(8,128)(2,1)S(1)} %copy.28), channel_id=1, replica_groups=mesh['seq_0'=4,'seq_1'=8,'head'=8,'var'=2] {'head'}, dimensions={0} | all-to-all | bytes 1048576 | tf_op jit(solution)/shard_map/all_to_all | solution.py:26
  167.9 0.6 fusion.20
  (41 shorter events, 2.6 us)
Async XLA Ops:
  6.5 8.0 %copy-start = (bf16[1,2,512]{2,1,0:T(2,128)(2,1)S(1)}, bf16[1,2,512]{2,1,0:T(2,128)(2,1)}, u32[]{:S(2)}) copy-start(bf16[1,2,512]{2,1,0:T(2,128)(2,1)} %param.16) | copy-start | bytes 6148
  6.5 114.8 %all-gather.3.cloned.1.call-start = ((), (), s32[]{:S(2)}) async-start(), calls=%async_computation.1 | async-start | bytes 4595712 | tf_op jit(solution)/shard_map/all_gather | solution.py:130
  8.1 6.2 %collective-permute-start = (bf16[1,3,512]{2,1,0:T(4,128)(2,1)S(1)}, bf16[1,3,512]{2,1,0:T(4,128)(2,1)S(1)}, u32[]{:S(2)}, u32[]{:S(2)}) collective-permute-start(bf16[1,3,512]{2,1,0:T(4,128)(2,1)S(1)} %slice.101), channel_id=1, source_target_pairs={{0,16},{16,32},{32,48},{48,64},{64,80},{80,96},{96,112},{112,128},... | collective-permute-start | bytes 9224 | tf_op jit(solution)/shard_map/ppermute | solution.py:15
  13.5 89.8 %copy-start.1 = (bf16[512,128]{1,0:T(8,128)(2,1)S(1)}, bf16[512,128]{1,0:T(8,128)(2,1)}, u32[]{:S(2)}) copy-start(bf16[512,128]{1,0:T(8,128)(2,1)} %param.19) | copy-start | bytes 393220
  24.1 8.0 %collective-permute-start.1 = (bf16[512,128]{1,0:T(8,128)(2,1)}, bf16[512,128]{1,0:T(8,128)(2,1)S(1)}, u32[]{:S(2)}, u32[]{:S(2)}) collective-permute-start(bf16[512,128]{1,0:T(8,128)(2,1)} %param.19), channel_id=1, source_target_pairs={{0,128},{128,256},{256,384},{384,0},{1,129},{129,257},{257,385},{3... | collective-permute-start | bytes 393224 | tf_op jit(solution)/shard_map/ppermute | solution.py:36
  28.3 5.9 %collective-permute-start.3 = (bf16[512,128]{1,0:T(8,128)(2,1)}, bf16[512,128]{1,0:T(8,128)(2,1)S(1)}, u32[]{:S(2)}, u32[]{:S(2)}) collective-permute-start(bf16[512,128]{1,0:T(8,128)(2,1)} %param.19), channel_id=1, source_target_pairs={{0,384},{128,0},{256,128},{384,256},{1,385},{129,1},{257,129},{385... | collective-permute-start | bytes 393224 | tf_op jit(solution)/shard_map/ppermute | solution.py:39
  32.1 6.9 %collective-permute-start.2 = (bf16[512,128]{1,0:T(8,128)(2,1)S(1)}, bf16[512,128]{1,0:T(8,128)(2,1)S(1)}, u32[]{:S(2)}, u32[]{:S(2)}) collective-permute-start(bf16[512,128]{1,0:T(8,128)(2,1)S(1)} %collective-permute-done.1), channel_id=1, source_target_pairs={{0,128},{128,256},{256,384},{384,0},{1,129},{129,257},{257,385},{3... | collective-permute-start | bytes 393224 | tf_op jit(solution)/shard_map/ppermute | solution.py:36
  40.0 12.5 %collective-permute-start.4 = (bf16[4,512,128]{2,1,0:T(8,128)(2,1)S(1)}, bf16[4,512,128]{2,1,0:T(8,128)(2,1)S(1)}, u32[]{:S(2)}, u32[]{:S(2)}) collective-permute-start(bf16[4,512,128]{2,1,0:T(8,128)(2,1)S(1)} %pad_maximum_fusion), channel_id=1, source_target_pairs={{0,16},{16,32},{32,48},{48,64},{64,80},{80,96},{96,112},{112,0},{1... | collective-permute-start | bytes 1572872 | tf_op jit(solution)/shard_map/ppermute | solution.py:36
  52.5 14.3 %collective-permute-start.5 = (bf16[4,512,128]{2,1,0:T(8,128)(2,1)S(1)}, bf16[4,512,128]{2,1,0:T(8,128)(2,1)S(1)}, u32[]{:S(2)}, u32[]{:S(2)}) collective-permute-start(bf16[4,512,128]{2,1,0:T(8,128)(2,1)S(1)} %collective-permute-done.4), channel_id=1, source_target_pairs={{0,16},{16,32},{32,48},{48,64},{64,80},{80,96},{96,112},{112,0},{1... | collective-permute-start | bytes 1572872 | tf_op jit(solution)/shard_map/ppermute | solution.py:36
  54.4 17.0 %collective-permute-start.8 = (bf16[4,512,128]{2,1,0:T(8,128)(2,1)S(1)}, bf16[4,512,128]{2,1,0:T(8,128)(2,1)S(1)}, u32[]{:S(2)}, u32[]{:S(2)}) collective-permute-start(bf16[4,512,128]{2,1,0:T(8,128)(2,1)S(1)} %pad_maximum_fusion), channel_id=1, source_target_pairs={{0,112},{16,0},{32,16},{48,32},{64,48},{80,64},{96,80},{112,96},{1... | collective-permute-start | bytes 1572872 | tf_op jit(solution)/shard_map/ppermute | solution.py:39
  66.8 12.1 %collective-permute-start.6 = (bf16[4,512,128]{2,1,0:T(8,128)(2,1)S(1)}, bf16[4,512,128]{2,1,0:T(8,128)(2,1)S(1)}, u32[]{:S(2)}, u32[]{:S(2)}) collective-permute-start(bf16[4,512,128]{2,1,0:T(8,128)(2,1)S(1)} %collective-permute-done.5), channel_id=1, source_target_pairs={{0,16},{16,32},{32,48},{48,64},{64,80},{80,96},{96,112},{112,0},{1... | collective-permute-start | bytes 1572872 | tf_op jit(solution)/shard_map/ppermute | solution.py:36
  71.4 12.5 %collective-permute-start.9 = (bf16[4,512,128]{2,1,0:T(8,128)(2,1)S(1)}, bf16[4,512,128]{2,1,0:T(8,128)(2,1)S(1)}, u32[]{:S(2)}, u32[]{:S(2)}) collective-permute-start(bf16[4,512,128]{2,1,0:T(8,128)(2,1)S(1)} %collective-permute-done.8), channel_id=1, source_target_pairs={{0,112},{16,0},{32,16},{48,32},{64,48},{80,64},{96,80},{112,96},{1... | collective-permute-start | bytes 1572872 | tf_op jit(solution)/shard_map/ppermute | solution.py:39
  78.9 20.0 %collective-permute-start.7 = (bf16[4,512,128]{2,1,0:T(8,128)(2,1)S(1)}, bf16[4,512,128]{2,1,0:T(8,128)(2,1)}, u32[]{:S(2)}, u32[]{:S(2)}) collective-permute-start(bf16[4,512,128]{2,1,0:T(8,128)(2,1)S(1)} %collective-permute-done.6), channel_id=1, source_target_pairs={{0,16},{16,32},{32,48},{48,64},{64,80},{80,96},{96,112},{112,0},{1... | collective-permute-start | bytes 1572872 | tf_op jit(solution)/shard_map/ppermute | solution.py:36
  83.8 22.1 %collective-permute-start.10 = (bf16[4,512,128]{2,1,0:T(8,128)(2,1)S(1)}, bf16[4,512,128]{2,1,0:T(8,128)(2,1)S(1)}, u32[]{:S(2)}, u32[]{:S(2)}) collective-permute-start(bf16[4,512,128]{2,1,0:T(8,128)(2,1)S(1)} %collective-permute-done.9), channel_id=1, source_target_pairs={{0,112},{16,0},{32,16},{48,32},{64,48},{80,64},{96,80},{112,96},{1... | collective-permute-start | bytes 1572872 | tf_op jit(solution)/shard_map/ppermute | solution.py:39
  122.2 9.8 %slice-start = ((s8[4456448]{0:T(1024)(128)(4,1)}), s8[262144]{0:T(1024)(128)(4,1)S(1)}, s32[]{:S(2)}) async-start(s8[4456448]{0:T(1024)(128)(4,1)} %bitcast.132), calls=%async_computation.2 | async-start | bytes 524288
  127.8 4.1 %slice-start.1 = ((s8[4456448]{0:T(1024)(128)(4,1)}), s8[4194304]{0:T(1024)(128)(4,1)S(1)}, s32[]{:S(2)}) async-start(s8[4456448]{0:T(1024)(128)(4,1)} %bitcast.132), calls=%async_computation.3 | async-start | bytes 8388608
  132.0 2.0 %copy-start.3 = (f32[512]{0:T(512)S(1)}, f32[512]{0:T(512)}, u32[]{:S(2)}) copy-start(f32[512]{0:T(512)} %param.18) | copy-start | bytes 6148
  137.0 30.8 %copy-start.2 = (bf16[64,512]{1,0:T(8,128)(2,1)S(1)}, bf16[64,512]{1,0:T(8,128)(2,1)}, u32[]{:S(2)}) copy-start(bf16[64,512]{1,0:T(8,128)(2,1)} %param.12) | copy-start | bytes 196612
Sparse Core Ops, SparseCore 0:
  24.2 97.0 all-gather.2

commit v7 on v6

--- a/solution.py
+++ b/solution.py
@@ -127,7 +127,9 @@
     extra = jnp.zeros((EXTRA, head_size), jnp.bfloat16)
     extra = extra.at[0, :3].set(three_parts(block_decay[0]))
     packed = jnp.concatenate([scaled_keys[0], values[0], extra], axis=0)
-    gathered = lax.all_gather(packed, SEQ, axis=0, tiled=False)
+    gathered = lax.all_gather(packed, SEQ[1], axis=0, tiled=False)
+    gathered = lax.all_gather(gathered, SEQ[0], axis=0, tiled=False)
+    gathered = gathered.reshape(-1, *packed.shape)
     block = lax.axis_index(SEQ)
     intra_part = local_terms(queries, key_rows, values, cumulated, input_log)
     numerator = carried_terms(queries, cumulated, gathered, block) + intra_part

time: 177 us -> 203 us (1.15)
  waiting for transfers between devices: 57.9 us -> 80.6 us
  blocking collectives: 29.5 us -> 35.2 us
  matrix products: 16.1 us -> 13.8 us
    all_gather x1 -> x2, waiting for transfers between devices: 14.5 us -> 42.2 us  [the longest x1 42.2 us: body(): gathered = lax.all_gather(packed, SEQ[1], axis=0, tiled=False)]
    all_to_all x1, blocking collectives: 29.5 us -> 35.2 us  [sent_and_summed(): lax.all_to_all(blocks, axis, split_axis=0, concat_axis=0, tiled=True)]
    ppermute x4, starting transfers between devices: 11.6 us -> 16.1 us  [ring_pieces(): backward = lax.ppermute(backward, axis, behind)]
    ppermute x6, starting transfers between devices: 18.8 us -> 14.8 us  [ring_pieces(): forward = lax.ppermute(forward, axis, ahead)]
    ppermute x6, waiting for transfers between devices: 42.2 us -> 38.2 us  [ring_pieces(): forward = lax.ppermute(forward, axis, ahead)]
    dot_general x1, matrix products: 3.78 us -> 1.42 us  [carried_terms(): jnp.einsum('vtbr,bre->vte', low, gathered, preferred_element_type=jnp.flo...]
  transfers between devices with their start and end apart: 12 -> 13, of which waited for: 9 -> 8; matrix products, arithmetic and copies ran while one was open for 6% -> 5% of each run, Pallas kernels for 0% -> 0%
where the time goes in v7:
time: 203 us; the launch traced here: 201 us
  waiting for transfers between devices  80.6 us (40%)
  blocking collectives  35.2 us (17%)
  starting transfers between devices  35 us (17%)
  between operations  18.9 us (9%)
  matrix products  13.8 us (7%)
  local copies, waits for them, and re-layouts  10.3 us (5%)
  other arithmetic  7.6 us (4%)
    all_gather x1, waiting for transfers between devices, body(): gathered = lax.all_gather(packed, SEQ[1], axis=0, tiled=False)  42.2 us
    ppermute x6, waiting for transfers between devices, ring_pieces(): forward = lax.ppermute(forward, axis, ahead)  38.2 us
    all_to_all x1, blocking collectives, sent_and_summed(): lax.all_to_all(blocks, axis, split_axis=0, concat_axis=0, tiled=True)  35.2 us
    ppermute x4, starting transfers between devices, ring_pieces(): backward = lax.ppermute(backward, axis, behind)  16.1 us
    ppermute x6, starting transfers between devices, ring_pieces(): forward = lax.ppermute(forward, axis, ahead)  14.8 us
    unnamed x20, local copies, waits for them, and re-layouts  6.18 us
  transfers between devices with their start and end apart: 13, of which 8 were waited for; matrix products, arithmetic and copies ran while one was open for 5% of the time, Pallas kernels for 0%

profile of v7, /device:TPU:1, one launch (start us, length us, event | category | flops | bytes accessed | tf_op | source)
XLA Modules:
  0.0 201.4 jit_solution(4082361586248439312)
XLA Ops:
  6.5 0.7 convert_bitcast_fusion
  7.2 0.9 multiply_bitcast_fusion
  8.2 4.0 %collective-permute-start = (bf16[1,3,512]{2,1,0:T(4,128)(2,1)S(1)}, bf16[1,3,512]{2,1,0:T(4,128)(2,1)S(1)}, u32[]{:S(2)}, u32[]{:S(2)}) collective-permute-start(bf16[1,3,512]{2,1,0:T(4,128)(2,1)S(1)} %slice.101), channel_id=1, source_target_pairs={{0,16},{16,32},{32,48},{48,64},{64,80},{80,96},{96,112},{112,128},... | collective-permute-start | bytes 9224 | tf_op jit(solution)/shard_map/ppermute | solution.py:15
  12.2 1.3 convolution_convert_fusion.1
  13.5 0.9 fusion.67
  14.5 0.7 fusion.4
  15.6 0.6 slice.92
  21.3 0.7 fusion.66
  21.9 1.5 convolution_bitcast_fusion.1
  23.6 0.7 pad_maximum_fusion.1
  24.3 42.2 %all-gather.5.cloned.1.call-done = bf16[1088,512]{1,0:T(8,128)(2,1)} async-done(((bf16[136,512]{1,0:T(8,128)(2,1)}), bf16[1088,512]{1,0:T(8,128)(2,1)}) %all-gather.5.cloned.1.call-update) | async-done | bytes 1114128 | tf_op jit(solution)/shard_map/all_gather | solution.py:130
  66.5 3.1 %collective-permute-start.1 = (bf16[512,128]{1,0:T(8,128)(2,1)S(1)}, bf16[512,128]{1,0:T(8,128)(2,1)S(1)}, u32[]{:S(2)}, u32[]{:S(2)}) collective-permute-start(bf16[512,128]{1,0:T(8,128)(2,1)S(1)} %copy-done.1), channel_id=1, source_target_pairs={{0,128},{128,256},{256,384},{384,0},{1,129},{129,257},{257,385},{3... | collective-permute-start | bytes 393224 | tf_op jit(solution)/shard_map/ppermute | solution.py:36
  69.6 3.4 %collective-permute-start.3 = (bf16[512,128]{1,0:T(8,128)(2,1)S(1)}, bf16[512,128]{1,0:T(8,128)(2,1)S(1)}, u32[]{:S(2)}, u32[]{:S(2)}) collective-permute-start(bf16[512,128]{1,0:T(8,128)(2,1)S(1)} %copy-done.1), channel_id=1, source_target_pairs={{0,384},{128,0},{256,128},{384,256},{1,385},{129,1},{257,129},{385... | collective-permute-start | bytes 393224 | tf_op jit(solution)/shard_map/ppermute | solution.py:39
  73.1 0.4 collective-permute-done.1
  73.5 1.9 collective-permute-start.2
  75.4 5.3 %collective-permute-done.2 = bf16[512,128]{1,0:T(8,128)(2,1)S(1)} collective-permute-done((bf16[512,128]{1,0:T(8,128)(2,1)S(1)}, bf16[512,128]{1,0:T(8,128)(2,1)S(1)}, u32[]{:S(2)}, u32[]{:S(2)}) %collective-permute-start.2) | collective-permute-done | bytes 131104 | tf_op jit(solution)/shard_map/ppermute | solution.py:36
  80.7 3.1 %collective-permute-start.4 = (bf16[4,512,128]{2,1,0:T(8,128)(2,1)S(1)}, bf16[4,512,128]{2,1,0:T(8,128)(2,1)S(1)}, u32[]{:S(2)}, u32[]{:S(2)}) collective-permute-start(bf16[4,512,128]{2,1,0:T(8,128)(2,1)S(1)} %pad_maximum_fusion), channel_id=1, source_target_pairs={{0,16},{16,32},{32,48},{48,64},{64,80},{80,96},{96,112},{112,0},{1... | collective-permute-start | bytes 1572872 | tf_op jit(solution)/shard_map/ppermute | solution.py:36
  83.8 8.0 %collective-permute-done.4 = bf16[4,512,128]{2,1,0:T(8,128)(2,1)S(1)} collective-permute-done((bf16[4,512,128]{2,1,0:T(8,128)(2,1)S(1)}, bf16[4,512,128]{2,1,0:T(8,128)(2,1)S(1)}, u32[]{:S(2)}, u32[]{:S(2)}) %collective-permute-start.4) | collective-permute-done | bytes 524320 | tf_op jit(solution)/shard_map/ppermute | solution.py:36
  91.9 1.9 collective-permute-start.5
  93.8 4.6 %collective-permute-start.8 = (bf16[4,512,128]{2,1,0:T(8,128)(2,1)S(1)}, bf16[4,512,128]{2,1,0:T(8,128)(2,1)S(1)}, u32[]{:S(2)}, u32[]{:S(2)}) collective-permute-start(bf16[4,512,128]{2,1,0:T(8,128)(2,1)S(1)} %pad_maximum_fusion), channel_id=1, source_target_pairs={{0,112},{16,0},{32,16},{48,32},{64,48},{80,64},{96,80},{112,96},{1... | collective-permute-start | bytes 1572872 | tf_op jit(solution)/shard_map/ppermute | solution.py:39
  98.4 7.6 %collective-permute-done.5 = bf16[4,512,128]{2,1,0:T(8,128)(2,1)S(1)} collective-permute-done((bf16[4,512,128]{2,1,0:T(8,128)(2,1)S(1)}, bf16[4,512,128]{2,1,0:T(8,128)(2,1)S(1)}, u32[]{:S(2)}, u32[]{:S(2)}) %collective-permute-start.5) | collective-permute-done | bytes 524320 | tf_op jit(solution)/shard_map/ppermute | solution.py:36
  106.0 2.2 %collective-permute-start.6 = (bf16[4,512,128]{2,1,0:T(8,128)(2,1)S(1)}, bf16[4,512,128]{2,1,0:T(8,128)(2,1)S(1)}, u32[]{:S(2)}, u32[]{:S(2)}) collective-permute-start(bf16[4,512,128]{2,1,0:T(8,128)(2,1)S(1)} %collective-permute-done.5), channel_id=1, source_target_pairs={{0,16},{16,32},{32,48},{48,64},{64,80},{80,96},{96,112},{112,0},{1... | collective-permute-start | bytes 1572872 | tf_op jit(solution)/shard_map/ppermute | solution.py:36
  108.2 4.2 %collective-permute-start.9 = (bf16[4,512,128]{2,1,0:T(8,128)(2,1)S(1)}, bf16[4,512,128]{2,1,0:T(8,128)(2,1)S(1)}, u32[]{:S(2)}, u32[]{:S(2)}) collective-permute-start(bf16[4,512,128]{2,1,0:T(8,128)(2,1)S(1)} %collective-permute-done.8), channel_id=1, source_target_pairs={{0,112},{16,0},{32,16},{48,32},{64,48},{80,64},{96,80},{112,96},{1... | collective-permute-start | bytes 1572872 | tf_op jit(solution)/shard_map/ppermute | solution.py:39
  112.5 8.3 %collective-permute-done.6 = bf16[4,512,128]{2,1,0:T(8,128)(2,1)S(1)} collective-permute-done((bf16[4,512,128]{2,1,0:T(8,128)(2,1)S(1)}, bf16[4,512,128]{2,1,0:T(8,128)(2,1)S(1)}, u32[]{:S(2)}, u32[]{:S(2)}) %collective-permute-start.6) | collective-permute-done | bytes 524320 | tf_op jit(solution)/shard_map/ppermute | solution.py:36
  120.8 2.6 %collective-permute-start.7 = (bf16[4,512,128]{2,1,0:T(8,128)(2,1)S(1)}, bf16[4,512,128]{2,1,0:T(8,128)(2,1)}, u32[]{:S(2)}, u32[]{:S(2)}) collective-permute-start(bf16[4,512,128]{2,1,0:T(8,128)(2,1)S(1)} %collective-permute-done.6), channel_id=1, source_target_pairs={{0,16},{16,32},{32,48},{48,64},{64,80},{80,96},{96,112},{112,0},{1... | collective-permute-start | bytes 1572872 | tf_op jit(solution)/shard_map/ppermute | solution.py:36
  123.7 3.9 %collective-permute-start.10 = (bf16[4,512,128]{2,1,0:T(8,128)(2,1)S(1)}, bf16[4,512,128]{2,1,0:T(8,128)(2,1)S(1)}, u32[]{:S(2)}, u32[]{:S(2)}) collective-permute-start(bf16[4,512,128]{2,1,0:T(8,128)(2,1)S(1)} %collective-permute-done.9), channel_id=1, source_target_pairs={{0,112},{16,0},{32,16},{48,32},{64,48},{80,64},{96,80},{112,96},{1... | collective-permute-start | bytes 1572872 | tf_op jit(solution)/shard_map/ppermute | solution.py:39
  127.6 8.5 %collective-permute-done.7 = bf16[4,512,128]{2,1,0:T(8,128)(2,1)} collective-permute-done((bf16[4,512,128]{2,1,0:T(8,128)(2,1)S(1)}, bf16[4,512,128]{2,1,0:T(8,128)(2,1)}, u32[]{:S(2)}, u32[]{:S(2)}) %collective-permute-start.7) | collective-permute-done | bytes 524320 | tf_op jit(solution)/shard_map/ppermute | solution.py:36
  136.1 1.9 bitcast_dynamic-update-slice_fusion.7
  138.0 0.8 bitcast_dynamic-update-slice_fusion.6
  138.9 0.8 bitcast_dynamic-update-slice_fusion.5
  139.7 0.9 bitcast_dynamic-update-slice_fusion.4
  140.5 0.8 bitcast_dynamic-update-slice_fusion.3
  141.4 0.8 bitcast_dynamic-update-slice_fusion.2
  142.2 0.8 bitcast_dynamic-update-slice_fusion.1
  143.0 0.9 bitcast_dynamic-update-slice_fusion
  143.9 0.9 slice.111
  144.9 0.6 fusion.53
  145.6 0.8 subtract_reduce_fusion
  146.5 4.0 %convolution_bitcast_fusion = f32[1,64,32,136]{3,1,2,0:T(8,128)S(1)} fusion(bf16[32,136,512]{2,1,0:T(8,128)(2,1)} %all-gather.7.cloned.1.call-done, f32[1,64,1024]{2,1,0:T(8,128)S(1)} %convolution_bitcast_fusion.1), kind=kOutput, calls=%fused_computation.3 | convolution fusion | flops 285212672 | bytes 5636096 | tf_op jit(solution)/shard_map/vtd,brd->vtbr/dot_general | solution.py:71
  150.5 0.3 slice_multiply_fusion
  150.9 1.4 convolution_bitcast_fusion.2
  152.3 1.3 fusion.2
  153.6 0.4 fusion.68
  154.3 3.1 %fusion.1 = bf16[1,64,8,4,128]{4,1,3,2,0:T(8,128)(2,1)S(1)} fusion(bf16[8,4,512,128]{3,2,1,0:T(8,128)(2,1)} %bitcast_dynamic-update-slice_fusion, f32[64,512]{1,0:T(8,128)S(1)} %get-tuple-element.26, f32[512]{0:T(512)S(1)} %copy-done.3, f32[64]{0:T(128)S(1)} %add_rsqrt_fusion, f32[64]{0:T(128)S(1)} %broadcast_multiply_fusion), kind=kOutput, calls=%fused_computation.5 | convolution fusion | flops 268828672 | bytes 4852224 | tf_op jit(solution)/shard_map/vtr,edrc->vtedc/dot_general | solution.py:140
  157.8 0.3 copy.21
  158.1 0.3 reshape_reshape.3
  158.6 35.2 %all_to_all.5 = bf16[8,1,64,512]{3,2,1,0:T(8,128)(2,1)S(1)} all-to-all(bf16[8,1,64,512]{3,2,1,0:T(8,128)(2,1)S(1)} %copy.22), channel_id=1, replica_groups=mesh['seq_0'=4,'seq_1'=8,'head'=8,'var'=2] {'head'}, dimensions={0} | all-to-all | bytes 1048576 | tf_op jit(solution)/shard_map/all_to_all | solution.py:26
  193.9 0.6 fusion.20
  (44 shorter events, 2.2 us)
Async XLA Ops:
  6.5 8.0 %copy-start = (bf16[1,2,512]{2,1,0:T(2,128)(2,1)S(1)}, bf16[1,2,512]{2,1,0:T(2,128)(2,1)}, u32[]{:S(2)}) copy-start(bf16[1,2,512]{2,1,0:T(2,128)(2,1)} %param.16) | copy-start | bytes 6148
  6.5 60.0 %copy-start.1 = (bf16[512,128]{1,0:T(8,128)(2,1)S(1)}, bf16[512,128]{1,0:T(8,128)(2,1)}, u32[]{:S(2)}) copy-start(bf16[512,128]{1,0:T(8,128)(2,1)} %param.19) | copy-start | bytes 393220
  6.5 60.0 %all-gather.5.cloned.1.call-start = ((), (), s32[]{:S(2)}) async-start(), calls=%async_computation.1 | async-start | bytes 1253376 | tf_op jit(solution)/shard_map/all_gather | solution.py:130
  8.2 6.2 %collective-permute-start = (bf16[1,3,512]{2,1,0:T(4,128)(2,1)S(1)}, bf16[1,3,512]{2,1,0:T(4,128)(2,1)S(1)}, u32[]{:S(2)}, u32[]{:S(2)}) collective-permute-start(bf16[1,3,512]{2,1,0:T(4,128)(2,1)S(1)} %slice.101), channel_id=1, source_target_pairs={{0,16},{16,32},{32,48},{48,64},{64,80},{80,96},{96,112},{112,128},... | collective-permute-start | bytes 9224 | tf_op jit(solution)/shard_map/ppermute | solution.py:15
  24.3 119.6 %all-gather.7.cloned.1.call-start = ((), (), s32[]{:S(2)}) async-start(), calls=%async_computation.2 | async-start | bytes 5570560 | tf_op jit(solution)/shard_map/all_gather | solution.py:131
  66.5 6.9 %collective-permute-start.1 = (bf16[512,128]{1,0:T(8,128)(2,1)S(1)}, bf16[512,128]{1,0:T(8,128)(2,1)S(1)}, u32[]{:S(2)}, u32[]{:S(2)}) collective-permute-start(bf16[512,128]{1,0:T(8,128)(2,1)S(1)} %copy-done.1), channel_id=1, source_target_pairs={{0,128},{128,256},{256,384},{384,0},{1,129},{129,257},{257,385},{3... | collective-permute-start | bytes 393224 | tf_op jit(solution)/shard_map/ppermute | solution.py:36
  69.6 5.7 %collective-permute-start.3 = (bf16[512,128]{1,0:T(8,128)(2,1)S(1)}, bf16[512,128]{1,0:T(8,128)(2,1)S(1)}, u32[]{:S(2)}, u32[]{:S(2)}) collective-permute-start(bf16[512,128]{1,0:T(8,128)(2,1)S(1)} %copy-done.1), channel_id=1, source_target_pairs={{0,384},{128,0},{256,128},{384,256},{1,385},{129,1},{257,129},{385... | collective-permute-start | bytes 393224 | tf_op jit(solution)/shard_map/ppermute | solution.py:39
  73.5 7.2 %collective-permute-start.2 = (bf16[512,128]{1,0:T(8,128)(2,1)S(1)}, bf16[512,128]{1,0:T(8,128)(2,1)S(1)}, u32[]{:S(2)}, u32[]{:S(2)}) collective-permute-start(bf16[512,128]{1,0:T(8,128)(2,1)S(1)} %collective-permute-done.1), channel_id=1, source_target_pairs={{0,128},{128,256},{256,384},{384,0},{1,129},{129,257},{257,385},{3... | collective-permute-start | bytes 393224 | tf_op jit(solution)/shard_map/ppermute | solution.py:36
  80.7 11.1 %collective-permute-start.4 = (bf16[4,512,128]{2,1,0:T(8,128)(2,1)S(1)}, bf16[4,512,128]{2,1,0:T(8,128)(2,1)S(1)}, u32[]{:S(2)}, u32[]{:S(2)}) collective-permute-start(bf16[4,512,128]{2,1,0:T(8,128)(2,1)S(1)} %pad_maximum_fusion), channel_id=1, source_target_pairs={{0,16},{16,32},{32,48},{48,64},{64,80},{80,96},{96,112},{112,0},{1... | collective-permute-start | bytes 1572872 | tf_op jit(solution)/shard_map/ppermute | solution.py:36
  91.9 14.1 %collective-permute-start.5 = (bf16[4,512,128]{2,1,0:T(8,128)(2,1)S(1)}, bf16[4,512,128]{2,1,0:T(8,128)(2,1)S(1)}, u32[]{:S(2)}, u32[]{:S(2)}) collective-permute-start(bf16[4,512,128]{2,1,0:T(8,128)(2,1)S(1)} %collective-permute-done.4), channel_id=1, source_target_pairs={{0,16},{16,32},{32,48},{48,64},{64,80},{80,96},{96,112},{112,0},{1... | collective-permute-start | bytes 1572872 | tf_op jit(solution)/shard_map/ppermute | solution.py:36
  93.8 14.4 %collective-permute-start.8 = (bf16[4,512,128]{2,1,0:T(8,128)(2,1)S(1)}, bf16[4,512,128]{2,1,0:T(8,128)(2,1)S(1)}, u32[]{:S(2)}, u32[]{:S(2)}) collective-permute-start(bf16[4,512,128]{2,1,0:T(8,128)(2,1)S(1)} %pad_maximum_fusion), channel_id=1, source_target_pairs={{0,112},{16,0},{32,16},{48,32},{64,48},{80,64},{96,80},{112,96},{1... | collective-permute-start | bytes 1572872 | tf_op jit(solution)/shard_map/ppermute | solution.py:39
  106.0 14.9 %collective-permute-start.6 = (bf16[4,512,128]{2,1,0:T(8,128)(2,1)S(1)}, bf16[4,512,128]{2,1,0:T(8,128)(2,1)S(1)}, u32[]{:S(2)}, u32[]{:S(2)}) collective-permute-start(bf16[4,512,128]{2,1,0:T(8,128)(2,1)S(1)} %collective-permute-done.5), channel_id=1, source_target_pairs={{0,16},{16,32},{32,48},{48,64},{64,80},{80,96},{96,112},{112,0},{1... | collective-permute-start | bytes 1572872 | tf_op jit(solution)/shard_map/ppermute | solution.py:36
  108.2 15.5 %collective-permute-start.9 = (bf16[4,512,128]{2,1,0:T(8,128)(2,1)S(1)}, bf16[4,512,128]{2,1,0:T(8,128)(2,1)S(1)}, u32[]{:S(2)}, u32[]{:S(2)}) collective-permute-start(bf16[4,512,128]{2,1,0:T(8,128)(2,1)S(1)} %collective-permute-done.8), channel_id=1, source_target_pairs={{0,112},{16,0},{32,16},{48,32},{64,48},{80,64},{96,80},{112,96},{1... | collective-permute-start | bytes 1572872 | tf_op jit(solution)/shard_map/ppermute | solution.py:39
  120.8 15.3 %collective-permute-start.7 = (bf16[4,512,128]{2,1,0:T(8,128)(2,1)S(1)}, bf16[4,512,128]{2,1,0:T(8,128)(2,1)}, u32[]{:S(2)}, u32[]{:S(2)}) collective-permute-start(bf16[4,512,128]{2,1,0:T(8,128)(2,1)S(1)} %collective-permute-done.6), channel_id=1, source_target_pairs={{0,16},{16,32},{32,48},{48,64},{64,80},{80,96},{96,112},{112,0},{1... | collective-permute-start | bytes 1572872 | tf_op jit(solution)/shard_map/ppermute | solution.py:36
  123.7 19.3 %collective-permute-start.10 = (bf16[4,512,128]{2,1,0:T(8,128)(2,1)S(1)}, bf16[4,512,128]{2,1,0:T(8,128)(2,1)S(1)}, u32[]{:S(2)}, u32[]{:S(2)}) collective-permute-start(bf16[4,512,128]{2,1,0:T(8,128)(2,1)S(1)} %collective-permute-done.9), channel_id=1, source_target_pairs={{0,112},{16,0},{32,16},{48,32},{64,48},{80,64},{96,80},{112,96},{1... | collective-permute-start | bytes 1572872 | tf_op jit(solution)/shard_map/ppermute | solution.py:39
  145.5 5.4 %slice-start = ((s8[4456448]{0:T(1024)(128)(4,1)}), s8[262144]{0:T(1024)(128)(4,1)S(1)}, s32[]{:S(2)}) async-start(s8[4456448]{0:T(1024)(128)(4,1)} %bitcast.129), calls=%async_computation.3 | async-start | bytes 524288
  146.5 4.4 %slice-start.1 = ((s8[4456448]{0:T(1024)(128)(4,1)}), s8[4194304]{0:T(1024)(128)(4,1)S(1)}, s32[]{:S(2)}) async-start(s8[4456448]{0:T(1024)(128)(4,1)} %bitcast.129), calls=%async_computation.4 | async-start | bytes 8388608
  152.3 2.0 copy-start.3
  157.3 36.5 %copy-start.2 = (bf16[64,512]{1,0:T(8,128)(2,1)S(1)}, bf16[64,512]{1,0:T(8,128)(2,1)}, u32[]{:S(2)}) copy-start(bf16[64,512]{1,0:T(8,128)(2,1)} %param.12) | copy-start | bytes 196612
Sparse Core Ops, SparseCore 0:
  24.4 42.0 all-gather.4
  68.6 59.3 all-gather.6

commit v8 on v2

--- a/solution.py
+++ b/solution.py
@@ -6,6 +6,7 @@
 
 CONV = 4
 SEQ = ("seq_0", "seq_1")
+HEAD = ("head_1", "head_0")
 EXTRA = 16
 
 
@@ -145,26 +146,32 @@
     head_terms = jnp.roll(head_terms, lax.axis_index(SEQ[1]) - inner_size // 2, axis=2)
     head_terms = jnp.roll(head_terms, lax.axis_index(SEQ[0]) - outer // 2, axis=3)
     head_terms = jnp.swapaxes(head_terms, 2, 3).reshape(*normed.shape[:2], -1)
-    summed = sent_and_summed(head_terms, "head", 2)
+    pair, across = HEAD
+    blocks = head_terms.reshape(*head_terms.shape[:2], lax.axis_size(across), lax.axis_size(pair), -1)
+    arrived = lax.all_to_all(blocks, pair, split_axis=3, concat_axis=3, tiled=True)
+    pair_sum = jnp.sum(arrived.astype(jnp.float32), axis=3).astype(jnp.bfloat16)
+    summed = lax.all_to_all(pair_sum, across, split_axis=2, concat_axis=2, tiled=True)
+    summed = jnp.sum(summed.astype(jnp.float32), axis=2)
     return (residual_in[None, :, :].astype(jnp.float32) + summed).astype(jnp.bfloat16)
 
 
 def solution(mesh):
     split = Mesh(
-        mesh.devices.reshape(4, 8, mesh.shape["head"], mesh.shape["var"]),
-        ("seq_0", "seq_1", "head", "var"),
+        mesh.devices.reshape(4, 8, mesh.shape["head"] // 2, 2, mesh.shape["var"]),
+        ("seq_0", "seq_1", "head_0", "head_1", "var"),
     )
+    heads = HEAD[::-1]
     placed = (
-        P(SEQ, "head"),
-        P(SEQ, "head"),
+        P(SEQ, heads),
+        P(SEQ, heads),
         P("var", SEQ),
-        P(None, "head"),
-        P("head", None, None),
-        P("head", None, None),
-        P("head", None),
-        P("head"),
-        P("head", SEQ),
+        P(None, heads),
+        P(heads, None, None),
+        P(heads, None, None),
+        P(heads, None),
+        P(heads),
+        P(heads, SEQ),
     )
     return jax.shard_map(
-        body, mesh=split, in_specs=placed, out_specs=P("var", SEQ, "head"), check_vma=False
+        body, mesh=split, in_specs=placed, out_specs=P("var", SEQ, heads), check_vma=False
     )

time: 176 us -> 175 us (level)
    all_to_all x1 -> x2, blocking collectives: 27.3 us -> 26 us  [the longest x1 19.5 us: body(): lax.all_to_all(pair_sum, across, split_axis=2, concat_axis=2, tiled=True)]
where the time goes in v8:
time: 175 us; the launch traced here: 173 us
  waiting for transfers between devices  57.8 us (33%)
  starting transfers between devices  35.7 us (20%)
  blocking collectives  26 us (15%)
  between operations  18.6 us (11%)
  local copies, waits for them, and re-layouts  14.8 us (8%)
  matrix products  11.3 us (6%)
  other arithmetic  8.74 us (5%)
    ppermute x6, waiting for transfers between devices, ring_pieces(): forward = lax.ppermute(forward, axis, ahead)  42.9 us
    all_to_all x1, blocking collectives, body(): lax.all_to_all(pair_sum, across, split_axis=2, concat_axis=2, tiled=True)  19.5 us
    ppermute x6, starting transfers between devices, ring_pieces(): forward = lax.ppermute(forward, axis, ahead)  19 us
    all_gather x1, waiting for transfers between devices, body(): gathered = lax.all_gather(packed, SEQ, axis=0, tiled=False)  14.6 us
    ppermute x4, starting transfers between devices, ring_pieces(): backward = lax.ppermute(backward, axis, behind)  12.7 us
    all_to_all x1, blocking collectives, body(): lax.all_to_all(blocks, pair, split_axis=3, concat_axis=3, tiled=True)  6.52 us
    unnamed x29, local copies, waits for them, and re-layouts  5.18 us
    slice x1, local copies, waits for them, and re-layouts, carried_terms(): gathered[:, :token_count, :].reshape(blocks * token_count, head_size)  4.03 us
  transfers between devices with their start and end apart: 12, of which 8 were waited for; matrix products, arithmetic and copies ran while one was open for 6% of the time, Pallas kernels for 0%

profile of v8, /device:TPU:1, one launch (start us, length us, event | category | flops | bytes accessed | tf_op | source)
XLA Modules:
  0.0 173.0 jit_solution(8328964076708865714)
XLA Ops:
  6.5 0.7 convert_bitcast_fusion
  7.2 0.9 multiply_bitcast_fusion
  8.1 4.0 %collective-permute-start = (bf16[1,3,512]{2,1,0:T(4,128)(2,1)S(1)}, bf16[1,3,512]{2,1,0:T(4,128)(2,1)S(1)}, u32[]{:S(2)}, u32[]{:S(2)}) collective-permute-start(bf16[1,3,512]{2,1,0:T(4,128)(2,1)S(1)} %slice.105), channel_id=1, source_target_pairs={{0,16},{16,32},{32,48},{48,64},{64,80},{80,96},{96,112},{112,128},... | collective-permute-start | bytes 9224 | tf_op jit(solution)/shard_map/ppermute | solution.py:16
  12.2 1.3 convolution_convert_fusion.1
  13.5 0.9 fusion.67
  14.5 0.7 fusion.4
  15.6 0.7 slice.95
  21.1 0.7 fusion.57
  21.8 1.5 convolution_bitcast_fusion
  23.5 0.7 pad_maximum_fusion.1
  24.2 4.2 %collective-permute-start.1 = (bf16[512,128]{1,0:T(8,128)(2,1)}, bf16[512,128]{1,0:T(8,128)(2,1)S(1)}, u32[]{:S(2)}, u32[]{:S(2)}) collective-permute-start(bf16[512,128]{1,0:T(8,128)(2,1)} %param.19), channel_id=1, source_target_pairs={{0,128},{128,256},{256,384},{384,0},{1,129},{129,257},{257,385},{3... | collective-permute-start | bytes 393224 | tf_op jit(solution)/shard_map/ppermute | solution.py:37
  28.3 3.2 %collective-permute-start.3 = (bf16[512,128]{1,0:T(8,128)(2,1)}, bf16[512,128]{1,0:T(8,128)(2,1)S(1)}, u32[]{:S(2)}, u32[]{:S(2)}) collective-permute-start(bf16[512,128]{1,0:T(8,128)(2,1)} %param.19), channel_id=1, source_target_pairs={{0,384},{128,0},{256,128},{384,256},{1,385},{129,1},{257,129},{385... | collective-permute-start | bytes 393224 | tf_op jit(solution)/shard_map/ppermute | solution.py:40
  31.5 0.6 collective-permute-done.1
  32.2 2.1 %collective-permute-start.2 = (bf16[512,128]{1,0:T(8,128)(2,1)S(1)}, bf16[512,128]{1,0:T(8,128)(2,1)S(1)}, u32[]{:S(2)}, u32[]{:S(2)}) collective-permute-start(bf16[512,128]{1,0:T(8,128)(2,1)S(1)} %collective-permute-done.1), channel_id=1, source_target_pairs={{0,128},{128,256},{256,384},{384,0},{1,129},{129,257},{257,385},{3... | collective-permute-start | bytes 393224 | tf_op jit(solution)/shard_map/ppermute | solution.py:37
  34.3 4.8 %collective-permute-done.2 = bf16[512,128]{1,0:T(8,128)(2,1)S(1)} collective-permute-done((bf16[512,128]{1,0:T(8,128)(2,1)S(1)}, bf16[512,128]{1,0:T(8,128)(2,1)S(1)}, u32[]{:S(2)}, u32[]{:S(2)}) %collective-permute-start.2) | collective-permute-done | bytes 131104 | tf_op jit(solution)/shard_map/ppermute | solution.py:37
  39.1 1.0 pad_maximum_fusion
  40.1 2.4 %collective-permute-start.4 = (bf16[4,512,128]{2,1,0:T(8,128)(2,1)S(1)}, bf16[4,512,128]{2,1,0:T(8,128)(2,1)S(1)}, u32[]{:S(2)}, u32[]{:S(2)}) collective-permute-start(bf16[4,512,128]{2,1,0:T(8,128)(2,1)S(1)} %pad_maximum_fusion), channel_id=1, source_target_pairs={{0,16},{16,32},{32,48},{48,64},{64,80},{80,96},{96,112},{112,0},{1... | collective-permute-start | bytes 1572872 | tf_op jit(solution)/shard_map/ppermute | solution.py:37
  42.5 10.2 %collective-permute-done.4 = bf16[4,512,128]{2,1,0:T(8,128)(2,1)S(1)} collective-permute-done((bf16[4,512,128]{2,1,0:T(8,128)(2,1)S(1)}, bf16[4,512,128]{2,1,0:T(8,128)(2,1)S(1)}, u32[]{:S(2)}, u32[]{:S(2)}) %collective-permute-start.4) | collective-permute-done | bytes 524320 | tf_op jit(solution)/shard_map/ppermute | solution.py:37
  52.7 1.9 %collective-permute-start.5 = (bf16[4,512,128]{2,1,0:T(8,128)(2,1)S(1)}, bf16[4,512,128]{2,1,0:T(8,128)(2,1)S(1)}, u32[]{:S(2)}, u32[]{:S(2)}) collective-permute-start(bf16[4,512,128]{2,1,0:T(8,128)(2,1)S(1)} %collective-permute-done.4), channel_id=1, source_target_pairs={{0,16},{16,32},{32,48},{48,64},{64,80},{80,96},{96,112},{112,0},{1... | collective-permute-start | bytes 1572872 | tf_op jit(solution)/shard_map/ppermute | solution.py:37
  54.6 4.6 %collective-permute-start.8 = (bf16[4,512,128]{2,1,0:T(8,128)(2,1)S(1)}, bf16[4,512,128]{2,1,0:T(8,128)(2,1)S(1)}, u32[]{:S(2)}, u32[]{:S(2)}) collective-permute-start(bf16[4,512,128]{2,1,0:T(8,128)(2,1)S(1)} %pad_maximum_fusion), channel_id=1, source_target_pairs={{0,112},{16,0},{32,16},{48,32},{64,48},{80,64},{96,80},{112,96},{1... | collective-permute-start | bytes 1572872 | tf_op jit(solution)/shard_map/ppermute | solution.py:40
  59.2 7.7 %collective-permute-done.5 = bf16[4,512,128]{2,1,0:T(8,128)(2,1)S(1)} collective-permute-done((bf16[4,512,128]{2,1,0:T(8,128)(2,1)S(1)}, bf16[4,512,128]{2,1,0:T(8,128)(2,1)S(1)}, u32[]{:S(2)}, u32[]{:S(2)}) %collective-permute-start.5) | collective-permute-done | bytes 524320 | tf_op jit(solution)/shard_map/ppermute | solution.py:37
  66.9 4.9 %collective-permute-start.6 = (bf16[4,512,128]{2,1,0:T(8,128)(2,1)S(1)}, bf16[4,512,128]{2,1,0:T(8,128)(2,1)S(1)}, u32[]{:S(2)}, u32[]{:S(2)}) collective-permute-start(bf16[4,512,128]{2,1,0:T(8,128)(2,1)S(1)} %collective-permute-done.5), channel_id=1, source_target_pairs={{0,16},{16,32},{32,48},{48,64},{64,80},{80,96},{96,112},{112,0},{1... | collective-permute-start | bytes 1572872 | tf_op jit(solution)/shard_map/ppermute | solution.py:37
  71.8 1.9 %collective-permute-start.9 = (bf16[4,512,128]{2,1,0:T(8,128)(2,1)S(1)}, bf16[4,512,128]{2,1,0:T(8,128)(2,1)S(1)}, u32[]{:S(2)}, u32[]{:S(2)}) collective-permute-start(bf16[4,512,128]{2,1,0:T(8,128)(2,1)S(1)} %collective-permute-done.8), channel_id=1, source_target_pairs={{0,112},{16,0},{32,16},{48,32},{64,48},{80,64},{96,80},{112,96},{1... | collective-permute-start | bytes 1572872 | tf_op jit(solution)/shard_map/ppermute | solution.py:40
  73.7 5.6 %collective-permute-done.6 = bf16[4,512,128]{2,1,0:T(8,128)(2,1)S(1)} collective-permute-done((bf16[4,512,128]{2,1,0:T(8,128)(2,1)S(1)}, bf16[4,512,128]{2,1,0:T(8,128)(2,1)S(1)}, u32[]{:S(2)}, u32[]{:S(2)}) %collective-permute-start.6) | collective-permute-done | bytes 524320 | tf_op jit(solution)/shard_map/ppermute | solution.py:37
  79.4 3.6 %collective-permute-start.7 = (bf16[4,512,128]{2,1,0:T(8,128)(2,1)S(1)}, bf16[4,512,128]{2,1,0:T(8,128)(2,1)S(1)}, u32[]{:S(2)}, u32[]{:S(2)}) collective-permute-start(bf16[4,512,128]{2,1,0:T(8,128)(2,1)S(1)} %collective-permute-done.6), channel_id=1, source_target_pairs={{0,16},{16,32},{32,48},{48,64},{64,80},{80,96},{96,112},{112,0},{1... | collective-permute-start | bytes 1572872 | tf_op jit(solution)/shard_map/ppermute | solution.py:37
  83.1 1.1 fusion.3
  84.3 3.0 %collective-permute-start.10 = (bf16[4,512,128]{2,1,0:T(8,128)(2,1)S(1)}, bf16[4,512,128]{2,1,0:T(8,128)(2,1)S(1)}, u32[]{:S(2)}, u32[]{:S(2)}) collective-permute-start(bf16[4,512,128]{2,1,0:T(8,128)(2,1)S(1)} %collective-permute-done.9), channel_id=1, source_target_pairs={{0,112},{16,0},{32,16},{48,32},{64,48},{80,64},{96,80},{112,96},{1... | collective-permute-start | bytes 1572872 | tf_op jit(solution)/shard_map/ppermute | solution.py:40
  87.3 13.9 %collective-permute-done.7 = bf16[4,512,128]{2,1,0:T(8,128)(2,1)S(1)} collective-permute-done((bf16[4,512,128]{2,1,0:T(8,128)(2,1)S(1)}, bf16[4,512,128]{2,1,0:T(8,128)(2,1)S(1)}, u32[]{:S(2)}, u32[]{:S(2)}) %collective-permute-start.7) | collective-permute-done | bytes 524320 | tf_op jit(solution)/shard_map/ppermute | solution.py:37
  101.2 0.8 bitcast_dynamic-update-slice_fusion.7
  102.0 0.8 bitcast_dynamic-update-slice_fusion.6
  102.9 0.8 bitcast_dynamic-update-slice_fusion.5
  103.7 0.9 bitcast_dynamic-update-slice_fusion.4
  104.5 0.8 bitcast_dynamic-update-slice_fusion.3
  105.4 0.8 bitcast_dynamic-update-slice_fusion.2
  106.2 0.9 bitcast_dynamic-update-slice_fusion.1
  107.4 0.9 bitcast_dynamic-update-slice_fusion
  108.3 14.6 %all-gather.3.cloned.1.call-done = bf16[4608,512]{1,0:T(8,128)(2,1)} async-done(((bf16[144,512]{1,0:T(8,128)(2,1)}), bf16[4608,512]{1,0:T(8,128)(2,1)}) %all-gather.3.cloned.1.call-update) | async-done | bytes 4718608 | tf_op jit(solution)/shard_map/all_gather | solution.py:134
  122.9 0.8 slice.115
  123.7 4.0 %fusion.66 = (bf16[32,64,512]{2,1,0:T(8,128)(2,1)}, bf16[32,64,512]{2,1,0:T(8,128)(2,1)S(1)}) fusion(bf16[32,144,512]{2,1,0:T(8,128)(2,1)} %bitcast.115), kind=kLoop, calls=%fused_computation.111 | loop fusion | bytes 8388608 | tf_op jit(solution)/shard_map/slice | solution.py:65
  127.8 0.6 fusion.54
  128.6 0.8 subtract_reduce_fusion
  129.8 1.2 broadcast_in_dim.20
  130.9 2.4 %convolution_multiply_fusion = f32[64,2048]{1,0:T(8,128)S(1)} fusion(f32[64,2048]{1,0:T(8,128)} %broadcast_in_dim.20, bf16[2048,512]{1,0:T(8,128)(2,1)} %bitcast.113, f32[1,64,1024]{2,1,0:T(8,128)S(1)} %convolution_bitcast_fusion), kind=kOutput, calls=%fused_computation | convolution fusion | flops 134348800 | bytes 3211264 | tf_op jit(solution)/shard_map/vtd,sd->vts/dot_general | solution.py:76
  133.9 0.6 fusion.68
  134.7 3.1 %fusion = bf16[1,64,8,4,128]{4,1,3,2,0:T(8,128)(2,1)S(1)} fusion(bf16[8,4,512,128]{3,2,1,0:T(8,128)(2,1)} %bitcast_dynamic-update-slice_fusion, f32[64,512]{1,0:T(8,128)S(1)} %get-tuple-element.28, f32[512]{0:T(512)S(1)} %copy-done.10, f32[64]{0:T(128)S(1)} %add_rsqrt_fusion, f32[64]{0:T(128)S(1)} %broadcast_multiply_fusion), kind=kOutput, calls=%fused_computation.2 | convolution fusion | flops 268828672 | bytes 4852224 | tf_op jit(solution)/shard_map/vtr,edrc->vtedc/dot_general | solution.py:142
  139.0 6.5 %all_to_all.10 = bf16[1,64,4,2,512]{4,2,1,0,3:T(4,128)(2,1)S(1)} all-to-all(bf16[1,64,4,2,512]{4,2,1,0,3:T(4,128)(2,1)S(1)} %copy.22), channel_id=1, replica_groups=mesh['seq_0'=4,'seq_1'=8,'head_0'=4,'head_1'=2,'var'=2] {'head_1'}, dimensions={3} | all-to-all | bytes 1048576 | tf_op jit(solution)/shard_map/all_to_all | solution.py:151
  146.0 19.5 %all_to_all.11 = bf16[1,64,4,512]{3,1,0,2:T(8,128)(2,1)S(1)} all-to-all(bf16[1,64,4,512]{3,1,0,2:T(8,128)(2,1)S(1)} %copy.23), channel_id=1, replica_groups=mesh['seq_0'=4,'seq_1'=8,'head_0'=4,'head_1'=2,'var'=2] {'head_0'}, dimensions={2} | all-to-all | bytes 524288 | tf_op jit(solution)/shard_map/all_to_all | solution.py:153
  165.6 0.6 fusion.20
  (55 shorter events, 4.1 us)
Async XLA Ops:
  6.5 8.0 %copy-start = (bf16[1,2,512]{2,1,0:T(2,128)(2,1)S(1)}, bf16[1,2,512]{2,1,0:T(2,128)(2,1)}, u32[]{:S(2)}) copy-start(bf16[1,2,512]{2,1,0:T(2,128)(2,1)} %param.16) | copy-start | bytes 6148
  6.5 116.3 %all-gather.3.cloned.1.call-start = ((), (), s32[]{:S(2)}) async-start(), calls=%async_computation.2 | async-start | bytes 4866048 | tf_op jit(solution)/shard_map/all_gather | solution.py:134
  8.1 6.2 %collective-permute-start = (bf16[1,3,512]{2,1,0:T(4,128)(2,1)S(1)}, bf16[1,3,512]{2,1,0:T(4,128)(2,1)S(1)}, u32[]{:S(2)}, u32[]{:S(2)}) collective-permute-start(bf16[1,3,512]{2,1,0:T(4,128)(2,1)S(1)} %slice.105), channel_id=1, source_target_pairs={{0,16},{16,32},{32,48},{48,64},{64,80},{80,96},{96,112},{112,128},... | collective-permute-start | bytes 9224 | tf_op jit(solution)/shard_map/ppermute | solution.py:16
  13.5 25.6 %copy-start.8 = (bf16[64,512]{1,0:T(8,128)(2,1)}, bf16[64,512]{1,0:T(8,128)(2,1)S(1)}, u32[]{:S(2)}) copy-start(bf16[64,512]{1,0:T(8,128)(2,1)S(1)} %convolution_convert_fusion.1) | copy-start | bytes 196612
  24.2 8.0 %collective-permute-start.1 = (bf16[512,128]{1,0:T(8,128)(2,1)}, bf16[512,128]{1,0:T(8,128)(2,1)S(1)}, u32[]{:S(2)}, u32[]{:S(2)}) collective-permute-start(bf16[512,128]{1,0:T(8,128)(2,1)} %param.19), channel_id=1, source_target_pairs={{0,128},{128,256},{256,384},{384,0},{1,129},{129,257},{257,385},{3... | collective-permute-start | bytes 393224 | tf_op jit(solution)/shard_map/ppermute | solution.py:37
  28.3 5.9 %collective-permute-start.3 = (bf16[512,128]{1,0:T(8,128)(2,1)}, bf16[512,128]{1,0:T(8,128)(2,1)S(1)}, u32[]{:S(2)}, u32[]{:S(2)}) collective-permute-start(bf16[512,128]{1,0:T(8,128)(2,1)} %param.19), channel_id=1, source_target_pairs={{0,384},{128,0},{256,128},{384,256},{1,385},{129,1},{257,129},{385... | collective-permute-start | bytes 393224 | tf_op jit(solution)/shard_map/ppermute | solution.py:40
  32.2 47.2 %copy-start.2 = (bf16[512,128]{1,0:T(8,128)(2,1)}, bf16[512,128]{1,0:T(8,128)(2,1)S(1)}, u32[]{:S(2)}) copy-start(bf16[512,128]{1,0:T(8,128)(2,1)S(1)} %collective-permute-done.1) | copy-start | bytes 393220
  32.2 6.9 %collective-permute-start.2 = (bf16[512,128]{1,0:T(8,128)(2,1)S(1)}, bf16[512,128]{1,0:T(8,128)(2,1)S(1)}, u32[]{:S(2)}, u32[]{:S(2)}) collective-permute-start(bf16[512,128]{1,0:T(8,128)(2,1)S(1)} %collective-permute-done.1), channel_id=1, source_target_pairs={{0,128},{128,256},{256,384},{384,0},{1,129},{129,257},{257,385},{3... | collective-permute-start | bytes 393224 | tf_op jit(solution)/shard_map/ppermute | solution.py:37
  34.3 48.7 %copy-start.4 = (bf16[512,128]{1,0:T(8,128)(2,1)}, bf16[512,128]{1,0:T(8,128)(2,1)S(1)}, u32[]{:S(2)}) copy-start(bf16[512,128]{1,0:T(8,128)(2,1)S(1)} %collective-permute-done.3) | copy-start | bytes 393220
  39.1 43.9 %copy-start.6 = (bf16[512,128]{1,0:T(8,128)(2,1)}, bf16[512,128]{1,0:T(8,128)(2,1)S(1)}, u32[]{:S(2)}) copy-start(bf16[512,128]{1,0:T(8,128)(2,1)S(1)} %collective-permute-done.2) | copy-start | bytes 393220
  40.1 12.6 %collective-permute-start.4 = (bf16[4,512,128]{2,1,0:T(8,128)(2,1)S(1)}, bf16[4,512,128]{2,1,0:T(8,128)(2,1)S(1)}, u32[]{:S(2)}, u32[]{:S(2)}) collective-permute-start(bf16[4,512,128]{2,1,0:T(8,128)(2,1)S(1)} %pad_maximum_fusion), channel_id=1, source_target_pairs={{0,16},{16,32},{32,48},{48,64},{64,80},{80,96},{96,112},{112,0},{1... | collective-permute-start | bytes 1572872 | tf_op jit(solution)/shard_map/ppermute | solution.py:37
  52.7 14.2 %collective-permute-start.5 = (bf16[4,512,128]{2,1,0:T(8,128)(2,1)S(1)}, bf16[4,512,128]{2,1,0:T(8,128)(2,1)S(1)}, u32[]{:S(2)}, u32[]{:S(2)}) collective-permute-start(bf16[4,512,128]{2,1,0:T(8,128)(2,1)S(1)} %collective-permute-done.4), channel_id=1, source_target_pairs={{0,16},{16,32},{32,48},{48,64},{64,80},{80,96},{96,112},{112,0},{1... | collective-permute-start | bytes 1572872 | tf_op jit(solution)/shard_map/ppermute | solution.py:37
  54.6 17.2 %collective-permute-start.8 = (bf16[4,512,128]{2,1,0:T(8,128)(2,1)S(1)}, bf16[4,512,128]{2,1,0:T(8,128)(2,1)S(1)}, u32[]{:S(2)}, u32[]{:S(2)}) collective-permute-start(bf16[4,512,128]{2,1,0:T(8,128)(2,1)S(1)} %pad_maximum_fusion), channel_id=1, source_target_pairs={{0,112},{16,0},{32,16},{48,32},{64,48},{80,64},{96,80},{112,96},{1... | collective-permute-start | bytes 1572872 | tf_op jit(solution)/shard_map/ppermute | solution.py:40
  66.9 12.5 %collective-permute-start.6 = (bf16[4,512,128]{2,1,0:T(8,128)(2,1)S(1)}, bf16[4,512,128]{2,1,0:T(8,128)(2,1)S(1)}, u32[]{:S(2)}, u32[]{:S(2)}) collective-permute-start(bf16[4,512,128]{2,1,0:T(8,128)(2,1)S(1)} %collective-permute-done.5), channel_id=1, source_target_pairs={{0,16},{16,32},{32,48},{48,64},{64,80},{80,96},{96,112},{112,0},{1... | collective-permute-start | bytes 1572872 | tf_op jit(solution)/shard_map/ppermute | solution.py:37
  71.8 12.4 %collective-permute-start.9 = (bf16[4,512,128]{2,1,0:T(8,128)(2,1)S(1)}, bf16[4,512,128]{2,1,0:T(8,128)(2,1)S(1)}, u32[]{:S(2)}, u32[]{:S(2)}) collective-permute-start(bf16[4,512,128]{2,1,0:T(8,128)(2,1)S(1)} %collective-permute-done.8), channel_id=1, source_target_pairs={{0,112},{16,0},{32,16},{48,32},{64,48},{80,64},{96,80},{112,96},{1... | collective-permute-start | bytes 1572872 | tf_op jit(solution)/shard_map/ppermute | solution.py:40
  79.4 21.8 %collective-permute-start.7 = (bf16[4,512,128]{2,1,0:T(8,128)(2,1)S(1)}, bf16[4,512,128]{2,1,0:T(8,128)(2,1)S(1)}, u32[]{:S(2)}, u32[]{:S(2)}) collective-permute-start(bf16[4,512,128]{2,1,0:T(8,128)(2,1)S(1)} %collective-permute-done.6), channel_id=1, source_target_pairs={{0,16},{16,32},{32,48},{48,64},{64,80},{80,96},{96,112},{112,0},{1... | collective-permute-start | bytes 1572872 | tf_op jit(solution)/shard_map/ppermute | solution.py:37
  84.2 20.3 %copy-start.1 = (bf16[512,128]{1,0:T(8,128)(2,1)S(1)}, bf16[512,128]{1,0:T(8,128)(2,1)}, u32[]{:S(2)}) copy-start(bf16[512,128]{1,0:T(8,128)(2,1)} %param.19) | copy-start | bytes 393220
  84.2 20.3 %copy-start.3 = (bf16[512,128]{1,0:T(8,128)(2,1)S(1)}, bf16[512,128]{1,0:T(8,128)(2,1)}, u32[]{:S(2)}) copy-start(bf16[512,128]{1,0:T(8,128)(2,1)} %copy-done.2) | copy-start | bytes 393220
  84.2 20.3 %copy-start.5 = (bf16[512,128]{1,0:T(8,128)(2,1)S(1)}, bf16[512,128]{1,0:T(8,128)(2,1)}, u32[]{:S(2)}) copy-start(bf16[512,128]{1,0:T(8,128)(2,1)} %copy-done.4) | copy-start | bytes 393220
  84.2 20.3 %copy-start.7 = (bf16[512,128]{1,0:T(8,128)(2,1)S(1)}, bf16[512,128]{1,0:T(8,128)(2,1)}, u32[]{:S(2)}) copy-start(bf16[512,128]{1,0:T(8,128)(2,1)} %copy-done.6) | copy-start | bytes 393220
  84.3 23.2 %collective-permute-start.10 = (bf16[4,512,128]{2,1,0:T(8,128)(2,1)S(1)}, bf16[4,512,128]{2,1,0:T(8,128)(2,1)S(1)}, u32[]{:S(2)}, u32[]{:S(2)}) collective-permute-start(bf16[4,512,128]{2,1,0:T(8,128)(2,1)S(1)} %collective-permute-done.9), channel_id=1, source_target_pairs={{0,112},{16,0},{32,16},{48,32},{64,48},{80,64},{96,80},{112,96},{1... | collective-permute-start | bytes 1572872 | tf_op jit(solution)/shard_map/ppermute | solution.py:40
  130.9 3.7 %copy-start.10 = (f32[512]{0:T(512)S(1)}, f32[512]{0:T(512)}, u32[]{:S(2)}) copy-start(f32[512]{0:T(512)} %param.18) | copy-start | bytes 6148
  137.7 27.8 %copy-start.9 = (bf16[64,512]{1,0:T(8,128)(2,1)S(1)}, bf16[64,512]{1,0:T(8,128)(2,1)}, u32[]{:S(2)}) copy-start(bf16[64,512]{1,0:T(8,128)(2,1)} %param.12) | copy-start | bytes 196612
Sparse Core Ops, SparseCore 0:
  24.3 98.5 all-gather.2

commit v9 on v8

--- a/solution.py
+++ b/solution.py
@@ -7,7 +7,7 @@
 CONV = 4
 SEQ = ("seq_0", "seq_1")
 HEAD = ("head_1", "head_0")
-EXTRA = 16
+EXTRA = 8
 
 
 def from_behind(value, axis, steps):
@@ -59,26 +59,25 @@
     return jnp.einsum("vts,vse->vte", weights, values, preferred_element_type=jnp.float32)
 
 
-def carried_terms(queries, cumulated, gathered, block):
-    blocks, rows, head_size = gathered.shape
+def carried_terms(queries, cumulated, gathered, values_ring, block, outer, inner_size):
+    blocks = gathered.shape[0]
     token_count = queries.shape[1]
-    keys_all = gathered[:, :token_count, :].reshape(blocks * token_count, head_size)
-    values_all = gathered[:, token_count : 2 * token_count, :].reshape(blocks * token_count, head_size)
-    parts = gathered[:, 2 * token_count, :3].astype(jnp.float32)
+    keys_all = gathered[:, :token_count, :]
+    parts = gathered[:, token_count, :3].astype(jnp.float32)
     decay = (parts[:, 0] + parts[:, 1]) + parts[:, 2]
     through = jnp.cumsum(decay)
-    before_own = jnp.sum(jnp.where(jnp.arange(blocks) < block, decay, 0.0))
     earlier = jnp.arange(blocks) < block
+    before_own = jnp.sum(jnp.where(earlier, decay, 0.0))
     block_exponent = jnp.where(earlier, before_own - through, -jnp.inf)
-    exponent = cumulated[:, :, None, None] + block_exponent[None, None, :, None]
-    scale = jnp.exp(jnp.broadcast_to(exponent, (*cumulated.shape, blocks, token_count)))
-    scale = scale.reshape(*cumulated.shape, blocks * token_count)
-    scores = jnp.einsum("vtd,sd->vts", queries, keys_all, preferred_element_type=jnp.float32)
-    weights = scores * scale
+    scale = jnp.exp(cumulated[:, :, None, None] + block_exponent[None, None, :, None])
+    scores = jnp.einsum("vtd,bsd->vtbs", queries, keys_all, preferred_element_type=jnp.float32)
+    weights = (scores * scale).reshape(*queries.shape[:2], outer, inner_size, token_count)
+    weights = jnp.roll(weights, outer // 2 - lax.axis_index(SEQ[0]), axis=2)
+    weights = jnp.roll(weights, inner_size // 2 - lax.axis_index(SEQ[1]), axis=3)
     high = weights.astype(jnp.bfloat16)
     low = (weights - high.astype(jnp.float32)).astype(jnp.bfloat16)
-    return jnp.einsum("vts,se->vte", high, values_all, preferred_element_type=jnp.float32) + jnp.einsum(
-        "vts,se->vte", low, values_all, preferred_element_type=jnp.float32
+    return jnp.einsum("vtqps,pqse->vte", high, values_ring, preferred_element_type=jnp.float32) + jnp.einsum(
+        "vtqps,pqse->vte", low, values_ring, preferred_element_type=jnp.float32
     )
 
 
@@ -130,11 +129,12 @@
     scaled_keys = (key_scale[..., None] * key_rows.astype(jnp.float32)).astype(jnp.bfloat16)
     extra = jnp.zeros((EXTRA, head_size), jnp.bfloat16)
     extra = extra.at[0, :3].set(three_parts(block_decay[0]))
-    packed = jnp.concatenate([scaled_keys[0], values[0], extra], axis=0)
+    packed = jnp.concatenate([scaled_keys[0], extra], axis=0)
     gathered = lax.all_gather(packed, SEQ, axis=0, tiled=False)
+    values_ring = ring_pieces(ring_pieces(values[0], SEQ[0], outer), SEQ[1], inner_size)
     block = lax.axis_index(SEQ)
     intra_part = local_terms(queries, key_rows, values, cumulated, input_log)
-    numerator = carried_terms(queries, cumulated, gathered, block) + intra_part
+    numerator = carried_terms(queries, cumulated, gathered, values_ring, block, outer, inner_size) + intra_part
     row_mean = jnp.mean(numerator, axis=-1, keepdims=True)
     centred = numerator - row_mean
     row_var = jnp.mean(centred * centred, axis=-1, keepdims=True)

time: 175 us -> 188 us (1.074)
  starting transfers between devices: 35.7 us -> 68.4 us
  waiting for transfers between devices: 57.8 us -> 36.4 us
  blocking collectives: 26 us -> 28.2 us
    ppermute x6 -> x12, starting transfers between devices: 19 us -> 37.2 us  [ring_pieces(): forward = lax.ppermute(forward, axis, ahead)]
    ppermute x4 -> x8, starting transfers between devices: 12.7 us -> 28 us  [ring_pieces(): backward = lax.ppermute(backward, axis, behind)]
    ppermute x6 -> x12, waiting for transfers between devices: 42.9 us -> 30.7 us  [ring_pieces(): forward = lax.ppermute(forward, axis, ahead)]
    all_gather x1, waiting for transfers between devices: 14.6 us -> 5.4 us  [body(): gathered = lax.all_gather(packed, SEQ, axis=0, tiled=False)]
    unnamed x29 -> x38, local copies, waits for them, and re-layouts: 5.18 us -> 9.48 us
    slice x2 -> x1, local copies, waits for them, and re-layouts: 4.88 us -> 0.85 us  [carried_terms(): parts = gathered[:, token_count, :3].astype(jnp.float32)]
    all_to_all x1, blocking collectives: 6.52 us -> 8.46 us  [body(): lax.all_to_all(blocks, pair, split_axis=3, concat_axis=3, tiled=True)]
  transfers between devices with their start and end apart: 12 -> 22, of which waited for: 8 -> 8; matrix products, arithmetic and copies ran while one was open for 6% -> 11% of each run, Pallas kernels for 0% -> 0%
where the time goes in v9:
time: 188 us; the launch traced here: 185 us
  starting transfers between devices  68.4 us (36%)
  waiting for transfers between devices  36.4 us (19%)
  blocking collectives  28.2 us (15%)
  between operations  18.9 us (10%)
  local copies, waits for them, and re-layouts  13.5 us (7%)
  matrix products  11.7 us (6%)
  other arithmetic  7.88 us (4%)
    ppermute x12, starting transfers between devices, ring_pieces(): forward = lax.ppermute(forward, axis, ahead)  37.2 us
    ppermute x12, waiting for transfers between devices, ring_pieces(): forward = lax.ppermute(forward, axis, ahead)  30.7 us
    ppermute x8, starting transfers between devices, ring_pieces(): backward = lax.ppermute(backward, axis, behind)  28 us
    all_to_all x1, blocking collectives, body(): lax.all_to_all(pair_sum, across, split_axis=2, concat_axis=2, tiled=True)  19.8 us
    unnamed x38, local copies, waits for them, and re-layouts  9.48 us
    all_to_all x1, blocking collectives, body(): lax.all_to_all(blocks, pair, split_axis=3, concat_axis=3, tiled=True)  8.46 us
    all_gather x1, waiting for transfers between devices, body(): gathered = lax.all_gather(packed, SEQ, axis=0, tiled=False)  5.4 us
  transfers between devices with their start and end apart: 22, of which 8 were waited for; matrix products, arithmetic and copies ran while one was open for 11% of the time, Pallas kernels for 0%

profile of v9, /device:TPU:1, one launch (start us, length us, event | category | flops | bytes accessed | tf_op | source)
XLA Modules:
  0.0 185.2 jit_solution(14890349398468032473)
XLA Ops:
  6.5 5.3 %collective-permute-start.13 = (bf16[512,128]{1,0:T(8,128)(2,1)}, bf16[512,128]{1,0:T(8,128)(2,1)S(1)}, u32[]{:S(2)}, u32[]{:S(2)}) collective-permute-start(bf16[512,128]{1,0:T(8,128)(2,1)} %param.19), channel_id=1, source_target_pairs={{0,384},{128,0},{256,128},{384,256},{1,385},{129,1},{257,129},{385... | collective-permute-start | bytes 393224 | tf_op jit(solution)/shard_map/ppermute | solution.py:40
  11.9 1.9 %collective-permute-start.11 = (bf16[512,128]{1,0:T(8,128)(2,1)}, bf16[512,128]{1,0:T(8,128)(2,1)S(1)}, u32[]{:S(2)}, u32[]{:S(2)}) collective-permute-start(bf16[512,128]{1,0:T(8,128)(2,1)} %param.19), channel_id=1, source_target_pairs={{0,128},{128,256},{256,384},{384,0},{1,129},{129,257},{257,385},{3... | collective-permute-start | bytes 393224 | tf_op jit(solution)/shard_map/ppermute | solution.py:37
  14.5 1.4 convolution_convert_fusion.1
  15.8 4.6 %collective-permute-start.3 = (bf16[64,512]{1,0:T(8,128)(2,1)S(1)}, bf16[64,512]{1,0:T(8,128)(2,1)S(1)}, u32[]{:S(2)}, u32[]{:S(2)}) collective-permute-start(bf16[64,512]{1,0:T(8,128)(2,1)S(1)} %convolution_convert_fusion.1), channel_id=1, source_target_pairs={{0,384},{128,0},{256,128},{384,256},{1,385},{129,1},{257,129},{385... | collective-permute-start | bytes 196616 | tf_op jit(solution)/shard_map/ppermute | solution.py:40
  20.4 1.9 %collective-permute-start.1 = (bf16[64,512]{1,0:T(8,128)(2,1)S(1)}, bf16[64,512]{1,0:T(8,128)(2,1)S(1)}, u32[]{:S(2)}, u32[]{:S(2)}) collective-permute-start(bf16[64,512]{1,0:T(8,128)(2,1)S(1)} %convolution_convert_fusion.1), channel_id=1, source_target_pairs={{0,128},{128,256},{256,384},{384,0},{1,129},{129,257},{257,385},{3... | collective-permute-start | bytes 196616 | tf_op jit(solution)/shard_map/ppermute | solution.py:37
  22.3 0.9 multiply_bitcast_fusion
  23.3 3.2 %collective-permute-start = (bf16[1,3,512]{2,1,0:T(4,128)(2,1)S(1)}, bf16[1,3,512]{2,1,0:T(4,128)(2,1)S(1)}, u32[]{:S(2)}, u32[]{:S(2)}) collective-permute-start(bf16[1,3,512]{2,1,0:T(4,128)(2,1)S(1)} %slice.101), channel_id=1, source_target_pairs={{0,16},{16,32},{32,48},{48,64},{64,80},{80,96},{96,112},{112,128},... | collective-permute-start | bytes 9224 | tf_op jit(solution)/shard_map/ppermute | solution.py:16
  26.5 0.9 fusion.74
  29.7 5.1 %collective-permute-start.2 = (bf16[64,512]{1,0:T(8,128)(2,1)S(1)}, bf16[64,512]{1,0:T(8,128)(2,1)S(1)}, u32[]{:S(2)}, u32[]{:S(2)}) collective-permute-start(bf16[64,512]{1,0:T(8,128)(2,1)S(1)} %collective-permute-done.1), channel_id=1, source_target_pairs={{0,128},{128,256},{256,384},{384,0},{1,129},{129,257},{257,385},{3... | collective-permute-start | bytes 196616 | tf_op jit(solution)/shard_map/ppermute | solution.py:37
  34.8 1.5 convolution_bitcast_fusion
  36.4 1.9 %collective-permute-done.2 = bf16[64,512]{1,0:T(8,128)(2,1)S(1)} collective-permute-done((bf16[64,512]{1,0:T(8,128)(2,1)S(1)}, bf16[64,512]{1,0:T(8,128)(2,1)S(1)}, u32[]{:S(2)}, u32[]{:S(2)}) %collective-permute-start.2) | collective-permute-done | bytes 65568 | tf_op jit(solution)/shard_map/ppermute | solution.py:37
  38.3 1.9 %collective-permute-start.4 = (bf16[4,64,512]{2,1,0:T(8,128)(2,1)S(1)}, bf16[4,64,512]{2,1,0:T(8,128)(2,1)S(1)}, u32[]{:S(2)}, u32[]{:S(2)}) collective-permute-start(bf16[4,64,512]{2,1,0:T(8,128)(2,1)S(1)} %pad_maximum_fusion.1), channel_id=1, source_target_pairs={{0,16},{16,32},{32,48},{48,64},{64,80},{80,96},{96,112},{112,0},{1... | collective-permute-start | bytes 786440 | tf_op jit(solution)/shard_map/ppermute | solution.py:37
  45.3 1.9 %collective-permute-start.12 = (bf16[512,128]{1,0:T(8,128)(2,1)S(1)}, bf16[512,128]{1,0:T(8,128)(2,1)S(1)}, u32[]{:S(2)}, u32[]{:S(2)}) collective-permute-start(bf16[512,128]{1,0:T(8,128)(2,1)S(1)} %collective-permute-done.11), channel_id=1, source_target_pairs={{0,128},{128,256},{256,384},{384,0},{1,129},{129,257},{257,385},{3... | collective-permute-start | bytes 393224 | tf_op jit(solution)/shard_map/ppermute | solution.py:37
  47.9 2.4 %collective-permute-start.5 = (bf16[4,64,512]{2,1,0:T(8,128)(2,1)S(1)}, bf16[4,64,512]{2,1,0:T(8,128)(2,1)S(1)}, u32[]{:S(2)}, u32[]{:S(2)}) collective-permute-start(bf16[4,64,512]{2,1,0:T(8,128)(2,1)S(1)} %collective-permute-done.4), channel_id=1, source_target_pairs={{0,16},{16,32},{32,48},{48,64},{64,80},{80,96},{96,112},{112,0},{1... | collective-permute-start | bytes 786440 | tf_op jit(solution)/shard_map/ppermute | solution.py:37
  50.3 2.2 %collective-permute-done.12 = bf16[512,128]{1,0:T(8,128)(2,1)S(1)} collective-permute-done((bf16[512,128]{1,0:T(8,128)(2,1)S(1)}, bf16[512,128]{1,0:T(8,128)(2,1)S(1)}, u32[]{:S(2)}, u32[]{:S(2)}) %collective-permute-start.12) | collective-permute-done | bytes 131104 | tf_op jit(solution)/shard_map/ppermute | solution.py:37
  52.6 2.1 %collective-permute-start.14 = (bf16[4,512,128]{2,1,0:T(8,128)(2,1)S(1)}, bf16[4,512,128]{2,1,0:T(8,128)(2,1)S(1)}, u32[]{:S(2)}, u32[]{:S(2)}) collective-permute-start(bf16[4,512,128]{2,1,0:T(8,128)(2,1)S(1)} %pad_maximum_fusion), channel_id=1, source_target_pairs={{0,16},{16,32},{32,48},{48,64},{64,80},{80,96},{96,112},{112,0},{1... | collective-permute-start | bytes 1572872 | tf_op jit(solution)/shard_map/ppermute | solution.py:37
  54.7 4.4 %collective-permute-start.8 = (bf16[4,64,512]{2,1,0:T(8,128)(2,1)S(1)}, bf16[4,64,512]{2,1,0:T(8,128)(2,1)S(1)}, u32[]{:S(2)}, u32[]{:S(2)}) collective-permute-start(bf16[4,64,512]{2,1,0:T(8,128)(2,1)S(1)} %pad_maximum_fusion.1), channel_id=1, source_target_pairs={{0,112},{16,0},{32,16},{48,32},{64,48},{80,64},{96,80},{112,96},{1... | collective-permute-start | bytes 786440 | tf_op jit(solution)/shard_map/ppermute | solution.py:40
  59.1 3.1 %collective-permute-start.18 = (bf16[4,512,128]{2,1,0:T(8,128)(2,1)S(1)}, bf16[4,512,128]{2,1,0:T(8,128)(2,1)S(1)}, u32[]{:S(2)}, u32[]{:S(2)}) collective-permute-start(bf16[4,512,128]{2,1,0:T(8,128)(2,1)S(1)} %pad_maximum_fusion), channel_id=1, source_target_pairs={{0,112},{16,0},{32,16},{48,32},{64,48},{80,64},{96,80},{112,96},{1... | collective-permute-start | bytes 1572872 | tf_op jit(solution)/shard_map/ppermute | solution.py:40
  62.2 2.2 %collective-permute-start.6 = (bf16[4,64,512]{2,1,0:T(8,128)(2,1)S(1)}, bf16[4,64,512]{2,1,0:T(8,128)(2,1)}, u32[]{:S(2)}, u32[]{:S(2)}) collective-permute-start(bf16[4,64,512]{2,1,0:T(8,128)(2,1)S(1)} %collective-permute-done.5), channel_id=1, source_target_pairs={{0,16},{16,32},{32,48},{48,64},{64,80},{80,96},{96,112},{112,0},{1... | collective-permute-start | bytes 786440 | tf_op jit(solution)/shard_map/ppermute | solution.py:37
  64.4 4.3 %collective-permute-start.9 = (bf16[4,64,512]{2,1,0:T(8,128)(2,1)S(1)}, bf16[4,64,512]{2,1,0:T(8,128)(2,1)}, u32[]{:S(2)}, u32[]{:S(2)}) collective-permute-start(bf16[4,64,512]{2,1,0:T(8,128)(2,1)S(1)} %collective-permute-done.8), channel_id=1, source_target_pairs={{0,112},{16,0},{32,16},{48,32},{64,48},{80,64},{96,80},{112,96},{1... | collective-permute-start | bytes 786440 | tf_op jit(solution)/shard_map/ppermute | solution.py:40
  68.7 4.9 %collective-permute-done.6 = bf16[4,64,512]{2,1,0:T(8,128)(2,1)} collective-permute-done((bf16[4,64,512]{2,1,0:T(8,128)(2,1)S(1)}, bf16[4,64,512]{2,1,0:T(8,128)(2,1)}, u32[]{:S(2)}, u32[]{:S(2)}) %collective-permute-start.6) | collective-permute-done | bytes 262176 | tf_op jit(solution)/shard_map/ppermute | solution.py:37
  73.6 2.7 %collective-permute-start.7 = (bf16[4,64,512]{2,1,0:T(8,128)(2,1)}, bf16[4,64,512]{2,1,0:T(8,128)(2,1)}, u32[]{:S(2)}, u32[]{:S(2)}) collective-permute-start(bf16[4,64,512]{2,1,0:T(8,128)(2,1)} %collective-permute-done.6), channel_id=1, source_target_pairs={{0,16},{16,32},{32,48},{48,64},{64,80},{80,96},{96,112},{112,0},{1... | collective-permute-start | bytes 786440 | tf_op jit(solution)/shard_map/ppermute | solution.py:37
  76.5 4.9 %collective-permute-start.15 = (bf16[4,512,128]{2,1,0:T(8,128)(2,1)S(1)}, bf16[4,512,128]{2,1,0:T(8,128)(2,1)S(1)}, u32[]{:S(2)}, u32[]{:S(2)}) collective-permute-start(bf16[4,512,128]{2,1,0:T(8,128)(2,1)S(1)} %collective-permute-done.14), channel_id=1, source_target_pairs={{0,16},{16,32},{32,48},{48,64},{64,80},{80,96},{96,112},{112,0},{1... | collective-permute-start | bytes 1572872 | tf_op jit(solution)/shard_map/ppermute | solution.py:37
  81.3 1.0 fusion.9
  82.3 2.0 %collective-permute-start.10 = (bf16[4,64,512]{2,1,0:T(8,128)(2,1)}, bf16[4,64,512]{2,1,0:T(8,128)(2,1)S(1)}, u32[]{:S(2)}, u32[]{:S(2)}) collective-permute-start(bf16[4,64,512]{2,1,0:T(8,128)(2,1)} %collective-permute-done.9), channel_id=1, source_target_pairs={{0,112},{16,0},{32,16},{48,32},{64,48},{80,64},{96,80},{112,96},{1... | collective-permute-start | bytes 786440 | tf_op jit(solution)/shard_map/ppermute | solution.py:40
  84.4 2.2 %collective-permute-start.19 = (bf16[4,512,128]{2,1,0:T(8,128)(2,1)S(1)}, bf16[4,512,128]{2,1,0:T(8,128)(2,1)S(1)}, u32[]{:S(2)}, u32[]{:S(2)}) collective-permute-start(bf16[4,512,128]{2,1,0:T(8,128)(2,1)S(1)} %collective-permute-done.18), channel_id=1, source_target_pairs={{0,112},{16,0},{32,16},{48,32},{64,48},{80,64},{96,80},{112,96},{1... | collective-permute-start | bytes 1572872 | tf_op jit(solution)/shard_map/ppermute | solution.py:40
  86.6 1.0 bitcast_dynamic-update-slice_fusion.15
  87.6 1.0 bitcast_dynamic-update-slice_fusion.14
  88.6 4.1 %collective-permute-done.15 = bf16[4,512,128]{2,1,0:T(8,128)(2,1)S(1)} collective-permute-done((bf16[4,512,128]{2,1,0:T(8,128)(2,1)S(1)}, bf16[4,512,128]{2,1,0:T(8,128)(2,1)S(1)}, u32[]{:S(2)}, u32[]{:S(2)}) %collective-permute-start.15) | collective-permute-done | bytes 524320 | tf_op jit(solution)/shard_map/ppermute | solution.py:37
  92.7 5.8 %collective-permute-start.16 = (bf16[4,512,128]{2,1,0:T(8,128)(2,1)S(1)}, bf16[4,512,128]{2,1,0:T(8,128)(2,1)S(1)}, u32[]{:S(2)}, u32[]{:S(2)}) collective-permute-start(bf16[4,512,128]{2,1,0:T(8,128)(2,1)S(1)} %collective-permute-done.15), channel_id=1, source_target_pairs={{0,16},{16,32},{32,48},{48,64},{64,80},{80,96},{96,112},{112,0},{1... | collective-permute-start | bytes 1572872 | tf_op jit(solution)/shard_map/ppermute | solution.py:37
  98.5 1.0 bitcast_dynamic-update-slice_fusion.13
  99.5 6.6 %collective-permute-done.16 = bf16[4,512,128]{2,1,0:T(8,128)(2,1)S(1)} collective-permute-done((bf16[4,512,128]{2,1,0:T(8,128)(2,1)S(1)}, bf16[4,512,128]{2,1,0:T(8,128)(2,1)S(1)}, u32[]{:S(2)}, u32[]{:S(2)}) %collective-permute-start.16) | collective-permute-done | bytes 524320 | tf_op jit(solution)/shard_map/ppermute | solution.py:37
  106.1 4.4 %collective-permute-start.17 = (bf16[4,512,128]{2,1,0:T(8,128)(2,1)S(1)}, bf16[4,512,128]{2,1,0:T(8,128)(2,1)S(1)}, u32[]{:S(2)}, u32[]{:S(2)}) collective-permute-start(bf16[4,512,128]{2,1,0:T(8,128)(2,1)S(1)} %collective-permute-done.16), channel_id=1, source_target_pairs={{0,16},{16,32},{32,48},{48,64},{64,80},{80,96},{96,112},{112,0},{1... | collective-permute-start | bytes 1572872 | tf_op jit(solution)/shard_map/ppermute | solution.py:37
  110.5 1.0 bitcast_dynamic-update-slice_fusion.9
  111.6 2.1 %collective-permute-start.20 = (bf16[4,512,128]{2,1,0:T(8,128)(2,1)S(1)}, bf16[4,512,128]{2,1,0:T(8,128)(2,1)S(1)}, u32[]{:S(2)}, u32[]{:S(2)}) collective-permute-start(bf16[4,512,128]{2,1,0:T(8,128)(2,1)S(1)} %collective-permute-done.19), channel_id=1, source_target_pairs={{0,112},{16,0},{32,16},{48,32},{64,48},{80,64},{96,80},{112,96},{1... | collective-permute-start | bytes 1572872 | tf_op jit(solution)/shard_map/ppermute | solution.py:40
  113.7 10.9 %collective-permute-done.17 = bf16[4,512,128]{2,1,0:T(8,128)(2,1)S(1)} collective-permute-done((bf16[4,512,128]{2,1,0:T(8,128)(2,1)S(1)}, bf16[4,512,128]{2,1,0:T(8,128)(2,1)S(1)}, u32[]{:S(2)}, u32[]{:S(2)}) %collective-permute-start.17) | collective-permute-done | bytes 524320 | tf_op jit(solution)/shard_map/ppermute | solution.py:37
  125.4 0.8 bitcast_dynamic-update-slice_fusion.6
  126.2 0.9 bitcast_dynamic-update-slice_fusion.5
  127.1 0.9 bitcast_dynamic-update-slice_fusion.4
  127.9 0.9 bitcast_dynamic-update-slice_fusion.3
  128.8 0.8 bitcast_dynamic-update-slice_fusion.2
  130.8 0.8 bitcast_dynamic-update-slice_fusion
  131.7 5.4 %all-gather.3.cloned.1.call-done = bf16[2304,512]{1,0:T(8,128)(2,1)} async-done(((bf16[72,512]{1,0:T(8,128)(2,1)}), bf16[2304,512]{1,0:T(8,128)(2,1)}) %all-gather.3.cloned.1.call-update) | async-done | bytes 2359312 | tf_op jit(solution)/shard_map/all_gather | solution.py:133
  137.1 0.8 slice.110
  139.6 2.9 %fusion.2 = f32[64,32,64]{2,0,1:T(8,128)S(1)} fusion(bf16[32,72,512]{2,1,0:T(8,128)(2,1)} %bitcast.153, f32[64,32]{0,1:T(8,128)S(1)} %add_exponential_fusion, f32[1,64,1024]{2,1,0:T(8,128)S(1)} %convolution_bitcast_fusion), kind=kOutput, calls=%fused_computation.6 | convolution fusion | flops 134348800 | bytes 2703360 | tf_op jit(solution)/shard_map/vtd,bsd->vtbs/dot_general | solution.py:73
  144.5 3.1 %fusion.5 = bf16[1,64,8,4,128]{4,1,3,2,0:T(8,128)(2,1)S(1)} fusion(bf16[8,4,512,128]{3,2,1,0:T(8,128)(2,1)} %bitcast_dynamic-update-slice_fusion, f32[64,512]{1,0:T(8,128)S(1)} %get-tuple-element.26, f32[512]{0:T(512)S(1)} %copy-done.11, f32[64]{0:T(128)S(1)} %add_rsqrt_fusion, f32[64]{0:T(128)S(1)} %broadcast_multiply_fusion), kind=kOutput, calls=%fused_computation.8 | convolution fusion | flops 268828672 | bytes 4852224 | tf_op jit(solution)/shard_map/vtr,edrc->vtedc/dot_general | solution.py:142
  148.8 8.5 %all_to_all.10 = bf16[1,64,4,2,512]{4,2,1,0,3:T(4,128)(2,1)S(1)} all-to-all(bf16[1,64,4,2,512]{4,2,1,0,3:T(4,128)(2,1)S(1)} %copy.44), channel_id=1, replica_groups=mesh['seq_0'=4,'seq_1'=8,'head_0'=4,'head_1'=2,'var'=2] {'head_1'}, dimensions={3} | all-to-all | bytes 1048576 | tf_op jit(solution)/shard_map/all_to_all | solution.py:151
  157.9 19.8 %all_to_all.11 = bf16[1,64,4,512]{3,1,0,2:T(8,128)(2,1)S(1)} all-to-all(bf16[1,64,4,512]{3,1,0,2:T(8,128)(2,1)S(1)} %copy.45), channel_id=1, replica_groups=mesh['seq_0'=4,'seq_1'=8,'head_0'=4,'head_1'=2,'var'=2] {'head_0'}, dimensions={2} | all-to-all | bytes 524288 | tf_op jit(solution)/shard_map/all_to_all | solution.py:153
  (84 shorter events, 12.1 us)
Async XLA Ops:
  6.5 20.9 %copy-start = (bf16[1,2,512]{2,1,0:T(2,128)(2,1)S(1)}, bf16[1,2,512]{2,1,0:T(2,128)(2,1)}, u32[]{:S(2)}) copy-start(bf16[1,2,512]{2,1,0:T(2,128)(2,1)} %param.16) | copy-start | bytes 6148
  6.5 130.5 %all-gather.3.cloned.1.call-start = ((), (), s32[]{:S(2)}) async-start(), calls=%async_computation.2 | async-start | bytes 2433024 | tf_op jit(solution)/shard_map/all_gather | solution.py:133
  6.5 43.7 %collective-permute-start.13 = (bf16[512,128]{1,0:T(8,128)(2,1)}, bf16[512,128]{1,0:T(8,128)(2,1)S(1)}, u32[]{:S(2)}, u32[]{:S(2)}) collective-permute-start(bf16[512,128]{1,0:T(8,128)(2,1)} %param.19), channel_id=1, source_target_pairs={{0,384},{128,0},{256,128},{384,256},{1,385},{129,1},{257,129},{385... | collective-permute-start | bytes 393224 | tf_op jit(solution)/shard_map/ppermute | solution.py:40
  11.9 33.4 %collective-permute-start.11 = (bf16[512,128]{1,0:T(8,128)(2,1)}, bf16[512,128]{1,0:T(8,128)(2,1)S(1)}, u32[]{:S(2)}, u32[]{:S(2)}) collective-permute-start(bf16[512,128]{1,0:T(8,128)(2,1)} %param.19), channel_id=1, source_target_pairs={{0,128},{128,256},{256,384},{384,0},{1,129},{129,257},{257,385},{3... | collective-permute-start | bytes 393224 | tf_op jit(solution)/shard_map/ppermute | solution.py:37
  14.5 38.0 %copy-start.1 = (bf16[512,128]{1,0:T(8,128)(2,1)S(1)}, bf16[512,128]{1,0:T(8,128)(2,1)}, u32[]{:S(2)}) copy-start(bf16[512,128]{1,0:T(8,128)(2,1)} %param.19) | copy-start | bytes 393220
  15.8 20.5 %collective-permute-start.3 = (bf16[64,512]{1,0:T(8,128)(2,1)S(1)}, bf16[64,512]{1,0:T(8,128)(2,1)S(1)}, u32[]{:S(2)}, u32[]{:S(2)}) collective-permute-start(bf16[64,512]{1,0:T(8,128)(2,1)S(1)} %convolution_convert_fusion.1), channel_id=1, source_target_pairs={{0,384},{128,0},{256,128},{384,256},{1,385},{129,1},{257,129},{385... | collective-permute-start | bytes 196616 | tf_op jit(solution)/shard_map/ppermute | solution.py:40
  20.4 9.3 %collective-permute-start.1 = (bf16[64,512]{1,0:T(8,128)(2,1)S(1)}, bf16[64,512]{1,0:T(8,128)(2,1)S(1)}, u32[]{:S(2)}, u32[]{:S(2)}) collective-permute-start(bf16[64,512]{1,0:T(8,128)(2,1)S(1)} %convolution_convert_fusion.1), channel_id=1, source_target_pairs={{0,128},{128,256},{256,384},{384,0},{1,129},{129,257},{257,385},{3... | collective-permute-start | bytes 196616 | tf_op jit(solution)/shard_map/ppermute | solution.py:37
  23.3 4.1 %collective-permute-start = (bf16[1,3,512]{2,1,0:T(4,128)(2,1)S(1)}, bf16[1,3,512]{2,1,0:T(4,128)(2,1)S(1)}, u32[]{:S(2)}, u32[]{:S(2)}) collective-permute-start(bf16[1,3,512]{2,1,0:T(4,128)(2,1)S(1)} %slice.101), channel_id=1, source_target_pairs={{0,16},{16,32},{32,48},{48,64},{64,80},{80,96},{96,112},{112,128},... | collective-permute-start | bytes 9224 | tf_op jit(solution)/shard_map/ppermute | solution.py:16
  29.7 46.8 %copy-start.3 = (bf16[64,512]{1,0:T(8,128)(2,1)}, bf16[64,512]{1,0:T(8,128)(2,1)S(1)}, u32[]{:S(2)}) copy-start(bf16[64,512]{1,0:T(8,128)(2,1)S(1)} %collective-permute-done.1) | copy-start | bytes 196612
  29.7 8.6 %collective-permute-start.2 = (bf16[64,512]{1,0:T(8,128)(2,1)S(1)}, bf16[64,512]{1,0:T(8,128)(2,1)S(1)}, u32[]{:S(2)}, u32[]{:S(2)}) collective-permute-start(bf16[64,512]{1,0:T(8,128)(2,1)S(1)} %collective-permute-done.1), channel_id=1, source_target_pairs={{0,128},{128,256},{256,384},{384,0},{1,129},{129,257},{257,385},{3... | collective-permute-start | bytes 196616 | tf_op jit(solution)/shard_map/ppermute | solution.py:37
  38.3 38.2 %copy-start.5 = (bf16[64,512]{1,0:T(8,128)(2,1)}, bf16[64,512]{1,0:T(8,128)(2,1)S(1)}, u32[]{:S(2)}) copy-start(bf16[64,512]{1,0:T(8,128)(2,1)S(1)} %collective-permute-done.2) | copy-start | bytes 196612
  38.3 9.6 %collective-permute-start.4 = (bf16[4,64,512]{2,1,0:T(8,128)(2,1)S(1)}, bf16[4,64,512]{2,1,0:T(8,128)(2,1)S(1)}, u32[]{:S(2)}, u32[]{:S(2)}) collective-permute-start(bf16[4,64,512]{2,1,0:T(8,128)(2,1)S(1)} %pad_maximum_fusion.1), channel_id=1, source_target_pairs={{0,16},{16,32},{32,48},{48,64},{64,80},{80,96},{96,112},{112,0},{1... | collective-permute-start | bytes 786440 | tf_op jit(solution)/shard_map/ppermute | solution.py:37
  45.3 7.2 %collective-permute-start.12 = (bf16[512,128]{1,0:T(8,128)(2,1)S(1)}, bf16[512,128]{1,0:T(8,128)(2,1)S(1)}, u32[]{:S(2)}, u32[]{:S(2)}) collective-permute-start(bf16[512,128]{1,0:T(8,128)(2,1)S(1)} %collective-permute-done.11), channel_id=1, source_target_pairs={{0,128},{128,256},{256,384},{384,0},{1,129},{129,257},{257,385},{3... | collective-permute-start | bytes 393224 | tf_op jit(solution)/shard_map/ppermute | solution.py:37
  47.9 14.3 %collective-permute-start.5 = (bf16[4,64,512]{2,1,0:T(8,128)(2,1)S(1)}, bf16[4,64,512]{2,1,0:T(8,128)(2,1)S(1)}, u32[]{:S(2)}, u32[]{:S(2)}) collective-permute-start(bf16[4,64,512]{2,1,0:T(8,128)(2,1)S(1)} %collective-permute-done.4), channel_id=1, source_target_pairs={{0,16},{16,32},{32,48},{48,64},{64,80},{80,96},{96,112},{112,0},{1... | collective-permute-start | bytes 786440 | tf_op jit(solution)/shard_map/ppermute | solution.py:37
  52.6 23.9 %collective-permute-start.14 = (bf16[4,512,128]{2,1,0:T(8,128)(2,1)S(1)}, bf16[4,512,128]{2,1,0:T(8,128)(2,1)S(1)}, u32[]{:S(2)}, u32[]{:S(2)}) collective-permute-start(bf16[4,512,128]{2,1,0:T(8,128)(2,1)S(1)} %pad_maximum_fusion), channel_id=1, source_target_pairs={{0,16},{16,32},{32,48},{48,64},{64,80},{80,96},{96,112},{112,0},{1... | collective-permute-start | bytes 1572872 | tf_op jit(solution)/shard_map/ppermute | solution.py:37
  54.7 9.7 %collective-permute-start.8 = (bf16[4,64,512]{2,1,0:T(8,128)(2,1)S(1)}, bf16[4,64,512]{2,1,0:T(8,128)(2,1)S(1)}, u32[]{:S(2)}, u32[]{:S(2)}) collective-permute-start(bf16[4,64,512]{2,1,0:T(8,128)(2,1)S(1)} %pad_maximum_fusion.1), channel_id=1, source_target_pairs={{0,112},{16,0},{32,16},{48,32},{64,48},{80,64},{96,80},{112,96},{1... | collective-permute-start | bytes 786440 | tf_op jit(solution)/shard_map/ppermute | solution.py:40
  59.1 25.3 %collective-permute-start.18 = (bf16[4,512,128]{2,1,0:T(8,128)(2,1)S(1)}, bf16[4,512,128]{2,1,0:T(8,128)(2,1)S(1)}, u32[]{:S(2)}, u32[]{:S(2)}) collective-permute-start(bf16[4,512,128]{2,1,0:T(8,128)(2,1)S(1)} %pad_maximum_fusion), channel_id=1, source_target_pairs={{0,112},{16,0},{32,16},{48,32},{64,48},{80,64},{96,80},{112,96},{1... | collective-permute-start | bytes 1572872 | tf_op jit(solution)/shard_map/ppermute | solution.py:40
  62.2 2.2 %copy-start.2 = (bf16[4,64,512]{2,1,0:T(8,128)(2,1)}, bf16[4,64,512]{2,1,0:T(8,128)(2,1)S(1)}, u32[]{:S(2)}) copy-start(bf16[4,64,512]{2,1,0:T(8,128)(2,1)S(1)} %collective-permute-done.5) | copy-start | bytes 786436
  62.2 11.4 %collective-permute-start.6 = (bf16[4,64,512]{2,1,0:T(8,128)(2,1)S(1)}, bf16[4,64,512]{2,1,0:T(8,128)(2,1)}, u32[]{:S(2)}, u32[]{:S(2)}) collective-permute-start(bf16[4,64,512]{2,1,0:T(8,128)(2,1)S(1)} %collective-permute-done.5), channel_id=1, source_target_pairs={{0,16},{16,32},{32,48},{48,64},{64,80},{80,96},{96,112},{112,0},{1... | collective-permute-start | bytes 786440 | tf_op jit(solution)/shard_map/ppermute | solution.py:37
  64.4 17.9 %collective-permute-start.9 = (bf16[4,64,512]{2,1,0:T(8,128)(2,1)S(1)}, bf16[4,64,512]{2,1,0:T(8,128)(2,1)}, u32[]{:S(2)}, u32[]{:S(2)}) collective-permute-start(bf16[4,64,512]{2,1,0:T(8,128)(2,1)S(1)} %collective-permute-done.8), channel_id=1, source_target_pairs={{0,112},{16,0},{32,16},{48,32},{64,48},{80,64},{96,80},{112,96},{1... | collective-permute-start | bytes 786440 | tf_op jit(solution)/shard_map/ppermute | solution.py:40
  73.6 13.0 %collective-permute-start.7 = (bf16[4,64,512]{2,1,0:T(8,128)(2,1)}, bf16[4,64,512]{2,1,0:T(8,128)(2,1)}, u32[]{:S(2)}, u32[]{:S(2)}) collective-permute-start(bf16[4,64,512]{2,1,0:T(8,128)(2,1)} %collective-permute-done.6), channel_id=1, source_target_pairs={{0,16},{16,32},{32,48},{48,64},{64,80},{80,96},{96,112},{112,0},{1... | collective-permute-start | bytes 786440 | tf_op jit(solution)/shard_map/ppermute | solution.py:37
  76.5 16.2 %collective-permute-start.15 = (bf16[4,512,128]{2,1,0:T(8,128)(2,1)S(1)}, bf16[4,512,128]{2,1,0:T(8,128)(2,1)S(1)}, u32[]{:S(2)}, u32[]{:S(2)}) collective-permute-start(bf16[4,512,128]{2,1,0:T(8,128)(2,1)S(1)} %collective-permute-done.14), channel_id=1, source_target_pairs={{0,16},{16,32},{32,48},{48,64},{64,80},{80,96},{96,112},{112,0},{1... | collective-permute-start | bytes 1572872 | tf_op jit(solution)/shard_map/ppermute | solution.py:37
  82.3 17.2 %copy-start.4 = (bf16[64,512]{1,0:T(8,128)(2,1)S(1)}, bf16[64,512]{1,0:T(8,128)(2,1)}, u32[]{:S(2)}) copy-start(bf16[64,512]{1,0:T(8,128)(2,1)} %copy-done.3) | copy-start | bytes 196612
  82.3 17.2 %copy-start.6 = (bf16[64,512]{1,0:T(8,128)(2,1)S(1)}, bf16[64,512]{1,0:T(8,128)(2,1)}, u32[]{:S(2)}) copy-start(bf16[64,512]{1,0:T(8,128)(2,1)} %copy-done.5) | copy-start | bytes 196612
  82.3 29.2 %collective-permute-start.10 = (bf16[4,64,512]{2,1,0:T(8,128)(2,1)}, bf16[4,64,512]{2,1,0:T(8,128)(2,1)S(1)}, u32[]{:S(2)}, u32[]{:S(2)}) collective-permute-start(bf16[4,64,512]{2,1,0:T(8,128)(2,1)} %collective-permute-done.9), channel_id=1, source_target_pairs={{0,112},{16,0},{32,16},{48,32},{64,48},{80,64},{96,80},{112,96},{1... | collective-permute-start | bytes 786440 | tf_op jit(solution)/shard_map/ppermute | solution.py:40
  84.4 27.2 %collective-permute-start.19 = (bf16[4,512,128]{2,1,0:T(8,128)(2,1)S(1)}, bf16[4,512,128]{2,1,0:T(8,128)(2,1)S(1)}, u32[]{:S(2)}, u32[]{:S(2)}) collective-permute-start(bf16[4,512,128]{2,1,0:T(8,128)(2,1)S(1)} %collective-permute-done.18), channel_id=1, source_target_pairs={{0,112},{16,0},{32,16},{48,32},{64,48},{80,64},{96,80},{112,96},{1... | collective-permute-start | bytes 1572872 | tf_op jit(solution)/shard_map/ppermute | solution.py:40
  92.7 13.4 %collective-permute-start.16 = (bf16[4,512,128]{2,1,0:T(8,128)(2,1)S(1)}, bf16[4,512,128]{2,1,0:T(8,128)(2,1)S(1)}, u32[]{:S(2)}, u32[]{:S(2)}) collective-permute-start(bf16[4,512,128]{2,1,0:T(8,128)(2,1)S(1)} %collective-permute-done.15), channel_id=1, source_target_pairs={{0,16},{16,32},{32,48},{48,64},{64,80},{80,96},{96,112},{112,0},{1... | collective-permute-start | bytes 1572872 | tf_op jit(solution)/shard_map/ppermute | solution.py:37
  106.1 18.5 %collective-permute-start.17 = (bf16[4,512,128]{2,1,0:T(8,128)(2,1)S(1)}, bf16[4,512,128]{2,1,0:T(8,128)(2,1)S(1)}, u32[]{:S(2)}, u32[]{:S(2)}) collective-permute-start(bf16[4,512,128]{2,1,0:T(8,128)(2,1)S(1)} %collective-permute-done.16), channel_id=1, source_target_pairs={{0,16},{16,32},{32,48},{48,64},{64,80},{80,96},{96,112},{112,0},{1... | collective-permute-start | bytes 1572872 | tf_op jit(solution)/shard_map/ppermute | solution.py:37
  111.6 16.4 %copy-start.9 = (bf16[8,4,64,512]{3,2,1,0:T(8,128)(2,1)}, bf16[8,4,64,512]{3,2,1,0:T(8,128)(2,1)S(1)}, u32[]{:S(2)}) copy-start(bf16[8,4,64,512]{3,2,1,0:T(8,128)(2,1)S(1)} %bitcast_dynamic-update-slice_fusion.8) | copy-start | bytes 6291460
  111.6 19.2 %collective-permute-start.20 = (bf16[4,512,128]{2,1,0:T(8,128)(2,1)S(1)}, bf16[4,512,128]{2,1,0:T(8,128)(2,1)S(1)}, u32[]{:S(2)}, u32[]{:S(2)}) collective-permute-start(bf16[4,512,128]{2,1,0:T(8,128)(2,1)S(1)} %collective-permute-done.19), channel_id=1, source_target_pairs={{0,112},{16,0},{32,16},{48,32},{64,48},{80,64},{96,80},{112,96},{1... | collective-permute-start | bytes 1572872 | tf_op jit(solution)/shard_map/ppermute | solution.py:40
  139.6 3.1 %copy-start.10 = (bf16[8,4,64,512]{3,2,1,0:T(8,128)(2,1)S(1)}, bf16[8,4,64,512]{3,2,1,0:T(8,128)(2,1)}, u32[]{:S(2)}) copy-start(bf16[8,4,64,512]{3,2,1,0:T(8,128)(2,1)} %copy-done.9) | copy-start | bytes 6291460
  142.8 0.9 copy-start.7
  143.7 0.9 copy-start.11
  148.6 29.1 %copy-start.8 = (bf16[64,512]{1,0:T(8,128)(2,1)S(1)}, bf16[64,512]{1,0:T(8,128)(2,1)}, u32[]{:S(2)}) copy-start(bf16[64,512]{1,0:T(8,128)(2,1)} %param.12) | copy-start | bytes 196612
Sparse Core Ops, SparseCore 0:
  48.0 89.0 all-gather.2

commit v10 on v8

--- a/solution.py
+++ b/solution.py
@@ -66,10 +66,13 @@
     values_all = gathered[:, token_count : 2 * token_count, :].reshape(blocks * token_count, head_size)
     parts = gathered[:, 2 * token_count, :3].astype(jnp.float32)
     decay = (parts[:, 0] + parts[:, 1]) + parts[:, 2]
+    outer, inner_size = (lax.axis_size(SEQ[0]), lax.axis_size(SEQ[1]))
+    decay = decay.reshape(inner_size, outer).T.reshape(-1)
     through = jnp.cumsum(decay)
     before_own = jnp.sum(jnp.where(jnp.arange(blocks) < block, decay, 0.0))
     earlier = jnp.arange(blocks) < block
     block_exponent = jnp.where(earlier, before_own - through, -jnp.inf)
+    block_exponent = block_exponent.reshape(outer, inner_size).T.reshape(-1)
     exponent = cumulated[:, :, None, None] + block_exponent[None, None, :, None]
     scale = jnp.exp(jnp.broadcast_to(exponent, (*cumulated.shape, blocks, token_count)))
     scale = scale.reshape(*cumulated.shape, blocks * token_count)
@@ -131,7 +134,8 @@
     extra = jnp.zeros((EXTRA, head_size), jnp.bfloat16)
     extra = extra.at[0, :3].set(three_parts(block_decay[0]))
     packed = jnp.concatenate([scaled_keys[0], values[0], extra], axis=0)
-    gathered = lax.all_gather(packed, SEQ, axis=0, tiled=False)
+    gathered = lax.all_gather(packed, SEQ[0], axis=0, tiled=False)
+    gathered = lax.all_gather(gathered, SEQ[1], axis=0, tiled=False).reshape(-1, *packed.shape)
     block = lax.axis_index(SEQ)
     intra_part = local_terms(queries, key_rows, values, cumulated, input_log)
     numerator = carried_terms(queries, cumulated, gathered, block) + intra_part

time: 175 us -> 200 us (1.14)
  blocking collectives: 26 us -> 45.1 us
  waiting for transfers between devices: 57.8 us -> 71.1 us
    ppermute x6, waiting for transfers between devices: 42.9 us -> 71.1 us  [ring_pieces(): forward = lax.ppermute(forward, axis, ahead)]
    all_gather x1, waiting for transfers between devices: 14.6 us -> 0.01 us  [body(): lax.all_gather(gathered, SEQ[1], axis=0, tiled=False)]
    all_gather x0 -> x1, blocking collectives: none -> 13.3 us  [body(): gathered = lax.all_gather(packed, SEQ[0], axis=0, tiled=False)]
    all_to_all x1, blocking collectives: 6.52 us -> 15.2 us  [body(): lax.all_to_all(blocks, pair, split_axis=3, concat_axis=3, tiled=True)]
    ppermute x6, starting transfers between devices: 19 us -> 15.4 us  [ring_pieces(): forward = lax.ppermute(forward, axis, ahead)]
    all_to_all x1, blocking collectives: 19.5 us -> 16.6 us  [body(): lax.all_to_all(pair_sum, across, split_axis=2, concat_axis=2, tiled=True)]
    ppermute x4, starting transfers between devices: 12.7 us -> 15.2 us  [ring_pieces(): backward = lax.ppermute(backward, axis, behind)]
    unnamed x29 -> x32, local copies, waits for them, and re-layouts: 5.18 us -> 5.2 us
  transfers between devices with their start and end apart: 12 -> 12, of which waited for: 8 -> 6; matrix products, arithmetic and copies ran while one was open for 6% -> 5% of each run, Pallas kernels for 0% -> 0%
where the time goes in v10:
time: 200 us; the launch traced here: 199 us
  waiting for transfers between devices  71.1 us (36%)
  blocking collectives  45.1 us (23%)
  starting transfers between devices  34.7 us (17%)
  between operations  18.5 us (9%)
  local copies, waits for them, and re-layouts  12.9 us (6%)
  matrix products  9.61 us (5%)
  other arithmetic  7.1 us (4%)
    ppermute x6, waiting for transfers between devices, ring_pieces(): forward = lax.ppermute(forward, axis, ahead)  71.1 us
    all_to_all x1, blocking collectives, body(): lax.all_to_all(pair_sum, across, split_axis=2, concat_axis=2, tiled=True)  16.6 us
    ppermute x6, starting transfers between devices, ring_pieces(): forward = lax.ppermute(forward, axis, ahead)  15.4 us
    all_to_all x1, blocking collectives, body(): lax.all_to_all(blocks, pair, split_axis=3, concat_axis=3, tiled=True)  15.2 us
    ppermute x4, starting transfers between devices, ring_pieces(): backward = lax.ppermute(backward, axis, behind)  15.2 us
    all_gather x1, blocking collectives, body(): gathered = lax.all_gather(packed, SEQ[0], axis=0, tiled=False)  13.3 us
    unnamed x32, local copies, waits for them, and re-layouts  5.2 us
    ppermute x1, starting transfers between devices, from_behind(): lax.ppermute(value, axis, [(source, source + steps) for source in range(i...  4.02 us
  transfers between devices with their start and end apart: 12, of which 6 were waited for; matrix products, arithmetic and copies ran while one was open for 5% of the time, Pallas kernels for 0%

profile of v10, /device:TPU:1, one launch (start us, length us, event | category | flops | bytes accessed | tf_op | source)
XLA Modules:
  0.0 199.0 jit_solution(806594387071993932)
XLA Ops:
  6.5 0.7 convert_bitcast_fusion
  7.2 0.9 multiply_bitcast_fusion
  8.2 4.0 %collective-permute-start = (bf16[1,3,512]{2,1,0:T(4,128)(2,1)S(1)}, bf16[1,3,512]{2,1,0:T(4,128)(2,1)S(1)}, u32[]{:S(2)}, u32[]{:S(2)}) collective-permute-start(bf16[1,3,512]{2,1,0:T(4,128)(2,1)S(1)} %slice.105), channel_id=1, source_target_pairs={{0,16},{16,32},{32,48},{48,64},{64,80},{80,96},{96,112},{112,128},... | collective-permute-start | bytes 9224 | tf_op jit(solution)/shard_map/ppermute | solution.py:16
  12.2 1.3 convolution_convert_fusion.1
  13.5 0.9 fusion.66
  14.5 0.7 fusion.4
  15.6 0.6 slice.95
  20.8 0.6 fusion.56
  21.5 1.5 convolution_bitcast_fusion
  23.2 13.3 %all-gather = bf16[576,512]{1,0:T(8,128)(2,1)} all-gather(bf16[144,512]{1,0:T(8,128)(2,1)S(1)} %pad_maximum_fusion.1), channel_id=2, replica_groups=mesh['seq_0'=4,'seq_1'=8,'head_0'=4,'head_1'=2,'var'=2] {'seq_0'}, dimensions={0}, use_global_device_ids=true | all-gather | bytes 737280 | tf_op jit(solution)/shard_map/all_gather | solution.py:137
  36.5 3.2 %collective-permute-start.1 = (bf16[512,128]{1,0:T(8,128)(2,1)S(1)}, bf16[512,128]{1,0:T(8,128)(2,1)S(1)}, u32[]{:S(2)}, u32[]{:S(2)}) collective-permute-start(bf16[512,128]{1,0:T(8,128)(2,1)S(1)} %copy-done.1), channel_id=1, source_target_pairs={{0,128},{128,256},{256,384},{384,0},{1,129},{129,257},{257,385},{3... | collective-permute-start | bytes 393224 | tf_op jit(solution)/shard_map/ppermute | solution.py:37
  39.7 3.3 %collective-permute-start.3 = (bf16[512,128]{1,0:T(8,128)(2,1)S(1)}, bf16[512,128]{1,0:T(8,128)(2,1)S(1)}, u32[]{:S(2)}, u32[]{:S(2)}) collective-permute-start(bf16[512,128]{1,0:T(8,128)(2,1)S(1)} %copy-done.1), channel_id=1, source_target_pairs={{0,384},{128,0},{256,128},{384,256},{1,385},{129,1},{257,129},{385... | collective-permute-start | bytes 393224 | tf_op jit(solution)/shard_map/ppermute | solution.py:40
  43.0 0.4 collective-permute-done.1
  43.4 2.0 collective-permute-start.2
  45.5 5.1 %collective-permute-done.2 = bf16[512,128]{1,0:T(8,128)(2,1)S(1)} collective-permute-done((bf16[512,128]{1,0:T(8,128)(2,1)S(1)}, bf16[512,128]{1,0:T(8,128)(2,1)S(1)}, u32[]{:S(2)}, u32[]{:S(2)}) %collective-permute-start.2) | collective-permute-done | bytes 131104 | tf_op jit(solution)/shard_map/ppermute | solution.py:37
  50.6 2.6 %collective-permute-start.4 = (bf16[4,512,128]{2,1,0:T(8,128)(2,1)S(1)}, bf16[4,512,128]{2,1,0:T(8,128)(2,1)S(1)}, u32[]{:S(2)}, u32[]{:S(2)}) collective-permute-start(bf16[4,512,128]{2,1,0:T(8,128)(2,1)S(1)} %pad_maximum_fusion), channel_id=1, source_target_pairs={{0,16},{16,32},{32,48},{48,64},{64,80},{80,96},{96,112},{112,0},{1... | collective-permute-start | bytes 1572872 | tf_op jit(solution)/shard_map/ppermute | solution.py:37
  53.2 11.7 %collective-permute-done.4 = bf16[4,512,128]{2,1,0:T(8,128)(2,1)S(1)} collective-permute-done((bf16[4,512,128]{2,1,0:T(8,128)(2,1)S(1)}, bf16[4,512,128]{2,1,0:T(8,128)(2,1)S(1)}, u32[]{:S(2)}, u32[]{:S(2)}) %collective-permute-start.4) | collective-permute-done | bytes 524320 | tf_op jit(solution)/shard_map/ppermute | solution.py:37
  65.0 2.5 %collective-permute-start.5 = (bf16[4,512,128]{2,1,0:T(8,128)(2,1)S(1)}, bf16[4,512,128]{2,1,0:T(8,128)(2,1)S(1)}, u32[]{:S(2)}, u32[]{:S(2)}) collective-permute-start(bf16[4,512,128]{2,1,0:T(8,128)(2,1)S(1)} %collective-permute-done.4), channel_id=1, source_target_pairs={{0,16},{16,32},{32,48},{48,64},{64,80},{80,96},{96,112},{112,0},{1... | collective-permute-start | bytes 1572872 | tf_op jit(solution)/shard_map/ppermute | solution.py:37
  67.5 4.0 %collective-permute-start.8 = (bf16[4,512,128]{2,1,0:T(8,128)(2,1)S(1)}, bf16[4,512,128]{2,1,0:T(8,128)(2,1)S(1)}, u32[]{:S(2)}, u32[]{:S(2)}) collective-permute-start(bf16[4,512,128]{2,1,0:T(8,128)(2,1)S(1)} %pad_maximum_fusion), channel_id=1, source_target_pairs={{0,112},{16,0},{32,16},{48,32},{64,48},{80,64},{96,80},{112,96},{1... | collective-permute-start | bytes 1572872 | tf_op jit(solution)/shard_map/ppermute | solution.py:40
  71.5 19.8 %collective-permute-done.5 = bf16[4,512,128]{2,1,0:T(8,128)(2,1)S(1)} collective-permute-done((bf16[4,512,128]{2,1,0:T(8,128)(2,1)S(1)}, bf16[4,512,128]{2,1,0:T(8,128)(2,1)S(1)}, u32[]{:S(2)}, u32[]{:S(2)}) %collective-permute-start.5) | collective-permute-done | bytes 524320 | tf_op jit(solution)/shard_map/ppermute | solution.py:37
  91.3 3.0 %collective-permute-start.6 = (bf16[4,512,128]{2,1,0:T(8,128)(2,1)S(1)}, bf16[4,512,128]{2,1,0:T(8,128)(2,1)S(1)}, u32[]{:S(2)}, u32[]{:S(2)}) collective-permute-start(bf16[4,512,128]{2,1,0:T(8,128)(2,1)S(1)} %collective-permute-done.5), channel_id=1, source_target_pairs={{0,16},{16,32},{32,48},{48,64},{64,80},{80,96},{96,112},{112,0},{1... | collective-permute-start | bytes 1572872 | tf_op jit(solution)/shard_map/ppermute | solution.py:37
  94.2 3.5 %collective-permute-start.9 = (bf16[4,512,128]{2,1,0:T(8,128)(2,1)S(1)}, bf16[4,512,128]{2,1,0:T(8,128)(2,1)S(1)}, u32[]{:S(2)}, u32[]{:S(2)}) collective-permute-start(bf16[4,512,128]{2,1,0:T(8,128)(2,1)S(1)} %collective-permute-done.8), channel_id=1, source_target_pairs={{0,112},{16,0},{32,16},{48,32},{64,48},{80,64},{96,80},{112,96},{1... | collective-permute-start | bytes 1572872 | tf_op jit(solution)/shard_map/ppermute | solution.py:40
  97.8 20.1 %collective-permute-done.6 = bf16[4,512,128]{2,1,0:T(8,128)(2,1)S(1)} collective-permute-done((bf16[4,512,128]{2,1,0:T(8,128)(2,1)S(1)}, bf16[4,512,128]{2,1,0:T(8,128)(2,1)S(1)}, u32[]{:S(2)}, u32[]{:S(2)}) %collective-permute-start.6) | collective-permute-done | bytes 524320 | tf_op jit(solution)/shard_map/ppermute | solution.py:37
  117.8 2.2 %collective-permute-start.7 = (bf16[4,512,128]{2,1,0:T(8,128)(2,1)S(1)}, bf16[4,512,128]{2,1,0:T(8,128)(2,1)S(1)}, u32[]{:S(2)}, u32[]{:S(2)}) collective-permute-start(bf16[4,512,128]{2,1,0:T(8,128)(2,1)S(1)} %collective-permute-done.6), channel_id=1, source_target_pairs={{0,16},{16,32},{32,48},{48,64},{64,80},{80,96},{96,112},{112,0},{1... | collective-permute-start | bytes 1572872 | tf_op jit(solution)/shard_map/ppermute | solution.py:37
  120.1 1.1 fusion.3
  121.3 4.4 %collective-permute-start.10 = (bf16[4,512,128]{2,1,0:T(8,128)(2,1)S(1)}, bf16[4,512,128]{2,1,0:T(8,128)(2,1)S(1)}, u32[]{:S(2)}, u32[]{:S(2)}) collective-permute-start(bf16[4,512,128]{2,1,0:T(8,128)(2,1)S(1)} %collective-permute-done.9), channel_id=1, source_target_pairs={{0,112},{16,0},{32,16},{48,32},{64,48},{80,64},{96,80},{112,96},{1... | collective-permute-start | bytes 1572872 | tf_op jit(solution)/shard_map/ppermute | solution.py:40
  125.7 14.0 %collective-permute-done.7 = bf16[4,512,128]{2,1,0:T(8,128)(2,1)S(1)} collective-permute-done((bf16[4,512,128]{2,1,0:T(8,128)(2,1)S(1)}, bf16[4,512,128]{2,1,0:T(8,128)(2,1)S(1)}, u32[]{:S(2)}, u32[]{:S(2)}) %collective-permute-start.7) | collective-permute-done | bytes 524320 | tf_op jit(solution)/shard_map/ppermute | solution.py:37
  139.7 0.9 bitcast_dynamic-update-slice_fusion.7
  140.5 0.9 bitcast_dynamic-update-slice_fusion.6
  141.4 0.8 bitcast_dynamic-update-slice_fusion.5
  142.2 0.8 bitcast_dynamic-update-slice_fusion.4
  143.1 0.8 bitcast_dynamic-update-slice_fusion.3
  143.9 0.8 bitcast_dynamic-update-slice_fusion.2
  144.7 0.9 bitcast_dynamic-update-slice_fusion.1
  145.6 0.9 bitcast_dynamic-update-slice_fusion
  146.5 0.9 slice.115
  147.8 0.6 select_reduce_fusion
  148.4 0.8 subtract_reduce_fusion
  149.8 0.4 broadcast_in_dim.20
  150.2 2.5 %fusion.65 = (bf16[32,64,512]{2,1,0:T(8,128)(2,1)S(1)}, bf16[32,64,512]{2,1,0:T(8,128)(2,1)S(1)}) fusion(bf16[32,144,512]{2,1,0:T(8,128)(2,1)} %all-gather.4.cloned.1.call-done), kind=kLoop, calls=%fused_computation.111 | loop fusion | bytes 8388608 | tf_op jit(solution)/shard_map/slice | solution.py:65
  152.7 0.8 convolution_multiply_fusion
  153.5 0.5 fusion.15
  154.0 0.6 fusion.67
  154.8 3.1 %fusion = bf16[1,64,8,4,128]{4,1,3,2,0:T(8,128)(2,1)S(1)} fusion(bf16[8,4,512,128]{3,2,1,0:T(8,128)(2,1)} %bitcast_dynamic-update-slice_fusion, f32[64,512]{1,0:T(8,128)S(1)} %get-tuple-element.26, f32[512]{0:T(512)S(1)} %copy-done.11, f32[64]{0:T(128)S(1)} %add_rsqrt_fusion, f32[64]{0:T(128)S(1)} %broadcast_multiply_fusion), kind=kOutput, calls=%fused_computation.2 | convolution fusion | flops 268828672 | bytes 4852224 | tf_op jit(solution)/shard_map/vtr,edrc->vtedc/dot_general | solution.py:146
  159.1 15.2 %all_to_all.10 = bf16[1,64,4,2,512]{4,2,1,0,3:T(4,128)(2,1)S(1)} all-to-all(bf16[1,64,4,2,512]{4,2,1,0,3:T(4,128)(2,1)S(1)} %copy.37), channel_id=1, replica_groups=mesh['seq_0'=4,'seq_1'=8,'head_0'=4,'head_1'=2,'var'=2] {'head_1'}, dimensions={3} | all-to-all | bytes 1048576 | tf_op jit(solution)/shard_map/all_to_all | solution.py:155
  174.3 0.5 reduce_sum.53
  174.9 16.6 %all_to_all.11 = bf16[1,64,4,512]{3,1,0,2:T(8,128)(2,1)S(1)} all-to-all(bf16[1,64,4,512]{3,1,0,2:T(8,128)(2,1)S(1)} %copy.38), channel_id=1, replica_groups=mesh['seq_0'=4,'seq_1'=8,'head_0'=4,'head_1'=2,'var'=2] {'head_0'}, dimensions={2} | all-to-all | bytes 524288 | tf_op jit(solution)/shard_map/all_to_all | solution.py:157
  191.5 0.6 fusion.20
  (64 shorter events, 3.3 us)
Async XLA Ops:
  6.5 8.0 %copy-start = (bf16[1,2,512]{2,1,0:T(2,128)(2,1)S(1)}, bf16[1,2,512]{2,1,0:T(2,128)(2,1)}, u32[]{:S(2)}) copy-start(bf16[1,2,512]{2,1,0:T(2,128)(2,1)} %param.16) | copy-start | bytes 6148
  6.5 30.0 %copy-start.1 = (bf16[512,128]{1,0:T(8,128)(2,1)S(1)}, bf16[512,128]{1,0:T(8,128)(2,1)}, u32[]{:S(2)}) copy-start(bf16[512,128]{1,0:T(8,128)(2,1)} %param.19) | copy-start | bytes 393220
  6.5 139.9 %all-gather.4.cloned.1.call-start = ((), (), s32[]{:S(2)}) async-start(), calls=%async_computation.2 | async-start | bytes 5308416 | tf_op jit(solution)/shard_map/all_gather | solution.py:138
  8.2 6.2 %collective-permute-start = (bf16[1,3,512]{2,1,0:T(4,128)(2,1)S(1)}, bf16[1,3,512]{2,1,0:T(4,128)(2,1)S(1)}, u32[]{:S(2)}, u32[]{:S(2)}) collective-permute-start(bf16[1,3,512]{2,1,0:T(4,128)(2,1)S(1)} %slice.105), channel_id=1, source_target_pairs={{0,16},{16,32},{32,48},{48,64},{64,80},{80,96},{96,112},{112,128},... | collective-permute-start | bytes 9224 | tf_op jit(solution)/shard_map/ppermute | solution.py:16
  13.5 37.0 %copy-start.9 = (bf16[64,512]{1,0:T(8,128)(2,1)}, bf16[64,512]{1,0:T(8,128)(2,1)S(1)}, u32[]{:S(2)}) copy-start(bf16[64,512]{1,0:T(8,128)(2,1)S(1)} %convolution_convert_fusion.1) | copy-start | bytes 196612
  36.5 6.9 %collective-permute-start.1 = (bf16[512,128]{1,0:T(8,128)(2,1)S(1)}, bf16[512,128]{1,0:T(8,128)(2,1)S(1)}, u32[]{:S(2)}, u32[]{:S(2)}) collective-permute-start(bf16[512,128]{1,0:T(8,128)(2,1)S(1)} %copy-done.1), channel_id=1, source_target_pairs={{0,128},{128,256},{256,384},{384,0},{1,129},{129,257},{257,385},{3... | collective-permute-start | bytes 393224 | tf_op jit(solution)/shard_map/ppermute | solution.py:37
  39.7 5.7 %collective-permute-start.3 = (bf16[512,128]{1,0:T(8,128)(2,1)S(1)}, bf16[512,128]{1,0:T(8,128)(2,1)S(1)}, u32[]{:S(2)}, u32[]{:S(2)}) collective-permute-start(bf16[512,128]{1,0:T(8,128)(2,1)S(1)} %copy-done.1), channel_id=1, source_target_pairs={{0,384},{128,0},{256,128},{384,256},{1,385},{129,1},{257,129},{385... | collective-permute-start | bytes 393224 | tf_op jit(solution)/shard_map/ppermute | solution.py:40
  43.4 9.8 %copy-start.3 = (bf16[512,128]{1,0:T(8,128)(2,1)}, bf16[512,128]{1,0:T(8,128)(2,1)S(1)}, u32[]{:S(2)}) copy-start(bf16[512,128]{1,0:T(8,128)(2,1)S(1)} %collective-permute-done.1) | copy-start | bytes 393220
  43.4 7.1 %collective-permute-start.2 = (bf16[512,128]{1,0:T(8,128)(2,1)S(1)}, bf16[512,128]{1,0:T(8,128)(2,1)S(1)}, u32[]{:S(2)}, u32[]{:S(2)}) collective-permute-start(bf16[512,128]{1,0:T(8,128)(2,1)S(1)} %collective-permute-done.1), channel_id=1, source_target_pairs={{0,128},{128,256},{256,384},{384,0},{1,129},{129,257},{257,385},{3... | collective-permute-start | bytes 393224 | tf_op jit(solution)/shard_map/ppermute | solution.py:37
  45.4 7.8 %copy-start.5 = (bf16[512,128]{1,0:T(8,128)(2,1)}, bf16[512,128]{1,0:T(8,128)(2,1)S(1)}, u32[]{:S(2)}) copy-start(bf16[512,128]{1,0:T(8,128)(2,1)S(1)} %collective-permute-done.3) | copy-start | bytes 393220
  50.5 2.7 %copy-start.7 = (bf16[512,128]{1,0:T(8,128)(2,1)}, bf16[512,128]{1,0:T(8,128)(2,1)S(1)}, u32[]{:S(2)}) copy-start(bf16[512,128]{1,0:T(8,128)(2,1)S(1)} %collective-permute-done.2) | copy-start | bytes 393220
  50.6 14.4 %collective-permute-start.4 = (bf16[4,512,128]{2,1,0:T(8,128)(2,1)S(1)}, bf16[4,512,128]{2,1,0:T(8,128)(2,1)S(1)}, u32[]{:S(2)}, u32[]{:S(2)}) collective-permute-start(bf16[4,512,128]{2,1,0:T(8,128)(2,1)S(1)} %pad_maximum_fusion), channel_id=1, source_target_pairs={{0,16},{16,32},{32,48},{48,64},{64,80},{80,96},{96,112},{112,0},{1... | collective-permute-start | bytes 1572872 | tf_op jit(solution)/shard_map/ppermute | solution.py:37
  65.0 26.3 %collective-permute-start.5 = (bf16[4,512,128]{2,1,0:T(8,128)(2,1)S(1)}, bf16[4,512,128]{2,1,0:T(8,128)(2,1)S(1)}, u32[]{:S(2)}, u32[]{:S(2)}) collective-permute-start(bf16[4,512,128]{2,1,0:T(8,128)(2,1)S(1)} %collective-permute-done.4), channel_id=1, source_target_pairs={{0,16},{16,32},{32,48},{48,64},{64,80},{80,96},{96,112},{112,0},{1... | collective-permute-start | bytes 1572872 | tf_op jit(solution)/shard_map/ppermute | solution.py:37
  67.5 26.8 %collective-permute-start.8 = (bf16[4,512,128]{2,1,0:T(8,128)(2,1)S(1)}, bf16[4,512,128]{2,1,0:T(8,128)(2,1)S(1)}, u32[]{:S(2)}, u32[]{:S(2)}) collective-permute-start(bf16[4,512,128]{2,1,0:T(8,128)(2,1)S(1)} %pad_maximum_fusion), channel_id=1, source_target_pairs={{0,112},{16,0},{32,16},{48,32},{64,48},{80,64},{96,80},{112,96},{1... | collective-permute-start | bytes 1572872 | tf_op jit(solution)/shard_map/ppermute | solution.py:40
  91.3 26.6 %collective-permute-start.6 = (bf16[4,512,128]{2,1,0:T(8,128)(2,1)S(1)}, bf16[4,512,128]{2,1,0:T(8,128)(2,1)S(1)}, u32[]{:S(2)}, u32[]{:S(2)}) collective-permute-start(bf16[4,512,128]{2,1,0:T(8,128)(2,1)S(1)} %collective-permute-done.5), channel_id=1, source_target_pairs={{0,16},{16,32},{32,48},{48,64},{64,80},{80,96},{96,112},{112,0},{1... | collective-permute-start | bytes 1572872 | tf_op jit(solution)/shard_map/ppermute | solution.py:37
  94.2 27.0 %collective-permute-start.9 = (bf16[4,512,128]{2,1,0:T(8,128)(2,1)S(1)}, bf16[4,512,128]{2,1,0:T(8,128)(2,1)S(1)}, u32[]{:S(2)}, u32[]{:S(2)}) collective-permute-start(bf16[4,512,128]{2,1,0:T(8,128)(2,1)S(1)} %collective-permute-done.8), channel_id=1, source_target_pairs={{0,112},{16,0},{32,16},{48,32},{64,48},{80,64},{96,80},{112,96},{1... | collective-permute-start | bytes 1572872 | tf_op jit(solution)/shard_map/ppermute | solution.py:40
  117.8 21.9 %collective-permute-start.7 = (bf16[4,512,128]{2,1,0:T(8,128)(2,1)S(1)}, bf16[4,512,128]{2,1,0:T(8,128)(2,1)S(1)}, u32[]{:S(2)}, u32[]{:S(2)}) collective-permute-start(bf16[4,512,128]{2,1,0:T(8,128)(2,1)S(1)} %collective-permute-done.6), channel_id=1, source_target_pairs={{0,16},{16,32},{32,48},{48,64},{64,80},{80,96},{96,112},{112,0},{1... | collective-permute-start | bytes 1572872 | tf_op jit(solution)/shard_map/ppermute | solution.py:37
  121.2 21.8 %copy-start.2 = (bf16[512,128]{1,0:T(8,128)(2,1)S(1)}, bf16[512,128]{1,0:T(8,128)(2,1)}, u32[]{:S(2)}) copy-start(bf16[512,128]{1,0:T(8,128)(2,1)} %param.19) | copy-start | bytes 393220
  121.2 21.8 %copy-start.4 = (bf16[512,128]{1,0:T(8,128)(2,1)S(1)}, bf16[512,128]{1,0:T(8,128)(2,1)}, u32[]{:S(2)}) copy-start(bf16[512,128]{1,0:T(8,128)(2,1)} %copy-done.3) | copy-start | bytes 393220
  121.3 21.8 %copy-start.6 = (bf16[512,128]{1,0:T(8,128)(2,1)S(1)}, bf16[512,128]{1,0:T(8,128)(2,1)}, u32[]{:S(2)}) copy-start(bf16[512,128]{1,0:T(8,128)(2,1)} %copy-done.5) | copy-start | bytes 393220
  121.3 21.8 %copy-start.8 = (bf16[512,128]{1,0:T(8,128)(2,1)S(1)}, bf16[512,128]{1,0:T(8,128)(2,1)}, u32[]{:S(2)}) copy-start(bf16[512,128]{1,0:T(8,128)(2,1)} %copy-done.7) | copy-start | bytes 393220
  121.3 24.3 %collective-permute-start.10 = (bf16[4,512,128]{2,1,0:T(8,128)(2,1)S(1)}, bf16[4,512,128]{2,1,0:T(8,128)(2,1)S(1)}, u32[]{:S(2)}, u32[]{:S(2)}) collective-permute-start(bf16[4,512,128]{2,1,0:T(8,128)(2,1)S(1)} %collective-permute-done.9), channel_id=1, source_target_pairs={{0,112},{16,0},{32,16},{48,32},{64,48},{80,64},{96,80},{112,96},{1... | collective-permute-start | bytes 1572872 | tf_op jit(solution)/shard_map/ppermute | solution.py:40
  152.7 2.0 %copy-start.11 = (f32[512]{0:T(512)S(1)}, f32[512]{0:T(512)}, u32[]{:S(2)}) copy-start(f32[512]{0:T(512)} %param.18) | copy-start | bytes 6148
  157.8 33.6 %copy-start.10 = (bf16[64,512]{1,0:T(8,128)(2,1)S(1)}, bf16[64,512]{1,0:T(8,128)(2,1)}, u32[]{:S(2)}) copy-start(bf16[64,512]{1,0:T(8,128)(2,1)} %param.12) | copy-start | bytes 196612
Sparse Core Ops, SparseCore 0:
  36.6 100.4 all-gather.3

commit v11 on v8

--- a/solution.py
+++ b/solution.py
@@ -70,16 +70,11 @@
     before_own = jnp.sum(jnp.where(jnp.arange(blocks) < block, decay, 0.0))
     earlier = jnp.arange(blocks) < block
     block_exponent = jnp.where(earlier, before_own - through, -jnp.inf)
-    exponent = cumulated[:, :, None, None] + block_exponent[None, None, :, None]
-    scale = jnp.exp(jnp.broadcast_to(exponent, (*cumulated.shape, blocks, token_count)))
-    scale = scale.reshape(*cumulated.shape, blocks * token_count)
+    scale = jnp.exp(cumulated[:, :, None] + block_exponent[None, None, :])
     scores = jnp.einsum("vtd,sd->vts", queries, keys_all, preferred_element_type=jnp.float32)
-    weights = scores * scale
-    high = weights.astype(jnp.bfloat16)
-    low = (weights - high.astype(jnp.float32)).astype(jnp.bfloat16)
-    return jnp.einsum("vts,se->vte", high, values_all, preferred_element_type=jnp.float32) + jnp.einsum(
-        "vts,se->vte", low, values_all, preferred_element_type=jnp.float32
-    )
+    scores = scores.reshape(*cumulated.shape, blocks, token_count) * scale[..., None]
+    weights = scores.reshape(*cumulated.shape, blocks * token_count).astype(jnp.bfloat16)
+    return jnp.einsum("vts,se->vte", weights, values_all, preferred_element_type=jnp.float32)
 
 
 def body(

time: 175 us -> 170 us (0.971)
  local copies, waits for them, and re-layouts: 14.8 us -> 9.34 us
    slice x1 -> x0, local copies, waits for them, and re-layouts: 4.03 us -> none  [carried_terms(): gathered[:, :token_count, :].reshape(blocks * token_count, head_size)]
    dot_general x3 -> x1, matrix products: 3.49 us -> 3.72 us  [carried_terms(): jnp.einsum('vts,se->vte', weights, values_all, preferred_element_type=jnp...]
    unnamed x29 -> x32, local copies, waits for them, and re-layouts: 5.18 us -> 5.2 us
where the time goes in v11:
time: 170 us; the launch traced here: 168 us
  waiting for transfers between devices  59.4 us (35%)
  starting transfers between devices  35.2 us (21%)
  blocking collectives  26 us (15%)
  between operations  18.6 us (11%)
  matrix products  10.8 us (6%)
  local copies, waits for them, and re-layouts  9.34 us (5%)
  other arithmetic  8.74 us (5%)
    ppermute x6, waiting for transfers between devices, ring_pieces(): forward = lax.ppermute(forward, axis, ahead)  44 us
    all_to_all x1, blocking collectives, body(): lax.all_to_all(pair_sum, across, split_axis=2, concat_axis=2, tiled=True)  19.5 us
    ppermute x6, starting transfers between devices, ring_pieces(): forward = lax.ppermute(forward, axis, ahead)  19.1 us
    all_gather x1, waiting for transfers between devices, body(): gathered = lax.all_gather(packed, SEQ, axis=0, tiled=False)  14.8 us
    ppermute x4, starting transfers between devices, ring_pieces(): backward = lax.ppermute(backward, axis, behind)  12.1 us
    all_to_all x1, blocking collectives, body(): lax.all_to_all(blocks, pair, split_axis=3, concat_axis=3, tiled=True)  6.49 us
    unnamed x32, local copies, waits for them, and re-layouts  5.2 us
    ppermute x1, starting transfers between devices, from_behind(): lax.ppermute(value, axis, [(source, source + steps) for source in range(i...  4.02 us
  transfers between devices with their start and end apart: 12, of which 8 were waited for; matrix products, arithmetic and copies ran while one was open for 6% of the time, Pallas kernels for 0%

profile of v11, /device:TPU:1, one launch (start us, length us, event | category | flops | bytes accessed | tf_op | source)
XLA Modules:
  0.0 168.2 jit_solution(12377816003872306472)
XLA Ops:
  6.5 0.7 convert_bitcast_fusion
  7.2 0.9 multiply_bitcast_fusion
  8.1 4.0 %collective-permute-start = (bf16[1,3,512]{2,1,0:T(4,128)(2,1)S(1)}, bf16[1,3,512]{2,1,0:T(4,128)(2,1)S(1)}, u32[]{:S(2)}, u32[]{:S(2)}) collective-permute-start(bf16[1,3,512]{2,1,0:T(4,128)(2,1)S(1)} %slice.105), channel_id=1, source_target_pairs={{0,16},{16,32},{32,48},{48,64},{64,80},{80,96},{96,112},{112,128},... | collective-permute-start | bytes 9224 | tf_op jit(solution)/shard_map/ppermute | solution.py:16
  12.2 1.3 convolution_convert_fusion.1
  13.5 0.9 fusion.79
  14.5 0.7 fusion.19
  15.6 0.7 slice.95
  21.1 0.7 fusion.78
  21.8 1.5 convolution_bitcast_fusion
  23.5 0.7 pad_maximum_fusion.1
  24.2 4.1 %collective-permute-start.1 = (bf16[512,128]{1,0:T(8,128)(2,1)}, bf16[512,128]{1,0:T(8,128)(2,1)S(1)}, u32[]{:S(2)}, u32[]{:S(2)}) collective-permute-start(bf16[512,128]{1,0:T(8,128)(2,1)} %param.19), channel_id=1, source_target_pairs={{0,128},{128,256},{256,384},{384,0},{1,129},{129,257},{257,385},{3... | collective-permute-start | bytes 393224 | tf_op jit(solution)/shard_map/ppermute | solution.py:37
  28.3 3.2 %collective-permute-start.3 = (bf16[512,128]{1,0:T(8,128)(2,1)}, bf16[512,128]{1,0:T(8,128)(2,1)S(1)}, u32[]{:S(2)}, u32[]{:S(2)}) collective-permute-start(bf16[512,128]{1,0:T(8,128)(2,1)} %param.19), channel_id=1, source_target_pairs={{0,384},{128,0},{256,128},{384,256},{1,385},{129,1},{257,129},{385... | collective-permute-start | bytes 393224 | tf_op jit(solution)/shard_map/ppermute | solution.py:40
  31.5 0.6 collective-permute-done.1
  32.2 2.1 %collective-permute-start.2 = (bf16[512,128]{1,0:T(8,128)(2,1)S(1)}, bf16[512,128]{1,0:T(8,128)(2,1)S(1)}, u32[]{:S(2)}, u32[]{:S(2)}) collective-permute-start(bf16[512,128]{1,0:T(8,128)(2,1)S(1)} %collective-permute-done.1), channel_id=1, source_target_pairs={{0,128},{128,256},{256,384},{384,0},{1,129},{129,257},{257,385},{3... | collective-permute-start | bytes 393224 | tf_op jit(solution)/shard_map/ppermute | solution.py:37
  34.3 4.8 %collective-permute-done.2 = bf16[512,128]{1,0:T(8,128)(2,1)S(1)} collective-permute-done((bf16[512,128]{1,0:T(8,128)(2,1)S(1)}, bf16[512,128]{1,0:T(8,128)(2,1)S(1)}, u32[]{:S(2)}, u32[]{:S(2)}) %collective-permute-start.2) | collective-permute-done | bytes 131104 | tf_op jit(solution)/shard_map/ppermute | solution.py:37
  39.1 1.0 pad_maximum_fusion
  40.1 2.4 %collective-permute-start.4 = (bf16[4,512,128]{2,1,0:T(8,128)(2,1)S(1)}, bf16[4,512,128]{2,1,0:T(8,128)(2,1)S(1)}, u32[]{:S(2)}, u32[]{:S(2)}) collective-permute-start(bf16[4,512,128]{2,1,0:T(8,128)(2,1)S(1)} %pad_maximum_fusion), channel_id=1, source_target_pairs={{0,16},{16,32},{32,48},{48,64},{64,80},{80,96},{96,112},{112,0},{1... | collective-permute-start | bytes 1572872 | tf_op jit(solution)/shard_map/ppermute | solution.py:37
  42.5 10.2 %collective-permute-done.4 = bf16[4,512,128]{2,1,0:T(8,128)(2,1)S(1)} collective-permute-done((bf16[4,512,128]{2,1,0:T(8,128)(2,1)S(1)}, bf16[4,512,128]{2,1,0:T(8,128)(2,1)S(1)}, u32[]{:S(2)}, u32[]{:S(2)}) %collective-permute-start.4) | collective-permute-done | bytes 524320 | tf_op jit(solution)/shard_map/ppermute | solution.py:37
  52.7 1.9 %collective-permute-start.5 = (bf16[4,512,128]{2,1,0:T(8,128)(2,1)S(1)}, bf16[4,512,128]{2,1,0:T(8,128)(2,1)S(1)}, u32[]{:S(2)}, u32[]{:S(2)}) collective-permute-start(bf16[4,512,128]{2,1,0:T(8,128)(2,1)S(1)} %collective-permute-done.4), channel_id=1, source_target_pairs={{0,16},{16,32},{32,48},{48,64},{64,80},{80,96},{96,112},{112,0},{1... | collective-permute-start | bytes 1572872 | tf_op jit(solution)/shard_map/ppermute | solution.py:37
  54.6 4.6 %collective-permute-start.8 = (bf16[4,512,128]{2,1,0:T(8,128)(2,1)S(1)}, bf16[4,512,128]{2,1,0:T(8,128)(2,1)S(1)}, u32[]{:S(2)}, u32[]{:S(2)}) collective-permute-start(bf16[4,512,128]{2,1,0:T(8,128)(2,1)S(1)} %pad_maximum_fusion), channel_id=1, source_target_pairs={{0,112},{16,0},{32,16},{48,32},{64,48},{80,64},{96,80},{112,96},{1... | collective-permute-start | bytes 1572872 | tf_op jit(solution)/shard_map/ppermute | solution.py:40
  59.2 7.7 %collective-permute-done.5 = bf16[4,512,128]{2,1,0:T(8,128)(2,1)S(1)} collective-permute-done((bf16[4,512,128]{2,1,0:T(8,128)(2,1)S(1)}, bf16[4,512,128]{2,1,0:T(8,128)(2,1)S(1)}, u32[]{:S(2)}, u32[]{:S(2)}) %collective-permute-start.5) | collective-permute-done | bytes 524320 | tf_op jit(solution)/shard_map/ppermute | solution.py:37
  66.9 4.9 %collective-permute-start.6 = (bf16[4,512,128]{2,1,0:T(8,128)(2,1)S(1)}, bf16[4,512,128]{2,1,0:T(8,128)(2,1)S(1)}, u32[]{:S(2)}, u32[]{:S(2)}) collective-permute-start(bf16[4,512,128]{2,1,0:T(8,128)(2,1)S(1)} %collective-permute-done.5), channel_id=1, source_target_pairs={{0,16},{16,32},{32,48},{48,64},{64,80},{80,96},{96,112},{112,0},{1... | collective-permute-start | bytes 1572872 | tf_op jit(solution)/shard_map/ppermute | solution.py:37
  71.8 1.9 %collective-permute-start.9 = (bf16[4,512,128]{2,1,0:T(8,128)(2,1)S(1)}, bf16[4,512,128]{2,1,0:T(8,128)(2,1)S(1)}, u32[]{:S(2)}, u32[]{:S(2)}) collective-permute-start(bf16[4,512,128]{2,1,0:T(8,128)(2,1)S(1)} %collective-permute-done.8), channel_id=1, source_target_pairs={{0,112},{16,0},{32,16},{48,32},{64,48},{80,64},{96,80},{112,96},{1... | collective-permute-start | bytes 1572872 | tf_op jit(solution)/shard_map/ppermute | solution.py:40
  73.8 5.6 %collective-permute-done.6 = bf16[4,512,128]{2,1,0:T(8,128)(2,1)S(1)} collective-permute-done((bf16[4,512,128]{2,1,0:T(8,128)(2,1)S(1)}, bf16[4,512,128]{2,1,0:T(8,128)(2,1)S(1)}, u32[]{:S(2)}, u32[]{:S(2)}) %collective-permute-start.6) | collective-permute-done | bytes 524320 | tf_op jit(solution)/shard_map/ppermute | solution.py:37
  79.4 3.6 %collective-permute-start.7 = (bf16[4,512,128]{2,1,0:T(8,128)(2,1)S(1)}, bf16[4,512,128]{2,1,0:T(8,128)(2,1)S(1)}, u32[]{:S(2)}, u32[]{:S(2)}) collective-permute-start(bf16[4,512,128]{2,1,0:T(8,128)(2,1)S(1)} %collective-permute-done.6), channel_id=1, source_target_pairs={{0,16},{16,32},{32,48},{48,64},{64,80},{80,96},{96,112},{112,0},{1... | collective-permute-start | bytes 1572872 | tf_op jit(solution)/shard_map/ppermute | solution.py:37
  83.1 0.5 collective-permute-done.9
  83.7 2.4 %collective-permute-start.10 = (bf16[4,512,128]{2,1,0:T(8,128)(2,1)S(1)}, bf16[4,512,128]{2,1,0:T(8,128)(2,1)S(1)}, u32[]{:S(2)}, u32[]{:S(2)}) collective-permute-start(bf16[4,512,128]{2,1,0:T(8,128)(2,1)S(1)} %collective-permute-done.9), channel_id=1, source_target_pairs={{0,112},{16,0},{32,16},{48,32},{64,48},{80,64},{96,80},{112,96},{1... | collective-permute-start | bytes 1572872 | tf_op jit(solution)/shard_map/ppermute | solution.py:40
  86.1 15.1 %collective-permute-done.7 = bf16[4,512,128]{2,1,0:T(8,128)(2,1)S(1)} collective-permute-done((bf16[4,512,128]{2,1,0:T(8,128)(2,1)S(1)}, bf16[4,512,128]{2,1,0:T(8,128)(2,1)S(1)}, u32[]{:S(2)}, u32[]{:S(2)}) %collective-permute-start.7) | collective-permute-done | bytes 524320 | tf_op jit(solution)/shard_map/ppermute | solution.py:37
  101.2 0.8 bitcast_dynamic-update-slice_fusion.7
  102.0 0.8 bitcast_dynamic-update-slice_fusion.6
  102.9 0.8 bitcast_dynamic-update-slice_fusion.5
  103.7 0.9 bitcast_dynamic-update-slice_fusion.4
  104.6 0.8 bitcast_dynamic-update-slice_fusion.3
  105.4 0.8 bitcast_dynamic-update-slice_fusion.2
  106.2 0.9 bitcast_dynamic-update-slice_fusion.1
  107.1 0.9 bitcast_dynamic-update-slice_fusion
  108.0 14.8 %all-gather.3.cloned.1.call-done = bf16[4608,512]{1,0:T(8,128)(2,1)} async-done(((bf16[144,512]{1,0:T(8,128)(2,1)}), bf16[4608,512]{1,0:T(8,128)(2,1)}) %all-gather.3.cloned.1.call-update) | async-done | bytes 4718608 | tf_op jit(solution)/shard_map/all_gather | solution.py:129
  122.8 0.8 slice.115
  123.8 0.6 fusion.67
  124.5 0.7 subtract_reduce_fusion
  125.4 3.7 %fusion.13 = f32[64,512]{1,0:T(8,128)S(1)} fusion(bf16[32,144,512]{2,1,0:T(8,128)(2,1)} %bitcast.134, f32[64,32]{0,1:T(8,128)S(1)} %add_exponential_fusion, f32[1,64,1024]{2,1,0:T(8,128)S(1)} %convolution_bitcast_fusion), kind=kOutput, calls=%fused_computation.9 | convolution fusion | flops 268697600 | bytes 4407296 | tf_op jit(solution)/shard_map/vts,se->vte/dot_general | solution.py:77
  129.1 0.4 fusion.80
  129.7 3.1 %fusion.12 = bf16[1,64,8,4,128]{4,1,3,2,0:T(8,128)(2,1)S(1)} fusion(bf16[8,4,512,128]{3,2,1,0:T(8,128)(2,1)} %bitcast_dynamic-update-slice_fusion, f32[64,512]{1,0:T(8,128)S(1)} %get-tuple-element.26, f32[512]{0:T(512)S(1)} %copy-done.11, f32[64]{0:T(128)S(1)} %add_rsqrt_fusion, f32[64]{0:T(128)S(1)} %broadcast_multiply_fusion), kind=kOutput, calls=%fused_computation.7 | convolution fusion | flops 268828672 | bytes 4852224 | tf_op jit(solution)/shard_map/vtr,edrc->vtedc/dot_general | solution.py:137
  133.3 0.3 copy.32
  134.0 6.5 %all_to_all.10 = bf16[1,64,4,2,512]{4,2,1,0,3:T(4,128)(2,1)S(1)} all-to-all(bf16[1,64,4,2,512]{4,2,1,0,3:T(4,128)(2,1)S(1)} %copy.33), channel_id=1, replica_groups=mesh['seq_0'=4,'seq_1'=8,'head_0'=4,'head_1'=2,'var'=2] {'head_1'}, dimensions={3} | all-to-all | bytes 1048576 | tf_op jit(solution)/shard_map/all_to_all | solution.py:146
  140.5 0.5 reduce_sum.53
  141.1 19.5 %all_to_all.11 = bf16[1,64,4,512]{3,1,0,2:T(8,128)(2,1)S(1)} all-to-all(bf16[1,64,4,512]{3,1,0,2:T(8,128)(2,1)S(1)} %copy.34), channel_id=1, replica_groups=mesh['seq_0'=4,'seq_1'=8,'head_0'=4,'head_1'=2,'var'=2] {'head_0'}, dimensions={2} | all-to-all | bytes 524288 | tf_op jit(solution)/shard_map/all_to_all | solution.py:148
  160.7 0.6 fusion.33
  (52 shorter events, 2.1 us)
Async XLA Ops:
  6.5 8.0 %copy-start = (bf16[1,2,512]{2,1,0:T(2,128)(2,1)S(1)}, bf16[1,2,512]{2,1,0:T(2,128)(2,1)}, u32[]{:S(2)}) copy-start(bf16[1,2,512]{2,1,0:T(2,128)(2,1)} %param.16) | copy-start | bytes 6148
  6.5 116.3 %all-gather.3.cloned.1.call-start = ((), (), s32[]{:S(2)}) async-start(), calls=%async_computation.2 | async-start | bytes 4866048 | tf_op jit(solution)/shard_map/all_gather | solution.py:129
  8.1 6.2 %collective-permute-start = (bf16[1,3,512]{2,1,0:T(4,128)(2,1)S(1)}, bf16[1,3,512]{2,1,0:T(4,128)(2,1)S(1)}, u32[]{:S(2)}, u32[]{:S(2)}) collective-permute-start(bf16[1,3,512]{2,1,0:T(4,128)(2,1)S(1)} %slice.105), channel_id=1, source_target_pairs={{0,16},{16,32},{32,48},{48,64},{64,80},{80,96},{96,112},{112,128},... | collective-permute-start | bytes 9224 | tf_op jit(solution)/shard_map/ppermute | solution.py:16
  13.5 25.6 %copy-start.8 = (bf16[64,512]{1,0:T(8,128)(2,1)}, bf16[64,512]{1,0:T(8,128)(2,1)S(1)}, u32[]{:S(2)}) copy-start(bf16[64,512]{1,0:T(8,128)(2,1)S(1)} %convolution_convert_fusion.1) | copy-start | bytes 196612
  13.5 91.0 %copy-start.1 = (bf16[512,128]{1,0:T(8,128)(2,1)S(1)}, bf16[512,128]{1,0:T(8,128)(2,1)}, u32[]{:S(2)}) copy-start(bf16[512,128]{1,0:T(8,128)(2,1)} %param.19) | copy-start | bytes 393220
  24.2 8.0 %collective-permute-start.1 = (bf16[512,128]{1,0:T(8,128)(2,1)}, bf16[512,128]{1,0:T(8,128)(2,1)S(1)}, u32[]{:S(2)}, u32[]{:S(2)}) collective-permute-start(bf16[512,128]{1,0:T(8,128)(2,1)} %param.19), channel_id=1, source_target_pairs={{0,128},{128,256},{256,384},{384,0},{1,129},{129,257},{257,385},{3... | collective-permute-start | bytes 393224 | tf_op jit(solution)/shard_map/ppermute | solution.py:37
  28.3 5.9 %collective-permute-start.3 = (bf16[512,128]{1,0:T(8,128)(2,1)}, bf16[512,128]{1,0:T(8,128)(2,1)S(1)}, u32[]{:S(2)}, u32[]{:S(2)}) collective-permute-start(bf16[512,128]{1,0:T(8,128)(2,1)} %param.19), channel_id=1, source_target_pairs={{0,384},{128,0},{256,128},{384,256},{1,385},{129,1},{257,129},{385... | collective-permute-start | bytes 393224 | tf_op jit(solution)/shard_map/ppermute | solution.py:40
  32.2 27.0 %copy-start.2 = (bf16[512,128]{1,0:T(8,128)(2,1)}, bf16[512,128]{1,0:T(8,128)(2,1)S(1)}, u32[]{:S(2)}) copy-start(bf16[512,128]{1,0:T(8,128)(2,1)S(1)} %collective-permute-done.1) | copy-start | bytes 393220
  32.2 6.9 %collective-permute-start.2 = (bf16[512,128]{1,0:T(8,128)(2,1)S(1)}, bf16[512,128]{1,0:T(8,128)(2,1)S(1)}, u32[]{:S(2)}, u32[]{:S(2)}) collective-permute-start(bf16[512,128]{1,0:T(8,128)(2,1)S(1)} %collective-permute-done.1), channel_id=1, source_target_pairs={{0,128},{128,256},{256,384},{384,0},{1,129},{129,257},{257,385},{3... | collective-permute-start | bytes 393224 | tf_op jit(solution)/shard_map/ppermute | solution.py:37
  34.3 24.9 %copy-start.4 = (bf16[512,128]{1,0:T(8,128)(2,1)}, bf16[512,128]{1,0:T(8,128)(2,1)S(1)}, u32[]{:S(2)}) copy-start(bf16[512,128]{1,0:T(8,128)(2,1)S(1)} %collective-permute-done.3) | copy-start | bytes 393220
  39.1 20.1 %copy-start.6 = (bf16[512,128]{1,0:T(8,128)(2,1)}, bf16[512,128]{1,0:T(8,128)(2,1)S(1)}, u32[]{:S(2)}) copy-start(bf16[512,128]{1,0:T(8,128)(2,1)S(1)} %collective-permute-done.2) | copy-start | bytes 393220
  40.1 12.6 %collective-permute-start.4 = (bf16[4,512,128]{2,1,0:T(8,128)(2,1)S(1)}, bf16[4,512,128]{2,1,0:T(8,128)(2,1)S(1)}, u32[]{:S(2)}, u32[]{:S(2)}) collective-permute-start(bf16[4,512,128]{2,1,0:T(8,128)(2,1)S(1)} %pad_maximum_fusion), channel_id=1, source_target_pairs={{0,16},{16,32},{32,48},{48,64},{64,80},{80,96},{96,112},{112,0},{1... | collective-permute-start | bytes 1572872 | tf_op jit(solution)/shard_map/ppermute | solution.py:37
  52.7 14.2 %collective-permute-start.5 = (bf16[4,512,128]{2,1,0:T(8,128)(2,1)S(1)}, bf16[4,512,128]{2,1,0:T(8,128)(2,1)S(1)}, u32[]{:S(2)}, u32[]{:S(2)}) collective-permute-start(bf16[4,512,128]{2,1,0:T(8,128)(2,1)S(1)} %collective-permute-done.4), channel_id=1, source_target_pairs={{0,16},{16,32},{32,48},{48,64},{64,80},{80,96},{96,112},{112,0},{1... | collective-permute-start | bytes 1572872 | tf_op jit(solution)/shard_map/ppermute | solution.py:37
  54.6 17.2 %collective-permute-start.8 = (bf16[4,512,128]{2,1,0:T(8,128)(2,1)S(1)}, bf16[4,512,128]{2,1,0:T(8,128)(2,1)S(1)}, u32[]{:S(2)}, u32[]{:S(2)}) collective-permute-start(bf16[4,512,128]{2,1,0:T(8,128)(2,1)S(1)} %pad_maximum_fusion), channel_id=1, source_target_pairs={{0,112},{16,0},{32,16},{48,32},{64,48},{80,64},{96,80},{112,96},{1... | collective-permute-start | bytes 1572872 | tf_op jit(solution)/shard_map/ppermute | solution.py:40
  66.9 12.5 %collective-permute-start.6 = (bf16[4,512,128]{2,1,0:T(8,128)(2,1)S(1)}, bf16[4,512,128]{2,1,0:T(8,128)(2,1)S(1)}, u32[]{:S(2)}, u32[]{:S(2)}) collective-permute-start(bf16[4,512,128]{2,1,0:T(8,128)(2,1)S(1)} %collective-permute-done.5), channel_id=1, source_target_pairs={{0,16},{16,32},{32,48},{48,64},{64,80},{80,96},{96,112},{112,0},{1... | collective-permute-start | bytes 1572872 | tf_op jit(solution)/shard_map/ppermute | solution.py:37
  71.8 11.8 %collective-permute-start.9 = (bf16[4,512,128]{2,1,0:T(8,128)(2,1)S(1)}, bf16[4,512,128]{2,1,0:T(8,128)(2,1)S(1)}, u32[]{:S(2)}, u32[]{:S(2)}) collective-permute-start(bf16[4,512,128]{2,1,0:T(8,128)(2,1)S(1)} %collective-permute-done.8), channel_id=1, source_target_pairs={{0,112},{16,0},{32,16},{48,32},{64,48},{80,64},{96,80},{112,96},{1... | collective-permute-start | bytes 1572872 | tf_op jit(solution)/shard_map/ppermute | solution.py:40
  79.4 21.8 %collective-permute-start.7 = (bf16[4,512,128]{2,1,0:T(8,128)(2,1)S(1)}, bf16[4,512,128]{2,1,0:T(8,128)(2,1)S(1)}, u32[]{:S(2)}, u32[]{:S(2)}) collective-permute-start(bf16[4,512,128]{2,1,0:T(8,128)(2,1)S(1)} %collective-permute-done.6), channel_id=1, source_target_pairs={{0,16},{16,32},{32,48},{48,64},{64,80},{80,96},{96,112},{112,0},{1... | collective-permute-start | bytes 1572872 | tf_op jit(solution)/shard_map/ppermute | solution.py:37
  83.1 21.5 %copy-start.3 = (bf16[512,128]{1,0:T(8,128)(2,1)S(1)}, bf16[512,128]{1,0:T(8,128)(2,1)}, u32[]{:S(2)}) copy-start(bf16[512,128]{1,0:T(8,128)(2,1)} %copy-done.2) | copy-start | bytes 393220
  83.1 21.5 %copy-start.5 = (bf16[512,128]{1,0:T(8,128)(2,1)S(1)}, bf16[512,128]{1,0:T(8,128)(2,1)}, u32[]{:S(2)}) copy-start(bf16[512,128]{1,0:T(8,128)(2,1)} %copy-done.4) | copy-start | bytes 393220
  83.1 21.5 %copy-start.7 = (bf16[512,128]{1,0:T(8,128)(2,1)S(1)}, bf16[512,128]{1,0:T(8,128)(2,1)}, u32[]{:S(2)}) copy-start(bf16[512,128]{1,0:T(8,128)(2,1)} %copy-done.6) | copy-start | bytes 393220
  83.7 23.4 %collective-permute-start.10 = (bf16[4,512,128]{2,1,0:T(8,128)(2,1)S(1)}, bf16[4,512,128]{2,1,0:T(8,128)(2,1)S(1)}, u32[]{:S(2)}, u32[]{:S(2)}) collective-permute-start(bf16[4,512,128]{2,1,0:T(8,128)(2,1)S(1)} %collective-permute-done.9), channel_id=1, source_target_pairs={{0,112},{16,0},{32,16},{48,32},{64,48},{80,64},{96,80},{112,96},{1... | collective-permute-start | bytes 1572872 | tf_op jit(solution)/shard_map/ppermute | solution.py:40
  106.2 22.9 %copy-start.9 = (bf16[64,512]{1,0:T(8,128)(2,1)S(1)}, bf16[64,512]{1,0:T(8,128)(2,1)}, u32[]{:S(2)}) copy-start(bf16[64,512]{1,0:T(8,128)(2,1)} %copy-done.8) | copy-start | bytes 196612
  107.1 22.6 %copy-start.11 = (f32[512]{0:T(512)S(1)}, f32[512]{0:T(512)}, u32[]{:S(2)}) copy-start(f32[512]{0:T(512)} %param.18) | copy-start | bytes 6148
  132.8 27.9 %copy-start.10 = (bf16[64,512]{1,0:T(8,128)(2,1)S(1)}, bf16[64,512]{1,0:T(8,128)(2,1)}, u32[]{:S(2)}) copy-start(bf16[64,512]{1,0:T(8,128)(2,1)} %param.12) | copy-start | bytes 196612
Sparse Core Ops, SparseCore 0:
  24.3 98.4 all-gather.2

commit v12 on v11

--- a/solution.py
+++ b/solution.py
@@ -7,7 +7,7 @@
 CONV = 4
 SEQ = ("seq_0", "seq_1")
 HEAD = ("head_1", "head_0")
-EXTRA = 16
+EXTRA = 8
 
 
 def from_behind(value, axis, steps):

time: 170 us -> 169 us (level)
  no operation moved by 1% of the time
where the time goes in v12:
time: 169 us; the launch traced here: 168 us
  waiting for transfers between devices  58.1 us (34%)
  starting transfers between devices  35.1 us (21%)
  blocking collectives  27.1 us (16%)
  between operations  18.6 us (11%)
  matrix products  10.8 us (6%)
  local copies, waits for them, and re-layouts  9.29 us (5%)
  other arithmetic  8.6 us (5%)
    ppermute x6, waiting for transfers between devices, ring_pieces(): forward = lax.ppermute(forward, axis, ahead)  43.2 us
    all_to_all x1, blocking collectives, body(): lax.all_to_all(pair_sum, across, split_axis=2, concat_axis=2, tiled=True)  20.5 us
    ppermute x6, starting transfers between devices, ring_pieces(): forward = lax.ppermute(forward, axis, ahead)  18.9 us
    all_gather x1, waiting for transfers between devices, body(): gathered = lax.all_gather(packed, SEQ, axis=0, tiled=False)  14.4 us
    ppermute x4, starting transfers between devices, ring_pieces(): backward = lax.ppermute(backward, axis, behind)  12.2 us
    all_to_all x1, blocking collectives, body(): lax.all_to_all(blocks, pair, split_axis=3, concat_axis=3, tiled=True)  6.58 us
    unnamed x32, local copies, waits for them, and re-layouts  5.15 us
    ppermute x1, starting transfers between devices, from_behind(): lax.ppermute(value, axis, [(source, source + steps) for source in range(i...  4.02 us
  transfers between devices with their start and end apart: 12, of which 8 were waited for; matrix products, arithmetic and copies ran while one was open for 6% of the time, Pallas kernels for 0%

profile of v12, /device:TPU:1, one launch (start us, length us, event | category | flops | bytes accessed | tf_op | source)
XLA Modules:
  0.0 167.5 jit_solution(7616951389691728160)
XLA Ops:
  6.5 0.7 convert_bitcast_fusion
  7.2 0.9 multiply_bitcast_fusion
  8.1 4.0 %collective-permute-start = (bf16[1,3,512]{2,1,0:T(4,128)(2,1)S(1)}, bf16[1,3,512]{2,1,0:T(4,128)(2,1)S(1)}, u32[]{:S(2)}, u32[]{:S(2)}) collective-permute-start(bf16[1,3,512]{2,1,0:T(4,128)(2,1)S(1)} %slice.105), channel_id=1, source_target_pairs={{0,16},{16,32},{32,48},{48,64},{64,80},{80,96},{96,112},{112,128},... | collective-permute-start | bytes 9224 | tf_op jit(solution)/shard_map/ppermute | solution.py:16
  12.2 1.3 convolution_convert_fusion.1
  13.5 0.9 fusion.79
  14.5 0.7 fusion.19
  15.6 0.7 slice.95
  21.1 0.7 fusion.78
  21.8 1.5 convolution_bitcast_fusion
  23.5 0.7 pad_maximum_fusion.1
  24.2 4.1 %collective-permute-start.1 = (bf16[512,128]{1,0:T(8,128)(2,1)}, bf16[512,128]{1,0:T(8,128)(2,1)S(1)}, u32[]{:S(2)}, u32[]{:S(2)}) collective-permute-start(bf16[512,128]{1,0:T(8,128)(2,1)} %param.19), channel_id=1, source_target_pairs={{0,128},{128,256},{256,384},{384,0},{1,129},{129,257},{257,385},{3... | collective-permute-start | bytes 393224 | tf_op jit(solution)/shard_map/ppermute | solution.py:37
  28.3 3.2 %collective-permute-start.3 = (bf16[512,128]{1,0:T(8,128)(2,1)}, bf16[512,128]{1,0:T(8,128)(2,1)S(1)}, u32[]{:S(2)}, u32[]{:S(2)}) collective-permute-start(bf16[512,128]{1,0:T(8,128)(2,1)} %param.19), channel_id=1, source_target_pairs={{0,384},{128,0},{256,128},{384,256},{1,385},{129,1},{257,129},{385... | collective-permute-start | bytes 393224 | tf_op jit(solution)/shard_map/ppermute | solution.py:40
  31.5 0.6 collective-permute-done.1
  32.1 2.1 %collective-permute-start.2 = (bf16[512,128]{1,0:T(8,128)(2,1)S(1)}, bf16[512,128]{1,0:T(8,128)(2,1)S(1)}, u32[]{:S(2)}, u32[]{:S(2)}) collective-permute-start(bf16[512,128]{1,0:T(8,128)(2,1)S(1)} %collective-permute-done.1), channel_id=1, source_target_pairs={{0,128},{128,256},{256,384},{384,0},{1,129},{129,257},{257,385},{3... | collective-permute-start | bytes 393224 | tf_op jit(solution)/shard_map/ppermute | solution.py:37
  34.3 4.8 %collective-permute-done.2 = bf16[512,128]{1,0:T(8,128)(2,1)S(1)} collective-permute-done((bf16[512,128]{1,0:T(8,128)(2,1)S(1)}, bf16[512,128]{1,0:T(8,128)(2,1)S(1)}, u32[]{:S(2)}, u32[]{:S(2)}) %collective-permute-start.2) | collective-permute-done | bytes 131104 | tf_op jit(solution)/shard_map/ppermute | solution.py:37
  39.1 1.0 pad_maximum_fusion
  40.1 2.4 %collective-permute-start.4 = (bf16[4,512,128]{2,1,0:T(8,128)(2,1)S(1)}, bf16[4,512,128]{2,1,0:T(8,128)(2,1)S(1)}, u32[]{:S(2)}, u32[]{:S(2)}) collective-permute-start(bf16[4,512,128]{2,1,0:T(8,128)(2,1)S(1)} %pad_maximum_fusion), channel_id=1, source_target_pairs={{0,16},{16,32},{32,48},{48,64},{64,80},{80,96},{96,112},{112,0},{1... | collective-permute-start | bytes 1572872 | tf_op jit(solution)/shard_map/ppermute | solution.py:37
  42.5 10.1 %collective-permute-done.4 = bf16[4,512,128]{2,1,0:T(8,128)(2,1)S(1)} collective-permute-done((bf16[4,512,128]{2,1,0:T(8,128)(2,1)S(1)}, bf16[4,512,128]{2,1,0:T(8,128)(2,1)S(1)}, u32[]{:S(2)}, u32[]{:S(2)}) %collective-permute-start.4) | collective-permute-done | bytes 524320 | tf_op jit(solution)/shard_map/ppermute | solution.py:37
  52.6 1.9 %collective-permute-start.5 = (bf16[4,512,128]{2,1,0:T(8,128)(2,1)S(1)}, bf16[4,512,128]{2,1,0:T(8,128)(2,1)S(1)}, u32[]{:S(2)}, u32[]{:S(2)}) collective-permute-start(bf16[4,512,128]{2,1,0:T(8,128)(2,1)S(1)} %collective-permute-done.4), channel_id=1, source_target_pairs={{0,16},{16,32},{32,48},{48,64},{64,80},{80,96},{96,112},{112,0},{1... | collective-permute-start | bytes 1572872 | tf_op jit(solution)/shard_map/ppermute | solution.py:37
  54.5 4.6 %collective-permute-start.8 = (bf16[4,512,128]{2,1,0:T(8,128)(2,1)S(1)}, bf16[4,512,128]{2,1,0:T(8,128)(2,1)S(1)}, u32[]{:S(2)}, u32[]{:S(2)}) collective-permute-start(bf16[4,512,128]{2,1,0:T(8,128)(2,1)S(1)} %pad_maximum_fusion), channel_id=1, source_target_pairs={{0,112},{16,0},{32,16},{48,32},{64,48},{80,64},{96,80},{112,96},{1... | collective-permute-start | bytes 1572872 | tf_op jit(solution)/shard_map/ppermute | solution.py:40
  59.1 7.6 %collective-permute-done.5 = bf16[4,512,128]{2,1,0:T(8,128)(2,1)S(1)} collective-permute-done((bf16[4,512,128]{2,1,0:T(8,128)(2,1)S(1)}, bf16[4,512,128]{2,1,0:T(8,128)(2,1)S(1)}, u32[]{:S(2)}, u32[]{:S(2)}) %collective-permute-start.5) | collective-permute-done | bytes 524320 | tf_op jit(solution)/shard_map/ppermute | solution.py:37
  66.7 4.8 %collective-permute-start.6 = (bf16[4,512,128]{2,1,0:T(8,128)(2,1)S(1)}, bf16[4,512,128]{2,1,0:T(8,128)(2,1)S(1)}, u32[]{:S(2)}, u32[]{:S(2)}) collective-permute-start(bf16[4,512,128]{2,1,0:T(8,128)(2,1)S(1)} %collective-permute-done.5), channel_id=1, source_target_pairs={{0,16},{16,32},{32,48},{48,64},{64,80},{80,96},{96,112},{112,0},{1... | collective-permute-start | bytes 1572872 | tf_op jit(solution)/shard_map/ppermute | solution.py:37
  71.5 1.9 %collective-permute-start.9 = (bf16[4,512,128]{2,1,0:T(8,128)(2,1)S(1)}, bf16[4,512,128]{2,1,0:T(8,128)(2,1)S(1)}, u32[]{:S(2)}, u32[]{:S(2)}) collective-permute-start(bf16[4,512,128]{2,1,0:T(8,128)(2,1)S(1)} %collective-permute-done.8), channel_id=1, source_target_pairs={{0,112},{16,0},{32,16},{48,32},{64,48},{80,64},{96,80},{112,96},{1... | collective-permute-start | bytes 1572872 | tf_op jit(solution)/shard_map/ppermute | solution.py:40
  73.4 5.7 %collective-permute-done.6 = bf16[4,512,128]{2,1,0:T(8,128)(2,1)S(1)} collective-permute-done((bf16[4,512,128]{2,1,0:T(8,128)(2,1)S(1)}, bf16[4,512,128]{2,1,0:T(8,128)(2,1)S(1)}, u32[]{:S(2)}, u32[]{:S(2)}) %collective-permute-start.6) | collective-permute-done | bytes 524320 | tf_op jit(solution)/shard_map/ppermute | solution.py:37
  79.1 3.6 %collective-permute-start.7 = (bf16[4,512,128]{2,1,0:T(8,128)(2,1)S(1)}, bf16[4,512,128]{2,1,0:T(8,128)(2,1)S(1)}, u32[]{:S(2)}, u32[]{:S(2)}) collective-permute-start(bf16[4,512,128]{2,1,0:T(8,128)(2,1)S(1)} %collective-permute-done.6), channel_id=1, source_target_pairs={{0,16},{16,32},{32,48},{48,64},{64,80},{80,96},{96,112},{112,0},{1... | collective-permute-start | bytes 1572872 | tf_op jit(solution)/shard_map/ppermute | solution.py:37
  82.7 0.6 collective-permute-done.9
  83.3 2.5 %collective-permute-start.10 = (bf16[4,512,128]{2,1,0:T(8,128)(2,1)S(1)}, bf16[4,512,128]{2,1,0:T(8,128)(2,1)S(1)}, u32[]{:S(2)}, u32[]{:S(2)}) collective-permute-start(bf16[4,512,128]{2,1,0:T(8,128)(2,1)S(1)} %collective-permute-done.9), channel_id=1, source_target_pairs={{0,112},{16,0},{32,16},{48,32},{64,48},{80,64},{96,80},{112,96},{1... | collective-permute-start | bytes 1572872 | tf_op jit(solution)/shard_map/ppermute | solution.py:40
  85.8 14.4 %collective-permute-done.7 = bf16[4,512,128]{2,1,0:T(8,128)(2,1)S(1)} collective-permute-done((bf16[4,512,128]{2,1,0:T(8,128)(2,1)S(1)}, bf16[4,512,128]{2,1,0:T(8,128)(2,1)S(1)}, u32[]{:S(2)}, u32[]{:S(2)}) %collective-permute-start.7) | collective-permute-done | bytes 524320 | tf_op jit(solution)/shard_map/ppermute | solution.py:37
  100.2 0.8 bitcast_dynamic-update-slice_fusion.7
  101.0 0.8 bitcast_dynamic-update-slice_fusion.6
  101.8 0.8 bitcast_dynamic-update-slice_fusion.5
  102.7 0.8 bitcast_dynamic-update-slice_fusion.4
  103.5 0.8 bitcast_dynamic-update-slice_fusion.3
  104.4 0.8 bitcast_dynamic-update-slice_fusion.2
  105.2 0.8 bitcast_dynamic-update-slice_fusion.1
  106.0 0.9 bitcast_dynamic-update-slice_fusion
  106.9 14.4 %all-gather.3.cloned.1.call-done = bf16[4352,512]{1,0:T(8,128)(2,1)} async-done(((bf16[136,512]{1,0:T(8,128)(2,1)}), bf16[4352,512]{1,0:T(8,128)(2,1)}) %all-gather.3.cloned.1.call-update) | async-done | bytes 4456464 | tf_op jit(solution)/shard_map/all_gather | solution.py:129
  121.2 0.8 slice.115
  122.2 0.6 fusion.67
  123.0 0.7 subtract_reduce_fusion
  123.7 3.7 %fusion.13 = f32[64,512]{1,0:T(8,128)S(1)} fusion(bf16[32,136,512]{2,1,0:T(8,128)(2,1)} %bitcast.134, f32[64,32]{0,1:T(8,128)S(1)} %add_exponential_fusion, f32[1,64,1024]{2,1,0:T(8,128)S(1)} %convolution_bitcast_fusion), kind=kOutput, calls=%fused_computation.9 | convolution fusion | flops 268697600 | bytes 4407296 | tf_op jit(solution)/shard_map/vts,se->vte/dot_general | solution.py:77
  127.4 0.4 fusion.80
  128.1 3.1 %fusion.12 = bf16[1,64,8,4,128]{4,1,3,2,0:T(8,128)(2,1)S(1)} fusion(bf16[8,4,512,128]{3,2,1,0:T(8,128)(2,1)} %bitcast_dynamic-update-slice_fusion, f32[64,512]{1,0:T(8,128)S(1)} %get-tuple-element.26, f32[512]{0:T(512)S(1)} %copy-done.11, f32[64]{0:T(128)S(1)} %add_rsqrt_fusion, f32[64]{0:T(128)S(1)} %broadcast_multiply_fusion), kind=kOutput, calls=%fused_computation.7 | convolution fusion | flops 268828672 | bytes 4852224 | tf_op jit(solution)/shard_map/vtr,edrc->vtedc/dot_general | solution.py:137
  131.6 0.3 copy.32
  132.4 6.6 %all_to_all.10 = bf16[1,64,4,2,512]{4,2,1,0,3:T(4,128)(2,1)S(1)} all-to-all(bf16[1,64,4,2,512]{4,2,1,0,3:T(4,128)(2,1)S(1)} %copy.33), channel_id=1, replica_groups=mesh['seq_0'=4,'seq_1'=8,'head_0'=4,'head_1'=2,'var'=2] {'head_1'}, dimensions={3} | all-to-all | bytes 1048576 | tf_op jit(solution)/shard_map/all_to_all | solution.py:146
  138.9 0.5 reduce_sum.53
  139.5 20.5 %all_to_all.11 = bf16[1,64,4,512]{3,1,0,2:T(8,128)(2,1)S(1)} all-to-all(bf16[1,64,4,512]{3,1,0,2:T(8,128)(2,1)S(1)} %copy.34), channel_id=1, replica_groups=mesh['seq_0'=4,'seq_1'=8,'head_0'=4,'head_1'=2,'var'=2] {'head_0'}, dimensions={2} | all-to-all | bytes 524288 | tf_op jit(solution)/shard_map/all_to_all | solution.py:148
  160.0 0.6 fusion.33
  (52 shorter events, 2.1 us)
Async XLA Ops:
  6.5 8.0 %copy-start = (bf16[1,2,512]{2,1,0:T(2,128)(2,1)S(1)}, bf16[1,2,512]{2,1,0:T(2,128)(2,1)}, u32[]{:S(2)}) copy-start(bf16[1,2,512]{2,1,0:T(2,128)(2,1)} %param.16) | copy-start | bytes 6148
  6.5 114.7 %all-gather.3.cloned.1.call-start = ((), (), s32[]{:S(2)}) async-start(), calls=%async_computation.2 | async-start | bytes 4595712 | tf_op jit(solution)/shard_map/all_gather | solution.py:129
  8.1 6.2 %collective-permute-start = (bf16[1,3,512]{2,1,0:T(4,128)(2,1)S(1)}, bf16[1,3,512]{2,1,0:T(4,128)(2,1)S(1)}, u32[]{:S(2)}, u32[]{:S(2)}) collective-permute-start(bf16[1,3,512]{2,1,0:T(4,128)(2,1)S(1)} %slice.105), channel_id=1, source_target_pairs={{0,16},{16,32},{32,48},{48,64},{64,80},{80,96},{96,112},{112,128},... | collective-permute-start | bytes 9224 | tf_op jit(solution)/shard_map/ppermute | solution.py:16
  13.5 25.6 %copy-start.8 = (bf16[64,512]{1,0:T(8,128)(2,1)}, bf16[64,512]{1,0:T(8,128)(2,1)S(1)}, u32[]{:S(2)}) copy-start(bf16[64,512]{1,0:T(8,128)(2,1)S(1)} %convolution_convert_fusion.1) | copy-start | bytes 196612
  13.5 90.0 %copy-start.1 = (bf16[512,128]{1,0:T(8,128)(2,1)S(1)}, bf16[512,128]{1,0:T(8,128)(2,1)}, u32[]{:S(2)}) copy-start(bf16[512,128]{1,0:T(8,128)(2,1)} %param.19) | copy-start | bytes 393220
  24.2 8.0 %collective-permute-start.1 = (bf16[512,128]{1,0:T(8,128)(2,1)}, bf16[512,128]{1,0:T(8,128)(2,1)S(1)}, u32[]{:S(2)}, u32[]{:S(2)}) collective-permute-start(bf16[512,128]{1,0:T(8,128)(2,1)} %param.19), channel_id=1, source_target_pairs={{0,128},{128,256},{256,384},{384,0},{1,129},{129,257},{257,385},{3... | collective-permute-start | bytes 393224 | tf_op jit(solution)/shard_map/ppermute | solution.py:37
  28.3 5.9 %collective-permute-start.3 = (bf16[512,128]{1,0:T(8,128)(2,1)}, bf16[512,128]{1,0:T(8,128)(2,1)S(1)}, u32[]{:S(2)}, u32[]{:S(2)}) collective-permute-start(bf16[512,128]{1,0:T(8,128)(2,1)} %param.19), channel_id=1, source_target_pairs={{0,384},{128,0},{256,128},{384,256},{1,385},{129,1},{257,129},{385... | collective-permute-start | bytes 393224 | tf_op jit(solution)/shard_map/ppermute | solution.py:40
  32.1 26.9 %copy-start.2 = (bf16[512,128]{1,0:T(8,128)(2,1)}, bf16[512,128]{1,0:T(8,128)(2,1)S(1)}, u32[]{:S(2)}) copy-start(bf16[512,128]{1,0:T(8,128)(2,1)S(1)} %collective-permute-done.1) | copy-start | bytes 393220
  32.1 6.9 %collective-permute-start.2 = (bf16[512,128]{1,0:T(8,128)(2,1)S(1)}, bf16[512,128]{1,0:T(8,128)(2,1)S(1)}, u32[]{:S(2)}, u32[]{:S(2)}) collective-permute-start(bf16[512,128]{1,0:T(8,128)(2,1)S(1)} %collective-permute-done.1), channel_id=1, source_target_pairs={{0,128},{128,256},{256,384},{384,0},{1,129},{129,257},{257,385},{3... | collective-permute-start | bytes 393224 | tf_op jit(solution)/shard_map/ppermute | solution.py:37
  34.2 24.8 %copy-start.4 = (bf16[512,128]{1,0:T(8,128)(2,1)}, bf16[512,128]{1,0:T(8,128)(2,1)S(1)}, u32[]{:S(2)}) copy-start(bf16[512,128]{1,0:T(8,128)(2,1)S(1)} %collective-permute-done.3) | copy-start | bytes 393220
  39.1 20.0 %copy-start.6 = (bf16[512,128]{1,0:T(8,128)(2,1)}, bf16[512,128]{1,0:T(8,128)(2,1)S(1)}, u32[]{:S(2)}) copy-start(bf16[512,128]{1,0:T(8,128)(2,1)S(1)} %collective-permute-done.2) | copy-start | bytes 393220
  40.1 12.5 %collective-permute-start.4 = (bf16[4,512,128]{2,1,0:T(8,128)(2,1)S(1)}, bf16[4,512,128]{2,1,0:T(8,128)(2,1)S(1)}, u32[]{:S(2)}, u32[]{:S(2)}) collective-permute-start(bf16[4,512,128]{2,1,0:T(8,128)(2,1)S(1)} %pad_maximum_fusion), channel_id=1, source_target_pairs={{0,16},{16,32},{32,48},{48,64},{64,80},{80,96},{96,112},{112,0},{1... | collective-permute-start | bytes 1572872 | tf_op jit(solution)/shard_map/ppermute | solution.py:37
  52.6 14.1 %collective-permute-start.5 = (bf16[4,512,128]{2,1,0:T(8,128)(2,1)S(1)}, bf16[4,512,128]{2,1,0:T(8,128)(2,1)S(1)}, u32[]{:S(2)}, u32[]{:S(2)}) collective-permute-start(bf16[4,512,128]{2,1,0:T(8,128)(2,1)S(1)} %collective-permute-done.4), channel_id=1, source_target_pairs={{0,16},{16,32},{32,48},{48,64},{64,80},{80,96},{96,112},{112,0},{1... | collective-permute-start | bytes 1572872 | tf_op jit(solution)/shard_map/ppermute | solution.py:37
  54.5 17.0 %collective-permute-start.8 = (bf16[4,512,128]{2,1,0:T(8,128)(2,1)S(1)}, bf16[4,512,128]{2,1,0:T(8,128)(2,1)S(1)}, u32[]{:S(2)}, u32[]{:S(2)}) collective-permute-start(bf16[4,512,128]{2,1,0:T(8,128)(2,1)S(1)} %pad_maximum_fusion), channel_id=1, source_target_pairs={{0,112},{16,0},{32,16},{48,32},{64,48},{80,64},{96,80},{112,96},{1... | collective-permute-start | bytes 1572872 | tf_op jit(solution)/shard_map/ppermute | solution.py:40
  66.7 12.4 %collective-permute-start.6 = (bf16[4,512,128]{2,1,0:T(8,128)(2,1)S(1)}, bf16[4,512,128]{2,1,0:T(8,128)(2,1)S(1)}, u32[]{:S(2)}, u32[]{:S(2)}) collective-permute-start(bf16[4,512,128]{2,1,0:T(8,128)(2,1)S(1)} %collective-permute-done.5), channel_id=1, source_target_pairs={{0,16},{16,32},{32,48},{48,64},{64,80},{80,96},{96,112},{112,0},{1... | collective-permute-start | bytes 1572872 | tf_op jit(solution)/shard_map/ppermute | solution.py:37
  71.5 11.8 %collective-permute-start.9 = (bf16[4,512,128]{2,1,0:T(8,128)(2,1)S(1)}, bf16[4,512,128]{2,1,0:T(8,128)(2,1)S(1)}, u32[]{:S(2)}, u32[]{:S(2)}) collective-permute-start(bf16[4,512,128]{2,1,0:T(8,128)(2,1)S(1)} %collective-permute-done.8), channel_id=1, source_target_pairs={{0,112},{16,0},{32,16},{48,32},{64,48},{80,64},{96,80},{112,96},{1... | collective-permute-start | bytes 1572872 | tf_op jit(solution)/shard_map/ppermute | solution.py:40
  79.1 21.1 %collective-permute-start.7 = (bf16[4,512,128]{2,1,0:T(8,128)(2,1)S(1)}, bf16[4,512,128]{2,1,0:T(8,128)(2,1)S(1)}, u32[]{:S(2)}, u32[]{:S(2)}) collective-permute-start(bf16[4,512,128]{2,1,0:T(8,128)(2,1)S(1)} %collective-permute-done.6), channel_id=1, source_target_pairs={{0,16},{16,32},{32,48},{48,64},{64,80},{80,96},{96,112},{112,0},{1... | collective-permute-start | bytes 1572872 | tf_op jit(solution)/shard_map/ppermute | solution.py:37
  82.7 20.8 %copy-start.3 = (bf16[512,128]{1,0:T(8,128)(2,1)S(1)}, bf16[512,128]{1,0:T(8,128)(2,1)}, u32[]{:S(2)}) copy-start(bf16[512,128]{1,0:T(8,128)(2,1)} %copy-done.2) | copy-start | bytes 393220
  82.7 20.8 %copy-start.5 = (bf16[512,128]{1,0:T(8,128)(2,1)S(1)}, bf16[512,128]{1,0:T(8,128)(2,1)}, u32[]{:S(2)}) copy-start(bf16[512,128]{1,0:T(8,128)(2,1)} %copy-done.4) | copy-start | bytes 393220
  82.7 20.8 %copy-start.7 = (bf16[512,128]{1,0:T(8,128)(2,1)S(1)}, bf16[512,128]{1,0:T(8,128)(2,1)}, u32[]{:S(2)}) copy-start(bf16[512,128]{1,0:T(8,128)(2,1)} %copy-done.6) | copy-start | bytes 393220
  83.3 22.7 %collective-permute-start.10 = (bf16[4,512,128]{2,1,0:T(8,128)(2,1)S(1)}, bf16[4,512,128]{2,1,0:T(8,128)(2,1)S(1)}, u32[]{:S(2)}, u32[]{:S(2)}) collective-permute-start(bf16[4,512,128]{2,1,0:T(8,128)(2,1)S(1)} %collective-permute-done.9), channel_id=1, source_target_pairs={{0,112},{16,0},{32,16},{48,32},{64,48},{80,64},{96,80},{112,96},{1... | collective-permute-start | bytes 1572872 | tf_op jit(solution)/shard_map/ppermute | solution.py:40
  105.2 22.2 %copy-start.9 = (bf16[64,512]{1,0:T(8,128)(2,1)S(1)}, bf16[64,512]{1,0:T(8,128)(2,1)}, u32[]{:S(2)}) copy-start(bf16[64,512]{1,0:T(8,128)(2,1)} %copy-done.8) | copy-start | bytes 196612
  106.0 22.0 %copy-start.11 = (f32[512]{0:T(512)S(1)}, f32[512]{0:T(512)}, u32[]{:S(2)}) copy-start(f32[512]{0:T(512)} %param.18) | copy-start | bytes 6148
  131.1 28.9 %copy-start.10 = (bf16[64,512]{1,0:T(8,128)(2,1)S(1)}, bf16[64,512]{1,0:T(8,128)(2,1)}, u32[]{:S(2)}) copy-start(bf16[64,512]{1,0:T(8,128)(2,1)} %param.12) | copy-start | bytes 196612
Sparse Core Ops, SparseCore 0:
  24.3 96.9 all-gather.2

commit v13 on v12

--- a/solution.py
+++ b/solution.py
@@ -89,7 +89,7 @@
     down_weight,
 ):
     outer, inner_size = (lax.axis_size(SEQ[0]), lax.axis_size(SEQ[1]))
-    columns_all = ring_pieces(ring_pieces(down_weight, SEQ[0], outer), SEQ[1], inner_size)
+    columns_all = ring_pieces(ring_pieces(down_weight, SEQ[1], inner_size), SEQ[0], outer)
     kept_mask = (1 - erase).astype(jnp.bfloat16)
     erased = inner[None, :, :] * kept_mask[:, :, None]
     row_count = inner.shape[0]
@@ -135,12 +135,12 @@
     row_var = jnp.mean(centred * centred, axis=-1, keepdims=True)
     normed = (centred * lax.rsqrt(row_var + 1e-05) * norm_gain).astype(jnp.bfloat16)
     head_terms = jnp.einsum(
-        "vtr,edrc->vtedc", normed, columns_all.reshape(inner_size, outer, head_size, -1),
+        "vtr,derc->vtdec", normed, columns_all.reshape(outer, inner_size, head_size, -1),
         preferred_element_type=jnp.float32,
     ).astype(jnp.bfloat16)
-    head_terms = jnp.roll(head_terms, lax.axis_index(SEQ[1]) - inner_size // 2, axis=2)
-    head_terms = jnp.roll(head_terms, lax.axis_index(SEQ[0]) - outer // 2, axis=3)
-    head_terms = jnp.swapaxes(head_terms, 2, 3).reshape(*normed.shape[:2], -1)
+    head_terms = jnp.roll(head_terms, lax.axis_index(SEQ[0]) - outer // 2, axis=2)
+    head_terms = jnp.roll(head_terms, lax.axis_index(SEQ[1]) - inner_size // 2, axis=3)
+    head_terms = head_terms.reshape(*normed.shape[:2], -1)
     pair, across = HEAD
     blocks = head_terms.reshape(*head_terms.shape[:2], lax.axis_size(across), lax.axis_size(pair), -1)
     arrived = lax.all_to_all(blocks, pair, split_axis=3, concat_axis=3, tiled=True)

time: 169 us -> 171 us (1.012)
  waiting for transfers between devices: 58.1 us -> 71.2 us
  local copies, waits for them, and re-layouts: 9.29 us -> 3.46 us
  blocking collectives: 27.1 us -> 21.5 us
  starting transfers between devices: 35.1 us -> 37 us
  other arithmetic: 8.6 us -> 6.84 us
    all_gather x1, waiting for transfers between devices: 14.4 us -> 50.2 us  [body(): gathered = lax.all_gather(packed, SEQ, axis=0, tiled=False)]
    ppermute x6, waiting for transfers between devices: 43.2 us -> 18.6 us  [ring_pieces(): forward = lax.ppermute(forward, axis, ahead)]
    ppermute x4, starting transfers between devices: 12.2 us -> 18.1 us  [ring_pieces(): backward = lax.ppermute(backward, axis, behind)]
    unnamed x32 -> x17, local copies, waits for them, and re-layouts: 5.15 us -> 0.25 us
    ppermute x6, starting transfers between devices: 18.9 us -> 14.8 us  [ring_pieces(): forward = lax.ppermute(forward, axis, ahead)]
    all_to_all x1, blocking collectives: 20.5 us -> 16.4 us  [body(): lax.all_to_all(pair_sum, across, split_axis=2, concat_axis=2, tiled=True)]
    ppermute x4, waiting for transfers between devices: 0.58 us -> 2.49 us  [ring_pieces(): backward = lax.ppermute(backward, axis, behind)]
  transfers between devices with their start and end apart: 12 -> 12, of which waited for: 8 -> 8; matrix products, arithmetic and copies ran while one was open for 6% -> 5% of each run, Pallas kernels for 0% -> 0%
where the time goes in v13:
time: 171 us; the launch traced here: 169 us
  waiting for transfers between devices  71.2 us (42%)
  starting transfers between devices  37 us (22%)
  blocking collectives  21.5 us (13%)
  between operations  18.9 us (11%)
  matrix products  10.2 us (6%)
  other arithmetic  6.84 us (4%)
  local copies, waits for them, and re-layouts  3.46 us (2%)
    all_gather x1, waiting for transfers between devices, body(): gathered = lax.all_gather(packed, SEQ, axis=0, tiled=False)  50.2 us
    ppermute x6, waiting for transfers between devices, ring_pieces(): forward = lax.ppermute(forward, axis, ahead)  18.6 us
    ppermute x4, starting transfers between devices, ring_pieces(): backward = lax.ppermute(backward, axis, behind)  18.1 us
    all_to_all x1, blocking collectives, body(): lax.all_to_all(pair_sum, across, split_axis=2, concat_axis=2, tiled=True)  16.4 us
    ppermute x6, starting transfers between devices, ring_pieces(): forward = lax.ppermute(forward, axis, ahead)  14.8 us
    all_to_all x1, blocking collectives, body(): lax.all_to_all(blocks, pair, split_axis=3, concat_axis=3, tiled=True)  5.08 us
    ppermute x1, starting transfers between devices, from_behind(): lax.ppermute(value, axis, [(source, source + steps) for source in range(i...  4.02 us
    dot_general x1, matrix products, carried_terms(): jnp.einsum('vts,se->vte', weights, values_all, preferred_element_type=jnp...  3.73 us
  transfers between devices with their start and end apart: 12, of which 8 were waited for; matrix products, arithmetic and copies ran while one was open for 5% of the time, Pallas kernels for 0%

profile of v13, /device:TPU:1, one launch (start us, length us, event | category | flops | bytes accessed | tf_op | source)
XLA Modules:
  0.0 169.1 jit_solution(322384207057204312)
XLA Ops:
  6.5 0.7 convert_bitcast_fusion
  7.2 0.9 multiply_bitcast_fusion
  8.2 4.0 %collective-permute-start = (bf16[1,3,512]{2,1,0:T(4,128)(2,1)S(1)}, bf16[1,3,512]{2,1,0:T(4,128)(2,1)S(1)}, u32[]{:S(2)}, u32[]{:S(2)}) collective-permute-start(bf16[1,3,512]{2,1,0:T(4,128)(2,1)S(1)} %slice.105), channel_id=1, source_target_pairs={{0,16},{16,32},{32,48},{48,64},{64,80},{80,96},{96,112},{112,128},... | collective-permute-start | bytes 9224 | tf_op jit(solution)/shard_map/ppermute | solution.py:16
  12.2 1.3 convolution_convert_fusion
  13.5 0.9 fusion.92
  14.4 0.1 multiply_convert_fusion.2
  14.5 0.7 fusion.32
  15.3 0.2 reduce_window_sum.18
  15.6 0.6 slice.95
  21.3 0.7 fusion.91
  22.0 1.5 convolution_bitcast_fusion
  23.7 0.7 pad_maximum_fusion
  24.4 3.2 %collective-permute-start.1 = (bf16[512,128]{1,0:T(8,128)(2,1)}, bf16[512,128]{1,0:T(8,128)(2,1)S(1)}, u32[]{:S(2)}, u32[]{:S(2)}) collective-permute-start(bf16[512,128]{1,0:T(8,128)(2,1)} %param.19), channel_id=1, source_target_pairs={{0,16},{16,32},{32,48},{48,64},{64,80},{80,96},{96,112},{112,0},{1... | collective-permute-start | bytes 393224 | tf_op jit(solution)/shard_map/ppermute | solution.py:37
  27.6 3.9 %collective-permute-done.1 = bf16[512,128]{1,0:T(8,128)(2,1)S(1)} collective-permute-done((bf16[512,128]{1,0:T(8,128)(2,1)}, bf16[512,128]{1,0:T(8,128)(2,1)S(1)}, u32[]{:S(2)}, u32[]{:S(2)}) %collective-permute-start.1) | collective-permute-done | bytes 131104 | tf_op jit(solution)/shard_map/ppermute | solution.py:37
  31.5 2.0 %collective-permute-start.2 = (bf16[512,128]{1,0:T(8,128)(2,1)S(1)}, bf16[512,128]{1,0:T(8,128)(2,1)S(1)}, u32[]{:S(2)}, u32[]{:S(2)}) collective-permute-start(bf16[512,128]{1,0:T(8,128)(2,1)S(1)} %collective-permute-done.1), channel_id=1, source_target_pairs={{0,16},{16,32},{32,48},{48,64},{64,80},{80,96},{96,112},{112,0},{1... | collective-permute-start | bytes 393224 | tf_op jit(solution)/shard_map/ppermute | solution.py:37
  33.5 4.5 %collective-permute-start.5 = (bf16[512,128]{1,0:T(8,128)(2,1)}, bf16[512,128]{1,0:T(8,128)(2,1)S(1)}, u32[]{:S(2)}, u32[]{:S(2)}) collective-permute-start(bf16[512,128]{1,0:T(8,128)(2,1)} %param.19), channel_id=1, source_target_pairs={{0,112},{16,0},{32,16},{48,32},{64,48},{80,64},{96,80},{112,96},{1... | collective-permute-start | bytes 393224 | tf_op jit(solution)/shard_map/ppermute | solution.py:40
  38.0 0.4 collective-permute-done.2
  38.4 1.9 %collective-permute-start.3 = (bf16[512,128]{1,0:T(8,128)(2,1)S(1)}, bf16[512,128]{1,0:T(8,128)(2,1)S(1)}, u32[]{:S(2)}, u32[]{:S(2)}) collective-permute-start(bf16[512,128]{1,0:T(8,128)(2,1)S(1)} %collective-permute-done.2), channel_id=1, source_target_pairs={{0,16},{16,32},{32,48},{48,64},{64,80},{80,96},{96,112},{112,0},{1... | collective-permute-start | bytes 393224 | tf_op jit(solution)/shard_map/ppermute | solution.py:37
  40.3 4.8 %collective-permute-start.6 = (bf16[512,128]{1,0:T(8,128)(2,1)S(1)}, bf16[512,128]{1,0:T(8,128)(2,1)S(1)}, u32[]{:S(2)}, u32[]{:S(2)}) collective-permute-start(bf16[512,128]{1,0:T(8,128)(2,1)S(1)} %collective-permute-done.5), channel_id=1, source_target_pairs={{0,112},{16,0},{32,16},{48,32},{64,48},{80,64},{96,80},{112,96},{1... | collective-permute-start | bytes 393224 | tf_op jit(solution)/shard_map/ppermute | solution.py:40
  45.1 0.4 collective-permute-done.3
  45.5 1.9 %collective-permute-start.4 = (bf16[512,128]{1,0:T(8,128)(2,1)S(1)}, bf16[512,128]{1,0:T(8,128)(2,1)S(1)}, u32[]{:S(2)}, u32[]{:S(2)}) collective-permute-start(bf16[512,128]{1,0:T(8,128)(2,1)S(1)} %collective-permute-done.3), channel_id=1, source_target_pairs={{0,16},{16,32},{32,48},{48,64},{64,80},{80,96},{96,112},{112,0},{1... | collective-permute-start | bytes 393224 | tf_op jit(solution)/shard_map/ppermute | solution.py:37
  47.4 0.4 collective-permute-done.6
  47.9 5.0 %collective-permute-start.7 = (bf16[512,128]{1,0:T(8,128)(2,1)S(1)}, bf16[512,128]{1,0:T(8,128)(2,1)S(1)}, u32[]{:S(2)}, u32[]{:S(2)}) collective-permute-start(bf16[512,128]{1,0:T(8,128)(2,1)S(1)} %collective-permute-done.6), channel_id=1, source_target_pairs={{0,112},{16,0},{32,16},{48,32},{64,48},{80,64},{96,80},{112,96},{1... | collective-permute-start | bytes 393224 | tf_op jit(solution)/shard_map/ppermute | solution.py:40
  52.9 1.3 collective-permute-done.4
  54.4 2.1 %collective-permute-done.7 = bf16[512,128]{1,0:T(8,128)(2,1)S(1)} collective-permute-done((bf16[512,128]{1,0:T(8,128)(2,1)S(1)}, bf16[512,128]{1,0:T(8,128)(2,1)S(1)}, u32[]{:S(2)}, u32[]{:S(2)}) %collective-permute-start.7) | collective-permute-done | bytes 131104 | tf_op jit(solution)/shard_map/ppermute | solution.py:40
  56.5 2.7 %collective-permute-start.8 = (bf16[8,512,128]{2,1,0:T(8,128)(2,1)S(1)}, bf16[8,512,128]{2,1,0:T(8,128)(2,1)S(1)}, u32[]{:S(2)}, u32[]{:S(2)}) collective-permute-start(bf16[8,512,128]{2,1,0:T(8,128)(2,1)S(1)} %bitcast_dynamic-update-slice_fusion), channel_id=1, source_target_pairs={{0,128},{128,256},{256,384},{384,0},{1,129},{129,257},{257,385},{3... | collective-permute-start | bytes 3145736 | tf_op jit(solution)/shard_map/ppermute | solution.py:37
  59.2 3.8 %collective-permute-start.10 = (bf16[8,512,128]{2,1,0:T(8,128)(2,1)S(1)}, bf16[8,512,128]{2,1,0:T(8,128)(2,1)}, u32[]{:S(2)}, u32[]{:S(2)}) collective-permute-start(bf16[8,512,128]{2,1,0:T(8,128)(2,1)S(1)} %bitcast_dynamic-update-slice_fusion), channel_id=1, source_target_pairs={{0,384},{128,0},{256,128},{384,256},{1,385},{129,1},{257,129},{385... | collective-permute-start | bytes 3145736 | tf_op jit(solution)/shard_map/ppermute | solution.py:40
  63.0 12.5 %collective-permute-done.8 = bf16[8,512,128]{2,1,0:T(8,128)(2,1)S(1)} collective-permute-done((bf16[8,512,128]{2,1,0:T(8,128)(2,1)S(1)}, bf16[8,512,128]{2,1,0:T(8,128)(2,1)S(1)}, u32[]{:S(2)}, u32[]{:S(2)}) %collective-permute-start.8) | collective-permute-done | bytes 1048608 | tf_op jit(solution)/shard_map/ppermute | solution.py:37
  75.5 3.1 %collective-permute-start.9 = (bf16[8,512,128]{2,1,0:T(8,128)(2,1)S(1)}, bf16[8,512,128]{2,1,0:T(8,128)(2,1)}, u32[]{:S(2)}, u32[]{:S(2)}) collective-permute-start(bf16[8,512,128]{2,1,0:T(8,128)(2,1)S(1)} %collective-permute-done.8), channel_id=1, source_target_pairs={{0,128},{128,256},{256,384},{384,0},{1,129},{129,257},{257,385},{3... | collective-permute-start | bytes 3145736 | tf_op jit(solution)/shard_map/ppermute | solution.py:37
  78.7 50.2 %all-gather.3.cloned.1.call-done = bf16[4352,512]{1,0:T(8,128)(2,1)} async-done(((bf16[136,512]{1,0:T(8,128)(2,1)}), bf16[4352,512]{1,0:T(8,128)(2,1)}) %all-gather.3.cloned.1.call-update) | async-done | bytes 4456464 | tf_op jit(solution)/shard_map/all_gather | solution.py:129
  128.9 0.8 slice.115
  129.7 0.1 copy.37
  129.8 0.6 fusion.79
  130.4 0.1 copy.31
  130.6 0.8 subtract_reduce_fusion
  131.4 3.7 %fusion.26 = f32[64,512]{1,0:T(8,128)S(1)} fusion(bf16[32,136,512]{2,1,0:T(8,128)(2,1)} %bitcast.124, f32[64,32]{0,1:T(8,128)S(1)} %add_exponential_fusion, f32[1,64,1024]{2,1,0:T(8,128)S(1)} %convolution_bitcast_fusion), kind=kOutput, calls=%fused_computation.17 | convolution fusion | flops 268697600 | bytes 4407296 | tf_op jit(solution)/shard_map/vts,se->vte/dot_general | solution.py:77
  135.1 0.4 fusion.93
  135.6 0.2 multiply_reduce_fusion
  135.8 2.4 %fusion.23 = bf16[1,64,4,8,128]{4,1,3,2,0:T(8,128)(2,1)S(1)} fusion(bf16[1,8,512,128]{3,2,1,0:T(8,128)(2,1)} %bitcast.41, bf16[1,8,512,128]{3,2,1,0:T(8,128)(2,1)S(1)} %bitcast.115, bf16[1,8,512,128]{3,2,1,0:T(8,128)(2,1)S(1)} %bitcast.125, bf16[1,8,512,128]{3,2,1,0:T(8,128)(2,1)} %bitcast.38, f32[64,512]{1,0:T(8,128)S(1)} %get-tuple-element.26, ...), kind=kOutput, calls=%fused_computation.15 | convolution fusion | flops 285605888 | bytes 4852224 | tf_op jit(solution)/shard_map/vtr,derc->vtdec/dot_general | solution.py:137
  138.2 0.2 fusion.35
  138.5 0.2 fusion.34
  138.7 0.3 copy.32
  139.0 0.2 reshape_reshape.3
  139.2 0.2 copy.33
  139.4 5.1 %all_to_all.10 = bf16[1,64,4,2,512]{4,2,1,0,3:T(4,128)(2,1)S(1)} all-to-all(bf16[1,64,4,2,512]{4,2,1,0,3:T(4,128)(2,1)S(1)} %copy.33), channel_id=1, replica_groups=mesh['seq_0'=4,'seq_1'=8,'head_0'=4,'head_1'=2,'var'=2] {'head_1'}, dimensions={3} | all-to-all | bytes 1048576 | tf_op jit(solution)/shard_map/all_to_all | solution.py:146
  144.5 0.5 reduce_sum.53
  145.1 16.4 %all_to_all.11 = bf16[1,64,4,512]{3,1,0,2:T(8,128)(2,1)S(1)} all-to-all(bf16[1,64,4,512]{3,1,0,2:T(8,128)(2,1)S(1)} %copy.34), channel_id=1, replica_groups=mesh['seq_0'=4,'seq_1'=8,'head_0'=4,'head_1'=2,'var'=2] {'head_0'}, dimensions={2} | all-to-all | bytes 524288 | tf_op jit(solution)/shard_map/all_to_all | solution.py:148
  161.6 0.6 fusion.45
  (35 shorter events, 0.7 us)
Async XLA Ops:
  6.5 8.0 %copy-start = (bf16[1,2,512]{2,1,0:T(2,128)(2,1)S(1)}, bf16[1,2,512]{2,1,0:T(2,128)(2,1)}, u32[]{:S(2)}) copy-start(bf16[1,2,512]{2,1,0:T(2,128)(2,1)} %param.16) | copy-start | bytes 6148
  6.5 47.8 %copy-start.1 = (bf16[512,128]{1,0:T(8,128)(2,1)S(1)}, bf16[512,128]{1,0:T(8,128)(2,1)}, u32[]{:S(2)}) copy-start(bf16[512,128]{1,0:T(8,128)(2,1)} %param.19) | copy-start | bytes 393220
  6.5 122.3 %all-gather.3.cloned.1.call-start = ((), (), s32[]{:S(2)}) async-start(), calls=%async_computation.2 | async-start | bytes 4595712 | tf_op jit(solution)/shard_map/all_gather | solution.py:129
  8.2 6.2 %collective-permute-start = (bf16[1,3,512]{2,1,0:T(4,128)(2,1)S(1)}, bf16[1,3,512]{2,1,0:T(4,128)(2,1)S(1)}, u32[]{:S(2)}, u32[]{:S(2)}) collective-permute-start(bf16[1,3,512]{2,1,0:T(4,128)(2,1)S(1)} %slice.105), channel_id=1, source_target_pairs={{0,16},{16,32},{32,48},{48,64},{64,80},{80,96},{96,112},{112,128},... | collective-permute-start | bytes 9224 | tf_op jit(solution)/shard_map/ppermute | solution.py:16
  24.4 7.1 %collective-permute-start.1 = (bf16[512,128]{1,0:T(8,128)(2,1)}, bf16[512,128]{1,0:T(8,128)(2,1)S(1)}, u32[]{:S(2)}, u32[]{:S(2)}) collective-permute-start(bf16[512,128]{1,0:T(8,128)(2,1)} %param.19), channel_id=1, source_target_pairs={{0,16},{16,32},{32,48},{48,64},{64,80},{80,96},{96,112},{112,0},{1... | collective-permute-start | bytes 393224 | tf_op jit(solution)/shard_map/ppermute | solution.py:37
  31.5 6.9 %collective-permute-start.2 = (bf16[512,128]{1,0:T(8,128)(2,1)S(1)}, bf16[512,128]{1,0:T(8,128)(2,1)S(1)}, u32[]{:S(2)}, u32[]{:S(2)}) collective-permute-start(bf16[512,128]{1,0:T(8,128)(2,1)S(1)} %collective-permute-done.1), channel_id=1, source_target_pairs={{0,16},{16,32},{32,48},{48,64},{64,80},{80,96},{96,112},{112,0},{1... | collective-permute-start | bytes 393224 | tf_op jit(solution)/shard_map/ppermute | solution.py:37
  33.5 6.8 %collective-permute-start.5 = (bf16[512,128]{1,0:T(8,128)(2,1)}, bf16[512,128]{1,0:T(8,128)(2,1)S(1)}, u32[]{:S(2)}, u32[]{:S(2)}) collective-permute-start(bf16[512,128]{1,0:T(8,128)(2,1)} %param.19), channel_id=1, source_target_pairs={{0,112},{16,0},{32,16},{48,32},{64,48},{80,64},{96,80},{112,96},{1... | collective-permute-start | bytes 393224 | tf_op jit(solution)/shard_map/ppermute | solution.py:40
  38.4 7.1 %collective-permute-start.3 = (bf16[512,128]{1,0:T(8,128)(2,1)S(1)}, bf16[512,128]{1,0:T(8,128)(2,1)S(1)}, u32[]{:S(2)}, u32[]{:S(2)}) collective-permute-start(bf16[512,128]{1,0:T(8,128)(2,1)S(1)} %collective-permute-done.2), channel_id=1, source_target_pairs={{0,16},{16,32},{32,48},{48,64},{64,80},{80,96},{96,112},{112,0},{1... | collective-permute-start | bytes 393224 | tf_op jit(solution)/shard_map/ppermute | solution.py:37
  40.3 7.5 %collective-permute-start.6 = (bf16[512,128]{1,0:T(8,128)(2,1)S(1)}, bf16[512,128]{1,0:T(8,128)(2,1)S(1)}, u32[]{:S(2)}, u32[]{:S(2)}) collective-permute-start(bf16[512,128]{1,0:T(8,128)(2,1)S(1)} %collective-permute-done.5), channel_id=1, source_target_pairs={{0,112},{16,0},{32,16},{48,32},{64,48},{80,64},{96,80},{112,96},{1... | collective-permute-start | bytes 393224 | tf_op jit(solution)/shard_map/ppermute | solution.py:40
  45.5 8.7 %collective-permute-start.4 = (bf16[512,128]{1,0:T(8,128)(2,1)S(1)}, bf16[512,128]{1,0:T(8,128)(2,1)S(1)}, u32[]{:S(2)}, u32[]{:S(2)}) collective-permute-start(bf16[512,128]{1,0:T(8,128)(2,1)S(1)} %collective-permute-done.3), channel_id=1, source_target_pairs={{0,16},{16,32},{32,48},{48,64},{64,80},{80,96},{96,112},{112,0},{1... | collective-permute-start | bytes 393224 | tf_op jit(solution)/shard_map/ppermute | solution.py:37
  47.9 8.6 %collective-permute-start.7 = (bf16[512,128]{1,0:T(8,128)(2,1)S(1)}, bf16[512,128]{1,0:T(8,128)(2,1)S(1)}, u32[]{:S(2)}, u32[]{:S(2)}) collective-permute-start(bf16[512,128]{1,0:T(8,128)(2,1)S(1)} %collective-permute-done.6), channel_id=1, source_target_pairs={{0,112},{16,0},{32,16},{48,32},{64,48},{80,64},{96,80},{112,96},{1... | collective-permute-start | bytes 393224 | tf_op jit(solution)/shard_map/ppermute | solution.py:40
  54.3 81.5 %copy-start.3 = (f32[512]{0:T(512)S(1)}, f32[512]{0:T(512)}, u32[]{:S(2)}) copy-start(f32[512]{0:T(512)} %param.18) | copy-start | bytes 6148
  56.5 19.1 %collective-permute-start.8 = (bf16[8,512,128]{2,1,0:T(8,128)(2,1)S(1)}, bf16[8,512,128]{2,1,0:T(8,128)(2,1)S(1)}, u32[]{:S(2)}, u32[]{:S(2)}) collective-permute-start(bf16[8,512,128]{2,1,0:T(8,128)(2,1)S(1)} %bitcast_dynamic-update-slice_fusion), channel_id=1, source_target_pairs={{0,128},{128,256},{256,384},{384,0},{1,129},{129,257},{257,385},{3... | collective-permute-start | bytes 3145736 | tf_op jit(solution)/shard_map/ppermute | solution.py:37
  59.2 76.6 %collective-permute-start.10 = (bf16[8,512,128]{2,1,0:T(8,128)(2,1)S(1)}, bf16[8,512,128]{2,1,0:T(8,128)(2,1)}, u32[]{:S(2)}, u32[]{:S(2)}) collective-permute-start(bf16[8,512,128]{2,1,0:T(8,128)(2,1)S(1)} %bitcast_dynamic-update-slice_fusion), channel_id=1, source_target_pairs={{0,384},{128,0},{256,128},{384,256},{1,385},{129,1},{257,129},{385... | collective-permute-start | bytes 3145736 | tf_op jit(solution)/shard_map/ppermute | solution.py:40
  75.5 60.2 %collective-permute-start.9 = (bf16[8,512,128]{2,1,0:T(8,128)(2,1)S(1)}, bf16[8,512,128]{2,1,0:T(8,128)(2,1)}, u32[]{:S(2)}, u32[]{:S(2)}) collective-permute-start(bf16[8,512,128]{2,1,0:T(8,128)(2,1)S(1)} %collective-permute-done.8), channel_id=1, source_target_pairs={{0,128},{128,256},{256,384},{384,0},{1,129},{129,257},{257,385},{3... | collective-permute-start | bytes 3145736 | tf_op jit(solution)/shard_map/ppermute | solution.py:37
  138.2 23.3 %copy-start.2 = (bf16[64,512]{1,0:T(8,128)(2,1)S(1)}, bf16[64,512]{1,0:T(8,128)(2,1)}, u32[]{:S(2)}) copy-start(bf16[64,512]{1,0:T(8,128)(2,1)} %param.12) | copy-start | bytes 196612
Sparse Core Ops, SparseCore 0:
  24.5 104.3 all-gather.2

commit v14 on v13

--- a/solution.py
+++ b/solution.py
@@ -89,7 +89,9 @@
     down_weight,
 ):
     outer, inner_size = (lax.axis_size(SEQ[0]), lax.axis_size(SEQ[1]))
-    columns_all = ring_pieces(ring_pieces(down_weight, SEQ[1], inner_size), SEQ[0], outer)
+    columns_all = ring_pieces(ring_pieces(down_weight, SEQ[0], outer), SEQ[1], inner_size)
+    columns_all = jnp.roll(columns_all, lax.axis_index(SEQ[1]) - inner_size // 2, axis=0)
+    columns_all = jnp.roll(columns_all, lax.axis_index(SEQ[0]) - outer // 2, axis=1)
     kept_mask = (1 - erase).astype(jnp.bfloat16)
     erased = inner[None, :, :] * kept_mask[:, :, None]
     row_count = inner.shape[0]
@@ -135,11 +137,8 @@
     row_var = jnp.mean(centred * centred, axis=-1, keepdims=True)
     normed = (centred * lax.rsqrt(row_var + 1e-05) * norm_gain).astype(jnp.bfloat16)
     head_terms = jnp.einsum(
-        "vtr,derc->vtdec", normed, columns_all.reshape(outer, inner_size, head_size, -1),
-        preferred_element_type=jnp.float32,
+        "vtr,edrc->vtdec", normed, columns_all, preferred_element_type=jnp.float32
     ).astype(jnp.bfloat16)
-    head_terms = jnp.roll(head_terms, lax.axis_index(SEQ[0]) - outer // 2, axis=2)
-    head_terms = jnp.roll(head_terms, lax.axis_index(SEQ[1]) - inner_size // 2, axis=3)
     head_terms = head_terms.reshape(*normed.shape[:2], -1)
     pair, across = HEAD
     blocks = head_terms.reshape(*head_terms.shape[:2], lax.axis_size(across), lax.axis_size(pair), -1)

time: 171 us -> 170 us (level)
  the two profiles are of different devices: /device:TPU:1 before, /device:TPU:24 now
where the time goes in v14:
time: 170 us
  waiting for transfers between devices  58 us (34%)
  starting transfers between devices  38.2 us (22%)
  blocking collectives  27.7 us (16%)
  between operations  18.7 us (11%)
  matrix products  11.8 us (7%)
  other arithmetic  8.56 us (5%)
  local copies, waits for them, and re-layouts  6.68 us (4%)
    ppermute x6, waiting for transfers between devices, ring_pieces(): forward = lax.ppermute(forward, axis, ahead)  47.2 us
    ppermute x6, starting transfers between devices, ring_pieces(): forward = lax.ppermute(forward, axis, ahead)  24.1 us
    all_to_all x1, blocking collectives, body(): lax.all_to_all(pair_sum, across, split_axis=2, concat_axis=2, tiled=True)  23.6 us
    ppermute x4, waiting for transfers between devices, ring_pieces(): backward = lax.ppermute(backward, axis, behind)  10.6 us
    ppermute x4, starting transfers between devices, ring_pieces(): backward = lax.ppermute(backward, axis, behind)  9.41 us
    ppermute x1, starting transfers between devices, from_behind(): lax.ppermute(value, axis, [(source, source + steps) for source in range(i...  4.7 us
    all_to_all x1, blocking collectives, body(): lax.all_to_all(blocks, pair, split_axis=3, concat_axis=3, tiled=True)  4.15 us
    dot_general x1, matrix products, body(): jnp.einsum('vtr,edrc->vtdec', normed, columns_all, preferred_element_type...  4.1 us
  transfers between devices with their start and end apart: 12, of which 9 were waited for; matrix products, arithmetic and copies ran while one was open for 5% of the time, Pallas kernels for 0%

profile of v14, /device:TPU:24, one launch (start us, length us, event | category | flops | bytes accessed | tf_op | source)
XLA Modules:
  0.0 169.7 jit_solution(3462607861276383051)
XLA Ops:
  6.5 0.7 convert_bitcast_fusion
  7.2 0.9 multiply_bitcast_fusion
  8.2 4.7 %collective-permute-start.10 = (bf16[1,3,512]{2,1,0:T(4,128)(2,1)S(1)}, bf16[1,3,512]{2,1,0:T(4,128)(2,1)S(1)}, u32[]{:S(2)}, u32[]{:S(2)}) collective-permute-start(bf16[1,3,512]{2,1,0:T(4,128)(2,1)S(1)} %slice.105), channel_id=1, source_target_pairs={{0,16},{16,32},{32,48},{48,64},{64,80},{80,96},{96,112},{112,128},... | collective-permute-start | bytes 9224 | tf_op jit(solution)/shard_map/ppermute | solution.py:16
  12.9 1.3 convolution_convert_fusion
  14.2 0.9 fusion.86
  15.1 0.1 multiply_convert_fusion.2
  15.2 0.7 fusion.27
  16.0 0.2 reduce_window_sum.18
  16.3 0.7 slice.95
  21.8 0.7 fusion.85
  22.5 1.5 convolution_bitcast_fusion
  24.2 0.7 pad_maximum_fusion.1
  24.9 3.4 %collective-permute-start = (bf16[512,128]{1,0:T(8,128)(2,1)}, bf16[512,128]{1,0:T(8,128)(2,1)S(1)}, u32[]{:S(2)}, u32[]{:S(2)}) collective-permute-start(bf16[512,128]{1,0:T(8,128)(2,1)} %param.19), channel_id=1, source_target_pairs={{0,128},{128,256},{256,384},{384,0},{1,129},{129,257},{257,385},{3... | collective-permute-start | bytes 393224 | tf_op jit(solution)/shard_map/ppermute | solution.py:37
  28.3 3.7 %collective-permute-start.2 = (bf16[512,128]{1,0:T(8,128)(2,1)}, bf16[512,128]{1,0:T(8,128)(2,1)S(1)}, u32[]{:S(2)}, u32[]{:S(2)}) collective-permute-start(bf16[512,128]{1,0:T(8,128)(2,1)} %param.19), channel_id=1, source_target_pairs={{0,384},{128,0},{256,128},{384,256},{1,385},{129,1},{257,129},{385... | collective-permute-start | bytes 393224 | tf_op jit(solution)/shard_map/ppermute | solution.py:40
  31.9 1.2 collective-permute-done
  33.1 2.2 %collective-permute-start.1 = (bf16[512,128]{1,0:T(8,128)(2,1)S(1)}, bf16[512,128]{1,0:T(8,128)(2,1)S(1)}, u32[]{:S(2)}, u32[]{:S(2)}) collective-permute-start(bf16[512,128]{1,0:T(8,128)(2,1)S(1)} %collective-permute-done), channel_id=1, source_target_pairs={{0,128},{128,256},{256,384},{384,0},{1,129},{129,257},{257,385},{3... | collective-permute-start | bytes 393224 | tf_op jit(solution)/shard_map/ppermute | solution.py:37
  35.4 5.9 %collective-permute-done.1 = bf16[512,128]{1,0:T(8,128)(2,1)S(1)} collective-permute-done((bf16[512,128]{1,0:T(8,128)(2,1)S(1)}, bf16[512,128]{1,0:T(8,128)(2,1)S(1)}, u32[]{:S(2)}, u32[]{:S(2)}) %collective-permute-start.1) | collective-permute-done | bytes 131104 | tf_op jit(solution)/shard_map/ppermute | solution.py:37
  41.2 1.0 pad_maximum_fusion
  42.2 4.5 %collective-permute-start.3 = (bf16[4,512,128]{2,1,0:T(8,128)(2,1)S(1)}, bf16[4,512,128]{2,1,0:T(8,128)(2,1)S(1)}, u32[]{:S(2)}, u32[]{:S(2)}) collective-permute-start(bf16[4,512,128]{2,1,0:T(8,128)(2,1)S(1)} %pad_maximum_fusion), channel_id=1, source_target_pairs={{0,16},{16,32},{32,48},{48,64},{64,80},{80,96},{96,112},{112,0},{1... | collective-permute-start | bytes 1572872 | tf_op jit(solution)/shard_map/ppermute | solution.py:37
  46.7 11.2 %collective-permute-done.3 = bf16[4,512,128]{2,1,0:T(8,128)(2,1)S(1)} collective-permute-done((bf16[4,512,128]{2,1,0:T(8,128)(2,1)S(1)}, bf16[4,512,128]{2,1,0:T(8,128)(2,1)S(1)}, u32[]{:S(2)}, u32[]{:S(2)}) %collective-permute-start.3) | collective-permute-done | bytes 524320 | tf_op jit(solution)/shard_map/ppermute | solution.py:37
  57.9 4.9 %collective-permute-start.4 = (bf16[4,512,128]{2,1,0:T(8,128)(2,1)S(1)}, bf16[4,512,128]{2,1,0:T(8,128)(2,1)S(1)}, u32[]{:S(2)}, u32[]{:S(2)}) collective-permute-start(bf16[4,512,128]{2,1,0:T(8,128)(2,1)S(1)} %collective-permute-done.3), channel_id=1, source_target_pairs={{0,16},{16,32},{32,48},{48,64},{64,80},{80,96},{96,112},{112,0},{1... | collective-permute-start | bytes 1572872 | tf_op jit(solution)/shard_map/ppermute | solution.py:37
  62.8 1.9 %collective-permute-start.7 = (bf16[4,512,128]{2,1,0:T(8,128)(2,1)S(1)}, bf16[4,512,128]{2,1,0:T(8,128)(2,1)S(1)}, u32[]{:S(2)}, u32[]{:S(2)}) collective-permute-start(bf16[4,512,128]{2,1,0:T(8,128)(2,1)S(1)} %pad_maximum_fusion), channel_id=1, source_target_pairs={{0,112},{16,0},{32,16},{48,32},{64,48},{80,64},{96,80},{112,96},{1... | collective-permute-start | bytes 1572872 | tf_op jit(solution)/shard_map/ppermute | solution.py:40
  64.8 7.6 %collective-permute-done.4 = bf16[4,512,128]{2,1,0:T(8,128)(2,1)S(1)} collective-permute-done((bf16[4,512,128]{2,1,0:T(8,128)(2,1)S(1)}, bf16[4,512,128]{2,1,0:T(8,128)(2,1)S(1)}, u32[]{:S(2)}, u32[]{:S(2)}) %collective-permute-start.4) | collective-permute-done | bytes 524320 | tf_op jit(solution)/shard_map/ppermute | solution.py:37
  72.4 4.6 %collective-permute-start.5 = (bf16[4,512,128]{2,1,0:T(8,128)(2,1)S(1)}, bf16[4,512,128]{2,1,0:T(8,128)(2,1)S(1)}, u32[]{:S(2)}, u32[]{:S(2)}) collective-permute-start(bf16[4,512,128]{2,1,0:T(8,128)(2,1)S(1)} %collective-permute-done.4), channel_id=1, source_target_pairs={{0,16},{16,32},{32,48},{48,64},{64,80},{80,96},{96,112},{112,0},{1... | collective-permute-start | bytes 1572872 | tf_op jit(solution)/shard_map/ppermute | solution.py:37
  77.0 1.9 %collective-permute-start.8 = (bf16[4,512,128]{2,1,0:T(8,128)(2,1)S(1)}, bf16[4,512,128]{2,1,0:T(8,128)(2,1)S(1)}, u32[]{:S(2)}, u32[]{:S(2)}) collective-permute-start(bf16[4,512,128]{2,1,0:T(8,128)(2,1)S(1)} %collective-permute-done.7), channel_id=1, source_target_pairs={{0,112},{16,0},{32,16},{48,32},{64,48},{80,64},{96,80},{112,96},{1... | collective-permute-start | bytes 1572872 | tf_op jit(solution)/shard_map/ppermute | solution.py:40
  78.9 5.9 %collective-permute-done.5 = bf16[4,512,128]{2,1,0:T(8,128)(2,1)S(1)} collective-permute-done((bf16[4,512,128]{2,1,0:T(8,128)(2,1)S(1)}, bf16[4,512,128]{2,1,0:T(8,128)(2,1)S(1)}, u32[]{:S(2)}, u32[]{:S(2)}) %collective-permute-start.5) | collective-permute-done | bytes 524320 | tf_op jit(solution)/shard_map/ppermute | solution.py:37
  84.8 4.6 %collective-permute-start.6 = (bf16[4,512,128]{2,1,0:T(8,128)(2,1)S(1)}, bf16[4,512,128]{2,1,0:T(8,128)(2,1)S(1)}, u32[]{:S(2)}, u32[]{:S(2)}) collective-permute-start(bf16[4,512,128]{2,1,0:T(8,128)(2,1)S(1)} %collective-permute-done.5), channel_id=1, source_target_pairs={{0,16},{16,32},{32,48},{48,64},{64,80},{80,96},{96,112},{112,0},{1... | collective-permute-start | bytes 1572872 | tf_op jit(solution)/shard_map/ppermute | solution.py:37
  89.5 3.7 %collective-permute-done.8 = bf16[4,512,128]{2,1,0:T(8,128)(2,1)S(1)} collective-permute-done((bf16[4,512,128]{2,1,0:T(8,128)(2,1)S(1)}, bf16[4,512,128]{2,1,0:T(8,128)(2,1)S(1)}, u32[]{:S(2)}, u32[]{:S(2)}) %collective-permute-start.8) | collective-permute-done | bytes 524320 | tf_op jit(solution)/shard_map/ppermute | solution.py:40
  93.2 1.9 %collective-permute-start.9 = (bf16[4,512,128]{2,1,0:T(8,128)(2,1)S(1)}, bf16[4,512,128]{2,1,0:T(8,128)(2,1)S(1)}, u32[]{:S(2)}, u32[]{:S(2)}) collective-permute-start(bf16[4,512,128]{2,1,0:T(8,128)(2,1)S(1)} %collective-permute-done.8), channel_id=1, source_target_pairs={{0,112},{16,0},{32,16},{48,32},{64,48},{80,64},{96,80},{112,96},{1... | collective-permute-start | bytes 1572872 | tf_op jit(solution)/shard_map/ppermute | solution.py:40
  95.1 15.4 %collective-permute-done.6 = bf16[4,512,128]{2,1,0:T(8,128)(2,1)S(1)} collective-permute-done((bf16[4,512,128]{2,1,0:T(8,128)(2,1)S(1)}, bf16[4,512,128]{2,1,0:T(8,128)(2,1)S(1)}, u32[]{:S(2)}, u32[]{:S(2)}) %collective-permute-start.6) | collective-permute-done | bytes 524320 | tf_op jit(solution)/shard_map/ppermute | solution.py:37
  110.8 1.1 bitcast_dynamic-update-slice_fusion.6
  112.1 6.9 %collective-permute-done.9 = bf16[4,512,128]{2,1,0:T(8,128)(2,1)S(1)} collective-permute-done((bf16[4,512,128]{2,1,0:T(8,128)(2,1)S(1)}, bf16[4,512,128]{2,1,0:T(8,128)(2,1)S(1)}, u32[]{:S(2)}, u32[]{:S(2)}) %collective-permute-start.9) | collective-permute-done | bytes 524320 | tf_op jit(solution)/shard_map/ppermute | solution.py:40
  119.7 2.3 %constant_dynamic-slice_fusion = bf16[8,4,512,128]{3,2,1,0:T(8,128)(2,1)} fusion(bf16[16,4,512,128]{3,2,1,0:T(8,128)(2,1)S(1)} %bitcast_dynamic-update-slice_fusion.1, s32[]{:T(128)S(6)} %select_n.53), kind=kLoop, calls=%fused_computation.100 | loop fusion | bytes 8388612 | tf_op jit(solution)/shard_map/jit(_roll_dynamic)/dynamic_slice | solution.py:93
  122.0 0.2 all-gather.3.cloned.1.call-done
  122.1 0.8 slice.115
  123.1 0.6 fusion.73
  123.9 0.7 subtract_reduce_fusion
  124.6 3.7 %fusion.21 = f32[64,512]{1,0:T(8,128)S(1)} fusion(bf16[32,136,512]{2,1,0:T(8,128)(2,1)} %bitcast.145, f32[64,32]{0,1:T(8,128)S(1)} %add_exponential_fusion, f32[1,64,1024]{2,1,0:T(8,128)S(1)} %convolution_bitcast_fusion), kind=kOutput, calls=%fused_computation.13 | convolution fusion | flops 268697600 | bytes 4407296 | tf_op jit(solution)/shard_map/vts,se->vte/dot_general | solution.py:77
  128.3 0.4 fusion.87
  128.8 0.2 multiply_reduce_fusion
  129.0 4.1 %fusion.18 = bf16[1,64,4,8,128]{4,1,2,3,0:T(8,128)(2,1)S(1)} fusion(s32[]{:T(128)S(6)} %select_n.55, bf16[8,4,512,128]{3,2,1,0:T(8,128)(2,1)} %constant_dynamic-slice_fusion, f32[64,512]{1,0:T(8,128)S(1)} %get-tuple-element.26, f32[512]{0:T(512)S(1)} %copy-done.11, f32[64]{0:T(128)S(1)} %add_rsqrt_fusion, f32[64]{0:T(128)S(1)} %broadcast_multiply_fusion), kind=kOutput, calls=%fused_computation.11 | convolution fusion | flops 277217280 | bytes 4852228 | tf_op jit(solution)/shard_map/vtr,edrc->vtdec/dot_general | solution.py:139
  133.1 0.3 copy.32
  133.4 0.2 reshape_reshape.3
  133.6 0.2 copy.33
  133.8 4.2 %all_to_all.10 = bf16[1,64,4,2,512]{4,2,1,0,3:T(4,128)(2,1)S(1)} all-to-all(bf16[1,64,4,2,512]{4,2,1,0,3:T(4,128)(2,1)S(1)} %copy.33), channel_id=1, replica_groups=mesh['seq_0'=4,'seq_1'=8,'head_0'=4,'head_1'=2,'var'=2] {'head_1'}, dimensions={3} | all-to-all | bytes 1048576 | tf_op jit(solution)/shard_map/all_to_all | solution.py:145
  138.0 0.5 reduce_sum.53
  138.6 23.6 %all_to_all.11 = bf16[1,64,4,512]{3,1,0,2:T(8,128)(2,1)S(1)} all-to-all(bf16[1,64,4,512]{3,1,0,2:T(8,128)(2,1)S(1)} %copy.34), channel_id=1, replica_groups=mesh['seq_0'=4,'seq_1'=8,'head_0'=4,'head_1'=2,'var'=2] {'head_0'}, dimensions={2} | all-to-all | bytes 524288 | tf_op jit(solution)/shard_map/all_to_all | solution.py:147
  162.2 0.6 fusion.38
  (59 shorter events, 1.8 us)
Async XLA Ops:
  6.5 8.7 %copy-start = (bf16[1,2,512]{2,1,0:T(2,128)(2,1)S(1)}, bf16[1,2,512]{2,1,0:T(2,128)(2,1)}, u32[]{:S(2)}) copy-start(bf16[1,2,512]{2,1,0:T(2,128)(2,1)} %param.16) | copy-start | bytes 6148
  6.5 104.2 %copy-start.1 = (bf16[512,128]{1,0:T(8,128)(2,1)S(1)}, bf16[512,128]{1,0:T(8,128)(2,1)}, u32[]{:S(2)}) copy-start(bf16[512,128]{1,0:T(8,128)(2,1)} %param.19) | copy-start | bytes 393220
  6.5 115.6 %all-gather.3.cloned.1.call-start = ((), (), s32[]{:S(2)}) async-start(), calls=%async_computation.2 | async-start | bytes 4595712 | tf_op jit(solution)/shard_map/all_gather | solution.py:131
  8.2 6.9 %collective-permute-start.10 = (bf16[1,3,512]{2,1,0:T(4,128)(2,1)S(1)}, bf16[1,3,512]{2,1,0:T(4,128)(2,1)S(1)}, u32[]{:S(2)}, u32[]{:S(2)}) collective-permute-start(bf16[1,3,512]{2,1,0:T(4,128)(2,1)S(1)} %slice.105), channel_id=1, source_target_pairs={{0,16},{16,32},{32,48},{48,64},{64,80},{80,96},{96,112},{112,128},... | collective-permute-start | bytes 9224 | tf_op jit(solution)/shard_map/ppermute | solution.py:16
  14.2 27.0 %copy-start.8 = (bf16[64,512]{1,0:T(8,128)(2,1)}, bf16[64,512]{1,0:T(8,128)(2,1)S(1)}, u32[]{:S(2)}) copy-start(bf16[64,512]{1,0:T(8,128)(2,1)S(1)} %convolution_convert_fusion) | copy-start | bytes 196612
  24.9 8.3 %collective-permute-start = (bf16[512,128]{1,0:T(8,128)(2,1)}, bf16[512,128]{1,0:T(8,128)(2,1)S(1)}, u32[]{:S(2)}, u32[]{:S(2)}) collective-permute-start(bf16[512,128]{1,0:T(8,128)(2,1)} %param.19), channel_id=1, source_target_pairs={{0,128},{128,256},{256,384},{384,0},{1,129},{129,257},{257,385},{3... | collective-permute-start | bytes 393224 | tf_op jit(solution)/shard_map/ppermute | solution.py:37
  28.3 7.1 %collective-permute-start.2 = (bf16[512,128]{1,0:T(8,128)(2,1)}, bf16[512,128]{1,0:T(8,128)(2,1)S(1)}, u32[]{:S(2)}, u32[]{:S(2)}) collective-permute-start(bf16[512,128]{1,0:T(8,128)(2,1)} %param.19), channel_id=1, source_target_pairs={{0,384},{128,0},{256,128},{384,256},{1,385},{129,1},{257,129},{385... | collective-permute-start | bytes 393224 | tf_op jit(solution)/shard_map/ppermute | solution.py:40
  33.1 51.6 %copy-start.2 = (bf16[512,128]{1,0:T(8,128)(2,1)}, bf16[512,128]{1,0:T(8,128)(2,1)S(1)}, u32[]{:S(2)}) copy-start(bf16[512,128]{1,0:T(8,128)(2,1)S(1)} %collective-permute-done) | copy-start | bytes 393220
  33.1 8.1 %collective-permute-start.1 = (bf16[512,128]{1,0:T(8,128)(2,1)S(1)}, bf16[512,128]{1,0:T(8,128)(2,1)S(1)}, u32[]{:S(2)}, u32[]{:S(2)}) collective-permute-start(bf16[512,128]{1,0:T(8,128)(2,1)S(1)} %collective-permute-done), channel_id=1, source_target_pairs={{0,128},{128,256},{256,384},{384,0},{1,129},{129,257},{257,385},{3... | collective-permute-start | bytes 393224 | tf_op jit(solution)/shard_map/ppermute | solution.py:37
  35.3 54.0 %copy-start.4 = (bf16[512,128]{1,0:T(8,128)(2,1)}, bf16[512,128]{1,0:T(8,128)(2,1)S(1)}, u32[]{:S(2)}) copy-start(bf16[512,128]{1,0:T(8,128)(2,1)S(1)} %collective-permute-done.2) | copy-start | bytes 393220
  41.2 48.2 %copy-start.6 = (bf16[512,128]{1,0:T(8,128)(2,1)}, bf16[512,128]{1,0:T(8,128)(2,1)S(1)}, u32[]{:S(2)}) copy-start(bf16[512,128]{1,0:T(8,128)(2,1)S(1)} %collective-permute-done.1) | copy-start | bytes 393220
  42.2 15.7 %collective-permute-start.3 = (bf16[4,512,128]{2,1,0:T(8,128)(2,1)S(1)}, bf16[4,512,128]{2,1,0:T(8,128)(2,1)S(1)}, u32[]{:S(2)}, u32[]{:S(2)}) collective-permute-start(bf16[4,512,128]{2,1,0:T(8,128)(2,1)S(1)} %pad_maximum_fusion), channel_id=1, source_target_pairs={{0,16},{16,32},{32,48},{48,64},{64,80},{80,96},{96,112},{112,0},{1... | collective-permute-start | bytes 1572872 | tf_op jit(solution)/shard_map/ppermute | solution.py:37
  57.9 14.5 %collective-permute-start.4 = (bf16[4,512,128]{2,1,0:T(8,128)(2,1)S(1)}, bf16[4,512,128]{2,1,0:T(8,128)(2,1)S(1)}, u32[]{:S(2)}, u32[]{:S(2)}) collective-permute-start(bf16[4,512,128]{2,1,0:T(8,128)(2,1)S(1)} %collective-permute-done.3), channel_id=1, source_target_pairs={{0,16},{16,32},{32,48},{48,64},{64,80},{80,96},{96,112},{112,0},{1... | collective-permute-start | bytes 1572872 | tf_op jit(solution)/shard_map/ppermute | solution.py:37
  62.8 14.1 %collective-permute-start.7 = (bf16[4,512,128]{2,1,0:T(8,128)(2,1)S(1)}, bf16[4,512,128]{2,1,0:T(8,128)(2,1)S(1)}, u32[]{:S(2)}, u32[]{:S(2)}) collective-permute-start(bf16[4,512,128]{2,1,0:T(8,128)(2,1)S(1)} %pad_maximum_fusion), channel_id=1, source_target_pairs={{0,112},{16,0},{32,16},{48,32},{64,48},{80,64},{96,80},{112,96},{1... | collective-permute-start | bytes 1572872 | tf_op jit(solution)/shard_map/ppermute | solution.py:40
  72.4 12.4 %collective-permute-start.5 = (bf16[4,512,128]{2,1,0:T(8,128)(2,1)S(1)}, bf16[4,512,128]{2,1,0:T(8,128)(2,1)S(1)}, u32[]{:S(2)}, u32[]{:S(2)}) collective-permute-start(bf16[4,512,128]{2,1,0:T(8,128)(2,1)S(1)} %collective-permute-done.4), channel_id=1, source_target_pairs={{0,16},{16,32},{32,48},{48,64},{64,80},{80,96},{96,112},{112,0},{1... | collective-permute-start | bytes 1572872 | tf_op jit(solution)/shard_map/ppermute | solution.py:37
  77.0 16.2 %collective-permute-start.8 = (bf16[4,512,128]{2,1,0:T(8,128)(2,1)S(1)}, bf16[4,512,128]{2,1,0:T(8,128)(2,1)S(1)}, u32[]{:S(2)}, u32[]{:S(2)}) collective-permute-start(bf16[4,512,128]{2,1,0:T(8,128)(2,1)S(1)} %collective-permute-done.7), channel_id=1, source_target_pairs={{0,112},{16,0},{32,16},{48,32},{64,48},{80,64},{96,80},{112,96},{1... | collective-permute-start | bytes 1572872 | tf_op jit(solution)/shard_map/ppermute | solution.py:40
  84.8 25.7 %collective-permute-start.6 = (bf16[4,512,128]{2,1,0:T(8,128)(2,1)S(1)}, bf16[4,512,128]{2,1,0:T(8,128)(2,1)S(1)}, u32[]{:S(2)}, u32[]{:S(2)}) collective-permute-start(bf16[4,512,128]{2,1,0:T(8,128)(2,1)S(1)} %collective-permute-done.5), channel_id=1, source_target_pairs={{0,16},{16,32},{32,48},{48,64},{64,80},{80,96},{96,112},{112,0},{1... | collective-permute-start | bytes 1572872 | tf_op jit(solution)/shard_map/ppermute | solution.py:37
  89.4 29.9 %copy-start.3 = (bf16[512,128]{1,0:T(8,128)(2,1)S(1)}, bf16[512,128]{1,0:T(8,128)(2,1)}, u32[]{:S(2)}) copy-start(bf16[512,128]{1,0:T(8,128)(2,1)} %copy-done.2) | copy-start | bytes 393220
  89.4 29.9 %copy-start.5 = (bf16[512,128]{1,0:T(8,128)(2,1)S(1)}, bf16[512,128]{1,0:T(8,128)(2,1)}, u32[]{:S(2)}) copy-start(bf16[512,128]{1,0:T(8,128)(2,1)} %copy-done.4) | copy-start | bytes 393220
  89.4 29.9 %copy-start.7 = (bf16[512,128]{1,0:T(8,128)(2,1)S(1)}, bf16[512,128]{1,0:T(8,128)(2,1)}, u32[]{:S(2)}) copy-start(bf16[512,128]{1,0:T(8,128)(2,1)} %copy-done.6) | copy-start | bytes 393220
  93.2 25.8 %collective-permute-start.9 = (bf16[4,512,128]{2,1,0:T(8,128)(2,1)S(1)}, bf16[4,512,128]{2,1,0:T(8,128)(2,1)S(1)}, u32[]{:S(2)}, u32[]{:S(2)}) collective-permute-start(bf16[4,512,128]{2,1,0:T(8,128)(2,1)S(1)} %collective-permute-done.8), channel_id=1, source_target_pairs={{0,112},{16,0},{32,16},{48,32},{64,48},{80,64},{96,80},{112,96},{1... | collective-permute-start | bytes 1572872 | tf_op jit(solution)/shard_map/ppermute | solution.py:40
  119.5 8.8 %copy-start.9 = (bf16[64,512]{1,0:T(8,128)(2,1)S(1)}, bf16[64,512]{1,0:T(8,128)(2,1)}, u32[]{:S(2)}) copy-start(bf16[64,512]{1,0:T(8,128)(2,1)} %copy-done.8) | copy-start | bytes 196612
  119.6 9.4 %copy-start.11 = (f32[512]{0:T(512)S(1)}, f32[512]{0:T(512)}, u32[]{:S(2)}) copy-start(f32[512]{0:T(512)} %param.18) | copy-start | bytes 6148
  129.0 33.2 %copy-start.10 = (bf16[64,512]{1,0:T(8,128)(2,1)S(1)}, bf16[64,512]{1,0:T(8,128)(2,1)}, u32[]{:S(2)}) copy-start(bf16[64,512]{1,0:T(8,128)(2,1)} %param.12) | copy-start | bytes 196612
Sparse Core Ops, SparseCore 0:
  25.0 97.1 all-gather.2

commit v15 on v12

--- a/solution.py
+++ b/solution.py
@@ -66,10 +66,10 @@
     values_all = gathered[:, token_count : 2 * token_count, :].reshape(blocks * token_count, head_size)
     parts = gathered[:, 2 * token_count, :3].astype(jnp.float32)
     decay = (parts[:, 0] + parts[:, 1]) + parts[:, 2]
-    through = jnp.cumsum(decay)
-    before_own = jnp.sum(jnp.where(jnp.arange(blocks) < block, decay, 0.0))
-    earlier = jnp.arange(blocks) < block
-    block_exponent = jnp.where(earlier, before_own - through, -jnp.inf)
+    index = jnp.arange(blocks)
+    between = (index[:, None] < index[None, :]) & (index[None, :] < block)
+    before_own = jnp.sum(jnp.where(index < block, decay, 0.0))
+    block_exponent = jnp.where(index < block, jnp.sum(jnp.where(between, decay[None, :], 0.0), axis=1), -jnp.inf)
     scale = jnp.exp(cumulated[:, :, None] + block_exponent[None, None, :])
     scores = jnp.einsum("vtd,sd->vts", queries, keys_all, preferred_element_type=jnp.float32)
     scores = scores.reshape(*cumulated.shape, blocks, token_count) * scale[..., None]

time: 169 us -> 168 us (level)
  no operation moved by 1% of the time
where the time goes in v15:
time: 168 us; the launch traced here: 166 us
  waiting for transfers between devices  57.6 us (34%)
  starting transfers between devices  35.4 us (21%)
  blocking collectives  27.2 us (16%)
  between operations  18.7 us (11%)
  matrix products  10.8 us (6%)
  local copies, waits for them, and re-layouts  9.19 us (5%)
  other arithmetic  7.37 us (4%)
    ppermute x6, waiting for transfers between devices, ring_pieces(): forward = lax.ppermute(forward, axis, ahead)  43 us
    all_to_all x1, blocking collectives, body(): lax.all_to_all(pair_sum, across, split_axis=2, concat_axis=2, tiled=True)  20.2 us
    ppermute x6, starting transfers between devices, ring_pieces(): forward = lax.ppermute(forward, axis, ahead)  19.2 us
    all_gather x1, waiting for transfers between devices, body(): gathered = lax.all_gather(packed, SEQ, axis=0, tiled=False)  14.2 us
    ppermute x4, starting transfers between devices, ring_pieces(): backward = lax.ppermute(backward, axis, behind)  12.2 us
    all_to_all x1, blocking collectives, body(): lax.all_to_all(blocks, pair, split_axis=3, concat_axis=3, tiled=True)  6.98 us
    unnamed x32, local copies, waits for them, and re-layouts  5.14 us
    ppermute x1, starting transfers between devices, from_behind(): lax.ppermute(value, axis, [(source, source + steps) for source in range(i...  4.02 us
  transfers between devices with their start and end apart: 12, of which 8 were waited for; matrix products, arithmetic and copies ran while one was open for 6% of the time, Pallas kernels for 0%

profile of v15, /device:TPU:1, one launch (start us, length us, event | category | flops | bytes accessed | tf_op | source)
XLA Modules:
  0.0 166.2 jit_solution(18085372864335441454)
XLA Ops:
  6.5 0.7 convert_bitcast_fusion
  7.2 0.9 multiply_bitcast_fusion
  8.1 4.0 %collective-permute-start = (bf16[1,3,512]{2,1,0:T(4,128)(2,1)S(1)}, bf16[1,3,512]{2,1,0:T(4,128)(2,1)S(1)}, u32[]{:S(2)}, u32[]{:S(2)}) collective-permute-start(bf16[1,3,512]{2,1,0:T(4,128)(2,1)S(1)} %slice.105), channel_id=1, source_target_pairs={{0,16},{16,32},{32,48},{48,64},{64,80},{80,96},{96,112},{112,128},... | collective-permute-start | bytes 9224 | tf_op jit(solution)/shard_map/ppermute | solution.py:16
  12.2 1.3 convolution_convert_fusion.1
  13.5 0.9 fusion.79
  14.5 0.7 fusion.19
  15.3 0.2 reduce_window_sum.11
  15.6 0.7 slice.95
  21.1 0.6 fusion.78
  21.8 1.5 convolution_bitcast_fusion
  23.5 0.7 pad_maximum_fusion.1
  24.2 4.1 %collective-permute-start.1 = (bf16[512,128]{1,0:T(8,128)(2,1)}, bf16[512,128]{1,0:T(8,128)(2,1)S(1)}, u32[]{:S(2)}, u32[]{:S(2)}) collective-permute-start(bf16[512,128]{1,0:T(8,128)(2,1)} %param.19), channel_id=1, source_target_pairs={{0,128},{128,256},{256,384},{384,0},{1,129},{129,257},{257,385},{3... | collective-permute-start | bytes 393224 | tf_op jit(solution)/shard_map/ppermute | solution.py:37
  28.3 3.2 %collective-permute-start.3 = (bf16[512,128]{1,0:T(8,128)(2,1)}, bf16[512,128]{1,0:T(8,128)(2,1)S(1)}, u32[]{:S(2)}, u32[]{:S(2)}) collective-permute-start(bf16[512,128]{1,0:T(8,128)(2,1)} %param.19), channel_id=1, source_target_pairs={{0,384},{128,0},{256,128},{384,256},{1,385},{129,1},{257,129},{385... | collective-permute-start | bytes 393224 | tf_op jit(solution)/shard_map/ppermute | solution.py:40
  31.5 0.6 collective-permute-done.1
  32.1 2.1 %collective-permute-start.2 = (bf16[512,128]{1,0:T(8,128)(2,1)S(1)}, bf16[512,128]{1,0:T(8,128)(2,1)S(1)}, u32[]{:S(2)}, u32[]{:S(2)}) collective-permute-start(bf16[512,128]{1,0:T(8,128)(2,1)S(1)} %collective-permute-done.1), channel_id=1, source_target_pairs={{0,128},{128,256},{256,384},{384,0},{1,129},{129,257},{257,385},{3... | collective-permute-start | bytes 393224 | tf_op jit(solution)/shard_map/ppermute | solution.py:37
  34.2 4.8 %collective-permute-done.2 = bf16[512,128]{1,0:T(8,128)(2,1)S(1)} collective-permute-done((bf16[512,128]{1,0:T(8,128)(2,1)S(1)}, bf16[512,128]{1,0:T(8,128)(2,1)S(1)}, u32[]{:S(2)}, u32[]{:S(2)}) %collective-permute-start.2) | collective-permute-done | bytes 131104 | tf_op jit(solution)/shard_map/ppermute | solution.py:37
  39.0 1.0 pad_maximum_fusion
  40.1 2.4 %collective-permute-start.4 = (bf16[4,512,128]{2,1,0:T(8,128)(2,1)S(1)}, bf16[4,512,128]{2,1,0:T(8,128)(2,1)S(1)}, u32[]{:S(2)}, u32[]{:S(2)}) collective-permute-start(bf16[4,512,128]{2,1,0:T(8,128)(2,1)S(1)} %pad_maximum_fusion), channel_id=1, source_target_pairs={{0,16},{16,32},{32,48},{48,64},{64,80},{80,96},{96,112},{112,0},{1... | collective-permute-start | bytes 1572872 | tf_op jit(solution)/shard_map/ppermute | solution.py:37
  42.5 10.1 %collective-permute-done.4 = bf16[4,512,128]{2,1,0:T(8,128)(2,1)S(1)} collective-permute-done((bf16[4,512,128]{2,1,0:T(8,128)(2,1)S(1)}, bf16[4,512,128]{2,1,0:T(8,128)(2,1)S(1)}, u32[]{:S(2)}, u32[]{:S(2)}) %collective-permute-start.4) | collective-permute-done | bytes 524320 | tf_op jit(solution)/shard_map/ppermute | solution.py:37
  52.6 1.9 %collective-permute-start.5 = (bf16[4,512,128]{2,1,0:T(8,128)(2,1)S(1)}, bf16[4,512,128]{2,1,0:T(8,128)(2,1)S(1)}, u32[]{:S(2)}, u32[]{:S(2)}) collective-permute-start(bf16[4,512,128]{2,1,0:T(8,128)(2,1)S(1)} %collective-permute-done.4), channel_id=1, source_target_pairs={{0,16},{16,32},{32,48},{48,64},{64,80},{80,96},{96,112},{112,0},{1... | collective-permute-start | bytes 1572872 | tf_op jit(solution)/shard_map/ppermute | solution.py:37
  54.5 4.6 %collective-permute-start.8 = (bf16[4,512,128]{2,1,0:T(8,128)(2,1)S(1)}, bf16[4,512,128]{2,1,0:T(8,128)(2,1)S(1)}, u32[]{:S(2)}, u32[]{:S(2)}) collective-permute-start(bf16[4,512,128]{2,1,0:T(8,128)(2,1)S(1)} %pad_maximum_fusion), channel_id=1, source_target_pairs={{0,112},{16,0},{32,16},{48,32},{64,48},{80,64},{96,80},{112,96},{1... | collective-permute-start | bytes 1572872 | tf_op jit(solution)/shard_map/ppermute | solution.py:40
  59.1 7.5 %collective-permute-done.5 = bf16[4,512,128]{2,1,0:T(8,128)(2,1)S(1)} collective-permute-done((bf16[4,512,128]{2,1,0:T(8,128)(2,1)S(1)}, bf16[4,512,128]{2,1,0:T(8,128)(2,1)S(1)}, u32[]{:S(2)}, u32[]{:S(2)}) %collective-permute-start.5) | collective-permute-done | bytes 524320 | tf_op jit(solution)/shard_map/ppermute | solution.py:37
  66.6 4.9 %collective-permute-start.6 = (bf16[4,512,128]{2,1,0:T(8,128)(2,1)S(1)}, bf16[4,512,128]{2,1,0:T(8,128)(2,1)S(1)}, u32[]{:S(2)}, u32[]{:S(2)}) collective-permute-start(bf16[4,512,128]{2,1,0:T(8,128)(2,1)S(1)} %collective-permute-done.5), channel_id=1, source_target_pairs={{0,16},{16,32},{32,48},{48,64},{64,80},{80,96},{96,112},{112,0},{1... | collective-permute-start | bytes 1572872 | tf_op jit(solution)/shard_map/ppermute | solution.py:37
  71.6 1.9 %collective-permute-start.9 = (bf16[4,512,128]{2,1,0:T(8,128)(2,1)S(1)}, bf16[4,512,128]{2,1,0:T(8,128)(2,1)S(1)}, u32[]{:S(2)}, u32[]{:S(2)}) collective-permute-start(bf16[4,512,128]{2,1,0:T(8,128)(2,1)S(1)} %collective-permute-done.8), channel_id=1, source_target_pairs={{0,112},{16,0},{32,16},{48,32},{64,48},{80,64},{96,80},{112,96},{1... | collective-permute-start | bytes 1572872 | tf_op jit(solution)/shard_map/ppermute | solution.py:40
  73.5 5.5 %collective-permute-done.6 = bf16[4,512,128]{2,1,0:T(8,128)(2,1)S(1)} collective-permute-done((bf16[4,512,128]{2,1,0:T(8,128)(2,1)S(1)}, bf16[4,512,128]{2,1,0:T(8,128)(2,1)S(1)}, u32[]{:S(2)}, u32[]{:S(2)}) %collective-permute-start.6) | collective-permute-done | bytes 524320 | tf_op jit(solution)/shard_map/ppermute | solution.py:37
  79.1 3.8 %collective-permute-start.7 = (bf16[4,512,128]{2,1,0:T(8,128)(2,1)S(1)}, bf16[4,512,128]{2,1,0:T(8,128)(2,1)S(1)}, u32[]{:S(2)}, u32[]{:S(2)}) collective-permute-start(bf16[4,512,128]{2,1,0:T(8,128)(2,1)S(1)} %collective-permute-done.6), channel_id=1, source_target_pairs={{0,16},{16,32},{32,48},{48,64},{64,80},{80,96},{96,112},{112,0},{1... | collective-permute-start | bytes 1572872 | tf_op jit(solution)/shard_map/ppermute | solution.py:37
  82.9 0.3 collective-permute-done.9
  83.3 2.5 %collective-permute-start.10 = (bf16[4,512,128]{2,1,0:T(8,128)(2,1)S(1)}, bf16[4,512,128]{2,1,0:T(8,128)(2,1)S(1)}, u32[]{:S(2)}, u32[]{:S(2)}) collective-permute-start(bf16[4,512,128]{2,1,0:T(8,128)(2,1)S(1)} %collective-permute-done.9), channel_id=1, source_target_pairs={{0,112},{16,0},{32,16},{48,32},{64,48},{80,64},{96,80},{112,96},{1... | collective-permute-start | bytes 1572872 | tf_op jit(solution)/shard_map/ppermute | solution.py:40
  85.8 14.4 %collective-permute-done.7 = bf16[4,512,128]{2,1,0:T(8,128)(2,1)S(1)} collective-permute-done((bf16[4,512,128]{2,1,0:T(8,128)(2,1)S(1)}, bf16[4,512,128]{2,1,0:T(8,128)(2,1)S(1)}, u32[]{:S(2)}, u32[]{:S(2)}) %collective-permute-start.7) | collective-permute-done | bytes 524320 | tf_op jit(solution)/shard_map/ppermute | solution.py:37
  100.2 0.8 bitcast_dynamic-update-slice_fusion.7
  101.0 0.8 bitcast_dynamic-update-slice_fusion.6
  101.8 0.8 bitcast_dynamic-update-slice_fusion.5
  102.7 0.8 bitcast_dynamic-update-slice_fusion.4
  103.5 0.8 bitcast_dynamic-update-slice_fusion.3
  104.4 0.8 bitcast_dynamic-update-slice_fusion.2
  105.2 0.8 bitcast_dynamic-update-slice_fusion.1
  106.0 0.9 bitcast_dynamic-update-slice_fusion
  106.9 14.2 %all-gather.3.cloned.1.call-done = bf16[4352,512]{1,0:T(8,128)(2,1)} async-done(((bf16[136,512]{1,0:T(8,128)(2,1)}), bf16[4352,512]{1,0:T(8,128)(2,1)}) %all-gather.3.cloned.1.call-update) | async-done | bytes 4456464 | tf_op jit(solution)/shard_map/all_gather | solution.py:129
  121.1 0.8 slice.115
  122.3 3.7 %fusion.13 = f32[64,512]{1,0:T(8,128)S(1)} fusion(bf16[32,136,512]{2,1,0:T(8,128)(2,1)} %bitcast.134, f32[64,32]{0,1:T(8,128)S(1)} %add_exponential_fusion, f32[1,64,1024]{2,1,0:T(8,128)S(1)} %convolution_bitcast_fusion), kind=kOutput, calls=%fused_computation.9 | convolution fusion | flops 268697600 | bytes 4407296 | tf_op jit(solution)/shard_map/vts,se->vte/dot_general | solution.py:77
  126.0 0.4 fusion.80
  126.6 3.1 %fusion.12 = bf16[1,64,8,4,128]{4,1,3,2,0:T(8,128)(2,1)S(1)} fusion(bf16[8,4,512,128]{3,2,1,0:T(8,128)(2,1)} %bitcast_dynamic-update-slice_fusion, f32[64,512]{1,0:T(8,128)S(1)} %get-tuple-element.24, f32[512]{0:T(512)S(1)} %copy-done.11, f32[64]{0:T(128)S(1)} %add_rsqrt_fusion, f32[64]{0:T(128)S(1)} %broadcast_multiply_fusion), kind=kOutput, calls=%fused_computation.7 | convolution fusion | flops 268828672 | bytes 4852224 | tf_op jit(solution)/shard_map/vtr,edrc->vtedc/dot_general | solution.py:137
  129.7 0.2 fusion.23
  130.2 0.3 copy.30
  130.9 7.0 %all_to_all.10 = bf16[1,64,4,2,512]{4,2,1,0,3:T(4,128)(2,1)S(1)} all-to-all(bf16[1,64,4,2,512]{4,2,1,0,3:T(4,128)(2,1)S(1)} %copy.31), channel_id=1, replica_groups=mesh['seq_0'=4,'seq_1'=8,'head_0'=4,'head_1'=2,'var'=2] {'head_1'}, dimensions={3} | all-to-all | bytes 1048576 | tf_op jit(solution)/shard_map/all_to_all | solution.py:146
  137.9 0.5 reduce_sum.53
  138.5 20.2 %all_to_all.11 = bf16[1,64,4,512]{3,1,0,2:T(8,128)(2,1)S(1)} all-to-all(bf16[1,64,4,512]{3,1,0,2:T(8,128)(2,1)S(1)} %copy.32), channel_id=1, replica_groups=mesh['seq_0'=4,'seq_1'=8,'head_0'=4,'head_1'=2,'var'=2] {'head_0'}, dimensions={2} | all-to-all | bytes 524288 | tf_op jit(solution)/shard_map/all_to_all | solution.py:148
  158.7 0.6 fusion.33
  (51 shorter events, 1.7 us)
Async XLA Ops:
  6.5 8.0 %copy-start = (bf16[1,2,512]{2,1,0:T(2,128)(2,1)S(1)}, bf16[1,2,512]{2,1,0:T(2,128)(2,1)}, u32[]{:S(2)}) copy-start(bf16[1,2,512]{2,1,0:T(2,128)(2,1)} %param.16) | copy-start | bytes 6148
  6.5 114.6 %all-gather.3.cloned.1.call-start = ((), (), s32[]{:S(2)}) async-start(), calls=%async_computation.2 | async-start | bytes 4595712 | tf_op jit(solution)/shard_map/all_gather | solution.py:129
  8.1 6.2 %collective-permute-start = (bf16[1,3,512]{2,1,0:T(4,128)(2,1)S(1)}, bf16[1,3,512]{2,1,0:T(4,128)(2,1)S(1)}, u32[]{:S(2)}, u32[]{:S(2)}) collective-permute-start(bf16[1,3,512]{2,1,0:T(4,128)(2,1)S(1)} %slice.105), channel_id=1, source_target_pairs={{0,16},{16,32},{32,48},{48,64},{64,80},{80,96},{96,112},{112,128},... | collective-permute-start | bytes 9224 | tf_op jit(solution)/shard_map/ppermute | solution.py:16
  13.5 25.5 %copy-start.8 = (bf16[64,512]{1,0:T(8,128)(2,1)}, bf16[64,512]{1,0:T(8,128)(2,1)S(1)}, u32[]{:S(2)}) copy-start(bf16[64,512]{1,0:T(8,128)(2,1)S(1)} %convolution_convert_fusion.1) | copy-start | bytes 196612
  13.5 90.0 %copy-start.1 = (bf16[512,128]{1,0:T(8,128)(2,1)S(1)}, bf16[512,128]{1,0:T(8,128)(2,1)}, u32[]{:S(2)}) copy-start(bf16[512,128]{1,0:T(8,128)(2,1)} %param.19) | copy-start | bytes 393220
  24.2 8.0 %collective-permute-start.1 = (bf16[512,128]{1,0:T(8,128)(2,1)}, bf16[512,128]{1,0:T(8,128)(2,1)S(1)}, u32[]{:S(2)}, u32[]{:S(2)}) collective-permute-start(bf16[512,128]{1,0:T(8,128)(2,1)} %param.19), channel_id=1, source_target_pairs={{0,128},{128,256},{256,384},{384,0},{1,129},{129,257},{257,385},{3... | collective-permute-start | bytes 393224 | tf_op jit(solution)/shard_map/ppermute | solution.py:37
  28.3 5.9 %collective-permute-start.3 = (bf16[512,128]{1,0:T(8,128)(2,1)}, bf16[512,128]{1,0:T(8,128)(2,1)S(1)}, u32[]{:S(2)}, u32[]{:S(2)}) collective-permute-start(bf16[512,128]{1,0:T(8,128)(2,1)} %param.19), channel_id=1, source_target_pairs={{0,384},{128,0},{256,128},{384,256},{1,385},{129,1},{257,129},{385... | collective-permute-start | bytes 393224 | tf_op jit(solution)/shard_map/ppermute | solution.py:40
  32.1 26.9 %copy-start.2 = (bf16[512,128]{1,0:T(8,128)(2,1)}, bf16[512,128]{1,0:T(8,128)(2,1)S(1)}, u32[]{:S(2)}) copy-start(bf16[512,128]{1,0:T(8,128)(2,1)S(1)} %collective-permute-done.1) | copy-start | bytes 393220
  32.1 6.9 %collective-permute-start.2 = (bf16[512,128]{1,0:T(8,128)(2,1)S(1)}, bf16[512,128]{1,0:T(8,128)(2,1)S(1)}, u32[]{:S(2)}, u32[]{:S(2)}) collective-permute-start(bf16[512,128]{1,0:T(8,128)(2,1)S(1)} %collective-permute-done.1), channel_id=1, source_target_pairs={{0,128},{128,256},{256,384},{384,0},{1,129},{129,257},{257,385},{3... | collective-permute-start | bytes 393224 | tf_op jit(solution)/shard_map/ppermute | solution.py:37
  34.2 24.9 %copy-start.4 = (bf16[512,128]{1,0:T(8,128)(2,1)}, bf16[512,128]{1,0:T(8,128)(2,1)S(1)}, u32[]{:S(2)}) copy-start(bf16[512,128]{1,0:T(8,128)(2,1)S(1)} %collective-permute-done.3) | copy-start | bytes 393220
  39.0 20.1 %copy-start.6 = (bf16[512,128]{1,0:T(8,128)(2,1)}, bf16[512,128]{1,0:T(8,128)(2,1)S(1)}, u32[]{:S(2)}) copy-start(bf16[512,128]{1,0:T(8,128)(2,1)S(1)} %collective-permute-done.2) | copy-start | bytes 393220
  40.1 12.5 %collective-permute-start.4 = (bf16[4,512,128]{2,1,0:T(8,128)(2,1)S(1)}, bf16[4,512,128]{2,1,0:T(8,128)(2,1)S(1)}, u32[]{:S(2)}, u32[]{:S(2)}) collective-permute-start(bf16[4,512,128]{2,1,0:T(8,128)(2,1)S(1)} %pad_maximum_fusion), channel_id=1, source_target_pairs={{0,16},{16,32},{32,48},{48,64},{64,80},{80,96},{96,112},{112,0},{1... | collective-permute-start | bytes 1572872 | tf_op jit(solution)/shard_map/ppermute | solution.py:37
  52.6 14.1 %collective-permute-start.5 = (bf16[4,512,128]{2,1,0:T(8,128)(2,1)S(1)}, bf16[4,512,128]{2,1,0:T(8,128)(2,1)S(1)}, u32[]{:S(2)}, u32[]{:S(2)}) collective-permute-start(bf16[4,512,128]{2,1,0:T(8,128)(2,1)S(1)} %collective-permute-done.4), channel_id=1, source_target_pairs={{0,16},{16,32},{32,48},{48,64},{64,80},{80,96},{96,112},{112,0},{1... | collective-permute-start | bytes 1572872 | tf_op jit(solution)/shard_map/ppermute | solution.py:37
  54.5 17.1 %collective-permute-start.8 = (bf16[4,512,128]{2,1,0:T(8,128)(2,1)S(1)}, bf16[4,512,128]{2,1,0:T(8,128)(2,1)S(1)}, u32[]{:S(2)}, u32[]{:S(2)}) collective-permute-start(bf16[4,512,128]{2,1,0:T(8,128)(2,1)S(1)} %pad_maximum_fusion), channel_id=1, source_target_pairs={{0,112},{16,0},{32,16},{48,32},{64,48},{80,64},{96,80},{112,96},{1... | collective-permute-start | bytes 1572872 | tf_op jit(solution)/shard_map/ppermute | solution.py:40
  66.6 12.4 %collective-permute-start.6 = (bf16[4,512,128]{2,1,0:T(8,128)(2,1)S(1)}, bf16[4,512,128]{2,1,0:T(8,128)(2,1)S(1)}, u32[]{:S(2)}, u32[]{:S(2)}) collective-permute-start(bf16[4,512,128]{2,1,0:T(8,128)(2,1)S(1)} %collective-permute-done.5), channel_id=1, source_target_pairs={{0,16},{16,32},{32,48},{48,64},{64,80},{80,96},{96,112},{112,0},{1... | collective-permute-start | bytes 1572872 | tf_op jit(solution)/shard_map/ppermute | solution.py:37
  71.6 11.7 %collective-permute-start.9 = (bf16[4,512,128]{2,1,0:T(8,128)(2,1)S(1)}, bf16[4,512,128]{2,1,0:T(8,128)(2,1)S(1)}, u32[]{:S(2)}, u32[]{:S(2)}) collective-permute-start(bf16[4,512,128]{2,1,0:T(8,128)(2,1)S(1)} %collective-permute-done.8), channel_id=1, source_target_pairs={{0,112},{16,0},{32,16},{48,32},{64,48},{80,64},{96,80},{112,96},{1... | collective-permute-start | bytes 1572872 | tf_op jit(solution)/shard_map/ppermute | solution.py:40
  79.1 21.1 %collective-permute-start.7 = (bf16[4,512,128]{2,1,0:T(8,128)(2,1)S(1)}, bf16[4,512,128]{2,1,0:T(8,128)(2,1)S(1)}, u32[]{:S(2)}, u32[]{:S(2)}) collective-permute-start(bf16[4,512,128]{2,1,0:T(8,128)(2,1)S(1)} %collective-permute-done.6), channel_id=1, source_target_pairs={{0,16},{16,32},{32,48},{48,64},{64,80},{80,96},{96,112},{112,0},{1... | collective-permute-start | bytes 1572872 | tf_op jit(solution)/shard_map/ppermute | solution.py:37
  82.9 20.6 %copy-start.3 = (bf16[512,128]{1,0:T(8,128)(2,1)S(1)}, bf16[512,128]{1,0:T(8,128)(2,1)}, u32[]{:S(2)}) copy-start(bf16[512,128]{1,0:T(8,128)(2,1)} %copy-done.2) | copy-start | bytes 393220
  82.9 20.6 %copy-start.5 = (bf16[512,128]{1,0:T(8,128)(2,1)S(1)}, bf16[512,128]{1,0:T(8,128)(2,1)}, u32[]{:S(2)}) copy-start(bf16[512,128]{1,0:T(8,128)(2,1)} %copy-done.4) | copy-start | bytes 393220
  82.9 20.6 %copy-start.7 = (bf16[512,128]{1,0:T(8,128)(2,1)S(1)}, bf16[512,128]{1,0:T(8,128)(2,1)}, u32[]{:S(2)}) copy-start(bf16[512,128]{1,0:T(8,128)(2,1)} %copy-done.6) | copy-start | bytes 393220
  83.3 22.7 %collective-permute-start.10 = (bf16[4,512,128]{2,1,0:T(8,128)(2,1)S(1)}, bf16[4,512,128]{2,1,0:T(8,128)(2,1)S(1)}, u32[]{:S(2)}, u32[]{:S(2)}) collective-permute-start(bf16[4,512,128]{2,1,0:T(8,128)(2,1)S(1)} %collective-permute-done.9), channel_id=1, source_target_pairs={{0,112},{16,0},{32,16},{48,32},{64,48},{80,64},{96,80},{112,96},{1... | collective-permute-start | bytes 1572872 | tf_op jit(solution)/shard_map/ppermute | solution.py:40
  105.2 20.8 %copy-start.9 = (bf16[64,512]{1,0:T(8,128)(2,1)S(1)}, bf16[64,512]{1,0:T(8,128)(2,1)}, u32[]{:S(2)}) copy-start(bf16[64,512]{1,0:T(8,128)(2,1)} %copy-done.8) | copy-start | bytes 196612
  106.0 20.6 %copy-start.11 = (f32[512]{0:T(512)S(1)}, f32[512]{0:T(512)}, u32[]{:S(2)}) copy-start(f32[512]{0:T(512)} %param.18) | copy-start | bytes 6148
  129.7 29.0 %copy-start.10 = (bf16[64,512]{1,0:T(8,128)(2,1)S(1)}, bf16[64,512]{1,0:T(8,128)(2,1)}, u32[]{:S(2)}) copy-start(bf16[64,512]{1,0:T(8,128)(2,1)} %param.12) | copy-start | bytes 196612
Sparse Core Ops, SparseCore 0:
  24.3 96.7 all-gather.2

commit v16 on v15

--- a/solution.py
+++ b/solution.py
@@ -140,13 +140,14 @@
     ).astype(jnp.bfloat16)
     head_terms = jnp.roll(head_terms, lax.axis_index(SEQ[1]) - inner_size // 2, axis=2)
     head_terms = jnp.roll(head_terms, lax.axis_index(SEQ[0]) - outer // 2, axis=3)
-    head_terms = jnp.swapaxes(head_terms, 2, 3).reshape(*normed.shape[:2], -1)
     pair, across = HEAD
-    blocks = head_terms.reshape(*head_terms.shape[:2], lax.axis_size(across), lax.axis_size(pair), -1)
-    arrived = lax.all_to_all(blocks, pair, split_axis=3, concat_axis=3, tiled=True)
-    pair_sum = jnp.sum(arrived.astype(jnp.float32), axis=3).astype(jnp.bfloat16)
-    summed = lax.all_to_all(pair_sum, across, split_axis=2, concat_axis=2, tiled=True)
-    summed = jnp.sum(summed.astype(jnp.float32), axis=2)
+    pairs = lax.axis_size(pair)
+    head_terms = head_terms.reshape(*normed.shape[:2], pairs, inner_size // pairs, outer, -1)
+    blocks = jnp.transpose(head_terms, (2, 4, 0, 1, 3, 5)).reshape(pairs, outer, *normed.shape[:2], -1)
+    arrived = lax.all_to_all(blocks, pair, split_axis=0, concat_axis=0, tiled=True)
+    pair_sum = jnp.sum(arrived.astype(jnp.float32), axis=0).astype(jnp.bfloat16)
+    summed = lax.all_to_all(pair_sum, across, split_axis=0, concat_axis=0, tiled=True)
+    summed = jnp.sum(summed.astype(jnp.float32), axis=0)
     return (residual_in[None, :, :].astype(jnp.float32) + summed).astype(jnp.bfloat16)
 
 

time: 168 us -> 167 us (level)
  no operation moved by 1% of the time
where the time goes in v16:
time: 167 us; the launch traced here: 165 us
  waiting for transfers between devices  57.6 us (34%)
  starting transfers between devices  35.4 us (21%)
  blocking collectives  27.2 us (16%)
  between operations  18.7 us (11%)
  matrix products  10.8 us (6%)
  local copies, waits for them, and re-layouts  8.49 us (5%)
  other arithmetic  6.95 us (4%)
    ppermute x6, waiting for transfers between devices, ring_pieces(): forward = lax.ppermute(forward, axis, ahead)  43 us
    all_to_all x1, blocking collectives, body(): lax.all_to_all(pair_sum, across, split_axis=0, concat_axis=0, tiled=True)  20.2 us
    ppermute x6, starting transfers between devices, ring_pieces(): forward = lax.ppermute(forward, axis, ahead)  19.2 us
    all_gather x1, waiting for transfers between devices, body(): gathered = lax.all_gather(packed, SEQ, axis=0, tiled=False)  14.2 us
    ppermute x4, starting transfers between devices, ring_pieces(): backward = lax.ppermute(backward, axis, behind)  12.2 us
    all_to_all x1, blocking collectives, body(): lax.all_to_all(blocks, pair, split_axis=0, concat_axis=0, tiled=True)  6.98 us
    unnamed x32, local copies, waits for them, and re-layouts  5.14 us
    ppermute x1, starting transfers between devices, from_behind(): lax.ppermute(value, axis, [(source, source + steps) for source in range(i...  4.02 us
  transfers between devices with their start and end apart: 12, of which 8 were waited for; matrix products, arithmetic and copies ran while one was open for 6% of the time, Pallas kernels for 0%

profile of v16, /device:TPU:1, one launch (start us, length us, event | category | flops | bytes accessed | tf_op | source)
XLA Modules:
  0.0 165.1 jit_solution(16972389005178806415)
XLA Ops:
  6.5 0.7 convert_bitcast_fusion
  7.2 0.9 multiply_bitcast_fusion
  8.1 4.0 %collective-permute-start = (bf16[1,3,512]{2,1,0:T(4,128)(2,1)S(1)}, bf16[1,3,512]{2,1,0:T(4,128)(2,1)S(1)}, u32[]{:S(2)}, u32[]{:S(2)}) collective-permute-start(bf16[1,3,512]{2,1,0:T(4,128)(2,1)S(1)} %slice.105), channel_id=1, source_target_pairs={{0,16},{16,32},{32,48},{48,64},{64,80},{80,96},{96,112},{112,128},... | collective-permute-start | bytes 9224 | tf_op jit(solution)/shard_map/ppermute | solution.py:16
  12.2 1.3 convolution_convert_fusion.1
  13.5 0.9 fusion.78
  14.5 0.7 fusion.19
  15.3 0.2 reduce_window_sum.11
  15.6 0.7 slice.95
  21.1 0.6 fusion.77
  21.8 1.5 convolution_bitcast_fusion
  23.5 0.7 pad_maximum_fusion.1
  24.2 4.1 %collective-permute-start.1 = (bf16[512,128]{1,0:T(8,128)(2,1)}, bf16[512,128]{1,0:T(8,128)(2,1)S(1)}, u32[]{:S(2)}, u32[]{:S(2)}) collective-permute-start(bf16[512,128]{1,0:T(8,128)(2,1)} %param.19), channel_id=1, source_target_pairs={{0,128},{128,256},{256,384},{384,0},{1,129},{129,257},{257,385},{3... | collective-permute-start | bytes 393224 | tf_op jit(solution)/shard_map/ppermute | solution.py:37
  28.3 3.2 %collective-permute-start.3 = (bf16[512,128]{1,0:T(8,128)(2,1)}, bf16[512,128]{1,0:T(8,128)(2,1)S(1)}, u32[]{:S(2)}, u32[]{:S(2)}) collective-permute-start(bf16[512,128]{1,0:T(8,128)(2,1)} %param.19), channel_id=1, source_target_pairs={{0,384},{128,0},{256,128},{384,256},{1,385},{129,1},{257,129},{385... | collective-permute-start | bytes 393224 | tf_op jit(solution)/shard_map/ppermute | solution.py:40
  31.5 0.6 collective-permute-done.1
  32.1 2.1 %collective-permute-start.2 = (bf16[512,128]{1,0:T(8,128)(2,1)S(1)}, bf16[512,128]{1,0:T(8,128)(2,1)S(1)}, u32[]{:S(2)}, u32[]{:S(2)}) collective-permute-start(bf16[512,128]{1,0:T(8,128)(2,1)S(1)} %collective-permute-done.1), channel_id=1, source_target_pairs={{0,128},{128,256},{256,384},{384,0},{1,129},{129,257},{257,385},{3... | collective-permute-start | bytes 393224 | tf_op jit(solution)/shard_map/ppermute | solution.py:37
  34.2 4.8 %collective-permute-done.2 = bf16[512,128]{1,0:T(8,128)(2,1)S(1)} collective-permute-done((bf16[512,128]{1,0:T(8,128)(2,1)S(1)}, bf16[512,128]{1,0:T(8,128)(2,1)S(1)}, u32[]{:S(2)}, u32[]{:S(2)}) %collective-permute-start.2) | collective-permute-done | bytes 131104 | tf_op jit(solution)/shard_map/ppermute | solution.py:37
  39.0 1.0 pad_maximum_fusion
  40.1 2.4 %collective-permute-start.4 = (bf16[4,512,128]{2,1,0:T(8,128)(2,1)S(1)}, bf16[4,512,128]{2,1,0:T(8,128)(2,1)S(1)}, u32[]{:S(2)}, u32[]{:S(2)}) collective-permute-start(bf16[4,512,128]{2,1,0:T(8,128)(2,1)S(1)} %pad_maximum_fusion), channel_id=1, source_target_pairs={{0,16},{16,32},{32,48},{48,64},{64,80},{80,96},{96,112},{112,0},{1... | collective-permute-start | bytes 1572872 | tf_op jit(solution)/shard_map/ppermute | solution.py:37
  42.5 10.1 %collective-permute-done.4 = bf16[4,512,128]{2,1,0:T(8,128)(2,1)S(1)} collective-permute-done((bf16[4,512,128]{2,1,0:T(8,128)(2,1)S(1)}, bf16[4,512,128]{2,1,0:T(8,128)(2,1)S(1)}, u32[]{:S(2)}, u32[]{:S(2)}) %collective-permute-start.4) | collective-permute-done | bytes 524320 | tf_op jit(solution)/shard_map/ppermute | solution.py:37
  52.6 1.9 %collective-permute-start.5 = (bf16[4,512,128]{2,1,0:T(8,128)(2,1)S(1)}, bf16[4,512,128]{2,1,0:T(8,128)(2,1)S(1)}, u32[]{:S(2)}, u32[]{:S(2)}) collective-permute-start(bf16[4,512,128]{2,1,0:T(8,128)(2,1)S(1)} %collective-permute-done.4), channel_id=1, source_target_pairs={{0,16},{16,32},{32,48},{48,64},{64,80},{80,96},{96,112},{112,0},{1... | collective-permute-start | bytes 1572872 | tf_op jit(solution)/shard_map/ppermute | solution.py:37
  54.5 4.6 %collective-permute-start.8 = (bf16[4,512,128]{2,1,0:T(8,128)(2,1)S(1)}, bf16[4,512,128]{2,1,0:T(8,128)(2,1)S(1)}, u32[]{:S(2)}, u32[]{:S(2)}) collective-permute-start(bf16[4,512,128]{2,1,0:T(8,128)(2,1)S(1)} %pad_maximum_fusion), channel_id=1, source_target_pairs={{0,112},{16,0},{32,16},{48,32},{64,48},{80,64},{96,80},{112,96},{1... | collective-permute-start | bytes 1572872 | tf_op jit(solution)/shard_map/ppermute | solution.py:40
  59.1 7.5 %collective-permute-done.5 = bf16[4,512,128]{2,1,0:T(8,128)(2,1)S(1)} collective-permute-done((bf16[4,512,128]{2,1,0:T(8,128)(2,1)S(1)}, bf16[4,512,128]{2,1,0:T(8,128)(2,1)S(1)}, u32[]{:S(2)}, u32[]{:S(2)}) %collective-permute-start.5) | collective-permute-done | bytes 524320 | tf_op jit(solution)/shard_map/ppermute | solution.py:37
  66.6 4.9 %collective-permute-start.6 = (bf16[4,512,128]{2,1,0:T(8,128)(2,1)S(1)}, bf16[4,512,128]{2,1,0:T(8,128)(2,1)S(1)}, u32[]{:S(2)}, u32[]{:S(2)}) collective-permute-start(bf16[4,512,128]{2,1,0:T(8,128)(2,1)S(1)} %collective-permute-done.5), channel_id=1, source_target_pairs={{0,16},{16,32},{32,48},{48,64},{64,80},{80,96},{96,112},{112,0},{1... | collective-permute-start | bytes 1572872 | tf_op jit(solution)/shard_map/ppermute | solution.py:37
  71.6 1.9 %collective-permute-start.9 = (bf16[4,512,128]{2,1,0:T(8,128)(2,1)S(1)}, bf16[4,512,128]{2,1,0:T(8,128)(2,1)S(1)}, u32[]{:S(2)}, u32[]{:S(2)}) collective-permute-start(bf16[4,512,128]{2,1,0:T(8,128)(2,1)S(1)} %collective-permute-done.8), channel_id=1, source_target_pairs={{0,112},{16,0},{32,16},{48,32},{64,48},{80,64},{96,80},{112,96},{1... | collective-permute-start | bytes 1572872 | tf_op jit(solution)/shard_map/ppermute | solution.py:40
  73.5 5.5 %collective-permute-done.6 = bf16[4,512,128]{2,1,0:T(8,128)(2,1)S(1)} collective-permute-done((bf16[4,512,128]{2,1,0:T(8,128)(2,1)S(1)}, bf16[4,512,128]{2,1,0:T(8,128)(2,1)S(1)}, u32[]{:S(2)}, u32[]{:S(2)}) %collective-permute-start.6) | collective-permute-done | bytes 524320 | tf_op jit(solution)/shard_map/ppermute | solution.py:37
  79.1 3.8 %collective-permute-start.7 = (bf16[4,512,128]{2,1,0:T(8,128)(2,1)S(1)}, bf16[4,512,128]{2,1,0:T(8,128)(2,1)S(1)}, u32[]{:S(2)}, u32[]{:S(2)}) collective-permute-start(bf16[4,512,128]{2,1,0:T(8,128)(2,1)S(1)} %collective-permute-done.6), channel_id=1, source_target_pairs={{0,16},{16,32},{32,48},{48,64},{64,80},{80,96},{96,112},{112,0},{1... | collective-permute-start | bytes 1572872 | tf_op jit(solution)/shard_map/ppermute | solution.py:37
  82.9 0.3 collective-permute-done.9
  83.3 2.5 %collective-permute-start.10 = (bf16[4,512,128]{2,1,0:T(8,128)(2,1)S(1)}, bf16[4,512,128]{2,1,0:T(8,128)(2,1)S(1)}, u32[]{:S(2)}, u32[]{:S(2)}) collective-permute-start(bf16[4,512,128]{2,1,0:T(8,128)(2,1)S(1)} %collective-permute-done.9), channel_id=1, source_target_pairs={{0,112},{16,0},{32,16},{48,32},{64,48},{80,64},{96,80},{112,96},{1... | collective-permute-start | bytes 1572872 | tf_op jit(solution)/shard_map/ppermute | solution.py:40
  85.8 14.4 %collective-permute-done.7 = bf16[4,512,128]{2,1,0:T(8,128)(2,1)S(1)} collective-permute-done((bf16[4,512,128]{2,1,0:T(8,128)(2,1)S(1)}, bf16[4,512,128]{2,1,0:T(8,128)(2,1)S(1)}, u32[]{:S(2)}, u32[]{:S(2)}) %collective-permute-start.7) | collective-permute-done | bytes 524320 | tf_op jit(solution)/shard_map/ppermute | solution.py:37
  100.2 0.8 bitcast_dynamic-update-slice_fusion.7
  101.0 0.8 bitcast_dynamic-update-slice_fusion.6
  101.8 0.8 bitcast_dynamic-update-slice_fusion.5
  102.7 0.8 bitcast_dynamic-update-slice_fusion.4
  103.5 0.8 bitcast_dynamic-update-slice_fusion.3
  104.4 0.8 bitcast_dynamic-update-slice_fusion.2
  105.2 0.8 bitcast_dynamic-update-slice_fusion.1
  106.0 0.9 bitcast_dynamic-update-slice_fusion
  106.9 14.2 %all-gather.3.cloned.1.call-done = bf16[4352,512]{1,0:T(8,128)(2,1)} async-done(((bf16[136,512]{1,0:T(8,128)(2,1)}), bf16[4352,512]{1,0:T(8,128)(2,1)}) %all-gather.3.cloned.1.call-update) | async-done | bytes 4456464 | tf_op jit(solution)/shard_map/all_gather | solution.py:129
  121.1 0.8 slice.115
  122.3 3.7 %fusion.13 = f32[64,512]{1,0:T(8,128)S(1)} fusion(bf16[32,136,512]{2,1,0:T(8,128)(2,1)} %bitcast.142, f32[64,32]{0,1:T(8,128)S(1)} %add_exponential_fusion, f32[1,64,1024]{2,1,0:T(8,128)S(1)} %convolution_bitcast_fusion), kind=kOutput, calls=%fused_computation.9 | convolution fusion | flops 268697600 | bytes 4407296 | tf_op jit(solution)/shard_map/vts,se->vte/dot_general | solution.py:77
  126.0 0.4 fusion.79
  126.4 0.2 multiply_reduce_fusion
  126.6 3.1 %fusion.12 = bf16[1,64,8,4,128]{4,1,3,2,0:T(8,128)(2,1)S(1)} fusion(bf16[8,4,512,128]{3,2,1,0:T(8,128)(2,1)} %bitcast_dynamic-update-slice_fusion, f32[64,512]{1,0:T(8,128)S(1)} %get-tuple-element.24, f32[512]{0:T(512)S(1)} %copy-done.11, f32[64]{0:T(128)S(1)} %add_rsqrt_fusion, f32[64]{0:T(128)S(1)} %broadcast_multiply_fusion), kind=kOutput, calls=%fused_computation.7 | convolution fusion | flops 268828672 | bytes 4852224 | tf_op jit(solution)/shard_map/vtr,edrc->vtedc/dot_general | solution.py:137
  129.8 0.2 fusion.22
  130.0 0.2 fusion.21
  130.3 7.0 %all_to_all.10 = bf16[2,4,1,64,512]{4,3,1,2,0:T(8,128)(2,1)S(1)} all-to-all(bf16[2,4,1,64,512]{4,3,1,2,0:T(8,128)(2,1)S(1)} %bitcast.122), channel_id=1, replica_groups=mesh['seq_0'=4,'seq_1'=8,'head_0'=4,'head_1'=2,'var'=2] {'head_1'}, dimensions={0} | all-to-all | bytes 1048576 | tf_op jit(solution)/shard_map/all_to_all | solution.py:147
  137.4 20.2 %all_to_all.11 = bf16[4,1,64,512]{3,2,1,0:T(8,128)(2,1)S(1)} all-to-all(bf16[4,1,64,512]{3,2,1,0:T(8,128)(2,1)S(1)} %bitcast.123), channel_id=1, replica_groups=mesh['seq_0'=4,'seq_1'=8,'head_0'=4,'head_1'=2,'var'=2] {'head_0'}, dimensions={0} | all-to-all | bytes 524288 | tf_op jit(solution)/shard_map/all_to_all | solution.py:149
  157.6 0.6 fusion.32
  (48 shorter events, 1.0 us)
Async XLA Ops:
  6.5 8.0 %copy-start = (bf16[1,2,512]{2,1,0:T(2,128)(2,1)S(1)}, bf16[1,2,512]{2,1,0:T(2,128)(2,1)}, u32[]{:S(2)}) copy-start(bf16[1,2,512]{2,1,0:T(2,128)(2,1)} %param.16) | copy-start | bytes 6148
  6.5 114.6 %all-gather.3.cloned.1.call-start = ((), (), s32[]{:S(2)}) async-start(), calls=%async_computation.2 | async-start | bytes 4595712 | tf_op jit(solution)/shard_map/all_gather | solution.py:129
  8.1 6.2 %collective-permute-start = (bf16[1,3,512]{2,1,0:T(4,128)(2,1)S(1)}, bf16[1,3,512]{2,1,0:T(4,128)(2,1)S(1)}, u32[]{:S(2)}, u32[]{:S(2)}) collective-permute-start(bf16[1,3,512]{2,1,0:T(4,128)(2,1)S(1)} %slice.105), channel_id=1, source_target_pairs={{0,16},{16,32},{32,48},{48,64},{64,80},{80,96},{96,112},{112,128},... | collective-permute-start | bytes 9224 | tf_op jit(solution)/shard_map/ppermute | solution.py:16
  13.5 25.5 %copy-start.8 = (bf16[64,512]{1,0:T(8,128)(2,1)}, bf16[64,512]{1,0:T(8,128)(2,1)S(1)}, u32[]{:S(2)}) copy-start(bf16[64,512]{1,0:T(8,128)(2,1)S(1)} %convolution_convert_fusion.1) | copy-start | bytes 196612
  13.5 90.0 %copy-start.1 = (bf16[512,128]{1,0:T(8,128)(2,1)S(1)}, bf16[512,128]{1,0:T(8,128)(2,1)}, u32[]{:S(2)}) copy-start(bf16[512,128]{1,0:T(8,128)(2,1)} %param.19) | copy-start | bytes 393220
  24.2 8.0 %collective-permute-start.1 = (bf16[512,128]{1,0:T(8,128)(2,1)}, bf16[512,128]{1,0:T(8,128)(2,1)S(1)}, u32[]{:S(2)}, u32[]{:S(2)}) collective-permute-start(bf16[512,128]{1,0:T(8,128)(2,1)} %param.19), channel_id=1, source_target_pairs={{0,128},{128,256},{256,384},{384,0},{1,129},{129,257},{257,385},{3... | collective-permute-start | bytes 393224 | tf_op jit(solution)/shard_map/ppermute | solution.py:37
  28.3 5.9 %collective-permute-start.3 = (bf16[512,128]{1,0:T(8,128)(2,1)}, bf16[512,128]{1,0:T(8,128)(2,1)S(1)}, u32[]{:S(2)}, u32[]{:S(2)}) collective-permute-start(bf16[512,128]{1,0:T(8,128)(2,1)} %param.19), channel_id=1, source_target_pairs={{0,384},{128,0},{256,128},{384,256},{1,385},{129,1},{257,129},{385... | collective-permute-start | bytes 393224 | tf_op jit(solution)/shard_map/ppermute | solution.py:40
  32.1 26.9 %copy-start.2 = (bf16[512,128]{1,0:T(8,128)(2,1)}, bf16[512,128]{1,0:T(8,128)(2,1)S(1)}, u32[]{:S(2)}) copy-start(bf16[512,128]{1,0:T(8,128)(2,1)S(1)} %collective-permute-done.1) | copy-start | bytes 393220
  32.1 6.9 %collective-permute-start.2 = (bf16[512,128]{1,0:T(8,128)(2,1)S(1)}, bf16[512,128]{1,0:T(8,128)(2,1)S(1)}, u32[]{:S(2)}, u32[]{:S(2)}) collective-permute-start(bf16[512,128]{1,0:T(8,128)(2,1)S(1)} %collective-permute-done.1), channel_id=1, source_target_pairs={{0,128},{128,256},{256,384},{384,0},{1,129},{129,257},{257,385},{3... | collective-permute-start | bytes 393224 | tf_op jit(solution)/shard_map/ppermute | solution.py:37
  34.2 24.9 %copy-start.4 = (bf16[512,128]{1,0:T(8,128)(2,1)}, bf16[512,128]{1,0:T(8,128)(2,1)S(1)}, u32[]{:S(2)}) copy-start(bf16[512,128]{1,0:T(8,128)(2,1)S(1)} %collective-permute-done.3) | copy-start | bytes 393220
  39.0 20.1 %copy-start.6 = (bf16[512,128]{1,0:T(8,128)(2,1)}, bf16[512,128]{1,0:T(8,128)(2,1)S(1)}, u32[]{:S(2)}) copy-start(bf16[512,128]{1,0:T(8,128)(2,1)S(1)} %collective-permute-done.2) | copy-start | bytes 393220
  40.1 12.5 %collective-permute-start.4 = (bf16[4,512,128]{2,1,0:T(8,128)(2,1)S(1)}, bf16[4,512,128]{2,1,0:T(8,128)(2,1)S(1)}, u32[]{:S(2)}, u32[]{:S(2)}) collective-permute-start(bf16[4,512,128]{2,1,0:T(8,128)(2,1)S(1)} %pad_maximum_fusion), channel_id=1, source_target_pairs={{0,16},{16,32},{32,48},{48,64},{64,80},{80,96},{96,112},{112,0},{1... | collective-permute-start | bytes 1572872 | tf_op jit(solution)/shard_map/ppermute | solution.py:37
  52.6 14.1 %collective-permute-start.5 = (bf16[4,512,128]{2,1,0:T(8,128)(2,1)S(1)}, bf16[4,512,128]{2,1,0:T(8,128)(2,1)S(1)}, u32[]{:S(2)}, u32[]{:S(2)}) collective-permute-start(bf16[4,512,128]{2,1,0:T(8,128)(2,1)S(1)} %collective-permute-done.4), channel_id=1, source_target_pairs={{0,16},{16,32},{32,48},{48,64},{64,80},{80,96},{96,112},{112,0},{1... | collective-permute-start | bytes 1572872 | tf_op jit(solution)/shard_map/ppermute | solution.py:37
  54.5 17.1 %collective-permute-start.8 = (bf16[4,512,128]{2,1,0:T(8,128)(2,1)S(1)}, bf16[4,512,128]{2,1,0:T(8,128)(2,1)S(1)}, u32[]{:S(2)}, u32[]{:S(2)}) collective-permute-start(bf16[4,512,128]{2,1,0:T(8,128)(2,1)S(1)} %pad_maximum_fusion), channel_id=1, source_target_pairs={{0,112},{16,0},{32,16},{48,32},{64,48},{80,64},{96,80},{112,96},{1... | collective-permute-start | bytes 1572872 | tf_op jit(solution)/shard_map/ppermute | solution.py:40
  66.6 12.4 %collective-permute-start.6 = (bf16[4,512,128]{2,1,0:T(8,128)(2,1)S(1)}, bf16[4,512,128]{2,1,0:T(8,128)(2,1)S(1)}, u32[]{:S(2)}, u32[]{:S(2)}) collective-permute-start(bf16[4,512,128]{2,1,0:T(8,128)(2,1)S(1)} %collective-permute-done.5), channel_id=1, source_target_pairs={{0,16},{16,32},{32,48},{48,64},{64,80},{80,96},{96,112},{112,0},{1... | collective-permute-start | bytes 1572872 | tf_op jit(solution)/shard_map/ppermute | solution.py:37
  71.6 11.7 %collective-permute-start.9 = (bf16[4,512,128]{2,1,0:T(8,128)(2,1)S(1)}, bf16[4,512,128]{2,1,0:T(8,128)(2,1)S(1)}, u32[]{:S(2)}, u32[]{:S(2)}) collective-permute-start(bf16[4,512,128]{2,1,0:T(8,128)(2,1)S(1)} %collective-permute-done.8), channel_id=1, source_target_pairs={{0,112},{16,0},{32,16},{48,32},{64,48},{80,64},{96,80},{112,96},{1... | collective-permute-start | bytes 1572872 | tf_op jit(solution)/shard_map/ppermute | solution.py:40
  79.1 21.1 %collective-permute-start.7 = (bf16[4,512,128]{2,1,0:T(8,128)(2,1)S(1)}, bf16[4,512,128]{2,1,0:T(8,128)(2,1)S(1)}, u32[]{:S(2)}, u32[]{:S(2)}) collective-permute-start(bf16[4,512,128]{2,1,0:T(8,128)(2,1)S(1)} %collective-permute-done.6), channel_id=1, source_target_pairs={{0,16},{16,32},{32,48},{48,64},{64,80},{80,96},{96,112},{112,0},{1... | collective-permute-start | bytes 1572872 | tf_op jit(solution)/shard_map/ppermute | solution.py:37
  82.9 20.6 %copy-start.3 = (bf16[512,128]{1,0:T(8,128)(2,1)S(1)}, bf16[512,128]{1,0:T(8,128)(2,1)}, u32[]{:S(2)}) copy-start(bf16[512,128]{1,0:T(8,128)(2,1)} %copy-done.2) | copy-start | bytes 393220
  82.9 20.6 %copy-start.5 = (bf16[512,128]{1,0:T(8,128)(2,1)S(1)}, bf16[512,128]{1,0:T(8,128)(2,1)}, u32[]{:S(2)}) copy-start(bf16[512,128]{1,0:T(8,128)(2,1)} %copy-done.4) | copy-start | bytes 393220
  82.9 20.6 %copy-start.7 = (bf16[512,128]{1,0:T(8,128)(2,1)S(1)}, bf16[512,128]{1,0:T(8,128)(2,1)}, u32[]{:S(2)}) copy-start(bf16[512,128]{1,0:T(8,128)(2,1)} %copy-done.6) | copy-start | bytes 393220
  83.3 22.7 %collective-permute-start.10 = (bf16[4,512,128]{2,1,0:T(8,128)(2,1)S(1)}, bf16[4,512,128]{2,1,0:T(8,128)(2,1)S(1)}, u32[]{:S(2)}, u32[]{:S(2)}) collective-permute-start(bf16[4,512,128]{2,1,0:T(8,128)(2,1)S(1)} %collective-permute-done.9), channel_id=1, source_target_pairs={{0,112},{16,0},{32,16},{48,32},{64,48},{80,64},{96,80},{112,96},{1... | collective-permute-start | bytes 1572872 | tf_op jit(solution)/shard_map/ppermute | solution.py:40
  105.2 20.8 %copy-start.9 = (bf16[64,512]{1,0:T(8,128)(2,1)S(1)}, bf16[64,512]{1,0:T(8,128)(2,1)}, u32[]{:S(2)}) copy-start(bf16[64,512]{1,0:T(8,128)(2,1)} %copy-done.8) | copy-start | bytes 196612
  106.0 20.6 %copy-start.11 = (f32[512]{0:T(512)S(1)}, f32[512]{0:T(512)}, u32[]{:S(2)}) copy-start(f32[512]{0:T(512)} %param.18) | copy-start | bytes 6148
  126.6 31.0 %copy-start.10 = (bf16[64,512]{1,0:T(8,128)(2,1)S(1)}, bf16[64,512]{1,0:T(8,128)(2,1)}, u32[]{:S(2)}) copy-start(bf16[64,512]{1,0:T(8,128)(2,1)} %param.12) | copy-start | bytes 196612
Sparse Core Ops, SparseCore 0:
  24.3 96.7 all-gather.2

commit v17 on v16

--- a/solution.py
+++ b/solution.py
@@ -64,8 +64,8 @@
     token_count = queries.shape[1]
     keys_all = gathered[:, :token_count, :].reshape(blocks * token_count, head_size)
     values_all = gathered[:, token_count : 2 * token_count, :].reshape(blocks * token_count, head_size)
-    parts = gathered[:, 2 * token_count, :3].astype(jnp.float32)
-    decay = (parts[:, 0] + parts[:, 1]) + parts[:, 2]
+    parts = gathered[:, 2 * token_count, :].astype(jnp.float32)
+    decay = jnp.sum(jnp.where(jnp.arange(head_size) < 3, parts, 0.0), axis=1)
     index = jnp.arange(blocks)
     between = (index[:, None] < index[None, :]) & (index[None, :] < block)
     before_own = jnp.sum(jnp.where(index < block, decay, 0.0))

time: 167 us -> 167 us (level)
  other arithmetic: 6.95 us -> 8.63 us
where the time goes in v17:
time: 167 us; the launch traced here: 165 us
  waiting for transfers between devices  56.8 us (34%)
  starting transfers between devices  35.6 us (21%)
  blocking collectives  27.2 us (16%)
  between operations  18.5 us (11%)
  matrix products  10.8 us (6%)
  other arithmetic  8.63 us (5%)
  local copies, waits for them, and re-layouts  7.53 us (5%)
    ppermute x6, waiting for transfers between devices, ring_pieces(): forward = lax.ppermute(forward, axis, ahead)  42.6 us
    all_to_all x1, blocking collectives, body(): lax.all_to_all(pair_sum, across, split_axis=0, concat_axis=0, tiled=True)  20.2 us
    ppermute x6, starting transfers between devices, ring_pieces(): forward = lax.ppermute(forward, axis, ahead)  19.2 us
    all_gather x1, waiting for transfers between devices, body(): gathered = lax.all_gather(packed, SEQ, axis=0, tiled=False)  13.6 us
    ppermute x4, starting transfers between devices, ring_pieces(): backward = lax.ppermute(backward, axis, behind)  12.4 us
    all_to_all x1, blocking collectives, body(): lax.all_to_all(blocks, pair, split_axis=0, concat_axis=0, tiled=True)  7.05 us
    unnamed x32, local copies, waits for them, and re-layouts  5.05 us
    ppermute x1, starting transfers between devices, from_behind(): lax.ppermute(value, axis, [(source, source + steps) for source in range(i...  4.02 us
  transfers between devices with their start and end apart: 12, of which 8 were waited for; matrix products, arithmetic and copies ran while one was open for 6% of the time, Pallas kernels for 0%

profile of v17, /device:TPU:1, one launch (start us, length us, event | category | flops | bytes accessed | tf_op | source)
XLA Modules:
  0.0 165.1 jit_solution(10807012482447167902)
XLA Ops:
  6.5 0.7 convert_bitcast_fusion
  7.2 0.9 multiply_bitcast_fusion
  8.1 4.0 %collective-permute-start = (bf16[1,3,512]{2,1,0:T(4,128)(2,1)S(1)}, bf16[1,3,512]{2,1,0:T(4,128)(2,1)S(1)}, u32[]{:S(2)}, u32[]{:S(2)}) collective-permute-start(bf16[1,3,512]{2,1,0:T(4,128)(2,1)S(1)} %slice.93), channel_id=1, source_target_pairs={{0,16},{16,32},{32,48},{48,64},{64,80},{80,96},{96,112},{112,128},... | collective-permute-start | bytes 9224 | tf_op jit(solution)/shard_map/ppermute | solution.py:16
  12.2 1.3 convolution_convert_fusion.1
  13.5 0.9 fusion.79
  14.5 0.7 fusion.19
  15.3 0.2 reduce_window_sum.11
  15.6 0.6 slice.86
  20.9 0.6 fusion.78
  21.6 1.5 convolution_bitcast_fusion
  23.3 0.7 pad_maximum_fusion.1
  24.0 4.1 %collective-permute-start.1 = (bf16[512,128]{1,0:T(8,128)(2,1)}, bf16[512,128]{1,0:T(8,128)(2,1)S(1)}, u32[]{:S(2)}, u32[]{:S(2)}) collective-permute-start(bf16[512,128]{1,0:T(8,128)(2,1)} %param.19), channel_id=1, source_target_pairs={{0,128},{128,256},{256,384},{384,0},{1,129},{129,257},{257,385},{3... | collective-permute-start | bytes 393224 | tf_op jit(solution)/shard_map/ppermute | solution.py:37
  28.1 3.2 %collective-permute-start.3 = (bf16[512,128]{1,0:T(8,128)(2,1)}, bf16[512,128]{1,0:T(8,128)(2,1)S(1)}, u32[]{:S(2)}, u32[]{:S(2)}) collective-permute-start(bf16[512,128]{1,0:T(8,128)(2,1)} %param.19), channel_id=1, source_target_pairs={{0,384},{128,0},{256,128},{384,256},{1,385},{129,1},{257,129},{385... | collective-permute-start | bytes 393224 | tf_op jit(solution)/shard_map/ppermute | solution.py:40
  31.3 0.6 collective-permute-done.1
  31.9 2.1 %collective-permute-start.2 = (bf16[512,128]{1,0:T(8,128)(2,1)S(1)}, bf16[512,128]{1,0:T(8,128)(2,1)S(1)}, u32[]{:S(2)}, u32[]{:S(2)}) collective-permute-start(bf16[512,128]{1,0:T(8,128)(2,1)S(1)} %collective-permute-done.1), channel_id=1, source_target_pairs={{0,128},{128,256},{256,384},{384,0},{1,129},{129,257},{257,385},{3... | collective-permute-start | bytes 393224 | tf_op jit(solution)/shard_map/ppermute | solution.py:37
  34.1 4.8 %collective-permute-done.2 = bf16[512,128]{1,0:T(8,128)(2,1)S(1)} collective-permute-done((bf16[512,128]{1,0:T(8,128)(2,1)S(1)}, bf16[512,128]{1,0:T(8,128)(2,1)S(1)}, u32[]{:S(2)}, u32[]{:S(2)}) %collective-permute-start.2) | collective-permute-done | bytes 131104 | tf_op jit(solution)/shard_map/ppermute | solution.py:37
  38.9 1.0 pad_maximum_fusion
  39.9 2.4 %collective-permute-start.4 = (bf16[4,512,128]{2,1,0:T(8,128)(2,1)S(1)}, bf16[4,512,128]{2,1,0:T(8,128)(2,1)S(1)}, u32[]{:S(2)}, u32[]{:S(2)}) collective-permute-start(bf16[4,512,128]{2,1,0:T(8,128)(2,1)S(1)} %pad_maximum_fusion), channel_id=1, source_target_pairs={{0,16},{16,32},{32,48},{48,64},{64,80},{80,96},{96,112},{112,0},{1... | collective-permute-start | bytes 1572872 | tf_op jit(solution)/shard_map/ppermute | solution.py:37
  42.3 10.1 %collective-permute-done.4 = bf16[4,512,128]{2,1,0:T(8,128)(2,1)S(1)} collective-permute-done((bf16[4,512,128]{2,1,0:T(8,128)(2,1)S(1)}, bf16[4,512,128]{2,1,0:T(8,128)(2,1)S(1)}, u32[]{:S(2)}, u32[]{:S(2)}) %collective-permute-start.4) | collective-permute-done | bytes 524320 | tf_op jit(solution)/shard_map/ppermute | solution.py:37
  52.4 1.9 %collective-permute-start.5 = (bf16[4,512,128]{2,1,0:T(8,128)(2,1)S(1)}, bf16[4,512,128]{2,1,0:T(8,128)(2,1)S(1)}, u32[]{:S(2)}, u32[]{:S(2)}) collective-permute-start(bf16[4,512,128]{2,1,0:T(8,128)(2,1)S(1)} %collective-permute-done.4), channel_id=1, source_target_pairs={{0,16},{16,32},{32,48},{48,64},{64,80},{80,96},{96,112},{112,0},{1... | collective-permute-start | bytes 1572872 | tf_op jit(solution)/shard_map/ppermute | solution.py:37
  54.3 4.6 %collective-permute-start.8 = (bf16[4,512,128]{2,1,0:T(8,128)(2,1)S(1)}, bf16[4,512,128]{2,1,0:T(8,128)(2,1)S(1)}, u32[]{:S(2)}, u32[]{:S(2)}) collective-permute-start(bf16[4,512,128]{2,1,0:T(8,128)(2,1)S(1)} %pad_maximum_fusion), channel_id=1, source_target_pairs={{0,112},{16,0},{32,16},{48,32},{64,48},{80,64},{96,80},{112,96},{1... | collective-permute-start | bytes 1572872 | tf_op jit(solution)/shard_map/ppermute | solution.py:40
  58.9 7.5 %collective-permute-done.5 = bf16[4,512,128]{2,1,0:T(8,128)(2,1)S(1)} collective-permute-done((bf16[4,512,128]{2,1,0:T(8,128)(2,1)S(1)}, bf16[4,512,128]{2,1,0:T(8,128)(2,1)S(1)}, u32[]{:S(2)}, u32[]{:S(2)}) %collective-permute-start.5) | collective-permute-done | bytes 524320 | tf_op jit(solution)/shard_map/ppermute | solution.py:37
  66.5 4.9 %collective-permute-start.6 = (bf16[4,512,128]{2,1,0:T(8,128)(2,1)S(1)}, bf16[4,512,128]{2,1,0:T(8,128)(2,1)S(1)}, u32[]{:S(2)}, u32[]{:S(2)}) collective-permute-start(bf16[4,512,128]{2,1,0:T(8,128)(2,1)S(1)} %collective-permute-done.5), channel_id=1, source_target_pairs={{0,16},{16,32},{32,48},{48,64},{64,80},{80,96},{96,112},{112,0},{1... | collective-permute-start | bytes 1572872 | tf_op jit(solution)/shard_map/ppermute | solution.py:37
  71.4 1.9 %collective-permute-start.9 = (bf16[4,512,128]{2,1,0:T(8,128)(2,1)S(1)}, bf16[4,512,128]{2,1,0:T(8,128)(2,1)S(1)}, u32[]{:S(2)}, u32[]{:S(2)}) collective-permute-start(bf16[4,512,128]{2,1,0:T(8,128)(2,1)S(1)} %collective-permute-done.8), channel_id=1, source_target_pairs={{0,112},{16,0},{32,16},{48,32},{64,48},{80,64},{96,80},{112,96},{1... | collective-permute-start | bytes 1572872 | tf_op jit(solution)/shard_map/ppermute | solution.py:40
  73.3 5.5 %collective-permute-done.6 = bf16[4,512,128]{2,1,0:T(8,128)(2,1)S(1)} collective-permute-done((bf16[4,512,128]{2,1,0:T(8,128)(2,1)S(1)}, bf16[4,512,128]{2,1,0:T(8,128)(2,1)S(1)}, u32[]{:S(2)}, u32[]{:S(2)}) %collective-permute-start.6) | collective-permute-done | bytes 524320 | tf_op jit(solution)/shard_map/ppermute | solution.py:37
  78.9 3.8 %collective-permute-start.7 = (bf16[4,512,128]{2,1,0:T(8,128)(2,1)S(1)}, bf16[4,512,128]{2,1,0:T(8,128)(2,1)S(1)}, u32[]{:S(2)}, u32[]{:S(2)}) collective-permute-start(bf16[4,512,128]{2,1,0:T(8,128)(2,1)S(1)} %collective-permute-done.6), channel_id=1, source_target_pairs={{0,16},{16,32},{32,48},{48,64},{64,80},{80,96},{96,112},{112,0},{1... | collective-permute-start | bytes 1572872 | tf_op jit(solution)/shard_map/ppermute | solution.py:37
  82.8 0.6 iota_compare_fusion.6
  83.4 2.7 %collective-permute-start.10 = (bf16[4,512,128]{2,1,0:T(8,128)(2,1)S(1)}, bf16[4,512,128]{2,1,0:T(8,128)(2,1)S(1)}, u32[]{:S(2)}, u32[]{:S(2)}) collective-permute-start(bf16[4,512,128]{2,1,0:T(8,128)(2,1)S(1)} %collective-permute-done.9), channel_id=1, source_target_pairs={{0,112},{16,0},{32,16},{48,32},{64,48},{80,64},{96,80},{112,96},{1... | collective-permute-start | bytes 1572872 | tf_op jit(solution)/shard_map/ppermute | solution.py:40
  86.0 13.9 %collective-permute-done.7 = bf16[4,512,128]{2,1,0:T(8,128)(2,1)S(1)} collective-permute-done((bf16[4,512,128]{2,1,0:T(8,128)(2,1)S(1)}, bf16[4,512,128]{2,1,0:T(8,128)(2,1)S(1)}, u32[]{:S(2)}, u32[]{:S(2)}) %collective-permute-start.7) | collective-permute-done | bytes 524320 | tf_op jit(solution)/shard_map/ppermute | solution.py:37
  100.0 0.8 bitcast_dynamic-update-slice_fusion.7
  100.8 0.8 bitcast_dynamic-update-slice_fusion.6
  101.7 0.8 bitcast_dynamic-update-slice_fusion.5
  102.5 0.8 bitcast_dynamic-update-slice_fusion.4
  103.3 0.8 bitcast_dynamic-update-slice_fusion.3
  104.2 0.8 bitcast_dynamic-update-slice_fusion.2
  105.0 0.8 bitcast_dynamic-update-slice_fusion.1
  105.9 0.5 collective-permute-done.10
  106.4 0.9 bitcast_dynamic-update-slice_fusion
  107.3 13.6 %all-gather.3.cloned.1.call-done = bf16[4352,512]{1,0:T(8,128)(2,1)} async-done(((bf16[136,512]{1,0:T(8,128)(2,1)}), bf16[4352,512]{1,0:T(8,128)(2,1)}) %all-gather.3.cloned.1.call-update) | async-done | bytes 4456464 | tf_op jit(solution)/shard_map/all_gather | solution.py:129
  120.9 1.0 slice_convert_fusion.1
  122.2 3.7 %fusion.13 = f32[64,512]{1,0:T(8,128)S(1)} fusion(bf16[32,136,512]{2,1,0:T(8,128)(2,1)} %bitcast.140, f32[64,32]{0,1:T(8,128)S(1)} %add_exponential_fusion, f32[1,64,1024]{2,1,0:T(8,128)S(1)} %convolution_bitcast_fusion), kind=kOutput, calls=%fused_computation.9 | convolution fusion | flops 268697600 | bytes 4407296 | tf_op jit(solution)/shard_map/vts,se->vte/dot_general | solution.py:77
  126.0 0.4 fusion.80
  126.6 3.1 %fusion.12 = bf16[1,64,8,4,128]{4,1,3,2,0:T(8,128)(2,1)S(1)} fusion(bf16[8,4,512,128]{3,2,1,0:T(8,128)(2,1)} %bitcast_dynamic-update-slice_fusion, f32[64,512]{1,0:T(8,128)S(1)} %get-tuple-element.24, f32[512]{0:T(512)S(1)} %copy-done.11, f32[64]{0:T(128)S(1)} %add_rsqrt_fusion, f32[64]{0:T(128)S(1)} %broadcast_multiply_fusion), kind=kOutput, calls=%fused_computation.7 | convolution fusion | flops 268828672 | bytes 4852224 | tf_op jit(solution)/shard_map/vtr,edrc->vtedc/dot_general | solution.py:137
  129.7 0.2 fusion.22
  129.9 0.2 fusion.21
  130.2 7.0 %all_to_all.10 = bf16[2,4,1,64,512]{4,3,1,2,0:T(8,128)(2,1)S(1)} all-to-all(bf16[2,4,1,64,512]{4,3,1,2,0:T(8,128)(2,1)S(1)} %bitcast.121), channel_id=1, replica_groups=mesh['seq_0'=4,'seq_1'=8,'head_0'=4,'head_1'=2,'var'=2] {'head_1'}, dimensions={0} | all-to-all | bytes 1048576 | tf_op jit(solution)/shard_map/all_to_all | solution.py:147
  137.4 20.2 %all_to_all.11 = bf16[4,1,64,512]{3,2,1,0:T(8,128)(2,1)S(1)} all-to-all(bf16[4,1,64,512]{3,2,1,0:T(8,128)(2,1)S(1)} %bitcast.122), channel_id=1, replica_groups=mesh['seq_0'=4,'seq_1'=8,'head_0'=4,'head_1'=2,'var'=2] {'head_0'}, dimensions={0} | all-to-all | bytes 524288 | tf_op jit(solution)/shard_map/all_to_all | solution.py:149
  157.6 0.6 fusion.32
  (49 shorter events, 1.2 us)
Async XLA Ops:
  6.5 8.0 %copy-start = (bf16[1,2,512]{2,1,0:T(2,128)(2,1)S(1)}, bf16[1,2,512]{2,1,0:T(2,128)(2,1)}, u32[]{:S(2)}) copy-start(bf16[1,2,512]{2,1,0:T(2,128)(2,1)} %param.16) | copy-start | bytes 6148
  6.5 114.4 %all-gather.3.cloned.1.call-start = ((), (), s32[]{:S(2)}) async-start(), calls=%async_computation.2 | async-start | bytes 4595712 | tf_op jit(solution)/shard_map/all_gather | solution.py:129
  8.1 6.2 %collective-permute-start = (bf16[1,3,512]{2,1,0:T(4,128)(2,1)S(1)}, bf16[1,3,512]{2,1,0:T(4,128)(2,1)S(1)}, u32[]{:S(2)}, u32[]{:S(2)}) collective-permute-start(bf16[1,3,512]{2,1,0:T(4,128)(2,1)S(1)} %slice.93), channel_id=1, source_target_pairs={{0,16},{16,32},{32,48},{48,64},{64,80},{80,96},{96,112},{112,128},... | collective-permute-start | bytes 9224 | tf_op jit(solution)/shard_map/ppermute | solution.py:16
  13.5 25.4 %copy-start.8 = (bf16[64,512]{1,0:T(8,128)(2,1)}, bf16[64,512]{1,0:T(8,128)(2,1)S(1)}, u32[]{:S(2)}) copy-start(bf16[64,512]{1,0:T(8,128)(2,1)S(1)} %convolution_convert_fusion.1) | copy-start | bytes 196612
  13.5 89.8 %copy-start.1 = (bf16[512,128]{1,0:T(8,128)(2,1)S(1)}, bf16[512,128]{1,0:T(8,128)(2,1)}, u32[]{:S(2)}) copy-start(bf16[512,128]{1,0:T(8,128)(2,1)} %param.19) | copy-start | bytes 393220
  24.0 8.0 %collective-permute-start.1 = (bf16[512,128]{1,0:T(8,128)(2,1)}, bf16[512,128]{1,0:T(8,128)(2,1)S(1)}, u32[]{:S(2)}, u32[]{:S(2)}) collective-permute-start(bf16[512,128]{1,0:T(8,128)(2,1)} %param.19), channel_id=1, source_target_pairs={{0,128},{128,256},{256,384},{384,0},{1,129},{129,257},{257,385},{3... | collective-permute-start | bytes 393224 | tf_op jit(solution)/shard_map/ppermute | solution.py:37
  28.1 5.9 %collective-permute-start.3 = (bf16[512,128]{1,0:T(8,128)(2,1)}, bf16[512,128]{1,0:T(8,128)(2,1)S(1)}, u32[]{:S(2)}, u32[]{:S(2)}) collective-permute-start(bf16[512,128]{1,0:T(8,128)(2,1)} %param.19), channel_id=1, source_target_pairs={{0,384},{128,0},{256,128},{384,256},{1,385},{129,1},{257,129},{385... | collective-permute-start | bytes 393224 | tf_op jit(solution)/shard_map/ppermute | solution.py:40
  31.9 26.9 %copy-start.2 = (bf16[512,128]{1,0:T(8,128)(2,1)}, bf16[512,128]{1,0:T(8,128)(2,1)S(1)}, u32[]{:S(2)}) copy-start(bf16[512,128]{1,0:T(8,128)(2,1)S(1)} %collective-permute-done.1) | copy-start | bytes 393220
  31.9 6.9 %collective-permute-start.2 = (bf16[512,128]{1,0:T(8,128)(2,1)S(1)}, bf16[512,128]{1,0:T(8,128)(2,1)S(1)}, u32[]{:S(2)}, u32[]{:S(2)}) collective-permute-start(bf16[512,128]{1,0:T(8,128)(2,1)S(1)} %collective-permute-done.1), channel_id=1, source_target_pairs={{0,128},{128,256},{256,384},{384,0},{1,129},{129,257},{257,385},{3... | collective-permute-start | bytes 393224 | tf_op jit(solution)/shard_map/ppermute | solution.py:37
  34.0 24.9 %copy-start.4 = (bf16[512,128]{1,0:T(8,128)(2,1)}, bf16[512,128]{1,0:T(8,128)(2,1)S(1)}, u32[]{:S(2)}) copy-start(bf16[512,128]{1,0:T(8,128)(2,1)S(1)} %collective-permute-done.3) | copy-start | bytes 393220
  38.9 20.1 %copy-start.6 = (bf16[512,128]{1,0:T(8,128)(2,1)}, bf16[512,128]{1,0:T(8,128)(2,1)S(1)}, u32[]{:S(2)}) copy-start(bf16[512,128]{1,0:T(8,128)(2,1)S(1)} %collective-permute-done.2) | copy-start | bytes 393220
  39.9 12.5 %collective-permute-start.4 = (bf16[4,512,128]{2,1,0:T(8,128)(2,1)S(1)}, bf16[4,512,128]{2,1,0:T(8,128)(2,1)S(1)}, u32[]{:S(2)}, u32[]{:S(2)}) collective-permute-start(bf16[4,512,128]{2,1,0:T(8,128)(2,1)S(1)} %pad_maximum_fusion), channel_id=1, source_target_pairs={{0,16},{16,32},{32,48},{48,64},{64,80},{80,96},{96,112},{112,0},{1... | collective-permute-start | bytes 1572872 | tf_op jit(solution)/shard_map/ppermute | solution.py:37
  52.4 14.1 %collective-permute-start.5 = (bf16[4,512,128]{2,1,0:T(8,128)(2,1)S(1)}, bf16[4,512,128]{2,1,0:T(8,128)(2,1)S(1)}, u32[]{:S(2)}, u32[]{:S(2)}) collective-permute-start(bf16[4,512,128]{2,1,0:T(8,128)(2,1)S(1)} %collective-permute-done.4), channel_id=1, source_target_pairs={{0,16},{16,32},{32,48},{48,64},{64,80},{80,96},{96,112},{112,0},{1... | collective-permute-start | bytes 1572872 | tf_op jit(solution)/shard_map/ppermute | solution.py:37
  54.3 17.1 %collective-permute-start.8 = (bf16[4,512,128]{2,1,0:T(8,128)(2,1)S(1)}, bf16[4,512,128]{2,1,0:T(8,128)(2,1)S(1)}, u32[]{:S(2)}, u32[]{:S(2)}) collective-permute-start(bf16[4,512,128]{2,1,0:T(8,128)(2,1)S(1)} %pad_maximum_fusion), channel_id=1, source_target_pairs={{0,112},{16,0},{32,16},{48,32},{64,48},{80,64},{96,80},{112,96},{1... | collective-permute-start | bytes 1572872 | tf_op jit(solution)/shard_map/ppermute | solution.py:40
  66.5 12.4 %collective-permute-start.6 = (bf16[4,512,128]{2,1,0:T(8,128)(2,1)S(1)}, bf16[4,512,128]{2,1,0:T(8,128)(2,1)S(1)}, u32[]{:S(2)}, u32[]{:S(2)}) collective-permute-start(bf16[4,512,128]{2,1,0:T(8,128)(2,1)S(1)} %collective-permute-done.5), channel_id=1, source_target_pairs={{0,16},{16,32},{32,48},{48,64},{64,80},{80,96},{96,112},{112,0},{1... | collective-permute-start | bytes 1572872 | tf_op jit(solution)/shard_map/ppermute | solution.py:37
  71.4 12.0 %collective-permute-start.9 = (bf16[4,512,128]{2,1,0:T(8,128)(2,1)S(1)}, bf16[4,512,128]{2,1,0:T(8,128)(2,1)S(1)}, u32[]{:S(2)}, u32[]{:S(2)}) collective-permute-start(bf16[4,512,128]{2,1,0:T(8,128)(2,1)S(1)} %collective-permute-done.8), channel_id=1, source_target_pairs={{0,112},{16,0},{32,16},{48,32},{64,48},{80,64},{96,80},{112,96},{1... | collective-permute-start | bytes 1572872 | tf_op jit(solution)/shard_map/ppermute | solution.py:40
  78.9 21.1 %collective-permute-start.7 = (bf16[4,512,128]{2,1,0:T(8,128)(2,1)S(1)}, bf16[4,512,128]{2,1,0:T(8,128)(2,1)S(1)}, u32[]{:S(2)}, u32[]{:S(2)}) collective-permute-start(bf16[4,512,128]{2,1,0:T(8,128)(2,1)S(1)} %collective-permute-done.6), channel_id=1, source_target_pairs={{0,16},{16,32},{32,48},{48,64},{64,80},{80,96},{96,112},{112,0},{1... | collective-permute-start | bytes 1572872 | tf_op jit(solution)/shard_map/ppermute | solution.py:37
  82.7 20.6 %copy-start.3 = (bf16[512,128]{1,0:T(8,128)(2,1)S(1)}, bf16[512,128]{1,0:T(8,128)(2,1)}, u32[]{:S(2)}) copy-start(bf16[512,128]{1,0:T(8,128)(2,1)} %copy-done.2) | copy-start | bytes 393220
  82.7 20.6 %copy-start.5 = (bf16[512,128]{1,0:T(8,128)(2,1)S(1)}, bf16[512,128]{1,0:T(8,128)(2,1)}, u32[]{:S(2)}) copy-start(bf16[512,128]{1,0:T(8,128)(2,1)} %copy-done.4) | copy-start | bytes 393220
  82.7 20.6 %copy-start.7 = (bf16[512,128]{1,0:T(8,128)(2,1)S(1)}, bf16[512,128]{1,0:T(8,128)(2,1)}, u32[]{:S(2)}) copy-start(bf16[512,128]{1,0:T(8,128)(2,1)} %copy-done.6) | copy-start | bytes 393220
  83.4 23.0 %collective-permute-start.10 = (bf16[4,512,128]{2,1,0:T(8,128)(2,1)S(1)}, bf16[4,512,128]{2,1,0:T(8,128)(2,1)S(1)}, u32[]{:S(2)}, u32[]{:S(2)}) collective-permute-start(bf16[4,512,128]{2,1,0:T(8,128)(2,1)S(1)} %collective-permute-done.9), channel_id=1, source_target_pairs={{0,112},{16,0},{32,16},{48,32},{64,48},{80,64},{96,80},{112,96},{1... | collective-permute-start | bytes 1572872 | tf_op jit(solution)/shard_map/ppermute | solution.py:40
  100.8 21.2 %copy-start.12 = (pred[32]{0:T(512)(128)(4,1)S(1)}, pred[32]{0:T(512)(128)(4,1)}, u32[]{:S(2)}) copy-start(pred[32]{0:T(512)(128)(4,1)} %iota_compare_fusion.6) | copy-start | bytes 100
  105.0 20.9 %copy-start.9 = (bf16[64,512]{1,0:T(8,128)(2,1)S(1)}, bf16[64,512]{1,0:T(8,128)(2,1)}, u32[]{:S(2)}) copy-start(bf16[64,512]{1,0:T(8,128)(2,1)} %copy-done.8) | copy-start | bytes 196612
  105.9 20.7 %copy-start.11 = (f32[512]{0:T(512)S(1)}, f32[512]{0:T(512)}, u32[]{:S(2)}) copy-start(f32[512]{0:T(512)} %param.18) | copy-start | bytes 6148
  126.6 31.0 %copy-start.10 = (bf16[64,512]{1,0:T(8,128)(2,1)S(1)}, bf16[64,512]{1,0:T(8,128)(2,1)}, u32[]{:S(2)}) copy-start(bf16[64,512]{1,0:T(8,128)(2,1)} %param.12) | copy-start | bytes 196612
Sparse Core Ops, SparseCore 0:
  24.1 96.7 all-gather.2

commit v18 on v17

--- a/solution.py
+++ b/solution.py
@@ -135,19 +135,20 @@
     row_var = jnp.mean(centred * centred, axis=-1, keepdims=True)
     normed = (centred * lax.rsqrt(row_var + 1e-05) * norm_gain).astype(jnp.bfloat16)
     head_terms = jnp.einsum(
-        "vtr,edrc->vtedc", normed, columns_all.reshape(inner_size, outer, head_size, -1),
+        "vtr,edrc->edvtc", normed, columns_all.reshape(inner_size, outer, head_size, -1),
         preferred_element_type=jnp.float32,
     ).astype(jnp.bfloat16)
-    head_terms = jnp.roll(head_terms, lax.axis_index(SEQ[1]) - inner_size // 2, axis=2)
-    head_terms = jnp.roll(head_terms, lax.axis_index(SEQ[0]) - outer // 2, axis=3)
+    head_terms = jnp.roll(head_terms, lax.axis_index(SEQ[1]) - inner_size // 2, axis=0)
+    head_terms = jnp.roll(head_terms, lax.axis_index(SEQ[0]) - outer // 2, axis=1)
     pair, across = HEAD
     pairs = lax.axis_size(pair)
-    head_terms = head_terms.reshape(*normed.shape[:2], pairs, inner_size // pairs, outer, -1)
-    blocks = jnp.transpose(head_terms, (2, 4, 0, 1, 3, 5)).reshape(pairs, outer, *normed.shape[:2], -1)
+    head_terms = head_terms.reshape(pairs, inner_size // pairs, *head_terms.shape[1:])
+    blocks = jnp.transpose(head_terms, (0, 2, 1, 3, 4, 5))
     arrived = lax.all_to_all(blocks, pair, split_axis=0, concat_axis=0, tiled=True)
     pair_sum = jnp.sum(arrived.astype(jnp.float32), axis=0).astype(jnp.bfloat16)
     summed = lax.all_to_all(pair_sum, across, split_axis=0, concat_axis=0, tiled=True)
     summed = jnp.sum(summed.astype(jnp.float32), axis=0)
+    summed = jnp.transpose(summed, (1, 2, 0, 3)).reshape(*normed.shape[:2], -1)
     return (residual_in[None, :, :].astype(jnp.float32) + summed).astype(jnp.bfloat16)
 
 

time: 167 us -> 167 us (level)
  no operation moved by 1% of the time
where the time goes in v18:
time: 167 us; the launch traced here: 165 us
  waiting for transfers between devices  56.8 us (34%)
  starting transfers between devices  35.6 us (21%)
  blocking collectives  27.2 us (16%)
  between operations  18.5 us (11%)
  matrix products  10.8 us (6%)
  other arithmetic  8.62 us (5%)
  local copies, waits for them, and re-layouts  7.55 us (5%)
    ppermute x6, waiting for transfers between devices, ring_pieces(): forward = lax.ppermute(forward, axis, ahead)  42.6 us
    all_to_all x1, blocking collectives, body(): lax.all_to_all(pair_sum, across, split_axis=0, concat_axis=0, tiled=True)  20.2 us
    ppermute x6, starting transfers between devices, ring_pieces(): forward = lax.ppermute(forward, axis, ahead)  19.2 us
    all_gather x1, waiting for transfers between devices, body(): gathered = lax.all_gather(packed, SEQ, axis=0, tiled=False)  13.6 us
    ppermute x4, starting transfers between devices, ring_pieces(): backward = lax.ppermute(backward, axis, behind)  12.4 us
    all_to_all x1, blocking collectives, body(): lax.all_to_all(blocks, pair, split_axis=0, concat_axis=0, tiled=True)  7.05 us
    unnamed x32, local copies, waits for them, and re-layouts  5.05 us
    ppermute x1, starting transfers between devices, from_behind(): lax.ppermute(value, axis, [(source, source + steps) for source in range(i...  4.02 us
  transfers between devices with their start and end apart: 12, of which 8 were waited for; matrix products, arithmetic and copies ran while one was open for 6% of the time, Pallas kernels for 0%

profile of v18, /device:TPU:1, one launch (start us, length us, event | category | flops | bytes accessed | tf_op | source)
XLA Modules:
  0.0 165.1 jit_solution(17205592855579354014)
XLA Ops:
  6.5 0.7 convert_bitcast_fusion
  7.2 0.9 multiply_bitcast_fusion
  8.1 4.0 %collective-permute-start.10 = (bf16[1,3,512]{2,1,0:T(4,128)(2,1)S(1)}, bf16[1,3,512]{2,1,0:T(4,128)(2,1)S(1)}, u32[]{:S(2)}, u32[]{:S(2)}) collective-permute-start(bf16[1,3,512]{2,1,0:T(4,128)(2,1)S(1)} %slice.93), channel_id=1, source_target_pairs={{0,16},{16,32},{32,48},{48,64},{64,80},{80,96},{96,112},{112,128},... | collective-permute-start | bytes 9224 | tf_op jit(solution)/shard_map/ppermute | solution.py:16
  12.2 1.3 convolution_convert_fusion.1
  13.5 0.9 fusion.80
  14.5 0.7 fusion.19
  15.3 0.2 reduce_window_sum.11
  15.6 0.6 slice.86
  20.9 0.6 fusion.79
  21.6 1.5 convolution_bitcast_fusion
  23.3 0.7 pad_maximum_fusion.1
  24.0 4.1 %collective-permute-start = (bf16[512,128]{1,0:T(8,128)(2,1)}, bf16[512,128]{1,0:T(8,128)(2,1)S(1)}, u32[]{:S(2)}, u32[]{:S(2)}) collective-permute-start(bf16[512,128]{1,0:T(8,128)(2,1)} %param.19), channel_id=1, source_target_pairs={{0,128},{128,256},{256,384},{384,0},{1,129},{129,257},{257,385},{3... | collective-permute-start | bytes 393224 | tf_op jit(solution)/shard_map/ppermute | solution.py:37
  28.1 3.2 %collective-permute-start.2 = (bf16[512,128]{1,0:T(8,128)(2,1)}, bf16[512,128]{1,0:T(8,128)(2,1)S(1)}, u32[]{:S(2)}, u32[]{:S(2)}) collective-permute-start(bf16[512,128]{1,0:T(8,128)(2,1)} %param.19), channel_id=1, source_target_pairs={{0,384},{128,0},{256,128},{384,256},{1,385},{129,1},{257,129},{385... | collective-permute-start | bytes 393224 | tf_op jit(solution)/shard_map/ppermute | solution.py:40
  31.3 0.6 collective-permute-done
  31.9 2.1 %collective-permute-start.1 = (bf16[512,128]{1,0:T(8,128)(2,1)S(1)}, bf16[512,128]{1,0:T(8,128)(2,1)S(1)}, u32[]{:S(2)}, u32[]{:S(2)}) collective-permute-start(bf16[512,128]{1,0:T(8,128)(2,1)S(1)} %collective-permute-done), channel_id=1, source_target_pairs={{0,128},{128,256},{256,384},{384,0},{1,129},{129,257},{257,385},{3... | collective-permute-start | bytes 393224 | tf_op jit(solution)/shard_map/ppermute | solution.py:37
  34.1 4.8 %collective-permute-done.1 = bf16[512,128]{1,0:T(8,128)(2,1)S(1)} collective-permute-done((bf16[512,128]{1,0:T(8,128)(2,1)S(1)}, bf16[512,128]{1,0:T(8,128)(2,1)S(1)}, u32[]{:S(2)}, u32[]{:S(2)}) %collective-permute-start.1) | collective-permute-done | bytes 131104 | tf_op jit(solution)/shard_map/ppermute | solution.py:37
  38.9 1.0 pad_maximum_fusion
  39.9 2.4 %collective-permute-start.3 = (bf16[4,512,128]{2,1,0:T(8,128)(2,1)S(1)}, bf16[4,512,128]{2,1,0:T(8,128)(2,1)S(1)}, u32[]{:S(2)}, u32[]{:S(2)}) collective-permute-start(bf16[4,512,128]{2,1,0:T(8,128)(2,1)S(1)} %pad_maximum_fusion), channel_id=1, source_target_pairs={{0,16},{16,32},{32,48},{48,64},{64,80},{80,96},{96,112},{112,0},{1... | collective-permute-start | bytes 1572872 | tf_op jit(solution)/shard_map/ppermute | solution.py:37
  42.3 10.1 %collective-permute-done.3 = bf16[4,512,128]{2,1,0:T(8,128)(2,1)S(1)} collective-permute-done((bf16[4,512,128]{2,1,0:T(8,128)(2,1)S(1)}, bf16[4,512,128]{2,1,0:T(8,128)(2,1)S(1)}, u32[]{:S(2)}, u32[]{:S(2)}) %collective-permute-start.3) | collective-permute-done | bytes 524320 | tf_op jit(solution)/shard_map/ppermute | solution.py:37
  52.4 1.9 %collective-permute-start.4 = (bf16[4,512,128]{2,1,0:T(8,128)(2,1)S(1)}, bf16[4,512,128]{2,1,0:T(8,128)(2,1)S(1)}, u32[]{:S(2)}, u32[]{:S(2)}) collective-permute-start(bf16[4,512,128]{2,1,0:T(8,128)(2,1)S(1)} %collective-permute-done.3), channel_id=1, source_target_pairs={{0,16},{16,32},{32,48},{48,64},{64,80},{80,96},{96,112},{112,0},{1... | collective-permute-start | bytes 1572872 | tf_op jit(solution)/shard_map/ppermute | solution.py:37
  54.3 4.6 %collective-permute-start.7 = (bf16[4,512,128]{2,1,0:T(8,128)(2,1)S(1)}, bf16[4,512,128]{2,1,0:T(8,128)(2,1)S(1)}, u32[]{:S(2)}, u32[]{:S(2)}) collective-permute-start(bf16[4,512,128]{2,1,0:T(8,128)(2,1)S(1)} %pad_maximum_fusion), channel_id=1, source_target_pairs={{0,112},{16,0},{32,16},{48,32},{64,48},{80,64},{96,80},{112,96},{1... | collective-permute-start | bytes 1572872 | tf_op jit(solution)/shard_map/ppermute | solution.py:40
  58.9 7.5 %collective-permute-done.4 = bf16[4,512,128]{2,1,0:T(8,128)(2,1)S(1)} collective-permute-done((bf16[4,512,128]{2,1,0:T(8,128)(2,1)S(1)}, bf16[4,512,128]{2,1,0:T(8,128)(2,1)S(1)}, u32[]{:S(2)}, u32[]{:S(2)}) %collective-permute-start.4) | collective-permute-done | bytes 524320 | tf_op jit(solution)/shard_map/ppermute | solution.py:37
  66.5 4.9 %collective-permute-start.5 = (bf16[4,512,128]{2,1,0:T(8,128)(2,1)S(1)}, bf16[4,512,128]{2,1,0:T(8,128)(2,1)S(1)}, u32[]{:S(2)}, u32[]{:S(2)}) collective-permute-start(bf16[4,512,128]{2,1,0:T(8,128)(2,1)S(1)} %collective-permute-done.4), channel_id=1, source_target_pairs={{0,16},{16,32},{32,48},{48,64},{64,80},{80,96},{96,112},{112,0},{1... | collective-permute-start | bytes 1572872 | tf_op jit(solution)/shard_map/ppermute | solution.py:37
  71.4 1.9 %collective-permute-start.8 = (bf16[4,512,128]{2,1,0:T(8,128)(2,1)S(1)}, bf16[4,512,128]{2,1,0:T(8,128)(2,1)S(1)}, u32[]{:S(2)}, u32[]{:S(2)}) collective-permute-start(bf16[4,512,128]{2,1,0:T(8,128)(2,1)S(1)} %collective-permute-done.7), channel_id=1, source_target_pairs={{0,112},{16,0},{32,16},{48,32},{64,48},{80,64},{96,80},{112,96},{1... | collective-permute-start | bytes 1572872 | tf_op jit(solution)/shard_map/ppermute | solution.py:40
  73.3 5.5 %collective-permute-done.5 = bf16[4,512,128]{2,1,0:T(8,128)(2,1)S(1)} collective-permute-done((bf16[4,512,128]{2,1,0:T(8,128)(2,1)S(1)}, bf16[4,512,128]{2,1,0:T(8,128)(2,1)S(1)}, u32[]{:S(2)}, u32[]{:S(2)}) %collective-permute-start.5) | collective-permute-done | bytes 524320 | tf_op jit(solution)/shard_map/ppermute | solution.py:37
  78.9 3.8 %collective-permute-start.6 = (bf16[4,512,128]{2,1,0:T(8,128)(2,1)S(1)}, bf16[4,512,128]{2,1,0:T(8,128)(2,1)S(1)}, u32[]{:S(2)}, u32[]{:S(2)}) collective-permute-start(bf16[4,512,128]{2,1,0:T(8,128)(2,1)S(1)} %collective-permute-done.5), channel_id=1, source_target_pairs={{0,16},{16,32},{32,48},{48,64},{64,80},{80,96},{96,112},{112,0},{1... | collective-permute-start | bytes 1572872 | tf_op jit(solution)/shard_map/ppermute | solution.py:37
  82.8 0.6 iota_compare_fusion.6
  83.4 2.7 %collective-permute-start.9 = (bf16[4,512,128]{2,1,0:T(8,128)(2,1)S(1)}, bf16[4,512,128]{2,1,0:T(8,128)(2,1)S(1)}, u32[]{:S(2)}, u32[]{:S(2)}) collective-permute-start(bf16[4,512,128]{2,1,0:T(8,128)(2,1)S(1)} %collective-permute-done.8), channel_id=1, source_target_pairs={{0,112},{16,0},{32,16},{48,32},{64,48},{80,64},{96,80},{112,96},{1... | collective-permute-start | bytes 1572872 | tf_op jit(solution)/shard_map/ppermute | solution.py:40
  86.0 13.9 %collective-permute-done.6 = bf16[4,512,128]{2,1,0:T(8,128)(2,1)S(1)} collective-permute-done((bf16[4,512,128]{2,1,0:T(8,128)(2,1)S(1)}, bf16[4,512,128]{2,1,0:T(8,128)(2,1)S(1)}, u32[]{:S(2)}, u32[]{:S(2)}) %collective-permute-start.6) | collective-permute-done | bytes 524320 | tf_op jit(solution)/shard_map/ppermute | solution.py:37
  100.0 0.8 bitcast_dynamic-update-slice_fusion.7
  100.8 0.8 bitcast_dynamic-update-slice_fusion.6
  101.7 0.8 bitcast_dynamic-update-slice_fusion.5
  102.5 0.8 bitcast_dynamic-update-slice_fusion.4
  103.3 0.8 bitcast_dynamic-update-slice_fusion.3
  104.2 0.8 bitcast_dynamic-update-slice_fusion.2
  105.0 0.8 bitcast_dynamic-update-slice_fusion.1
  105.9 0.5 collective-permute-done.9
  106.4 0.9 bitcast_dynamic-update-slice_fusion
  107.3 13.6 %all-gather.3.cloned.1.call-done = bf16[4352,512]{1,0:T(8,128)(2,1)} async-done(((bf16[136,512]{1,0:T(8,128)(2,1)}), bf16[4352,512]{1,0:T(8,128)(2,1)}) %all-gather.3.cloned.1.call-update) | async-done | bytes 4456464 | tf_op jit(solution)/shard_map/all_gather | solution.py:129
  120.9 1.0 slice_convert_fusion.1
  122.2 3.7 %fusion.13 = f32[64,512]{1,0:T(8,128)S(1)} fusion(bf16[32,136,512]{2,1,0:T(8,128)(2,1)} %bitcast.149, f32[64,32]{0,1:T(8,128)S(1)} %add_exponential_fusion, f32[1,64,1024]{2,1,0:T(8,128)S(1)} %convolution_bitcast_fusion), kind=kOutput, calls=%fused_computation.9 | convolution fusion | flops 268697600 | bytes 4407296 | tf_op jit(solution)/shard_map/vts,se->vte/dot_general | solution.py:77
  126.0 0.4 fusion.81
  126.6 3.1 %fusion.12 = bf16[8,4,1,64,128]{4,3,1,0,2:T(8,128)(2,1)S(1)} fusion(bf16[8,4,512,128]{3,2,1,0:T(8,128)(2,1)} %bitcast_dynamic-update-slice_fusion, f32[64,512]{1,0:T(8,128)S(1)} %get-tuple-element.24, f32[512]{0:T(512)S(1)} %copy-done.11, f32[64]{0:T(128)S(1)} %add_rsqrt_fusion, f32[64]{0:T(128)S(1)} %broadcast_multiply_fusion), kind=kOutput, calls=%fused_computation.7 | convolution fusion | flops 268828672 | bytes 4852224 | tf_op jit(solution)/shard_map/vtr,edrc->edvtc/dot_general | solution.py:137
  129.7 0.2 fusion.22
  129.9 0.2 fusion.21
  130.1 7.0 %all_to_all.10 = bf16[2,4,4,1,64,128]{5,4,1,2,3,0:T(8,128)(2,1)S(1)} all-to-all(bf16[2,4,4,1,64,128]{5,4,1,2,3,0:T(8,128)(2,1)S(1)} %bitcast.128), channel_id=1, replica_groups=mesh['seq_0'=4,'seq_1'=8,'head_0'=4,'head_1'=2,'var'=2] {'head_1'}, dimensions={0} | all-to-all | bytes 1048576 | tf_op jit(solution)/shard_map/all_to_all | solution.py:147
  137.3 20.2 %all_to_all.11 = bf16[4,4,1,64,128]{4,3,1,2,0:T(8,128)(2,1)S(1)} all-to-all(bf16[4,4,1,64,128]{4,3,1,2,0:T(8,128)(2,1)S(1)} %copy.18), channel_id=1, replica_groups=mesh['seq_0'=4,'seq_1'=8,'head_0'=4,'head_1'=2,'var'=2] {'head_0'}, dimensions={0} | all-to-all | bytes 524288 | tf_op jit(solution)/shard_map/all_to_all | solution.py:149
  157.6 0.6 fusion.33
  (50 shorter events, 1.2 us)
Async XLA Ops:
  6.5 8.0 %copy-start = (bf16[1,2,512]{2,1,0:T(2,128)(2,1)S(1)}, bf16[1,2,512]{2,1,0:T(2,128)(2,1)}, u32[]{:S(2)}) copy-start(bf16[1,2,512]{2,1,0:T(2,128)(2,1)} %param.16) | copy-start | bytes 6148
  6.5 114.4 %all-gather.3.cloned.1.call-start = ((), (), s32[]{:S(2)}) async-start(), calls=%async_computation.2 | async-start | bytes 4595712 | tf_op jit(solution)/shard_map/all_gather | solution.py:129
  8.1 6.2 %collective-permute-start.10 = (bf16[1,3,512]{2,1,0:T(4,128)(2,1)S(1)}, bf16[1,3,512]{2,1,0:T(4,128)(2,1)S(1)}, u32[]{:S(2)}, u32[]{:S(2)}) collective-permute-start(bf16[1,3,512]{2,1,0:T(4,128)(2,1)S(1)} %slice.93), channel_id=1, source_target_pairs={{0,16},{16,32},{32,48},{48,64},{64,80},{80,96},{96,112},{112,128},... | collective-permute-start | bytes 9224 | tf_op jit(solution)/shard_map/ppermute | solution.py:16
  13.5 25.4 %copy-start.8 = (bf16[64,512]{1,0:T(8,128)(2,1)}, bf16[64,512]{1,0:T(8,128)(2,1)S(1)}, u32[]{:S(2)}) copy-start(bf16[64,512]{1,0:T(8,128)(2,1)S(1)} %convolution_convert_fusion.1) | copy-start | bytes 196612
  13.5 89.8 %copy-start.1 = (bf16[512,128]{1,0:T(8,128)(2,1)S(1)}, bf16[512,128]{1,0:T(8,128)(2,1)}, u32[]{:S(2)}) copy-start(bf16[512,128]{1,0:T(8,128)(2,1)} %param.19) | copy-start | bytes 393220
  24.0 8.0 %collective-permute-start = (bf16[512,128]{1,0:T(8,128)(2,1)}, bf16[512,128]{1,0:T(8,128)(2,1)S(1)}, u32[]{:S(2)}, u32[]{:S(2)}) collective-permute-start(bf16[512,128]{1,0:T(8,128)(2,1)} %param.19), channel_id=1, source_target_pairs={{0,128},{128,256},{256,384},{384,0},{1,129},{129,257},{257,385},{3... | collective-permute-start | bytes 393224 | tf_op jit(solution)/shard_map/ppermute | solution.py:37
  28.1 5.9 %collective-permute-start.2 = (bf16[512,128]{1,0:T(8,128)(2,1)}, bf16[512,128]{1,0:T(8,128)(2,1)S(1)}, u32[]{:S(2)}, u32[]{:S(2)}) collective-permute-start(bf16[512,128]{1,0:T(8,128)(2,1)} %param.19), channel_id=1, source_target_pairs={{0,384},{128,0},{256,128},{384,256},{1,385},{129,1},{257,129},{385... | collective-permute-start | bytes 393224 | tf_op jit(solution)/shard_map/ppermute | solution.py:40
  31.9 26.9 %copy-start.2 = (bf16[512,128]{1,0:T(8,128)(2,1)}, bf16[512,128]{1,0:T(8,128)(2,1)S(1)}, u32[]{:S(2)}) copy-start(bf16[512,128]{1,0:T(8,128)(2,1)S(1)} %collective-permute-done) | copy-start | bytes 393220
  31.9 6.9 %collective-permute-start.1 = (bf16[512,128]{1,0:T(8,128)(2,1)S(1)}, bf16[512,128]{1,0:T(8,128)(2,1)S(1)}, u32[]{:S(2)}, u32[]{:S(2)}) collective-permute-start(bf16[512,128]{1,0:T(8,128)(2,1)S(1)} %collective-permute-done), channel_id=1, source_target_pairs={{0,128},{128,256},{256,384},{384,0},{1,129},{129,257},{257,385},{3... | collective-permute-start | bytes 393224 | tf_op jit(solution)/shard_map/ppermute | solution.py:37
  34.0 24.9 %copy-start.4 = (bf16[512,128]{1,0:T(8,128)(2,1)}, bf16[512,128]{1,0:T(8,128)(2,1)S(1)}, u32[]{:S(2)}) copy-start(bf16[512,128]{1,0:T(8,128)(2,1)S(1)} %collective-permute-done.2) | copy-start | bytes 393220
  38.9 20.1 %copy-start.6 = (bf16[512,128]{1,0:T(8,128)(2,1)}, bf16[512,128]{1,0:T(8,128)(2,1)S(1)}, u32[]{:S(2)}) copy-start(bf16[512,128]{1,0:T(8,128)(2,1)S(1)} %collective-permute-done.1) | copy-start | bytes 393220
  39.9 12.5 %collective-permute-start.3 = (bf16[4,512,128]{2,1,0:T(8,128)(2,1)S(1)}, bf16[4,512,128]{2,1,0:T(8,128)(2,1)S(1)}, u32[]{:S(2)}, u32[]{:S(2)}) collective-permute-start(bf16[4,512,128]{2,1,0:T(8,128)(2,1)S(1)} %pad_maximum_fusion), channel_id=1, source_target_pairs={{0,16},{16,32},{32,48},{48,64},{64,80},{80,96},{96,112},{112,0},{1... | collective-permute-start | bytes 1572872 | tf_op jit(solution)/shard_map/ppermute | solution.py:37
  52.4 14.1 %collective-permute-start.4 = (bf16[4,512,128]{2,1,0:T(8,128)(2,1)S(1)}, bf16[4,512,128]{2,1,0:T(8,128)(2,1)S(1)}, u32[]{:S(2)}, u32[]{:S(2)}) collective-permute-start(bf16[4,512,128]{2,1,0:T(8,128)(2,1)S(1)} %collective-permute-done.3), channel_id=1, source_target_pairs={{0,16},{16,32},{32,48},{48,64},{64,80},{80,96},{96,112},{112,0},{1... | collective-permute-start | bytes 1572872 | tf_op jit(solution)/shard_map/ppermute | solution.py:37
  54.3 17.1 %collective-permute-start.7 = (bf16[4,512,128]{2,1,0:T(8,128)(2,1)S(1)}, bf16[4,512,128]{2,1,0:T(8,128)(2,1)S(1)}, u32[]{:S(2)}, u32[]{:S(2)}) collective-permute-start(bf16[4,512,128]{2,1,0:T(8,128)(2,1)S(1)} %pad_maximum_fusion), channel_id=1, source_target_pairs={{0,112},{16,0},{32,16},{48,32},{64,48},{80,64},{96,80},{112,96},{1... | collective-permute-start | bytes 1572872 | tf_op jit(solution)/shard_map/ppermute | solution.py:40
  66.5 12.4 %collective-permute-start.5 = (bf16[4,512,128]{2,1,0:T(8,128)(2,1)S(1)}, bf16[4,512,128]{2,1,0:T(8,128)(2,1)S(1)}, u32[]{:S(2)}, u32[]{:S(2)}) collective-permute-start(bf16[4,512,128]{2,1,0:T(8,128)(2,1)S(1)} %collective-permute-done.4), channel_id=1, source_target_pairs={{0,16},{16,32},{32,48},{48,64},{64,80},{80,96},{96,112},{112,0},{1... | collective-permute-start | bytes 1572872 | tf_op jit(solution)/shard_map/ppermute | solution.py:37
  71.4 12.0 %collective-permute-start.8 = (bf16[4,512,128]{2,1,0:T(8,128)(2,1)S(1)}, bf16[4,512,128]{2,1,0:T(8,128)(2,1)S(1)}, u32[]{:S(2)}, u32[]{:S(2)}) collective-permute-start(bf16[4,512,128]{2,1,0:T(8,128)(2,1)S(1)} %collective-permute-done.7), channel_id=1, source_target_pairs={{0,112},{16,0},{32,16},{48,32},{64,48},{80,64},{96,80},{112,96},{1... | collective-permute-start | bytes 1572872 | tf_op jit(solution)/shard_map/ppermute | solution.py:40
  78.9 21.1 %collective-permute-start.6 = (bf16[4,512,128]{2,1,0:T(8,128)(2,1)S(1)}, bf16[4,512,128]{2,1,0:T(8,128)(2,1)S(1)}, u32[]{:S(2)}, u32[]{:S(2)}) collective-permute-start(bf16[4,512,128]{2,1,0:T(8,128)(2,1)S(1)} %collective-permute-done.5), channel_id=1, source_target_pairs={{0,16},{16,32},{32,48},{48,64},{64,80},{80,96},{96,112},{112,0},{1... | collective-permute-start | bytes 1572872 | tf_op jit(solution)/shard_map/ppermute | solution.py:37
  82.7 20.6 %copy-start.3 = (bf16[512,128]{1,0:T(8,128)(2,1)S(1)}, bf16[512,128]{1,0:T(8,128)(2,1)}, u32[]{:S(2)}) copy-start(bf16[512,128]{1,0:T(8,128)(2,1)} %copy-done.2) | copy-start | bytes 393220
  82.7 20.6 %copy-start.5 = (bf16[512,128]{1,0:T(8,128)(2,1)S(1)}, bf16[512,128]{1,0:T(8,128)(2,1)}, u32[]{:S(2)}) copy-start(bf16[512,128]{1,0:T(8,128)(2,1)} %copy-done.4) | copy-start | bytes 393220
  82.7 20.6 %copy-start.7 = (bf16[512,128]{1,0:T(8,128)(2,1)S(1)}, bf16[512,128]{1,0:T(8,128)(2,1)}, u32[]{:S(2)}) copy-start(bf16[512,128]{1,0:T(8,128)(2,1)} %copy-done.6) | copy-start | bytes 393220
  83.4 23.0 %collective-permute-start.9 = (bf16[4,512,128]{2,1,0:T(8,128)(2,1)S(1)}, bf16[4,512,128]{2,1,0:T(8,128)(2,1)S(1)}, u32[]{:S(2)}, u32[]{:S(2)}) collective-permute-start(bf16[4,512,128]{2,1,0:T(8,128)(2,1)S(1)} %collective-permute-done.8), channel_id=1, source_target_pairs={{0,112},{16,0},{32,16},{48,32},{64,48},{80,64},{96,80},{112,96},{1... | collective-permute-start | bytes 1572872 | tf_op jit(solution)/shard_map/ppermute | solution.py:40
  100.8 21.2 %copy-start.12 = (pred[32]{0:T(512)(128)(4,1)S(1)}, pred[32]{0:T(512)(128)(4,1)}, u32[]{:S(2)}) copy-start(pred[32]{0:T(512)(128)(4,1)} %iota_compare_fusion.6) | copy-start | bytes 100
  105.0 20.9 %copy-start.9 = (bf16[64,512]{1,0:T(8,128)(2,1)S(1)}, bf16[64,512]{1,0:T(8,128)(2,1)}, u32[]{:S(2)}) copy-start(bf16[64,512]{1,0:T(8,128)(2,1)} %copy-done.8) | copy-start | bytes 196612
  105.9 20.7 %copy-start.11 = (f32[512]{0:T(512)S(1)}, f32[512]{0:T(512)}, u32[]{:S(2)}) copy-start(f32[512]{0:T(512)} %param.18) | copy-start | bytes 6148
  126.6 31.1 %copy-start.10 = (bf16[64,512]{1,0:T(8,128)(2,1)S(1)}, bf16[64,512]{1,0:T(8,128)(2,1)}, u32[]{:S(2)}) copy-start(bf16[64,512]{1,0:T(8,128)(2,1)} %param.12) | copy-start | bytes 196612
Sparse Core Ops, SparseCore 0:
  24.1 96.7 all-gather.2
